TPU v7x, 32 devices: a whole 2x2x4 slice. The times are simulated.
32 devices in a mesh: rep: 4 (over z), fsdp: 4 (over x, core), ctx: 2 (over y).
Axes of the slice: x: 2, y: 2, z: 4, core: 2. Of those that a mesh axis runs over, the one named last changes fastest.
Arguments:
- tokens: bfloat16 [16, 1024, 1024], P(('rep', 'fsdp'), 'ctx'), may hold values from -6 to 6
- initial_layer_values: bfloat16 [16, 1024, 1024], P(('rep', 'fsdp'), 'ctx'), may hold values from -6 to 6
- cotangent: bfloat16 [16, 1024, 1024], P(('rep', 'fsdp'), 'ctx'), may hold values from -6 to 6
- lengths: int32 [16], P(('rep', 'fsdp')), may hold values from 256 to 1024, as said below
- w_query: bfloat16 [1024, 1024], P(('fsdp', 'ctx')), may hold values from -0.1875 to 0.1875
- w_key: bfloat16 [1024, 1024], P(('fsdp', 'ctx')), may hold values from -0.1875 to 0.1875
- w_value: bfloat16 [1024, 1024], P(('fsdp', 'ctx')), may hold values from -0.1875 to 0.1875
- w_out: bfloat16 [1024, 1024], P(('fsdp', 'ctx')), may hold values from -1.5 to 1.5
- w_gate: bfloat16 [1024, 2816], P(('fsdp', 'ctx')), may hold values from -0.1875 to 0.1875
- w_up: bfloat16 [1024, 2816], P(('fsdp', 'ctx')), may hold values from -0.1875 to 0.1875
- w_down: bfloat16 [2816, 1024], P(('fsdp', 'ctx')), may hold values from -0.109375 to 0.109375
- gain_attn: bfloat16 [1024], P(('fsdp', 'ctx')), may hold values from 0.099609375 to 1.8984375
- gain_mlp: bfloat16 [1024], P(('fsdp', 'ctx')), may hold values from 0.099609375 to 1.8984375
Outputs:
- output: bfloat16 [16, 1024, 1024], P(('rep', 'fsdp'), 'ctx')
- d_tokens: float32 [16, 1024, 1024], P(('rep', 'fsdp'), 'ctx')
- d_first: float32 [16, 1024, 1024], P(('rep', 'fsdp'), 'ctx')
- grad_query: float32 [1024, 1024], P(('fsdp', 'ctx'))
- grad_key: float32 [1024, 1024], P(('fsdp', 'ctx'))
- grad_value: float32 [1024, 1024], P(('fsdp', 'ctx'))
- grad_out: float32 [1024, 1024], P(('fsdp', 'ctx'))
- grad_gate: float32 [1024, 2816], P(('fsdp', 'ctx'))
- grad_up: float32 [1024, 2816], P(('fsdp', 'ctx'))
- grad_down: float32 [2816, 1024], P(('fsdp', 'ctx'))
- grad_gain_attn: float32 [1024], P(('fsdp', 'ctx'))
- grad_gain_mlp: float32 [1024], P(('fsdp', 'ctx'))
Inputs may be any that keep to these rules, and one draw needn't show every extreme that they name: Slot s holds one sequence at positions below lengths[s]; the rest of the slot is padding. Some slot is full and some slot holds a quarter of 1024.
All inputs are finite; a program needn't handle non-finite values.
Results may differ from a plain program's by a relative error of at most 0.019.
Values may be sent and summed in bfloat16 or wider, within the bound.
No kernel may reach another device: no remote copies, remote signals or barrier semaphores. Data moves between devices by JAX's collectives and lax.ppermute only.
A program may use at most 320 MiB of HBM per device.

v0:
```python
import jax
import jax.numpy as jnp
from jax import lax
from jax.sharding import PartitionSpec as P

HEADS = 16
HEAD_DIM = 64


EPS = 1e-06
NEG = -1e30
THETA = 10000.0
SCORE_CAP = 4194304


def rotate(field, positions, direction):
    head_width = field.shape[-1]
    half_width = head_width // 2
    frequency = THETA ** (-(jnp.arange(half_width, dtype=jnp.float32) * 2.0) / head_width)
    angles = positions.astype(jnp.float32)[:, None] * frequency[None, :]
    cosine = jnp.cos(angles)[:, None, :]
    sine_part = direction * jnp.sin(angles)[:, None, :]
    former = field[..., :half_width]
    latter = field[..., half_width:]
    return jnp.concatenate(
        [former * cosine - latter * sine_part, latter * cosine + former * sine_part], axis=-1
    )


def normalize(values, gain):
    inverse = lax.rsqrt(jnp.mean(values * values, axis=-1, keepdims=True) + EPS)
    return (values * inverse * gain, inverse)


def normalize_back(values, inverse, gain, upstream):
    unit_rows = values * inverse
    scaled = upstream * gain
    grad_gain = jnp.sum(upstream * unit_rows, axis=(0, 1))
    grad_values = inverse * (
        scaled - unit_rows * jnp.mean(scaled * unit_rows, axis=-1, keepdims=True)
    )
    return (grad_values, grad_gain)


def head_groups(n_slots, q_len, n_heads, k_len):
    q_block = min(q_len, 512)
    per_group = max(1, min(n_heads, SCORE_CAP // (n_slots * q_block * k_len)))
    while n_heads % per_group:
        per_group = per_group - 1
    return (q_block, per_group)


def split_heads(packed, n_groups):
    n_slots, length, n_heads, head_width = packed.shape
    return jnp.moveaxis(
        packed.reshape(n_slots, length, n_groups, n_heads // n_groups, head_width), 2, 0
    )


def join_heads(grouped):
    n_groups, n_slots, length, per_group, head_width = grouped.shape
    return jnp.moveaxis(grouped, 0, 2).reshape(n_slots, length, n_groups * per_group, head_width)


def score_block(q_rows, k_rows, q_pos, lengths):
    k_pos = jnp.arange(k_rows.shape[1])
    products = jnp.einsum(
        "sqhe,skhe->shqk", q_rows, k_rows, preferred_element_type=jnp.float32
    ) * q_rows.shape[-1] ** (-0.5)
    causal = k_pos[None, None, None, :] <= q_pos[None, None, :, None]
    filled = k_pos[None, None, None, :] < lengths[:, None, None, None]
    return jnp.where(causal & filled, products, NEG)


def attend_forward(queries, keys, values, q_pos, lengths):
    n_slots, q_len, n_heads, head_width = queries.shape
    q_block, per_group = head_groups(n_slots, q_len, n_heads, keys.shape[1])
    n_groups = n_heads // per_group
    n_blocks = q_len // q_block
    pos_blocks = q_pos.reshape(n_blocks, q_block)

    def one_group(packed):
        q_group, k_group, v_group = packed
        q_blocks = jnp.moveaxis(
            q_group.reshape(n_slots, n_blocks, q_block, per_group, head_width), 1, 0
        )

        def one_block(streams):
            q_rows, pos_rows = streams
            scores = score_block(q_rows, k_group, pos_rows, lengths)
            highest = jnp.max(scores, axis=-1, keepdims=True)
            exponent = jnp.exp(scores - highest)
            totals = jnp.sum(exponent, axis=-1, keepdims=True)
            probabilities = (exponent / totals).astype(jnp.bfloat16)
            mixture = jnp.einsum(
                "shqk,skhe->sqhe", probabilities, v_group, preferred_element_type=jnp.float32
            )
            return (mixture, (highest + jnp.log(totals))[..., 0])

        mixture, log_sums = lax.map(one_block, (q_blocks, pos_blocks))
        return (
            jnp.moveaxis(mixture, 0, 1).reshape(n_slots, q_len, per_group, head_width),
            log_sums,
        )

    grouped = (
        split_heads(queries, n_groups),
        split_heads(keys, n_groups),
        split_heads(values, n_groups),
    )
    mixture, log_sums = lax.map(one_group, grouped)
    return (join_heads(mixture), log_sums)


def attend_backward(queries, keys, values, upstream, row_dots, log_sums, q_pos, lengths):
    n_slots, q_len, n_heads, head_width = queries.shape
    q_block, per_group = head_groups(n_slots, q_len, n_heads, keys.shape[1])
    n_groups = n_heads // per_group
    n_blocks = q_len // q_block
    score_scale = head_width ** (-0.5)
    pos_blocks = q_pos.reshape(n_blocks, q_block)
    dot_groups = jnp.moveaxis(row_dots.reshape(n_slots, q_len, n_groups, per_group), 2, 0)

    def blocks_of(grouped):
        return jnp.moveaxis(grouped.reshape((n_slots, n_blocks, q_block) + grouped.shape[2:]), 1, 0)

    def one_group(packed):
        q_group, k_group, v_group, g_group, d_group, l_group = packed

        def one_block(running, streams):
            k_grad, v_grad = running
            q_rows, g_rows, d_rows, l_rows, pos_rows = streams
            scores = score_block(q_rows, k_group, pos_rows, lengths)
            probabilities = jnp.exp(scores - l_rows[..., None])
            v_grad = v_grad + jnp.einsum(
                "shqk,sqhe->skhe",
                probabilities.astype(jnp.bfloat16),
                g_rows,
                preferred_element_type=jnp.float32,
            )
            p_grad = jnp.einsum(
                "sqhe,skhe->shqk", g_rows, v_group, preferred_element_type=jnp.float32
            )
            s_grad = (probabilities * (p_grad - jnp.moveaxis(d_rows, 2, 1)[..., None])).astype(
                jnp.bfloat16
            )
            q_grad = (
                jnp.einsum("shqk,skhe->sqhe", s_grad, k_group, preferred_element_type=jnp.float32)
                * score_scale
            )
            k_grad = (
                k_grad
                + jnp.einsum("shqk,sqhe->skhe", s_grad, q_rows, preferred_element_type=jnp.float32)
                * score_scale
            )
            return ((k_grad, v_grad), q_grad)

        empty_grads = jnp.zeros(k_group.shape, jnp.float32)
        streams = (blocks_of(q_group), blocks_of(g_group), blocks_of(d_group), l_group, pos_blocks)
        (k_grad, v_grad), q_grads = lax.scan(one_block, (empty_grads, empty_grads), streams)
        return (
            jnp.moveaxis(q_grads, 0, 1).reshape(n_slots, q_len, per_group, head_width),
            k_grad,
            v_grad,
        )

    grouped = (
        split_heads(queries, n_groups),
        split_heads(keys, n_groups),
        split_heads(values, n_groups),
        split_heads(upstream, n_groups),
        dot_groups,
        log_sums,
    )
    q_grads, k_grads, v_grads = lax.map(one_group, grouped)
    return (join_heads(q_grads), join_heads(k_grads), join_heads(v_grads))


def shards(
    tokens,
    initial_layer_values,
    cotangent,
    lengths,
    w_query,
    w_key,
    w_value,
    w_out,
    w_gate,
    w_up,
    w_down,
    gain_attn,
    gain_mlp,
):
    n_slots, slot_rows, model_width = tokens.shape
    (
        full_query,
        full_key,
        full_value,
        full_out,
        full_gate,
        full_up,
        full_down,
        full_gain_attn,
        full_gain_mlp,
    ) = (
        lax.all_gather(w_query, ("fsdp", "ctx"), axis=0, tiled=True),
        lax.all_gather(w_key, ("fsdp", "ctx"), axis=0, tiled=True),
        lax.all_gather(w_value, ("fsdp", "ctx"), axis=0, tiled=True),
        lax.all_gather(w_out, ("fsdp", "ctx"), axis=0, tiled=True),
        lax.all_gather(w_gate, ("fsdp", "ctx"), axis=0, tiled=True),
        lax.all_gather(w_up, ("fsdp", "ctx"), axis=0, tiled=True),
        lax.all_gather(w_down, ("fsdp", "ctx"), axis=0, tiled=True),
        lax.all_gather(gain_attn, ("fsdp", "ctx"), axis=0, tiled=True),
        lax.all_gather(gain_mlp, ("fsdp", "ctx"), axis=0, tiled=True),
    )
    q_pos = lax.axis_index("ctx") * slot_rows + jnp.arange(slot_rows)
    live_rows = q_pos[None, :] < lengths[:, None]
    head_shape = (n_slots, slot_rows, HEADS, HEAD_DIM)
    inputs = tokens.astype(jnp.float32)
    attn_scale = full_gain_attn.astype(jnp.float32)
    mlp_scale = full_gain_mlp.astype(jnp.float32)
    normed, inv_attn = normalize(inputs, attn_scale)
    normed_low = normed.astype(jnp.bfloat16)
    q_pre = jnp.einsum("srd,de->sre", normed_low, full_query, preferred_element_type=jnp.float32)
    k_pre = jnp.einsum("srd,de->sre", normed_low, full_key, preferred_element_type=jnp.float32)
    v_pre = jnp.einsum("srd,de->sre", normed_low, full_value, preferred_element_type=jnp.float32)
    queries = rotate(q_pre.reshape(head_shape), q_pos, 1.0).astype(jnp.bfloat16)
    keys = rotate(k_pre.reshape(head_shape), q_pos, 1.0).astype(jnp.bfloat16)
    values = (
        (0.5 * v_pre + 0.5 * initial_layer_values.astype(jnp.float32))
        .astype(jnp.bfloat16)
        .reshape(head_shape)
    )
    slot_k, slot_v = (
        lax.all_gather(keys, "ctx", axis=1, tiled=True),
        lax.all_gather(values, "ctx", axis=1, tiled=True),
    )
    attn_raw, attn_lse = attend_forward(queries, slot_k, slot_v, q_pos, lengths)
    attended = attn_raw.astype(jnp.bfloat16)
    att_flat = attended.reshape(n_slots, slot_rows, model_width)
    branch = jnp.einsum("sre,ed->srd", att_flat, full_out, preferred_element_type=jnp.float32)
    residual = inputs + branch
    normed_mlp, inv_mlp = normalize(residual, mlp_scale)
    mlp_low = normed_mlp.astype(jnp.bfloat16)
    gate_proj = jnp.einsum("srd,df->srf", mlp_low, full_gate, preferred_element_type=jnp.float32)
    up_proj = jnp.einsum("srd,df->srf", mlp_low, full_up, preferred_element_type=jnp.float32)
    sigmoid_gate = jax.nn.sigmoid(gate_proj)
    hidden = (gate_proj * sigmoid_gate * up_proj).astype(jnp.bfloat16)
    final = residual + jnp.einsum(
        "srf,fd->srd", hidden, full_down, preferred_element_type=jnp.float32
    )
    output = jnp.where(live_rows[..., None], final, 0.0).astype(jnp.bfloat16)
    (
        full_query,
        full_key,
        full_value,
        full_out,
        full_gate,
        full_up,
        full_down,
        full_gain_attn,
        full_gain_mlp,
    ) = (
        lax.all_gather(w_query, ("fsdp", "ctx"), axis=0, tiled=True),
        lax.all_gather(w_key, ("fsdp", "ctx"), axis=0, tiled=True),
        lax.all_gather(w_value, ("fsdp", "ctx"), axis=0, tiled=True),
        lax.all_gather(w_out, ("fsdp", "ctx"), axis=0, tiled=True),
        lax.all_gather(w_gate, ("fsdp", "ctx"), axis=0, tiled=True),
        lax.all_gather(w_up, ("fsdp", "ctx"), axis=0, tiled=True),
        lax.all_gather(w_down, ("fsdp", "ctx"), axis=0, tiled=True),
        lax.all_gather(gain_attn, ("fsdp", "ctx"), axis=0, tiled=True),
        lax.all_gather(gain_mlp, ("fsdp", "ctx"), axis=0, tiled=True),
    )
    output_gradient = jnp.where(live_rows[..., None], cotangent.astype(jnp.float32), 0.0)
    g_low = output_gradient.astype(jnp.bfloat16)
    grad_down = jnp.einsum("srf,srd->fd", hidden, g_low, preferred_element_type=jnp.float32)
    g_hidden = jnp.einsum("srd,fd->srf", g_low, full_down, preferred_element_type=jnp.float32)
    gate_gradient = (
        g_hidden * up_proj * sigmoid_gate * (1.0 + gate_proj * (1.0 - sigmoid_gate))
    ).astype(jnp.bfloat16)
    up_gradient = (g_hidden * gate_proj * sigmoid_gate).astype(jnp.bfloat16)
    grad_gate = jnp.einsum(
        "srd,srf->df", mlp_low, gate_gradient, preferred_element_type=jnp.float32
    )
    grad_up = jnp.einsum("srd,srf->df", mlp_low, up_gradient, preferred_element_type=jnp.float32)
    g_normed_mlp = jnp.einsum(
        "srf,df->srd", gate_gradient, full_gate, preferred_element_type=jnp.float32
    ) + jnp.einsum("srf,df->srd", up_gradient, full_up, preferred_element_type=jnp.float32)
    g_mlp_in, grad_gain_mlp = normalize_back(residual, inv_mlp, mlp_scale, g_normed_mlp)
    g_residual = output_gradient + g_mlp_in
    g_branch = g_residual.astype(jnp.bfloat16)
    grad_out = jnp.einsum("sre,srd->ed", att_flat, g_branch, preferred_element_type=jnp.float32)
    g_attended = (
        jnp.einsum("srd,ed->sre", g_branch, full_out, preferred_element_type=jnp.float32)
        .astype(jnp.bfloat16)
        .reshape(head_shape)
    )
    row_dots = jnp.sum(g_attended.astype(jnp.float32) * attended.astype(jnp.float32), axis=-1)
    g_queries, slot_dk, slot_dv = attend_backward(
        queries, slot_k, slot_v, g_attended, row_dots, attn_lse, q_pos, lengths
    )
    g_keys, g_values = (
        lax.psum_scatter(
            slot_dk.astype(jnp.bfloat16), "ctx", scatter_dimension=1, tiled=True
        ).astype(jnp.float32),
        lax.psum_scatter(
            slot_dv.astype(jnp.bfloat16), "ctx", scatter_dimension=1, tiled=True
        ).astype(jnp.float32),
    )
    flat_shape = (n_slots, slot_rows, model_width)
    gq_low = rotate(g_queries, q_pos, -1.0).reshape(flat_shape).astype(jnp.bfloat16)
    gk_low = rotate(g_keys, q_pos, -1.0).reshape(flat_shape).astype(jnp.bfloat16)
    gv_rounded = g_values.reshape(flat_shape).astype(jnp.bfloat16).astype(jnp.float32)
    d_first = 0.5 * gv_rounded
    gv_half = d_first.astype(jnp.bfloat16)
    grad_query = jnp.einsum("srd,sre->de", normed_low, gq_low, preferred_element_type=jnp.float32)
    grad_key = jnp.einsum("srd,sre->de", normed_low, gk_low, preferred_element_type=jnp.float32)
    grad_value = jnp.einsum("srd,sre->de", normed_low, gv_half, preferred_element_type=jnp.float32)
    g_normed = jnp.einsum("sre,de->srd", gq_low, full_query, preferred_element_type=jnp.float32)
    g_normed = g_normed + jnp.einsum(
        "sre,de->srd", gk_low, full_key, preferred_element_type=jnp.float32
    )
    g_normed = g_normed + jnp.einsum(
        "sre,de->srd", gv_half, full_value, preferred_element_type=jnp.float32
    )
    g_attn_in, grad_gain_attn = normalize_back(inputs, inv_attn, attn_scale, g_normed)
    d_tokens = g_residual + g_attn_in
    (
        part_query,
        part_key,
        part_value,
        part_out,
        part_gate,
        part_up,
        part_down,
        part_gain_attn,
        part_gain_mlp,
    ) = (
        lax.psum_scatter(grad_query, ("fsdp", "ctx"), scatter_dimension=0, tiled=True),
        lax.psum_scatter(grad_key, ("fsdp", "ctx"), scatter_dimension=0, tiled=True),
        lax.psum_scatter(grad_value, ("fsdp", "ctx"), scatter_dimension=0, tiled=True),
        lax.psum_scatter(grad_out, ("fsdp", "ctx"), scatter_dimension=0, tiled=True),
        lax.psum_scatter(grad_gate, ("fsdp", "ctx"), scatter_dimension=0, tiled=True),
        lax.psum_scatter(grad_up, ("fsdp", "ctx"), scatter_dimension=0, tiled=True),
        lax.psum_scatter(grad_down, ("fsdp", "ctx"), scatter_dimension=0, tiled=True),
        lax.psum_scatter(grad_gain_attn, ("fsdp", "ctx"), scatter_dimension=0, tiled=True),
        lax.psum_scatter(grad_gain_mlp, ("fsdp", "ctx"), scatter_dimension=0, tiled=True),
    )
    (
        sum_query,
        sum_key,
        sum_value,
        sum_out,
        sum_gate,
        sum_up,
        sum_down,
        sum_gain_attn,
        sum_gain_mlp,
    ) = (
        lax.psum(part_query.astype(jnp.bfloat16), "rep").astype(jnp.float32),
        lax.psum(part_key.astype(jnp.bfloat16), "rep").astype(jnp.float32),
        lax.psum(part_value.astype(jnp.bfloat16), "rep").astype(jnp.float32),
        lax.psum(part_out.astype(jnp.bfloat16), "rep").astype(jnp.float32),
        lax.psum(part_gate.astype(jnp.bfloat16), "rep").astype(jnp.float32),
        lax.psum(part_up.astype(jnp.bfloat16), "rep").astype(jnp.float32),
        lax.psum(part_down.astype(jnp.bfloat16), "rep").astype(jnp.float32),
        lax.psum(part_gain_attn.astype(jnp.bfloat16), "rep").astype(jnp.float32),
        lax.psum(part_gain_mlp.astype(jnp.bfloat16), "rep").astype(jnp.float32),
    )
    return (
        output,
        d_tokens,
        d_first,
        sum_query,
        sum_key,
        sum_value,
        sum_out,
        sum_gate,
        sum_up,
        sum_down,
        sum_gain_attn,
        sum_gain_mlp,
    )


def solution(mesh):
    in_specs = (
        P(("rep", "fsdp"), "ctx", None),
        P(("rep", "fsdp"), "ctx", None),
        P(("rep", "fsdp"), "ctx", None),
        P(("rep", "fsdp")),
        P(("fsdp", "ctx"), None),
        P(("fsdp", "ctx"), None),
        P(("fsdp", "ctx"), None),
        P(("fsdp", "ctx"), None),
        P(("fsdp", "ctx"), None),
        P(("fsdp", "ctx"), None),
        P(("fsdp", "ctx"), None),
        P(("fsdp", "ctx")),
        P(("fsdp", "ctx")),
    )
    out_specs = (
        P(("rep", "fsdp"), "ctx", None),
        P(("rep", "fsdp"), "ctx", None),
        P(("rep", "fsdp"), "ctx", None),
        P(("fsdp", "ctx"), None),
        P(("fsdp", "ctx"), None),
        P(("fsdp", "ctx"), None),
        P(("fsdp", "ctx"), None),
        P(("fsdp", "ctx"), None),
        P(("fsdp", "ctx"), None),
        P(("fsdp", "ctx"), None),
        P(("fsdp", "ctx")),
        P(("fsdp", "ctx")),
    )
    return jax.shard_map(shards, mesh=mesh, in_specs=in_specs, out_specs=out_specs, check_vma=False)
```

profile of v0, /device:TPU:0, one launch (start us, length us, event | category | flops | bytes accessed | tf_op | source)
XLA Modules:
  0.0 1133.7 jit_solution(15939326894527541994)
XLA Ops:
  9.4 13.3 %all-gather = bf16[8,1,128]{2,1,0:T(2,128)(2,1)S(1)} all-gather(bf16[1,1,128]{2,1,0:T(2,128)(2,1)} %bitcast.334), channel_id=1, replica_groups=mesh['rep'=4,'fsdp'=4,'ctx'=2] {'fsdp','ctx'}, dimensions={0}, use_global_device_ids=true | all-gather | bytes 2304 | tf_op jit(solution)/shard_map/all_gather | solution.py:213
  24.3 16.1 %all-gather.12.cloned.1.call-done = bf16[1024,1024]{1,0:T(8,128)(2,1)} async-done(((bf16[128,1024]{1,0:T(8,128)(2,1)}), bf16[1024,1024]{1,0:T(8,128)(2,1)}) %all-gather.12.cloned.1.call-update) | async-done | bytes 2097168 | tf_op jit(solution)/shard_map/all_gather | solution.py:208
  46.3 23.8 %all-gather.18.cloned.1.call-done = bf16[1024,1024]{1,0:T(8,128)(2,1)} async-done(((bf16[128,1024]{1,0:T(8,128)(2,1)}), bf16[1024,1024]{1,0:T(8,128)(2,1)}) %all-gather.18.cloned.1.call-update) | async-done | bytes 2097168 | tf_op jit(solution)/shard_map/all_gather | solution.py:207
  73.0 26.8 %all-gather.16.cloned.1.call-done = bf16[1024,1024]{1,0:T(8,128)(2,1)} async-done(((bf16[128,1024]{1,0:T(8,128)(2,1)}), bf16[1024,1024]{1,0:T(8,128)(2,1)}) %all-gather.16.cloned.1.call-update) | async-done | bytes 2097168 | tf_op jit(solution)/shard_map/all_gather | solution.py:206
  111.6 12.8 %all-gather.1 = bf16[8,1,128]{2,1,0:T(2,128)(2,1)S(1)} all-gather(bf16[1,1,128]{2,1,0:T(2,128)(2,1)S(1)} %bitcast.335), channel_id=1, replica_groups=mesh['rep'=4,'fsdp'=4,'ctx'=2] {'fsdp','ctx'}, dimensions={0}, use_global_device_ids=true | all-gather | bytes 2304 | tf_op jit(solution)/shard_map/all_gather | solution.py:214
  126.2 8.7 all-gather.14.cloned.1.call-done
  134.9 35.1 %all-gather.20.cloned.1.call-done = bf16[1,1024,16,64]{1,3,2,0:T(8,128)(2,1)} async-done(((bf16[1,512,16,64]{1,3,2,0:T(8,128)(2,1)}), bf16[1,1024,16,64]{1,3,2,0:T(8,128)(2,1)}) %all-gather.20.cloned.1.call-update) | async-done | bytes 2097168 | tf_op jit(solution)/shard_map/all_gather | solution.py:235
  170.0 30.6 %while.30 = (s32[]{:T(128)}, bf16[2,1,512,8,64]{2,4,3,1,0:T(8,128)(2,1)S(1)}, f32[2,1,1,8,512]{4,3,2,1,0:T(8,128)S(1)}, bf16[2,1,1024,8,64]{2,4,3,1,0:T(8,128)(2...) while((s32[]{:T(128)}, ...), condition=%wide.region_4.5_spmd.clone.clone, body=%wide.region_1.4_spmd.clone.sunk.clone | while | flops 1125119488 | bytes 64626820 | solution.py:111
  205.6 39.1 %all-gather.24.cloned.1.call-done = bf16[1024,2816]{1,0:T(8,128)(2,1)} async-done(((bf16[128,2816]{1,0:T(8,128)(2,1)}), bf16[1024,2816]{1,0:T(8,128)(2,1)}) %all-gather.24.cloned.1.call-update) | async-done | bytes 5767184 | tf_op jit(solution)/shard_map/all_gather | solution.py:210
  252.2 37.6 %all-gather.26.cloned.1.call-done = bf16[1024,2816]{1,0:T(8,128)(2,1)} async-done(((bf16[128,2816]{1,0:T(8,128)(2,1)}), bf16[1024,2816]{1,0:T(8,128)(2,1)}) %all-gather.26.cloned.1.call-update) | async-done | bytes 5767184 | tf_op jit(solution)/shard_map/all_gather | solution.py:211
  297.3 37.6 %all-gather.28.cloned.1.call-done = bf16[2816,1024]{1,0:T(8,128)(2,1)} async-done(((bf16[352,1024]{1,0:T(8,128)(2,1)}), bf16[2816,1024]{1,0:T(8,128)(2,1)}) %all-gather.28.cloned.1.call-update) | async-done | bytes 5767184 | tf_op jit(solution)/shard_map/all_gather | solution.py:212
  334.8 11.3 multiply_convert_fusion.1
  366.3 68.0 %while.31 = (s32[]{:T(128)}, f32[2,1,512,8,64]{2,4,3,1,0:T(8,128)}, bf16[2,1,1024,8,64]{2,4,3,1,0:T(8,128)(2,1)}, bf16[2,1,1024,8,64]{2,4,3,1,0:T(8,128)(2,1)}, ...) while((s32[]{:T(128)}, f32[2,1,512,8,64]{2,4,3,1,0:T(8,128)}, ...), condition=%wide.region_9.10_spmd.clone.clone, body=%wide.region_8.9_spmd.clone.sunk.clone | while | flops 2728134144 | bytes 142208368 | solution.py:175
  376.0 9.9 multiply_convert_fusion.7
  390.9 8.2 bitcast_dynamic-update-slice_fusion.11
  409.8 9.9 multiply_convert_fusion.7
  439.7 26.7 %reduce-scatter.10.cloned.1.call-done = bf16[1,512,16,64]{1,3,2,0:T(8,128)(2,1)} async-done(((bf16[1,1024,16,64]{1,3,2,0:T(8,128)(2,1)}), bf16[1,512,16,64]{1,3,2,0:T(8,128)(2,1)}) %reduce-scatter.10.cloned.1.call-update) | async-done | bytes 1048592 | tf_op jit(solution)/shard_map/reduce_scatter | solution.py:303
  479.5 21.1 %reduce-scatter.12.cloned.1.call-done = bf16[1,512,16,64]{1,3,2,0:T(8,128)(2,1)} async-done(((bf16[1,1024,16,64]{1,3,2,0:T(8,128)(2,1)}), bf16[1,512,16,64]{1,3,2,0:T(8,128)(2,1)}) %reduce-scatter.12.cloned.1.call-update) | async-done | bytes 1048592 | tf_op jit(solution)/shard_map/reduce_scatter | solution.py:306
  507.9 10.3 fusion.109
  518.3 9.9 fusion.110
  528.8 9.5 fusion.89
  538.4 16.6 %reduce-scatter.20.cloned.1.call-done = f32[128,1024]{1,0:T(8,128)} async-done(((f32[1024,1024]{1,0:T(8,128)}), f32[128,1024]{1,0:T(8,128)}) %reduce-scatter.20.cloned.1.call-update) | async-done | bytes 524304 | tf_op jit(solution)/shard_map/reduce_scatter | solution.py:342
  556.7 52.8 %reduce-scatter.14.cloned.1.call-done = f32[128,1024]{1,0:T(8,128)} async-done(((f32[1024,1024]{1,0:T(8,128)}), f32[128,1024]{1,0:T(8,128)}) %reduce-scatter.14.cloned.1.call-update) | async-done | bytes 524304 | tf_op jit(solution)/shard_map/reduce_scatter | solution.py:339
  611.3 52.6 %reduce-scatter.16.cloned.1.call-done = f32[128,1024]{1,0:T(8,128)} async-done(((f32[1024,1024]{1,0:T(8,128)}), f32[128,1024]{1,0:T(8,128)}) %reduce-scatter.16.cloned.1.call-update) | async-done | bytes 524304 | tf_op jit(solution)/shard_map/reduce_scatter | solution.py:340
  665.7 52.6 %reduce-scatter.18.cloned.1.call-done = f32[128,1024]{1,0:T(8,128)} async-done(((f32[1024,1024]{1,0:T(8,128)}), f32[128,1024]{1,0:T(8,128)}) %reduce-scatter.18.cloned.1.call-update) | async-done | bytes 524304 | tf_op jit(solution)/shard_map/reduce_scatter | solution.py:341
  720.1 88.7 %reduce-scatter.22.cloned.1.call-done = f32[128,2816]{1,0:T(8,128)} async-done(((f32[1024,2816]{1,0:T(8,128)}), f32[128,2816]{1,0:T(8,128)}) %reduce-scatter.22.cloned.1.call-update) | async-done | bytes 1441808 | tf_op jit(solution)/shard_map/reduce_scatter | solution.py:343
  811.1 88.2 %reduce-scatter.24.cloned.1.call-done = f32[128,2816]{1,0:T(8,128)} async-done(((f32[1024,2816]{1,0:T(8,128)}), f32[128,2816]{1,0:T(8,128)}) %reduce-scatter.24.cloned.1.call-update) | async-done | bytes 1441808 | tf_op jit(solution)/shard_map/reduce_scatter | solution.py:344
  901.6 88.2 %reduce-scatter.26.cloned.1.call-done = f32[352,1024]{1,0:T(8,128)} async-done(((f32[2816,1024]{1,0:T(8,128)}), f32[352,1024]{1,0:T(8,128)}) %reduce-scatter.26.cloned.1.call-update) | async-done | bytes 1441808 | tf_op jit(solution)/shard_map/reduce_scatter | solution.py:345
  994.0 8.2 fusion.69
  1013.6 14.3 %all-reduce.2 = (bf16[1024]{0:T(1024)(128)(2,1)S(1)}, bf16[1024]{0:T(1024)(128)(2,1)S(1)}) all-reduce(f32[1024]{0:T(1024)S(1)} %get-tuple-element.280, f32[1024]{0:T(1024)S(1)} %copy-done.40), channel_id=11, replica_groups=mesh['rep'=4,'fsdp'=4,'ctx'=2] {'fsdp','ctx'}, use_global_device_ids=true, to_apply=%region_28.29.clone | all-reduce | flops 2048 | bytes 12288
  1028.0 12.4 %all-reduce.3 = (bf16[128]{0:T(256)(128)(2,1)S(1)}, bf16[128]{0:T(256)(128)(2,1)S(1)}) all-reduce(bf16[128]{0:T(256)(128)(2,1)S(1)} %dynamic-slice.7, bf16[128]{0:T(256)(128)(2,1)S(1)} %dynamic-slice.6), channel_id=1, replica_groups=mesh['rep'=4,'fsdp'=4,'ctx'=2] {'rep'}, use_global_device_ids=true, to_apply=%region_29.30 | all-reduce | flops 256 | bytes 1024 | tf_op jit(solution)/shard_map/psum | solution.py:367
  1044.9 72.0 %all-reduce.7.cloned.1.call-done = (bf16[128,1024]{1,0:T(8,128)(2,1)}, bf16[128,1024]{1,0:T(8,128)(2,1)}, bf16[128,1024]{1,0:T(8,128)(2,1)}, bf16[128,1024]{1,0:...) async-done(((bf16[128,1024]{1,0:T(8,128)(2,1)}, bf16[128,1024]{1,0:T(8,128)(2,1)}, bf16[128,1024]{1,0:T(8,128)(2,1)}, ...) | async-done | bytes 3211280 | tf_op jit(solution)/shard_map/psum | solution.py:360
  (252 shorter events, 202.7 us)
Async XLA Ops:
  7.2 33.2 %all-gather.12.cloned.1.call-start = ((), (), s32[]{:S(2)}) async-start(), calls=%async_computation.9 | async-start | bytes 2359296 | tf_op jit(solution)/shard_map/all_gather | solution.py:208
  7.9 62.2 %all-gather.18.cloned.1.call-start = ((), (), s32[]{:S(2)}) async-start(), calls=%async_computation.12 | async-start | bytes 2359296 | tf_op jit(solution)/shard_map/all_gather | solution.py:207
  8.7 91.1 %all-gather.16.cloned.1.call-start = ((), (), s32[]{:S(2)}) async-start(), calls=%async_computation.11 | async-start | bytes 2359296 | tf_op jit(solution)/shard_map/all_gather | solution.py:206
  9.4 125.5 %all-gather.14.cloned.1.call-start = ((), (), s32[]{:S(2)}) async-start(), calls=%async_computation.10 | async-start | bytes 3145728 | tf_op jit(solution)/shard_map/all_gather | solution.py:236
  22.8 82.4 %copy-start.35 = (f32[8,1,128]{2,1,0:T(1,128)}, f32[8,1,128]{2,1,0:T(1,128)S(1)}, u32[]{:S(2)}) copy-start(f32[8,1,128]{2,1,0:T(1,128)S(1)} %convert_element_type.385) | copy-start | bytes 12292
  24.3 80.9 %copy-start.38 = (f32[512]{0:T(512)}, f32[512]{0:T(512)S(1)}, u32[]{:S(2)}) copy-start(f32[512]{0:T(512)S(1)} %add_rsqrt_fusion.1) | copy-start | bytes 6148
  45.2 124.8 %all-gather.20.cloned.1.call-start = ((), (), s32[]{:S(2)}) async-start(), calls=%async_computation.13 | async-start | bytes 3145728 | tf_op jit(solution)/shard_map/all_gather | solution.py:235
  46.3 60.5 %copy-start.31 = (f32[512,32]{0,1:T(8,128)}, f32[512,32]{0,1:T(8,128)S(1)}, u32[]{:S(2)}) copy-start(f32[512,32]{0,1:T(8,128)S(1)} %get-tuple-element.354) | copy-start | bytes 196612
  108.6 92.1 %all-gather.22.cloned.1.call-start = ((), (), s32[]{:S(2)}) async-start(), calls=%async_computation.14 | async-start | bytes 2359296 | tf_op jit(solution)/shard_map/all_gather | solution.py:209
  109.1 135.5 %all-gather.24.cloned.1.call-start = ((), (), s32[]{:S(2)}) async-start(), calls=%async_computation.15 | async-start | bytes 6488064 | tf_op jit(solution)/shard_map/all_gather | solution.py:210
  109.9 179.8 %all-gather.26.cloned.1.call-start = ((), (), s32[]{:S(2)}) async-start(), calls=%async_computation.16 | async-start | bytes 6488064 | tf_op jit(solution)/shard_map/all_gather | solution.py:211
  110.6 224.2 %all-gather.28.cloned.1.call-start = ((), (), s32[]{:S(2)}) async-start(), calls=%async_computation.17 | async-start | bytes 6488064 | tf_op jit(solution)/shard_map/all_gather | solution.py:212
  111.4 355.0 %reduce-scatter.10.cloned.1.call-start = ((), (), s32[]{:S(2)}) async-start(), calls=%async_computation.18 | async-start | bytes 3145728 | tf_op jit(solution)/shard_map/reduce_scatter | solution.py:303
  170.0 30.7 %copy-start.8 = (bf16[1,512,1024]{2,1,0:T(8,128)(2,1)S(1)}, bf16[1,512,1024]{2,1,0:T(8,128)(2,1)}, u32[]{:S(2)}) copy-start(bf16[1,512,1024]{2,1,0:T(8,128)(2,1)} %param.17) | copy-start | bytes 3145732
  205.6 84.2 %copy-start.23 = (bf16[512,1024]{1,0:T(8,128)(2,1)}, bf16[512,1024]{1,0:T(8,128)(2,1)S(1)}, u32[]{:S(2)}) copy-start(bf16[512,1024]{1,0:T(8,128)(2,1)S(1)} %fusion.73) | copy-start | bytes 3145732
  252.2 82.7 %copy-start.25 = (bf16[1,512,1024]{2,1,0:T(8,128)(2,1)S(1)}, bf16[1,512,1024]{2,1,0:T(8,128)(2,1)}, u32[]{:S(2)}) copy-start(bf16[1,512,1024]{2,1,0:T(8,128)(2,1)} %param.19) | copy-start | bytes 3145732
  252.2 82.7 %copy-start.41 = (pred[512]{0:T(512)(128)(4,1)S(1)}, pred[512]{0:T(512)(128)(4,1)}, u32[]{:S(2)}) copy-start(pred[512]{0:T(512)(128)(4,1)} %fusion.95) | copy-start | bytes 1540
  366.7 9.3 copy-start.24
  376.0 9.9 copy-start.12
  400.5 9.3 copy-start.24
  409.7 9.9 copy-start.12
  434.3 66.3 %reduce-scatter.12.cloned.1.call-start = ((), (), s32[]{:S(2)}) async-start(), calls=%async_computation.19 | async-start | bytes 3145728 | tf_op jit(solution)/shard_map/reduce_scatter | solution.py:306
  435.0 119.9 %reduce-scatter.20.cloned.1.call-start = ((), (), s32[]{:S(2)}) async-start(), calls=%async_computation.23 | async-start | bytes 4718592 | tf_op jit(solution)/shard_map/reduce_scatter | solution.py:342
  439.4 28.6 %copy-start.32 = (f32[512,32]{0,1:T(8,128)S(1)}, f32[512,32]{0,1:T(8,128)}, u32[]{:S(2)}) copy-start(f32[512,32]{0,1:T(8,128)} %copy-done.31) | copy-start | bytes 196612
  439.4 28.6 %copy-start.33 = (f32[512,32]{0,1:T(8,128)S(1)}, f32[512,32]{0,1:T(8,128)}, u32[]{:S(2)}) copy-start(f32[512,32]{0,1:T(8,128)} %get-tuple-element.352) | copy-start | bytes 196612
  439.4 170.1 %reduce-scatter.14.cloned.1.call-start = ((), (), s32[]{:S(2)}) async-start(), calls=%async_computation.20 | async-start | bytes 4718592 | tf_op jit(solution)/shard_map/reduce_scatter | solution.py:339
  474.6 189.4 %reduce-scatter.16.cloned.1.call-start = ((), (), s32[]{:S(2)}) async-start(), calls=%async_computation.21 | async-start | bytes 4718592 | tf_op jit(solution)/shard_map/reduce_scatter | solution.py:340
  479.4 238.9 %reduce-scatter.18.cloned.1.call-start = ((), (), s32[]{:S(2)}) async-start(), calls=%async_computation.22 | async-start | bytes 4718592 | tf_op jit(solution)/shard_map/reduce_scatter | solution.py:341
  507.9 300.9 %reduce-scatter.22.cloned.1.call-start = ((), (), s32[]{:S(2)}) async-start(), calls=%async_computation.24 | async-start | bytes 12976128 | tf_op jit(solution)/shard_map/reduce_scatter | solution.py:343
  518.3 381.0 %reduce-scatter.24.cloned.1.call-start = ((), (), s32[]{:S(2)}) async-start(), calls=%async_computation.25 | async-start | bytes 12976128 | tf_op jit(solution)/shard_map/reduce_scatter | solution.py:344
  528.2 461.6 %reduce-scatter.26.cloned.1.call-start = ((), (), s32[]{:S(2)}) async-start(), calls=%async_computation.26 | async-start | bytes 12976128 | tf_op jit(solution)/shard_map/reduce_scatter | solution.py:345
  538.3 578.6 %all-reduce.7.cloned.1.call-start = ((), (), s32[]{:S(2)}) async-start(), calls=%async_computation.27 | async-start | bytes 6422528 | tf_op jit(solution)/shard_map/psum | solution.py:360
  (44 other events, 143.7 us)
Sparse Core Ops, SparseCore 0:
  9.9 30.4 all-gather.11
  42.3 27.7 all-gather.17
  72.0 27.7 all-gather.15
  101.8 33.0 all-gather.13
  136.9 33.0 all-gather.19
  171.7 27.7 all-gather.21
  201.4 43.1 all-gather.23
  246.5 43.1 all-gather.25
  291.6 43.1 all-gather.27
  434.4 31.8 reduce-scatter.9
  468.6 31.8 reduce-scatter.11
  503.8 51.1 reduce-scatter.19
  558.3 51.1 reduce-scatter.13
  612.7 51.1 reduce-scatter.15
  667.1 51.1 reduce-scatter.17
  721.7 87.0 reduce-scatter.21
  812.1 87.0 reduce-scatter.23
  902.6 87.1 reduce-scatter.25
  993.3 123.5 all-reduce.6
where the time goes:
time: 1140 us; the launch traced here: 1130 us
  waiting for transfers between devices  790 us (69%)
  matrix products  190 us (17%)
  other arithmetic  56.9 us (5%)
  blocking collectives  52.7 us (5%)
  local copies, waits for them, and re-layouts  26.7 us (2%)
  between operations  16 us (1%)
    reduce_scatter x1, waiting for transfers between devices, shards(): lax.psum_scatter(grad_gate, ('fsdp', 'ctx'), scatter_dimension=0, tiled=T...  88.7 us
    reduce_scatter x1, waiting for transfers between devices, shards(): lax.psum_scatter(grad_down, ('fsdp', 'ctx'), scatter_dimension=0, tiled=T...  88.2 us
    reduce_scatter x1, waiting for transfers between devices, shards(): lax.psum_scatter(grad_up, ('fsdp', 'ctx'), scatter_dimension=0, tiled=True)  88.2 us
    psum x1, waiting for transfers between devices, shards(): lax.psum(part_query.astype(jnp.bfloat16), 'rep').astype(jnp.float32)  72 us
    reduce_scatter x1, waiting for transfers between devices, shards(): lax.psum_scatter(grad_query, ('fsdp', 'ctx'), scatter_dimension=0, tiled=...  52.8 us
    reduce_scatter x1, waiting for transfers between devices, shards(): lax.psum_scatter(grad_key, ('fsdp', 'ctx'), scatter_dimension=0, tiled=True)  52.6 us
    reduce_scatter x1, waiting for transfers between devices, shards(): lax.psum_scatter(grad_value, ('fsdp', 'ctx'), scatter_dimension=0, tiled=...  52.6 us
    all_gather x1, waiting for transfers between devices, shards(): lax.all_gather(w_gate, ('fsdp', 'ctx'), axis=0, tiled=True)  39.1 us
  transfers between devices with their start and end apart: 19, of which 18 were waited for; matrix products, arithmetic and copies ran while one was open for 14% of the time, Pallas kernels for 0%

commit v1 on v0

--- a/solution.py
+++ b/solution.py
@@ -62,17 +62,18 @@
     return jnp.moveaxis(grouped, 0, 2).reshape(n_slots, length, n_groups * per_group, head_width)
 
 
-def score_block(q_rows, k_rows, q_pos, lengths):
-    k_pos = jnp.arange(k_rows.shape[1])
+def score_block(q_rows, k_rows, q_pos, k_pos, lengths):
     products = jnp.einsum(
         "sqhe,skhe->shqk", q_rows, k_rows, preferred_element_type=jnp.float32
     ) * q_rows.shape[-1] ** (-0.5)
-    causal = k_pos[None, None, None, :] <= q_pos[None, None, :, None]
+    causal = (k_pos[None, None, None, :] <= q_pos[None, None, :, None]) & (
+        k_pos[None, None, None, :] >= 0
+    )
     filled = k_pos[None, None, None, :] < lengths[:, None, None, None]
     return jnp.where(causal & filled, products, NEG)
 
 
-def attend_forward(queries, keys, values, q_pos, lengths):
+def attend_forward(queries, keys, values, q_pos, k_pos, lengths):
     n_slots, q_len, n_heads, head_width = queries.shape
     q_block, per_group = head_groups(n_slots, q_len, n_heads, keys.shape[1])
     n_groups = n_heads // per_group
@@ -87,7 +88,7 @@
 
         def one_block(streams):
             q_rows, pos_rows = streams
-            scores = score_block(q_rows, k_group, pos_rows, lengths)
+            scores = score_block(q_rows, k_group, pos_rows, k_pos, lengths)
             highest = jnp.max(scores, axis=-1, keepdims=True)
             exponent = jnp.exp(scores - highest)
             totals = jnp.sum(exponent, axis=-1, keepdims=True)
@@ -112,7 +113,7 @@
     return (join_heads(mixture), log_sums)
 
 
-def attend_backward(queries, keys, values, upstream, row_dots, log_sums, q_pos, lengths):
+def attend_backward(queries, keys, values, upstream, row_dots, log_sums, q_pos, k_pos, lengths):
     n_slots, q_len, n_heads, head_width = queries.shape
     q_block, per_group = head_groups(n_slots, q_len, n_heads, keys.shape[1])
     n_groups = n_heads // per_group
@@ -130,7 +131,7 @@
         def one_block(running, streams):
             k_grad, v_grad = running
             q_rows, g_rows, d_rows, l_rows, pos_rows = streams
-            scores = score_block(q_rows, k_group, pos_rows, lengths)
+            scores = score_block(q_rows, k_group, pos_rows, k_pos, lengths)
             probabilities = jnp.exp(scores - l_rows[..., None])
             v_grad = v_grad + jnp.einsum(
                 "shqk,sqhe->skhe",
@@ -174,6 +175,50 @@
     )
     q_grads, k_grads, v_grads = lax.map(one_group, grouped)
     return (join_heads(q_grads), join_heads(k_grads), join_heads(v_grads))
+
+
+GROUP = ("fsdp", "ctx")
+
+
+def as_rows(block, width):
+    return block.reshape(-1, width)
+
+
+def gather_rows(pieces, width):
+    flat = [as_rows(p, width) for p in pieces]
+    gathered = lax.all_gather(jnp.concatenate(flat, axis=0), GROUP, axis=0, tiled=False)
+    n_group = gathered.shape[0]
+    fulls, offset = [], 0
+    for piece, rows in zip(pieces, flat):
+        part = gathered[:, offset : offset + rows.shape[0], :]
+        fulls.append(part.reshape((n_group * piece.shape[0],) + piece.shape[1:]))
+        offset += rows.shape[0]
+    return fulls
+
+
+def scatter_rows(fulls, width, n_group):
+    flat = [f.reshape(n_group, -1, width) for f in fulls]
+    packed = jnp.concatenate(flat, axis=1).astype(jnp.bfloat16)
+    summed = lax.psum_scatter(packed, GROUP, scatter_dimension=0, tiled=True)
+    summed = lax.psum(summed, "rep")[0].astype(jnp.float32)
+    parts, offset = [], 0
+    for full, rows in zip(fulls, flat):
+        part = summed[offset : offset + rows.shape[1], :]
+        parts.append(part.reshape((full.shape[0] // n_group,) + full.shape[1:]))
+        offset += rows.shape[1]
+    return parts
+
+
+def gain_block(full, n_group, width):
+    own = full.reshape(n_group, 1, -1)
+    padded = jnp.pad(own, ((0, 0), (0, 7), (0, width - own.shape[-1])))
+    return padded.reshape(n_group * 8, width)
+
+
+def gain_rows(first, second, width):
+    row = jnp.zeros((8, width), first.dtype)
+    row = row.at[0, : first.shape[-1]].set(first)
+    return row.at[0, first.shape[-1] : first.shape[-1] + second.shape[-1]].set(second)
 
 
 def shards(
@@ -192,28 +237,20 @@
     gain_mlp,
 ):
     n_slots, slot_rows, model_width = tokens.shape
-    (
-        full_query,
-        full_key,
-        full_value,
-        full_out,
-        full_gate,
-        full_up,
-        full_down,
-        full_gain_attn,
-        full_gain_mlp,
-    ) = (
-        lax.all_gather(w_query, ("fsdp", "ctx"), axis=0, tiled=True),
-        lax.all_gather(w_key, ("fsdp", "ctx"), axis=0, tiled=True),
-        lax.all_gather(w_value, ("fsdp", "ctx"), axis=0, tiled=True),
-        lax.all_gather(w_out, ("fsdp", "ctx"), axis=0, tiled=True),
-        lax.all_gather(w_gate, ("fsdp", "ctx"), axis=0, tiled=True),
-        lax.all_gather(w_up, ("fsdp", "ctx"), axis=0, tiled=True),
-        lax.all_gather(w_down, ("fsdp", "ctx"), axis=0, tiled=True),
-        lax.all_gather(gain_attn, ("fsdp", "ctx"), axis=0, tiled=True),
-        lax.all_gather(gain_mlp, ("fsdp", "ctx"), axis=0, tiled=True),
-    )
-    q_pos = lax.axis_index("ctx") * slot_rows + jnp.arange(slot_rows)
+    n_ctx = lax.axis_size("ctx")
+    n_group = lax.axis_size("fsdp") * n_ctx
+    own_rows = gain_attn.shape[0]
+    full_query, full_key, full_value, gains = gather_rows(
+        [w_query, w_key, w_value, gain_rows(gain_attn, gain_mlp, model_width)], model_width
+    )
+    gains = gains.reshape(n_group, 8, model_width)[:, 0, :]
+    full_gain_attn = gains[:, :own_rows].reshape(-1)
+    full_gain_mlp = gains[:, own_rows : 2 * own_rows].reshape(-1)
+    full_out, full_gate, full_up, full_down = gather_rows(
+        [w_out, w_gate, w_up, w_down], model_width
+    )
+    ctx_index = lax.axis_index("ctx")
+    q_pos = ctx_index * slot_rows + jnp.arange(slot_rows)
     live_rows = q_pos[None, :] < lengths[:, None]
     head_shape = (n_slots, slot_rows, HEADS, HEAD_DIM)
     inputs = tokens.astype(jnp.float32)
@@ -231,11 +268,19 @@
         .astype(jnp.bfloat16)
         .reshape(head_shape)
     )
-    slot_k, slot_v = (
-        lax.all_gather(keys, "ctx", axis=1, tiled=True),
-        lax.all_gather(values, "ctx", axis=1, tiled=True),
-    )
-    attn_raw, attn_lse = attend_forward(queries, slot_k, slot_v, q_pos, lengths)
+    if n_ctx == 2:
+        shift_up = [(0, 1)]
+        earlier = lax.ppermute(jnp.stack([keys, values]), "ctx", shift_up)
+        slot_k = jnp.concatenate([earlier[0], keys], axis=1)
+        slot_v = jnp.concatenate([earlier[1], values], axis=1)
+        k_pos = jnp.concatenate([q_pos - slot_rows, q_pos])
+    else:
+        slot_k, slot_v = (
+            lax.all_gather(keys, "ctx", axis=1, tiled=True),
+            lax.all_gather(values, "ctx", axis=1, tiled=True),
+        )
+        k_pos = jnp.arange(n_ctx * slot_rows)
+    attn_raw, attn_lse = attend_forward(queries, slot_k, slot_v, q_pos, k_pos, lengths)
     attended = attn_raw.astype(jnp.bfloat16)
     att_flat = attended.reshape(n_slots, slot_rows, model_width)
     branch = jnp.einsum("sre,ed->srd", att_flat, full_out, preferred_element_type=jnp.float32)
@@ -250,27 +295,6 @@
         "srf,fd->srd", hidden, full_down, preferred_element_type=jnp.float32
     )
     output = jnp.where(live_rows[..., None], final, 0.0).astype(jnp.bfloat16)
-    (
-        full_query,
-        full_key,
-        full_value,
-        full_out,
-        full_gate,
-        full_up,
-        full_down,
-        full_gain_attn,
-        full_gain_mlp,
-    ) = (
-        lax.all_gather(w_query, ("fsdp", "ctx"), axis=0, tiled=True),
-        lax.all_gather(w_key, ("fsdp", "ctx"), axis=0, tiled=True),
-        lax.all_gather(w_value, ("fsdp", "ctx"), axis=0, tiled=True),
-        lax.all_gather(w_out, ("fsdp", "ctx"), axis=0, tiled=True),
-        lax.all_gather(w_gate, ("fsdp", "ctx"), axis=0, tiled=True),
-        lax.all_gather(w_up, ("fsdp", "ctx"), axis=0, tiled=True),
-        lax.all_gather(w_down, ("fsdp", "ctx"), axis=0, tiled=True),
-        lax.all_gather(gain_attn, ("fsdp", "ctx"), axis=0, tiled=True),
-        lax.all_gather(gain_mlp, ("fsdp", "ctx"), axis=0, tiled=True),
-    )
     output_gradient = jnp.where(live_rows[..., None], cotangent.astype(jnp.float32), 0.0)
     g_low = output_gradient.astype(jnp.bfloat16)
     grad_down = jnp.einsum("srf,srd->fd", hidden, g_low, preferred_element_type=jnp.float32)
@@ -290,6 +314,11 @@
     g_residual = output_gradient + g_mlp_in
     g_branch = g_residual.astype(jnp.bfloat16)
     grad_out = jnp.einsum("sre,srd->ed", att_flat, g_branch, preferred_element_type=jnp.float32)
+    part_down, part_gate, part_up, part_out, part_gain_mlp = scatter_rows(
+        [grad_down, grad_gate, grad_up, grad_out, gain_block(grad_gain_mlp, n_group, model_width)],
+        model_width,
+        n_group,
+    )
     g_attended = (
         jnp.einsum("srd,ed->sre", g_branch, full_out, preferred_element_type=jnp.float32)
         .astype(jnp.bfloat16)
@@ -297,16 +326,26 @@
     )
     row_dots = jnp.sum(g_attended.astype(jnp.float32) * attended.astype(jnp.float32), axis=-1)
     g_queries, slot_dk, slot_dv = attend_backward(
-        queries, slot_k, slot_v, g_attended, row_dots, attn_lse, q_pos, lengths
-    )
-    g_keys, g_values = (
-        lax.psum_scatter(
-            slot_dk.astype(jnp.bfloat16), "ctx", scatter_dimension=1, tiled=True
-        ).astype(jnp.float32),
-        lax.psum_scatter(
-            slot_dv.astype(jnp.bfloat16), "ctx", scatter_dimension=1, tiled=True
-        ).astype(jnp.float32),
-    )
+        queries, slot_k, slot_v, g_attended, row_dots, attn_lse, q_pos, k_pos, lengths
+    )
+    if n_ctx == 2:
+        shift_down = [(1, 0)]
+        later = lax.ppermute(
+            jnp.stack([slot_dk[:, :slot_rows], slot_dv[:, :slot_rows]]).astype(jnp.bfloat16),
+            "ctx",
+            shift_down,
+        ).astype(jnp.float32)
+        g_keys = slot_dk[:, slot_rows:] + later[0]
+        g_values = slot_dv[:, slot_rows:] + later[1]
+    else:
+        g_keys, g_values = (
+            lax.psum_scatter(
+                slot_dk.astype(jnp.bfloat16), "ctx", scatter_dimension=1, tiled=True
+            ).astype(jnp.float32),
+            lax.psum_scatter(
+                slot_dv.astype(jnp.bfloat16), "ctx", scatter_dimension=1, tiled=True
+            ).astype(jnp.float32),
+        )
     flat_shape = (n_slots, slot_rows, model_width)
     gq_low = rotate(g_queries, q_pos, -1.0).reshape(flat_shape).astype(jnp.bfloat16)
     gk_low = rotate(g_keys, q_pos, -1.0).reshape(flat_shape).astype(jnp.bfloat16)
@@ -325,7 +364,15 @@
     )
     g_attn_in, grad_gain_attn = normalize_back(inputs, inv_attn, attn_scale, g_normed)
     d_tokens = g_residual + g_attn_in
-    (
+    part_query, part_key, part_value, part_gain_attn = scatter_rows(
+        [grad_query, grad_key, grad_value, gain_block(grad_gain_attn, n_group, model_width)],
+        model_width,
+        n_group,
+    )
+    return (
+        output,
+        d_tokens,
+        d_first,
         part_query,
         part_key,
         part_value,
@@ -333,53 +380,8 @@
         part_gate,
         part_up,
         part_down,
-        part_gain_attn,
-        part_gain_mlp,
-    ) = (
-        lax.psum_scatter(grad_query, ("fsdp", "ctx"), scatter_dimension=0, tiled=True),
-        lax.psum_scatter(grad_key, ("fsdp", "ctx"), scatter_dimension=0, tiled=True),
-        lax.psum_scatter(grad_value, ("fsdp", "ctx"), scatter_dimension=0, tiled=True),
-        lax.psum_scatter(grad_out, ("fsdp", "ctx"), scatter_dimension=0, tiled=True),
-        lax.psum_scatter(grad_gate, ("fsdp", "ctx"), scatter_dimension=0, tiled=True),
-        lax.psum_scatter(grad_up, ("fsdp", "ctx"), scatter_dimension=0, tiled=True),
-        lax.psum_scatter(grad_down, ("fsdp", "ctx"), scatter_dimension=0, tiled=True),
-        lax.psum_scatter(grad_gain_attn, ("fsdp", "ctx"), scatter_dimension=0, tiled=True),
-        lax.psum_scatter(grad_gain_mlp, ("fsdp", "ctx"), scatter_dimension=0, tiled=True),
-    )
-    (
-        sum_query,
-        sum_key,
-        sum_value,
-        sum_out,
-        sum_gate,
-        sum_up,
-        sum_down,
-        sum_gain_attn,
-        sum_gain_mlp,
-    ) = (
-        lax.psum(part_query.astype(jnp.bfloat16), "rep").astype(jnp.float32),
-        lax.psum(part_key.astype(jnp.bfloat16), "rep").astype(jnp.float32),
-        lax.psum(part_value.astype(jnp.bfloat16), "rep").astype(jnp.float32),
-        lax.psum(part_out.astype(jnp.bfloat16), "rep").astype(jnp.float32),
-        lax.psum(part_gate.astype(jnp.bfloat16), "rep").astype(jnp.float32),
-        lax.psum(part_up.astype(jnp.bfloat16), "rep").astype(jnp.float32),
-        lax.psum(part_down.astype(jnp.bfloat16), "rep").astype(jnp.float32),
-        lax.psum(part_gain_attn.astype(jnp.bfloat16), "rep").astype(jnp.float32),
-        lax.psum(part_gain_mlp.astype(jnp.bfloat16), "rep").astype(jnp.float32),
-    )
-    return (
-        output,
-        d_tokens,
-        d_first,
-        sum_query,
-        sum_key,
-        sum_value,
-        sum_out,
-        sum_gate,
-        sum_up,
-        sum_down,
-        sum_gain_attn,
-        sum_gain_mlp,
+        part_gain_attn[0, :own_rows],
+        part_gain_mlp[0, :own_rows],
     )
 
 

time: 1140 us -> 794 us (0.70)
  waiting for transfers between devices: 790 us -> 416 us
  local copies, waits for them, and re-layouts: 26.7 us -> 143 us
  blocking collectives: 52.7 us -> 0 us
  matrix products: 190 us -> 153 us
    reduce_scatter x9 -> x2, waiting for transfers between devices: 487 us -> 134 us  [scatter_rows(): summed = lax.psum_scatter(packed, GROUP, scatter_dimension=0, tiled=True)]
    all_gather x9 -> x2, waiting for transfers between devices: 225 us -> 44 us  [gather_rows(): lax.all_gather(jnp.concatenate(flat, axis=0), GROUP, axis=0, tiled=False)]
    ppermute x0 -> x2, waiting for transfers between devices: none -> 125 us  [the longest x1 77.3 us: shards(): earlier = lax.ppermute(jnp.stack([keys, values]), 'ctx', shift_up)]
    reshape x0 -> x10, local copies, waits for them, and re-layouts: none -> 52.3 us  [the longest x2 23.8 us: scatter_rows(): flat = [f.reshape(n_group, -1, width) for f in fulls]]
    psum x1, waiting for transfers between devices: 72 us -> 113 us  [scatter_rows(): summed = lax.psum(summed, 'rep')[0].astype(jnp.float32)]
    slice x0 -> x9, local copies, waits for them, and re-layouts: none -> 30.5 us  [the longest x3 22.8 us: gather_rows(): part = gathered[:, offset:offset + rows.shape[0], :]]
    all_gather x2 -> x0, blocking collectives: 26.1 us -> none  [the longest x1 13.3 us: shards(): lax.all_gather(gain_attn, ('fsdp', 'ctx'), axis=0, tiled=True)]
    convert_element_type x19 -> x4, other arithmetic: 27.9 us -> 8.11 us  [the longest x1 4.18 us: shards(): gv_half = d_first.astype(jnp.bfloat16)]
  transfers between devices with their start and end apart: 19 -> 7, of which waited for: 18 -> 6; matrix products, arithmetic and copies ran while one was open for 14% -> 17% of each run, Pallas kernels for 0% -> 0%
where the time goes in v1:
time: 794 us; the launch traced here: 786 us
  waiting for transfers between devices  416 us (52%)
  matrix products  153 us (19%)
  local copies, waits for them, and re-layouts  143 us (18%)
  other arithmetic  50.5 us (6%)
  between operations  15.7 us (2%)
    reduce_scatter x2, waiting for transfers between devices, scatter_rows(): summed = lax.psum_scatter(packed, GROUP, scatter_dimension=0, tiled=True)  134 us
    psum x1, waiting for transfers between devices, scatter_rows(): summed = lax.psum(summed, 'rep')[0].astype(jnp.float32)  113 us
    ppermute x1, waiting for transfers between devices, shards(): earlier = lax.ppermute(jnp.stack([keys, values]), 'ctx', shift_up)  77.3 us
    ppermute x1, waiting for transfers between devices, shards(): lax.ppermute(jnp.stack([slot_dk[:, :slot_rows], slot_dv[:, :slot_rows]])....  47.6 us
    all_gather x2, waiting for transfers between devices, gather_rows(): lax.all_gather(jnp.concatenate(flat, axis=0), GROUP, axis=0, tiled=False)  44 us
    reshape x2, local copies, waits for them, and re-layouts, scatter_rows(): flat = [f.reshape(n_group, -1, width) for f in fulls]  23.8 us
    reshape x2, local copies, waits for them, and re-layouts, gather_rows(): fulls.append(part.reshape((n_group * piece.shape[0],) + piece.shape[1:]))  23.6 us
    slice x3, local copies, waits for them, and re-layouts, gather_rows(): part = gathered[:, offset:offset + rows.shape[0], :]  22.8 us
  transfers between devices with their start and end apart: 7, of which 6 were waited for; matrix products, arithmetic and copies ran while one was open for 17% of the time, Pallas kernels for 0%

profile of v1, /device:TPU:0, one launch (start us, length us, event | category | flops | bytes accessed | tf_op | source)
XLA Modules:
  0.0 786.2 jit_solution(12189413384773454407)
XLA Ops:
  21.0 44.0 %all-gather.5.cloned.1.call-done = bf16[3136,1024]{1,0:T(8,128)(2,1)} async-done(((bf16[392,1024]{1,0:T(8,128)(2,1)}), bf16[3136,1024]{1,0:T(8,128)(2,1)}) %all-gather.5.cloned.1.call-update) | async-done | bytes 6422544 | tf_op jit(solution)/shard_map/all_gather | solution.py:189
  66.6 6.0 fusion.110
  91.8 4.7 collective-permute-start
  100.2 77.3 %collective-permute-done = bf16[2,1,512,16,64]{2,4,3,1,0:T(8,128)(2,1)} collective-permute-done((bf16[2,1,512,16,64]{2,4,3,1,0:T(8,128)(2,1)}, bf16[2,1,512,16,64]{2,4,3,1,0:T(8,128)(2,1)}, u32[]{:S(2)}, u32[]{:S(2)}) %collective-permute-start) | collective-permute-done | bytes 2097184 | tf_op jit(solution)/shard_map/ppermute | solution.py:273
  181.1 29.3 %while.32 = (s32[]{:T(128)}, bf16[2,1,512,8,64]{2,4,3,1,0:T(8,128)(2,1)}, f32[2,1,1,8,512]{4,3,2,1,0:T(8,128)S(1)}, bf16[2,1,1024,8,64]{2,4,3,1,0:T(8,128)(2,1)}...) while((s32[]{:T(128)}, ...), condition=%wide.region_5.6_spmd.clone.clone, body=%wide.region_2.5_spmd.clone.sunk.clone | while | flops 1125644800 | bytes 73025728 | solution.py:112
  189.8 5.0 fusion.189
  200.0 4.4 fusion.188
  204.4 5.0 fusion.189
  213.5 13.7 %fusion.109 = (bf16[8,352,1024]{2,1,0:T(8,128)(2,1)}, bf16[8,352,1024]{2,1,0:T(8,128)(2,1)}, bf16[8,352,1024]{2,1,0:T(8,128)(2,1)}) fusion(bf16[8,1184,1024]{2,1,0:T(8,128)(2,1)} %bitcast.404), kind=kLoop, calls=%fused_computation.203 | loop fusion | bytes 34603008 | tf_op jit(solution)/shard_map/slice | solution.py:193
  227.2 11.7 %reshape.1061 = bf16[1024,2816]{1,0:T(8,128)(2,1)} reshape(bf16[8,352,1024]{2,1,0:T(8,128)(2,1)} %get-tuple-element.412) | data formatting | bytes 11534336 | tf_op jit(solution)/shard_map/reshape | solution.py:194
  238.9 4.8 multiply_reduce_fusion
  243.8 11.9 %reshape.1062 = bf16[1024,2816]{1,0:T(8,128)(2,1)} reshape(bf16[8,352,1024]{2,1,0:T(8,128)(2,1)} %get-tuple-element.414) | data formatting | bytes 11534336 | tf_op jit(solution)/shard_map/reshape | solution.py:194
  257.7 6.2 fusion.114
  264.0 5.9 fusion.52
  270.4 11.1 %multiply_convert_fusion.1 = (bf16[512,2816]{1,0:T(8,128)(2,1)}, bf16[512,2816]{1,0:T(8,128)(2,1)}) fusion(f32[512,2816]{1,0:T(8,128)} %copy-done.56, f32[512,2816]{1,0:T(8,128)} %get-tuple-element.458, bf16[2816,1024]{1,0:T(8,128)(2,1)} %bitcast.426, bf16[1,512,1024]{2,1,0:T(8,128)(2,1)S(1)} %copy-done.36, pred[512]{0:T(512)(128)(4,1)S(1)} %copy-done.53), kind=kOutput, calls=%fused_computation.75 | convolution fusion | flops 2973106176 | bytes 24117760 | tf_op jit(solution)/shard_map/srd,fd->srf/dot_general | solution.py:301
  281.5 5.1 fusion.115
  302.0 64.7 %while.44 = (s32[]{:T(128)}, f32[2,1,512,8,64]{2,4,3,1,0:T(8,128)}, f32[2,1,1024,8,64]{2,4,3,1,0:T(8,128)}, f32[2,1,1024,8,64]{2,4,3,1,0:T(8,128)}, bf16[2,1,102...) while((s32[]{:T(128)}, f32[2,1,512,8,64]{2,4,3,1,0:T(8,128)}, ...), condition=%wide.region_10.11_spmd.clone.clone, body=%wide.region_9.10_spmd.clone.sunk.clone | while | flops 2728659456 | bytes 200938768 | solution.py:176
  306.0 5.8 copy-done
  311.8 5.9 bitcast_dynamic-update-slice_fusion.11
  317.7 9.5 %multiply_convert_fusion.10 = bf16[8,512,1024]{2,1,0:T(8,128)(2,1)S(1)} fusion(f32[8,512,1024]{2,1,0:T(8,128)} %copy-done, f32[8,512]{1,0:T(8,128)S(1)} %dynamic-slice_bitcast_fusion.6, f32[8,512]{1,0:T(8,128)S(1)} %dynamic-slice_bitcast_fusion.7, pred[512,1024]{1,0:T(8,128)(4,1)S(1)} %and_and_fusion.7, ...), kind=kOutput, calls=%fused_computation.26.clone.1.clone | convolution fusion | flops 562036736 | bytes 27296768 | tf_op jit(solution)/shard_map/while/body/eval_jaxpr/while/body/eval_jaxpr/sqhe,skhe->shqk/dot_general | solution.py:142
  338.2 5.8 copy-done
  343.9 5.8 bitcast_dynamic-update-slice_fusion.11
  349.8 9.5 %multiply_convert_fusion.10 = bf16[8,512,1024]{2,1,0:T(8,128)(2,1)S(1)} fusion(f32[8,512,1024]{2,1,0:T(8,128)} %copy-done, f32[8,512]{1,0:T(8,128)S(1)} %dynamic-slice_bitcast_fusion.6, f32[8,512]{1,0:T(8,128)S(1)} %dynamic-slice_bitcast_fusion.7, pred[512,1024]{1,0:T(8,128)(4,1)S(1)} %and_and_fusion.7, ...), kind=kOutput, calls=%fused_computation.26.clone.1.clone | convolution fusion | flops 562036736 | bytes 27296768 | tf_op jit(solution)/shard_map/while/body/eval_jaxpr/while/body/eval_jaxpr/sqhe,skhe->shqk/dot_general | solution.py:142
  372.1 47.6 %collective-permute-done.1 = bf16[2,1,512,16,64]{2,4,3,1,0:T(8,128)(2,1)S(1)} collective-permute-done((bf16[2,1,512,16,64]{2,4,3,1,0:T(8,128)(2,1)S(1)}, bf16[2,1,512,16,64]{2,4,3,1,0:T(8,128)(2,1)S(1)}, u32[]{:S(2)}, u32[]{:S(2)}) %collective-permute-start.1) | collective-permute-done | bytes 2097184 | tf_op jit(solution)/shard_map/ppermute | solution.py:333
  447.9 8.7 %convolution_convert_fusion = bf16[1024,2816]{1,0:T(8,128)(2,1)} fusion(bf16[512,1024]{1,0:T(8,128)(2,1)} %copy-done.30, bf16[512,2816]{1,0:T(8,128)(2,1)} %get-tuple-element.415), kind=kOutput, calls=%fused_computation.79 | convolution fusion | flops 2955673600 | bytes 9699328 | tf_op jit(solution)/shard_map/srd,srf->df/dot_general | solution.py:309
  456.7 11.9 %reshape.1072 = bf16[8,352,1024]{2,1,0:T(8,128)(2,1)} reshape(bf16[1024,2816]{1,0:T(8,128)(2,1)} %convolution_convert_fusion) | data formatting | bytes 11534336 | tf_op jit(solution)/shard_map/reshape | solution.py:200
  468.6 6.9 convolution_convert_fusion.1
  475.4 11.9 %reshape.1071 = bf16[8,352,1024]{2,1,0:T(8,128)(2,1)} reshape(bf16[1024,2816]{1,0:T(8,128)(2,1)} %convolution_convert_fusion.1) | data formatting | bytes 11534336 | tf_op jit(solution)/shard_map/reshape | solution.py:200
  487.4 7.3 convert_dynamic-update-slice_fusion
  506.0 133.0 %reduce-scatter.5.cloned.1.call-done = bf16[1,1192,1024]{2,1,0:T(8,128)(2,1)} async-done(((bf16[8,1192,1024]{2,1,0:T(8,128)(2,1)}), bf16[1,1192,1024]{2,1,0:T(8,128)(2,1)}) %reduce-scatter.5.cloned.1.call-update) | async-done | bytes 2441232 | tf_op jit(solution)/shard_map/reduce_scatter | solution.py:202
  639.1 10.2 %fusion.77 = bf16[1,512,1024]{2,1,0:T(8,128)(2,1)} fusion(f32[1,512,1024]{2,1,0:T(8,128)S(1)} %copy-done.3, bf16[2816,1024]{1,0:T(8,128)(2,1)} %bitcast.427, f32[512,2816]{1,0:T(8,128)} %get-tuple-element.458, f32[512,2816]{1,0:T(8,128)} %copy-done.56, pred[512]{0:T(512)(128)(4,1)S(1)} %copy-done.54), kind=kOutput, calls=%fused_computation.119 | convolution fusion | flops 2963013632 | bytes 20447744 | tf_op jit(solution)/shard_map/srf,fd->srd/dot_general | solution.py:294
  652.1 113.5 %all-reduce.6.cloned.1.call-done = (bf16[1,392,1024]{2,1,0:T(8,128)(2,1)}, bf16[1,1192,1024]{2,1,0:T(8,128)(2,1)}) async-done(((bf16[1,392,1024]{2,1,0:T(8,128)(2,1)}, bf16[1,1192,1024]{2,1,0:T(8,128)(2,1)}), (bf16[1,392,1024]{2,1,0:T(8,128)(2,1)}, bf16[1,1192,1024]{2,1,0:T(8,128)(2,1)})) %all-reduce.6.cloned.1.call-update) | async-done | bytes 3244048 | tf_op jit(solution)/shard_map/psum | solution.py:203
  (269 shorter events, 159.6 us)
Async XLA Ops:
  7.2 9.1 %copy-start.41 = (bf16[128,2816]{1,0:T(8,128)(2,1)S(1)}, bf16[128,2816]{1,0:T(8,128)(2,1)}, u32[]{:S(2)}) copy-start(bf16[128,2816]{1,0:T(8,128)(2,1)} %param.29) | copy-start | bytes 2162692
  7.2 9.9 %copy-start.42 = (bf16[128,2816]{1,0:T(8,128)(2,1)S(1)}, bf16[128,2816]{1,0:T(8,128)(2,1)}, u32[]{:S(2)}) copy-start(bf16[128,2816]{1,0:T(8,128)(2,1)} %param.30) | copy-start | bytes 2162692
  7.2 57.8 %all-gather.5.cloned.1.call-start = ((), (), s32[]{:S(2)}) async-start(), calls=%async_computation.4 | async-start | bytes 7225344 | tf_op jit(solution)/shard_map/all_gather | solution.py:189
  16.2 194.2 %all-gather.7.cloned.1.call-start = ((), (), s32[]{:S(2)}) async-start(), calls=%async_computation.5 | async-start | bytes 21823488 | tf_op jit(solution)/shard_map/all_gather | solution.py:189
  19.7 486.4 %reduce-scatter.3.cloned.1.call-start = ((), (), s32[]{:S(2)}) async-start(), calls=%async_computation.2 | async-start | bytes 7225344 | tf_op jit(solution)/shard_map/reduce_scatter | solution.py:202
  20.0 67.0 %copy-start.50 = (f32[512]{0:T(512)}, f32[512]{0:T(512)S(1)}, u32[]{:S(2)}) copy-start(f32[512]{0:T(512)S(1)} %add_rsqrt_fusion.1) | copy-start | bytes 6148
  21.0 67.4 %copy-start.43 = (f32[512,32]{0,1:T(8,128)}, f32[512,32]{0,1:T(8,128)S(1)}, u32[]{:S(2)}) copy-start(f32[512,32]{0,1:T(8,128)S(1)} %get-tuple-element.450) | copy-start | bytes 196612
  66.6 20.5 %copy-start.47 = (f32[1024]{0:T(1024)}, f32[1024]{0:T(1024)S(1)}, u32[]{:S(2)}) copy-start(f32[1024]{0:T(1024)S(1)} %get-tuple-element.447) | copy-start | bytes 12292
  66.6 7.4 copy-start.55
  90.1 8.8 %copy-start.18 = (bf16[1,512,16,32]{1,3,2,0:T(8,128)(2,1)}, bf16[1,512,16,32]{1,3,2,0:T(8,128)(2,1)S(1)}, u32[]{:S(2)}) copy-start(bf16[1,512,16,32]{1,3,2,0:T(8,128)(2,1)S(1)} %get-tuple-element.444) | copy-start | bytes 1572868
  90.1 8.8 %copy-start.20 = (bf16[1,512,16,32]{1,3,2,0:T(8,128)(2,1)}, bf16[1,512,16,32]{1,3,2,0:T(8,128)(2,1)S(1)}, u32[]{:S(2)}) copy-start(bf16[1,512,16,32]{1,3,2,0:T(8,128)(2,1)S(1)} %get-tuple-element.445) | copy-start | bytes 1572868
  91.8 85.7 %collective-permute-start = (bf16[2,1,512,16,64]{2,4,3,1,0:T(8,128)(2,1)}, bf16[2,1,512,16,64]{2,4,3,1,0:T(8,128)(2,1)}, u32[]{:S(2)}, u32[]{:S(2)}) collective-permute-start(bf16[2,1,512,16,64]{2,4,3,1,0:T(8,128)(2,1)} %pad_maximum_fusion.1), channel_id=1, source_target_pairs={{0,1},{2,3},{4,5},{6,7},{8,9},{10,11},{12,13},{14,15},{16,17},{18,... | collective-permute-start | bytes 6291464 | tf_op jit(solution)/shard_map/ppermute | solution.py:273
  243.7 11.9 %copy-start.49 = (f32[1024]{0:T(1024)S(1)}, f32[1024]{0:T(1024)}, u32[]{:S(2)}) copy-start(f32[1024]{0:T(1024)} %get-tuple-element.446) | copy-start | bytes 12292
  255.7 8.2 %slice-start.4 = ((s8[5767168]{0:T(1024)(128)(4,1)}), s8[4194304]{0:T(1024)(128)(4,1)S(1)}, s32[]{:S(2)}) async-start(s8[5767168]{0:T(1024)(128)(4,1)} %bitcast.424), calls=%async_computation.11 | async-start | bytes 8388608
  263.9 6.4 copy-start.56
  263.9 6.4 copy-start.36
  264.0 6.4 copy-start.53
  264.0 17.5 %slice-start.2 = ((s8[5767168]{0:T(1024)(128)(4,1)}), s8[4194304]{0:T(1024)(128)(4,1)S(1)}, s32[]{:S(2)}) async-start(s8[5767168]{0:T(1024)(128)(4,1)} %bitcast.422), calls=%async_computation.9 | async-start | bytes 8388608
  270.4 11.1 %slice-start.3 = ((s8[5767168]{0:T(1024)(128)(4,1)}), s8[1572864]{0:T(1024)(128)(4,1)S(1)}, s32[]{:S(2)}) async-start(s8[5767168]{0:T(1024)(128)(4,1)} %bitcast.422), calls=%async_computation.10 | async-start | bytes 3145728
  303.6 8.2 %copy-start.32 = (bf16[2,1,512,8,64]{2,4,3,1,0:T(8,128)(2,1)S(1)}, bf16[2,1,512,8,64]{2,4,3,1,0:T(8,128)(2,1)}, u32[]{:S(2)}) copy-start(bf16[2,1,512,8,64]{2,4,3,1,0:T(8,128)(2,1)} %get-tuple-element.723) | copy-start | bytes 3145732 | tf_op jit(solution)/shard_map/while
  335.8 8.2 %copy-start.32 = (bf16[2,1,512,8,64]{2,4,3,1,0:T(8,128)(2,1)S(1)}, bf16[2,1,512,8,64]{2,4,3,1,0:T(8,128)(2,1)}, u32[]{:S(2)}) copy-start(bf16[2,1,512,8,64]{2,4,3,1,0:T(8,128)(2,1)} %get-tuple-element.723) | copy-start | bytes 3145732 | tf_op jit(solution)/shard_map/while
  370.4 49.9 %copy-start.25 = (f32[2,1,1024,8,64]{2,4,3,1,0:T(8,128)S(1)}, f32[2,1,1024,8,64]{2,4,3,1,0:T(8,128)}, u32[]{:S(2)}) copy-start(f32[2,1,1024,8,64]{2,4,3,1,0:T(8,128)} %get-tuple-element.222) | copy-start | bytes 12582916
  370.4 49.3 %collective-permute-start.1 = (bf16[2,1,512,16,64]{2,4,3,1,0:T(8,128)(2,1)S(1)}, bf16[2,1,512,16,64]{2,4,3,1,0:T(8,128)(2,1)S(1)}, u32[]{:S(2)}, u32[]{:S(2)}) collective-permute-start(bf16[2,1,512,16,64]{2,4,3,1,0:T(8,128)(2,1)S(1)} %pad_maximum_fusion.2), channel_id=1, source_target_pairs={{1,0},{3,2},{5,4},{7,6},{9,8},{11,10},{13,12},{15,14},{17,16},{19,... | collective-permute-start | bytes 6291464 | tf_op jit(solution)/shard_map/ppermute | solution.py:333
  443.3 195.7 %reduce-scatter.5.cloned.1.call-start = ((), (), s32[]{:S(2)}) async-start(), calls=%async_computation.3 | async-start | bytes 21970944 | tf_op jit(solution)/shard_map/reduce_scatter | solution.py:202
  456.7 11.9 %copy-start.31 = (bf16[512,1024]{1,0:T(8,128)(2,1)S(1)}, bf16[512,1024]{1,0:T(8,128)(2,1)}, u32[]{:S(2)}) copy-start(bf16[512,1024]{1,0:T(8,128)(2,1)} %copy-done.30) | copy-start | bytes 3145732
  475.4 11.9 %copy-start.38 = (bf16[1,512,1024]{2,1,0:T(8,128)(2,1)S(1)}, bf16[1,512,1024]{2,1,0:T(8,128)(2,1)}, u32[]{:S(2)}) copy-start(bf16[1,512,1024]{2,1,0:T(8,128)(2,1)} %param.23) | copy-start | bytes 3145732
  475.4 11.9 %copy-start.54 = (pred[512]{0:T(512)(128)(4,1)S(1)}, pred[512]{0:T(512)(128)(4,1)}, u32[]{:S(2)}) copy-start(pred[512]{0:T(512)(128)(4,1)} %fusion.100) | copy-start | bytes 1540
  475.4 22.4 %slice-start = ((s8[5767168]{0:T(1024)(128)(4,1)}), s8[1572864]{0:T(1024)(128)(4,1)S(1)}, s32[]{:S(2)}) async-start(s8[5767168]{0:T(1024)(128)(4,1)} %bitcast.401), calls=%async_computation.7 | async-start | bytes 3145728
  487.4 7.3 copy-start.1
  487.4 10.5 %slice-start.1 = ((s8[5767168]{0:T(1024)(128)(4,1)}), s8[4194304]{0:T(1024)(128)(4,1)S(1)}, s32[]{:S(2)}) async-start(s8[5767168]{0:T(1024)(128)(4,1)} %bitcast.401), calls=%async_computation.8 | async-start | bytes 8388608
  504.8 134.3 %copy-start.3 = (f32[1,512,1024]{2,1,0:T(8,128)S(1)}, f32[1,512,1024]{2,1,0:T(8,128)}, u32[]{:S(2)}) copy-start(f32[1,512,1024]{2,1,0:T(8,128)} %get-tuple-element.454) | copy-start | bytes 6291460
  504.8 260.8 %all-reduce.6.cloned.1.call-start = ((), (), s32[]{:S(2)}) async-start(), calls=%async_computation.6 | async-start | bytes 6488064 | tf_op jit(solution)/shard_map/psum | solution.py:203
  (47 other events, 148.7 us)
Sparse Core Ops, SparseCore 0:
  16.3 48.6 all-gather.4
  66.9 133.4 all-gather.6
  443.5 62.5 reduce-scatter.2
  509.5 129.4 reduce-scatter.4
  641.3 124.2 all-reduce.5

commit v2 on v1

--- a/solution.py
+++ b/solution.py
@@ -2,6 +2,7 @@
 import jax.numpy as jnp
 from jax import lax
 from jax.sharding import PartitionSpec as P
+
 
 HEADS = 16
 HEAD_DIM = 64
@@ -180,45 +181,45 @@
 GROUP = ("fsdp", "ctx")
 
 
-def as_rows(block, width):
-    return block.reshape(-1, width)
-
-
-def gather_rows(pieces, width):
-    flat = [as_rows(p, width) for p in pieces]
-    gathered = lax.all_gather(jnp.concatenate(flat, axis=0), GROUP, axis=0, tiled=False)
-    n_group = gathered.shape[0]
+def gather_blocks(pieces):
+    packed = jnp.concatenate(pieces, axis=0)
+    gathered = lax.all_gather(packed, GROUP, axis=0, tiled=False)
     fulls, offset = [], 0
-    for piece, rows in zip(pieces, flat):
-        part = gathered[:, offset : offset + rows.shape[0], :]
-        fulls.append(part.reshape((n_group * piece.shape[0],) + piece.shape[1:]))
-        offset += rows.shape[0]
+    for piece in pieces:
+        fulls.append(gathered[:, offset : offset + piece.shape[0], :])
+        offset += piece.shape[0]
     return fulls
 
 
-def scatter_rows(fulls, width, n_group):
-    flat = [f.reshape(n_group, -1, width) for f in fulls]
-    packed = jnp.concatenate(flat, axis=1).astype(jnp.bfloat16)
+def rep_sum(x):
+    n_rep = lax.axis_size("rep")
+    if n_rep != 4:
+        return lax.psum(x, "rep")
+    me = lax.axis_index("rep")
+    folded = (x.astype(jnp.float32) + lax.ppermute(x, "rep", [(0, 1), (3, 2)]).astype(jnp.float32)).astype(x.dtype)
+    total = (
+        folded.astype(jnp.float32) + lax.ppermute(folded, "rep", [(1, 2), (2, 1)]).astype(jnp.float32)
+    ).astype(x.dtype)
+    sent_out = lax.ppermute(total, "rep", [(1, 0), (2, 3)])
+    return jnp.where((me == 0) | (me == 3), sent_out, total)
+
+
+def scatter_blocks(blocks, by_permutes):
+    packed = jnp.concatenate(blocks, axis=1).astype(jnp.bfloat16)
     summed = lax.psum_scatter(packed, GROUP, scatter_dimension=0, tiled=True)
-    summed = lax.psum(summed, "rep")[0].astype(jnp.float32)
+    summed = (rep_sum(summed) if by_permutes else lax.psum(summed, "rep"))[0].astype(jnp.float32)
     parts, offset = [], 0
-    for full, rows in zip(fulls, flat):
-        part = summed[offset : offset + rows.shape[1], :]
-        parts.append(part.reshape((full.shape[0] // n_group,) + full.shape[1:]))
-        offset += rows.shape[1]
+    for block in blocks:
+        parts.append(summed[offset : offset + block.shape[1], :])
+        offset += block.shape[1]
     return parts
 
 
-def gain_block(full, n_group, width):
-    own = full.reshape(n_group, 1, -1)
-    padded = jnp.pad(own, ((0, 0), (0, 7), (0, width - own.shape[-1])))
-    return padded.reshape(n_group * 8, width)
-
-
-def gain_rows(first, second, width):
-    row = jnp.zeros((8, width), first.dtype)
-    row = row.at[0, : first.shape[-1]].set(first)
-    return row.at[0, first.shape[-1] : first.shape[-1] + second.shape[-1]].set(second)
+def gain_block(first, second, width):
+    lead = first.shape[:-1]
+    row = jnp.concatenate([first, second], axis=-1)
+    row = jnp.pad(row, [(0, 0)] * len(lead) + [(0, width - row.shape[-1])])
+    return jnp.pad(row[..., None, :], [(0, 0)] * len(lead) + [(0, 7), (0, 0)])
 
 
 def shards(
@@ -240,15 +241,23 @@
     n_ctx = lax.axis_size("ctx")
     n_group = lax.axis_size("fsdp") * n_ctx
     own_rows = gain_attn.shape[0]
-    full_query, full_key, full_value, gains = gather_rows(
-        [w_query, w_key, w_value, gain_rows(gain_attn, gain_mlp, model_width)], model_width
-    )
-    gains = gains.reshape(n_group, 8, model_width)[:, 0, :]
-    full_gain_attn = gains[:, :own_rows].reshape(-1)
-    full_gain_mlp = gains[:, own_rows : 2 * own_rows].reshape(-1)
-    full_out, full_gate, full_up, full_down = gather_rows(
-        [w_out, w_gate, w_up, w_down], model_width
-    )
+    ff_width = w_gate.shape[1]
+    attn_width = w_query.shape[1]
+    qkv_width = 3 * attn_width
+    (qkv_blocks, gain_rows) = gather_blocks(
+        [
+            jnp.concatenate([w_query, w_key, w_value], axis=1),
+            gain_block(gain_attn, gain_mlp, qkv_width),
+        ]
+    )
+    full_qkv = qkv_blocks.reshape(n_group * own_rows, qkv_width)
+    full_gain_attn = gain_rows[:, 0, :own_rows].reshape(-1)
+    full_gain_mlp = gain_rows[:, 0, own_rows : 2 * own_rows].reshape(-1)
+    out_blocks, down_blocks = gather_blocks([w_out, w_down])
+    full_out = out_blocks.reshape(-1, model_width)
+    full_down = down_blocks.reshape(-1, model_width)
+    (gu_blocks,) = gather_blocks([jnp.concatenate([w_gate, w_up], axis=1)])
+    full_gu = gu_blocks.reshape(n_group * own_rows, 2 * ff_width)
     ctx_index = lax.axis_index("ctx")
     q_pos = ctx_index * slot_rows + jnp.arange(slot_rows)
     live_rows = q_pos[None, :] < lengths[:, None]
@@ -258,9 +267,10 @@
     mlp_scale = full_gain_mlp.astype(jnp.float32)
     normed, inv_attn = normalize(inputs, attn_scale)
     normed_low = normed.astype(jnp.bfloat16)
-    q_pre = jnp.einsum("srd,de->sre", normed_low, full_query, preferred_element_type=jnp.float32)
-    k_pre = jnp.einsum("srd,de->sre", normed_low, full_key, preferred_element_type=jnp.float32)
-    v_pre = jnp.einsum("srd,de->sre", normed_low, full_value, preferred_element_type=jnp.float32)
+    qkv_pre = jnp.einsum("srd,de->sre", normed_low, full_qkv, preferred_element_type=jnp.float32)
+    q_pre = qkv_pre[..., :attn_width]
+    k_pre = qkv_pre[..., attn_width : 2 * attn_width]
+    v_pre = qkv_pre[..., 2 * attn_width :]
     queries = rotate(q_pre.reshape(head_shape), q_pos, 1.0).astype(jnp.bfloat16)
     keys = rotate(k_pre.reshape(head_shape), q_pos, 1.0).astype(jnp.bfloat16)
     values = (
@@ -269,8 +279,7 @@
         .reshape(head_shape)
     )
     if n_ctx == 2:
-        shift_up = [(0, 1)]
-        earlier = lax.ppermute(jnp.stack([keys, values]), "ctx", shift_up)
+        earlier = lax.ppermute(jnp.stack([keys, values]), "ctx", [(0, 1)])
         slot_k = jnp.concatenate([earlier[0], keys], axis=1)
         slot_v = jnp.concatenate([earlier[1], values], axis=1)
         k_pos = jnp.concatenate([q_pos - slot_rows, q_pos])
@@ -287,8 +296,9 @@
     residual = inputs + branch
     normed_mlp, inv_mlp = normalize(residual, mlp_scale)
     mlp_low = normed_mlp.astype(jnp.bfloat16)
-    gate_proj = jnp.einsum("srd,df->srf", mlp_low, full_gate, preferred_element_type=jnp.float32)
-    up_proj = jnp.einsum("srd,df->srf", mlp_low, full_up, preferred_element_type=jnp.float32)
+    gu_proj = jnp.einsum("srd,df->srf", mlp_low, full_gu, preferred_element_type=jnp.float32)
+    gate_proj = gu_proj[..., :ff_width]
+    up_proj = gu_proj[..., ff_width:]
     sigmoid_gate = jax.nn.sigmoid(gate_proj)
     hidden = (gate_proj * sigmoid_gate * up_proj).astype(jnp.bfloat16)
     final = residual + jnp.einsum(
@@ -303,37 +313,37 @@
         g_hidden * up_proj * sigmoid_gate * (1.0 + gate_proj * (1.0 - sigmoid_gate))
     ).astype(jnp.bfloat16)
     up_gradient = (g_hidden * gate_proj * sigmoid_gate).astype(jnp.bfloat16)
-    grad_gate = jnp.einsum(
-        "srd,srf->df", mlp_low, gate_gradient, preferred_element_type=jnp.float32
-    )
-    grad_up = jnp.einsum("srd,srf->df", mlp_low, up_gradient, preferred_element_type=jnp.float32)
+    gu_gradient = jnp.concatenate([gate_gradient, up_gradient], axis=-1)
+    grad_gu = jnp.einsum("srd,srf->df", mlp_low, gu_gradient, preferred_element_type=jnp.float32)
     g_normed_mlp = jnp.einsum(
-        "srf,df->srd", gate_gradient, full_gate, preferred_element_type=jnp.float32
-    ) + jnp.einsum("srf,df->srd", up_gradient, full_up, preferred_element_type=jnp.float32)
+        "srf,df->srd", gu_gradient, full_gu, preferred_element_type=jnp.float32
+    )
     g_mlp_in, grad_gain_mlp = normalize_back(residual, inv_mlp, mlp_scale, g_normed_mlp)
     g_residual = output_gradient + g_mlp_in
     g_branch = g_residual.astype(jnp.bfloat16)
     grad_out = jnp.einsum("sre,srd->ed", att_flat, g_branch, preferred_element_type=jnp.float32)
-    part_down, part_gate, part_up, part_out, part_gain_mlp = scatter_rows(
-        [grad_down, grad_gate, grad_up, grad_out, gain_block(grad_gain_mlp, n_group, model_width)],
-        model_width,
-        n_group,
-    )
+    gu_block = grad_gu.reshape(n_group, own_rows, 2 * ff_width).astype(jnp.bfloat16)
+    od_blocks = [
+        grad_out.reshape(n_group, -1, model_width).astype(jnp.bfloat16),
+        grad_down.reshape(n_group, -1, model_width).astype(jnp.bfloat16),
+    ]
     g_attended = (
         jnp.einsum("srd,ed->sre", g_branch, full_out, preferred_element_type=jnp.float32)
         .astype(jnp.bfloat16)
         .reshape(head_shape)
     )
+    gu_block, od_blocks, g_attended = lax.optimization_barrier((gu_block, od_blocks, g_attended))
+    (part_gu,) = scatter_blocks([gu_block], True)
+    part_out, part_down = scatter_blocks(od_blocks, True)
     row_dots = jnp.sum(g_attended.astype(jnp.float32) * attended.astype(jnp.float32), axis=-1)
     g_queries, slot_dk, slot_dv = attend_backward(
         queries, slot_k, slot_v, g_attended, row_dots, attn_lse, q_pos, k_pos, lengths
     )
     if n_ctx == 2:
-        shift_down = [(1, 0)]
         later = lax.ppermute(
             jnp.stack([slot_dk[:, :slot_rows], slot_dv[:, :slot_rows]]).astype(jnp.bfloat16),
             "ctx",
-            shift_down,
+            [(1, 0)],
         ).astype(jnp.float32)
         g_keys = slot_dk[:, slot_rows:] + later[0]
         g_values = slot_dv[:, slot_rows:] + later[1]
@@ -352,36 +362,35 @@
     gv_rounded = g_values.reshape(flat_shape).astype(jnp.bfloat16).astype(jnp.float32)
     d_first = 0.5 * gv_rounded
     gv_half = d_first.astype(jnp.bfloat16)
-    grad_query = jnp.einsum("srd,sre->de", normed_low, gq_low, preferred_element_type=jnp.float32)
-    grad_key = jnp.einsum("srd,sre->de", normed_low, gk_low, preferred_element_type=jnp.float32)
-    grad_value = jnp.einsum("srd,sre->de", normed_low, gv_half, preferred_element_type=jnp.float32)
-    g_normed = jnp.einsum("sre,de->srd", gq_low, full_query, preferred_element_type=jnp.float32)
-    g_normed = g_normed + jnp.einsum(
-        "sre,de->srd", gk_low, full_key, preferred_element_type=jnp.float32
-    )
-    g_normed = g_normed + jnp.einsum(
-        "sre,de->srd", gv_half, full_value, preferred_element_type=jnp.float32
-    )
+    g_qkv = jnp.concatenate([gq_low, gk_low, gv_half], axis=-1)
+    grad_qkv = jnp.einsum("srd,sre->de", normed_low, g_qkv, preferred_element_type=jnp.float32)
+    g_normed = jnp.einsum("sre,de->srd", g_qkv, full_qkv, preferred_element_type=jnp.float32)
     g_attn_in, grad_gain_attn = normalize_back(inputs, inv_attn, attn_scale, g_normed)
     d_tokens = g_residual + g_attn_in
-    part_query, part_key, part_value, part_gain_attn = scatter_rows(
-        [grad_query, grad_key, grad_value, gain_block(grad_gain_attn, n_group, model_width)],
-        model_width,
-        n_group,
+    part_qkv, part_gains = scatter_blocks(
+        [
+            grad_qkv.reshape(n_group, own_rows, qkv_width),
+            gain_block(
+                grad_gain_attn.reshape(n_group, own_rows),
+                grad_gain_mlp.reshape(n_group, own_rows),
+                qkv_width,
+            ),
+        ],
+        False,
     )
     return (
         output,
         d_tokens,
         d_first,
-        part_query,
-        part_key,
-        part_value,
+        part_qkv[:, :attn_width],
+        part_qkv[:, attn_width : 2 * attn_width],
+        part_qkv[:, 2 * attn_width :],
         part_out,
-        part_gate,
-        part_up,
+        part_gu[:, :ff_width],
+        part_gu[:, ff_width:],
         part_down,
-        part_gain_attn[0, :own_rows],
-        part_gain_mlp[0, :own_rows],
+        part_gains[0, :own_rows],
+        part_gains[0, own_rows : 2 * own_rows],
     )
 
 
@@ -415,4 +424,5 @@
         P(("fsdp", "ctx")),
         P(("fsdp", "ctx")),
     )
+
     return jax.shard_map(shards, mesh=mesh, in_specs=in_specs, out_specs=out_specs, check_vma=False)

time: 794 us -> 648 us (0.82)
  waiting for transfers between devices: 416 us -> 323 us
  local copies, waits for them, and re-layouts: 143 us -> 65 us
  other arithmetic: 50.5 us -> 69 us
  starting transfers between devices: 7.11 us -> 17.1 us
    reduce_scatter x2 -> x3, waiting for transfers between devices: 134 us -> 7.14 us  [scatter_blocks(): summed = lax.psum_scatter(packed, GROUP, scatter_dimension=0, tiled=True)]
    psum x1, waiting for transfers between devices: 113 us -> 44.3 us  [scatter_blocks(): lax.psum(summed, 'rep')]
    all_gather x2 -> x3, waiting for transfers between devices: 44 us -> 100 us  [gather_blocks(): gathered = lax.all_gather(packed, GROUP, axis=0, tiled=False)]
    reshape x10 -> x0, local copies, waits for them, and re-layouts: 52.3 us -> none  [the longest x2 23.8 us: scatter_rows(): flat = [f.reshape(n_group, -1, width) for f in fulls]]
    ppermute x1 -> x7, waiting for transfers between devices: 77.3 us -> 108 us  [the longest x2 47 us: rep_sum(): lax.ppermute(x, 'rep', [(0, 1), (3, 2)]).astype(jnp.float32)]
    ppermute x1, waiting for transfers between devices: 47.6 us -> 62.5 us  [shards(): lax.ppermute(jnp.stack([slot_dk[:, :slot_rows], slot_dv[:, :slot_rows]])....]
    unnamed x116 -> x92, local copies, waits for them, and re-layouts: 16.7 us -> 3.23 us
    concatenate x3 -> x6, other arithmetic: 6.95 us -> 17.4 us  [the longest x2 11.4 us: scatter_blocks(): packed = jnp.concatenate(blocks, axis=1).astype(jnp.bfloat16)]
  transfers between devices with their start and end apart: 7 -> 15, of which waited for: 6 -> 11; matrix products, arithmetic and copies ran while one was open for 17% -> 29% of each run, Pallas kernels for 0% -> 0%
where the time goes in v2:
time: 648 us; the launch traced here: 640 us
  waiting for transfers between devices  323 us (50%)
  matrix products  150 us (23%)
  other arithmetic  69 us (11%)
  local copies, waits for them, and re-layouts  65 us (10%)
  starting transfers between devices  17.1 us (3%)
  between operations  15.7 us (2%)
    all_gather x3, waiting for transfers between devices, gather_blocks(): gathered = lax.all_gather(packed, GROUP, axis=0, tiled=False)  100 us
    ppermute x1, waiting for transfers between devices, shards(): lax.ppermute(jnp.stack([slot_dk[:, :slot_rows], slot_dv[:, :slot_rows]])....  62.5 us
    ppermute x2, waiting for transfers between devices, rep_sum(): lax.ppermute(x, 'rep', [(0, 1), (3, 2)]).astype(jnp.float32)  47 us
    psum x1, waiting for transfers between devices, scatter_blocks(): lax.psum(summed, 'rep')  44.3 us
    ppermute x2, waiting for transfers between devices, rep_sum(): sent_out = lax.ppermute(total, 'rep', [(1, 0), (2, 3)])  42.2 us
    dot_general x2, matrix products, one_block(): jnp.einsum('sqhe,skhe->shqk', g_rows, v_group, preferred_element_type=jnp...  20 us
    ppermute x1, waiting for transfers between devices, shards(): earlier = lax.ppermute(jnp.stack([keys, values]), 'ctx', [(0, 1)])  19.2 us
    while x24, local copies, waits for them, and re-layouts  17.2 us
  transfers between devices with their start and end apart: 15, of which 11 were waited for; matrix products, arithmetic and copies ran while one was open for 29% of the time, Pallas kernels for 0%

profile of v2, /device:TPU:0, one launch (start us, length us, event | category | flops | bytes accessed | tf_op | source)
XLA Modules:
  0.0 640.2 jit_solution(2237879931814931933)
XLA Ops:
  14.9 45.3 %all-gather.7.cloned.1.call-done = bf16[1088,3072]{1,0:T(8,128)(2,1)} async-done(((bf16[136,3072]{1,0:T(8,128)(2,1)}), bf16[1088,3072]{1,0:T(8,128)(2,1)}) %all-gather.7.cloned.1.call-update) | async-done | bytes 6684688 | tf_op jit(solution)/shard_map/all_gather | solution.py:186
  90.7 41.3 %all-gather.9.cloned.1.call-done = bf16[3840,1024]{1,0:T(8,128)(2,1)} async-done(((bf16[480,1024]{1,0:T(8,128)(2,1)}), bf16[3840,1024]{1,0:T(8,128)(2,1)}) %all-gather.9.cloned.1.call-update) | async-done | bytes 7864336 | tf_op jit(solution)/shard_map/all_gather | solution.py:186
  135.0 5.8 slice.175
  140.8 19.2 %collective-permute-done = bf16[2,1,512,16,64]{2,4,3,1,0:T(8,128)(2,1)} collective-permute-done((bf16[2,1,512,16,64]{2,4,3,1,0:T(8,128)(2,1)}, bf16[2,1,512,16,64]{2,4,3,1,0:T(8,128)(2,1)}, u32[]{:S(2)}, u32[]{:S(2)}) %collective-permute-start) | collective-permute-done | bytes 2097184 | tf_op jit(solution)/shard_map/ppermute | solution.py:282
  163.7 28.9 %while.30 = (s32[]{:T(128)}, bf16[2,1,512,8,64]{2,4,3,1,0:T(8,128)(2,1)}, f32[2,1,1,8,512]{4,3,2,1,0:T(8,128)S(1)}, bf16[2,1,1024,8,64]{2,4,3,1,0:T(8,128)(2,1)}...) while((s32[]{:T(128)}, ...), condition=%wide.region_4.5_spmd.clone.clone, body=%wide.region_1.4_spmd.clone.sunk.clone | while | flops 1125644800 | bytes 64637068 | solution.py:113
  172.5 5.7 fusion.179
  186.8 5.7 fusion.179
  192.6 4.7 multiply_reduce_fusion
  197.3 13.5 %all-gather.11.cloned.1.call-done = bf16[1024,5632]{1,0:T(8,128)(2,1)} async-done(((bf16[128,5632]{1,0:T(8,128)(2,1)}), bf16[1024,5632]{1,0:T(8,128)(2,1)}) %all-gather.11.cloned.1.call-update) | async-done | bytes 11534352 | tf_op jit(solution)/shard_map/all_gather | solution.py:186
  210.8 12.4 %convolution_bitcast_fusion = f32[1,512,5632]{2,1,0:T(8,128)} fusion(bf16[1024,5632]{1,0:T(8,128)(2,1)} %all-gather.11.cloned.1.call-done, f32[1,512,1024]{2,1,0:T(8,128)} %get-tuple-element.385, f32[1024]{0:T(1024)S(1)} %bitcast.400, f32[512]{0:T(512)S(1)} %add_rsqrt_fusion), kind=kOutput, calls=%fused_computation.67 | convolution fusion | flops 5907152896 | bytes 25171968 | tf_op jit(solution)/shard_map/srd,df->srf/dot_general | solution.py:299
  223.3 10.5 %fusion.57 = (bf16[1,512,2816]{2,1,0:T(8,128)(2,1)}, bf16[1,512,2816]{2,1,0:T(8,128)(2,1)}, bf16[1,512,2816]{2,1,0:T(8,128)(2,1)}) fusion(f32[1,512,5632]{2,1,0:T(8,128)} %convolution_bitcast_fusion, bf16[2816,1024]{1,0:T(8,128)(2,1)S(1)} %bitcast.373, bf16[1,512,1024]{2,1,0:T(8,128)(2,1)S(1)} %copy-done.30, pred[512]{0:T(512)(128)(4,1)S(1)} %copy-done.48), kind=kOutput, calls=%fused_computation.78 | convolution fusion | flops 2977431552 | bytes 27001344 | tf_op jit(solution)/shard_map/srd,fd->srf/dot_general | solution.py:311
  238.3 13.7 %fusion.82 = (bf16[1024]{0:T(1024)(128)(2,1)}, f32[512]{0:T(512)S(1)}, f32[512,1024]{1,0:T(8,128)}) fusion(f32[1,512,1024]{2,1,0:T(8,128)} %get-tuple-element.385, f32[512]{0:T(512)S(1)} %add_rsqrt_fusion, f32[1024]{0:T(1024)S(1)} %bitcast.401, bf16[1024,5632]{1,0:T(8,128)(2,1)} %all-gather.11.cloned.1.call-done, ...), kind=kOutput, calls=%fused_computation.125 | convolution fusion | flops 5920258560 | bytes 21506048 | tf_op jit(solution)/shard_map/srf,df->srd/dot_general | solution.py:318
  268.2 5.2 convolution_convert_fusion.2
  273.4 9.1 %convolution_convert_fusion = bf16[8,128,5632]{2,1,0:T(8,128)(2,1)} fusion(bf16[8,128,512]{2,1,0:T(8,128)(2,1)S(1)} %bitcast.392, bf16[1,512,2816]{2,1,0:T(8,128)(2,1)S(1)} %copy-done.51, bf16[1,512,2816]{2,1,0:T(8,128)(2,1)S(1)} %copy-done.50), kind=kOutput, calls=%fused_computation.66 | convolution fusion | flops 5922881536 | bytes 18350080 | tf_op jit(solution)/shard_map/srd,srf->df/dot_general | solution.py:317
  284.5 7.9 %pad_maximum_fusion = bf16[8,480,1024]{2,1,0:T(8,128)(2,1)} fusion(bf16[8,352,1024]{2,1,0:T(8,128)(2,1)} %convolution_convert_fusion.2, bf16[8,128,1024]{2,1,0:T(8,128)(2,1)} %convolution_convert_fusion.3), kind=kLoop, calls=%fused_computation.68 | loop fusion | flops 15728640 | bytes 15728640 | tf_op jit(solution)/shard_map/concatenate | solution.py:208
  292.5 67.0 %while.31 = (s32[]{:T(128)}, f32[2,1,512,8,64]{2,4,3,1,0:T(8,128)}, f32[2,1,1024,8,64]{2,4,3,1,0:T(8,128)}, f32[2,1,1024,8,64]{2,4,3,1,0:T(8,128)}, bf16[2,1,102...) while((s32[]{:T(128)}, f32[2,1,512,8,64]{2,4,3,1,0:T(8,128)}, ...), condition=%wide.region_9.10_spmd.clone.clone, body=%wide.region_8.9_spmd.clone.sunk.clone | while | flops 2728659456 | bytes 200938768 | solution.py:177
  296.5 7.5 %copy-done = f32[8,512,1024]{2,1,0:T(8,128)} copy-done((f32[8,512,1024]{2,1,0:T(8,128)}, f32[8,512,1024]{2,1,0:T(8,128)S(1)}, u32[]{:S(2)}) %copy-start) | copy-done | bytes 16777240 | tf_op jit(solution)/shard_map/while
  304.0 5.8 bitcast_dynamic-update-slice_fusion.11
  309.8 10.4 %multiply_convert_fusion.6 = bf16[8,512,1024]{2,1,0:T(8,128)(2,1)S(1)} fusion(f32[8,512,1024]{2,1,0:T(8,128)} %copy-done, f32[8,512]{1,0:T(8,128)S(1)} %dynamic-slice_bitcast_fusion.6, f32[8,512]{1,0:T(8,128)S(1)} %dynamic-slice_bitcast_fusion.7, pred[512,1024]{1,0:T(8,128)(4,1)S(1)} %and_and_fusion.7, ...), kind=kOutput, calls=%fused_computation.26.clone.1.clone | convolution fusion | flops 562036736 | bytes 27296768 | tf_op jit(solution)/shard_map/while/body/eval_jaxpr/while/body/eval_jaxpr/sqhe,skhe->shqk/dot_general | solution.py:143
  331.0 5.8 copy-done
  336.8 5.9 bitcast_dynamic-update-slice_fusion.11
  342.7 9.5 %multiply_convert_fusion.6 = bf16[8,512,1024]{2,1,0:T(8,128)(2,1)S(1)} fusion(f32[8,512,1024]{2,1,0:T(8,128)} %copy-done, f32[8,512]{1,0:T(8,128)S(1)} %dynamic-slice_bitcast_fusion.6, f32[8,512]{1,0:T(8,128)S(1)} %dynamic-slice_bitcast_fusion.7, pred[512,1024]{1,0:T(8,128)(4,1)S(1)} %and_and_fusion.7, ...), kind=kOutput, calls=%fused_computation.26.clone.1.clone | convolution fusion | flops 562036736 | bytes 27296768 | tf_op jit(solution)/shard_map/while/body/eval_jaxpr/while/body/eval_jaxpr/sqhe,skhe->shqk/dot_general | solution.py:143
  365.0 62.5 %collective-permute-done.1 = bf16[2,1,512,16,64]{2,4,3,1,0:T(8,128)(2,1)S(1)} collective-permute-done((bf16[2,1,512,16,64]{2,4,3,1,0:T(8,128)(2,1)S(1)}, bf16[2,1,512,16,64]{2,4,3,1,0:T(8,128)(2,1)S(1)}, u32[]{:S(2)}, u32[]{:S(2)}) %collective-permute-start.1) | collective-permute-done | bytes 2097184 | tf_op jit(solution)/shard_map/ppermute | solution.py:343
  442.7 7.5 %fusion.74 = (bf16[1024]{0:T(1024)(128)(2,1)S(1)}, f32[512]{0:T(512)S(1)}, f32[512,1024]{1,0:T(8,128)S(1)}) fusion(bf16[1,512,1024]{2,1,0:T(8,128)(2,1)S(1)} %copy-done.2, f32[512]{0:T(512)S(1)} %copy-done.46, f32[1024]{0:T(1024)S(1)} %bitcast.398, bf16[1024,3072]{1,0:T(8,128)(2,1)} %bitcast.369, bf16[1,512,1024]{2,1,0:T(8,128)(2,1)} %convert_element_type.336, ...), kind=kOutput, calls=%fused_computation.106 | convolution fusion | flops 3234331136 | bytes 12593152 | tf_op jit(solution)/shard_map/sre,de->srd/dot_general | solution.py:367
  452.9 5.0 convolution_convert_fusion.1
  466.5 30.7 %collective-permute-done.5 = bf16[1,128,5632]{2,1,0:T(8,128)(2,1)S(1)} collective-permute-done((bf16[1,128,5632]{2,1,0:T(8,128)(2,1)}, bf16[1,128,5632]{2,1,0:T(8,128)(2,1)S(1)}, u32[]{:S(2)}, u32[]{:S(2)}) %collective-permute-start.5) | collective-permute-done | bytes 1441824 | tf_op jit(solution)/shard_map/ppermute | solution.py:199
  500.7 16.3 %collective-permute-done.2 = bf16[1,480,1024]{2,1,0:T(8,128)(2,1)S(1)} collective-permute-done((bf16[1,480,1024]{2,1,0:T(8,128)(2,1)}, bf16[1,480,1024]{2,1,0:T(8,128)(2,1)S(1)}, u32[]{:S(2)}, u32[]{:S(2)}) %collective-permute-start.2) | collective-permute-done | bytes 983072 | tf_op jit(solution)/shard_map/ppermute | solution.py:199
  518.1 7.1 %reduce-scatter.4.cloned.1.call-done = bf16[1,136,3072]{2,1,0:T(8,128)(2,1)} async-done(((bf16[8,136,3072]{2,1,0:T(8,128)(2,1)}), bf16[1,136,3072]{2,1,0:T(8,128)(2,1)}) %reduce-scatter.4.cloned.1.call-update) | async-done | bytes 835600 | tf_op jit(solution)/shard_map/reduce_scatter | solution.py:209
  531.3 6.9 %fusion.87 = bf16[1,512,1024]{2,1,0:T(8,128)(2,1)} fusion(f32[1,512,1024]{2,1,0:T(8,128)S(1)} %copy-done.6, bf16[2816,1024]{1,0:T(8,128)(2,1)} %bitcast.372, bf16[1,512,2816]{2,1,0:T(8,128)(2,1)S(1)} %copy-done.17, pred[512]{0:T(512)(128)(4,1)S(1)} %copy-done.49), kind=kOutput, calls=%fused_computation.133 | convolution fusion | flops 2954362880 | bytes 11796992 | tf_op jit(solution)/shard_map/srf,fd->srd/dot_general | solution.py:304
  538.2 44.3 %all-reduce.6.cloned.1.call-done = bf16[136,3072]{1,0:T(8,128)(2,1)} async-done(((bf16[136,3072]{1,0:T(8,128)(2,1)}), bf16[136,3072]{1,0:T(8,128)(2,1)}) %all-reduce.6.cloned.1.call-update) | async-done | bytes 835600 | tf_op jit(solution)/shard_map/psum | solution.py:210
  585.5 21.1 %collective-permute-done.4 = bf16[1,480,1024]{2,1,0:T(8,128)(2,1)} collective-permute-done((bf16[1,480,1024]{2,1,0:T(8,128)(2,1)}, bf16[1,480,1024]{2,1,0:T(8,128)(2,1)}, u32[]{:S(2)}, u32[]{:S(2)}) %collective-permute-start.4) | collective-permute-done | bytes 983072 | tf_op jit(solution)/shard_map/ppermute | solution.py:203
  610.1 21.1 %collective-permute-done.7 = bf16[1,128,5632]{2,1,0:T(8,128)(2,1)S(1)} collective-permute-done((bf16[1,128,5632]{2,1,0:T(8,128)(2,1)S(1)}, bf16[1,128,5632]{2,1,0:T(8,128)(2,1)S(1)}, u32[]{:S(2)}, u32[]{:S(2)}) %collective-permute-start.7) | collective-permute-done | bytes 1441824 | tf_op jit(solution)/shard_map/ppermute | solution.py:203
  (239 shorter events, 156.1 us)
Async XLA Ops:
  7.2 53.1 %all-gather.7.cloned.1.call-start = ((), (), s32[]{:S(2)}) async-start(), calls=%async_computation.7 | async-start | bytes 7520256 | tf_op jit(solution)/shard_map/all_gather | solution.py:186
  10.2 121.7 %all-gather.9.cloned.1.call-start = ((), (), s32[]{:S(2)}) async-start(), calls=%async_computation.8 | async-start | bytes 8847360 | tf_op jit(solution)/shard_map/all_gather | solution.py:186
  12.2 198.6 %all-gather.11.cloned.1.call-start = ((), (), s32[]{:S(2)}) async-start(), calls=%async_computation.9 | async-start | bytes 12976128 | tf_op jit(solution)/shard_map/all_gather | solution.py:186
  13.5 448.0 %reduce-scatter.8.cloned.1.call-start = ((), (), s32[]{:S(2)}) async-start(), calls=%async_computation.6 | async-start | bytes 12976128 | tf_op jit(solution)/shard_map/reduce_scatter | solution.py:209
  14.0 51.4 %copy-start.45 = (f32[512]{0:T(512)}, f32[512]{0:T(512)S(1)}, u32[]{:S(2)}) copy-start(f32[512]{0:T(512)S(1)} %add_rsqrt_fusion.1) | copy-start | bytes 6148
  14.9 63.3 %copy-start.39 = (f32[512,32]{0,1:T(8,128)}, f32[512,32]{0,1:T(8,128)S(1)}, u32[]{:S(2)}) copy-start(f32[512,32]{0,1:T(8,128)S(1)} %get-tuple-element.383) | copy-start | bytes 196612
  81.4 9.2 %copy-start.25 = (bf16[1,512,16,32]{1,3,2,0:T(8,128)(2,1)S(1)}, bf16[1,512,16,32]{1,3,2,0:T(8,128)(2,1)}, u32[]{:S(2)}) copy-start(bf16[1,512,16,32]{1,3,2,0:T(8,128)(2,1)} %get-tuple-element.362) | copy-start | bytes 1572868
  81.4 9.2 %copy-start.26 = (bf16[1,512,16,32]{1,3,2,0:T(8,128)(2,1)S(1)}, bf16[1,512,16,32]{1,3,2,0:T(8,128)(2,1)}, u32[]{:S(2)}) copy-start(bf16[1,512,16,32]{1,3,2,0:T(8,128)(2,1)} %get-tuple-element.363) | copy-start | bytes 1572868
  83.7 76.4 %collective-permute-start = (bf16[2,1,512,16,64]{2,4,3,1,0:T(8,128)(2,1)}, bf16[2,1,512,16,64]{2,4,3,1,0:T(8,128)(2,1)}, u32[]{:S(2)}, u32[]{:S(2)}) collective-permute-start(bf16[2,1,512,16,64]{2,4,3,1,0:T(8,128)(2,1)} %pad_maximum_fusion.5), channel_id=1, source_target_pairs={{0,1},{2,3},{4,5},{6,7},{8,9},{10,11},{12,13},{14,15},{16,17},{18,... | collective-permute-start | bytes 6291464 | tf_op jit(solution)/shard_map/ppermute | solution.py:282
  192.6 18.3 %copy-start.44 = (f32[8,1,128]{2,1,0:T(1,128)S(1)}, f32[8,1,128]{2,1,0:T(1,128)}, u32[]{:S(2)}) copy-start(f32[8,1,128]{2,1,0:T(1,128)} %get-tuple-element.349) | copy-start | bytes 12292
  210.8 12.5 %copy-start.11 = (bf16[8,352,1024]{2,1,0:T(8,128)(2,1)S(1)}, bf16[8,352,1024]{2,1,0:T(8,128)(2,1)}, u32[]{:S(2)}) copy-start(bf16[8,352,1024]{2,1,0:T(8,128)(2,1)} %slice.175) | copy-start | bytes 17301508
  210.8 12.5 %copy-start.30 = (bf16[1,512,1024]{2,1,0:T(8,128)(2,1)S(1)}, bf16[1,512,1024]{2,1,0:T(8,128)(2,1)}, u32[]{:S(2)}) copy-start(bf16[1,512,1024]{2,1,0:T(8,128)(2,1)} %param.19) | copy-start | bytes 3145732
  210.8 12.5 %copy-start.48 = (pred[512]{0:T(512)(128)(4,1)S(1)}, pred[512]{0:T(512)(128)(4,1)}, u32[]{:S(2)}) copy-start(pred[512]{0:T(512)(128)(4,1)} %fusion.117) | copy-start | bytes 1540
  238.3 13.7 %copy-start.5 = (f32[1,512,1024]{2,1,0:T(8,128)S(1)}, f32[1,512,1024]{2,1,0:T(8,128)}, u32[]{:S(2)}) copy-start(f32[1,512,1024]{2,1,0:T(8,128)} %get-tuple-element.385) | copy-start | bytes 6291460
  238.3 13.7 %copy-start.31 = (bf16[1,512,1024]{2,1,0:T(8,128)(2,1)S(1)}, bf16[1,512,1024]{2,1,0:T(8,128)(2,1)}, u32[]{:S(2)}) copy-start(bf16[1,512,1024]{2,1,0:T(8,128)(2,1)} %param.19) | copy-start | bytes 3145732
  282.5 182.5 %reduce-scatter.6.cloned.1.call-start = ((), (), s32[]{:S(2)}) async-start(), calls=%async_computation.5 | async-start | bytes 8847360 | tf_op jit(solution)/shard_map/reduce_scatter | solution.py:209
  292.4 232.8 %reduce-scatter.4.cloned.1.call-start = ((), (), s32[]{:S(2)}) async-start(), calls=%async_computation.3 | async-start | bytes 7520256 | tf_op jit(solution)/shard_map/reduce_scatter | solution.py:209
  294.1 9.9 %copy-start.16 = (bf16[2,1,512,8,64]{2,4,3,1,0:T(8,128)(2,1)S(1)}, bf16[2,1,512,8,64]{2,4,3,1,0:T(8,128)(2,1)}, u32[]{:S(2)}) copy-start(bf16[2,1,512,8,64]{2,4,3,1,0:T(8,128)(2,1)} %get-tuple-element.652) | copy-start | bytes 3145732 | tf_op jit(solution)/shard_map/while
  296.5 7.5 %copy-start = (f32[8,512,1024]{2,1,0:T(8,128)}, f32[8,512,1024]{2,1,0:T(8,128)S(1)}, u32[]{:S(2)}) copy-start(f32[8,512,1024]{2,1,0:T(8,128)S(1)} %fusion.190) | copy-start | bytes 50331652 | tf_op jit(solution)/shard_map/while
  328.6 8.2 %copy-start.16 = (bf16[2,1,512,8,64]{2,4,3,1,0:T(8,128)(2,1)S(1)}, bf16[2,1,512,8,64]{2,4,3,1,0:T(8,128)(2,1)}, u32[]{:S(2)}) copy-start(bf16[2,1,512,8,64]{2,4,3,1,0:T(8,128)(2,1)} %get-tuple-element.652) | copy-start | bytes 3145732 | tf_op jit(solution)/shard_map/while
  363.2 64.9 %copy-start.21 = (f32[2,1,1024,8,64]{2,4,3,1,0:T(8,128)S(1)}, f32[2,1,1024,8,64]{2,4,3,1,0:T(8,128)}, u32[]{:S(2)}) copy-start(f32[2,1,1024,8,64]{2,4,3,1,0:T(8,128)} %get-tuple-element.203) | copy-start | bytes 12582916
  363.3 64.3 %collective-permute-start.1 = (bf16[2,1,512,16,64]{2,4,3,1,0:T(8,128)(2,1)S(1)}, bf16[2,1,512,16,64]{2,4,3,1,0:T(8,128)(2,1)S(1)}, u32[]{:S(2)}, u32[]{:S(2)}) collective-permute-start(bf16[2,1,512,16,64]{2,4,3,1,0:T(8,128)(2,1)S(1)} %pad_maximum_fusion.6), channel_id=1, source_target_pairs={{1,0},{3,2},{5,4},{7,6},{9,8},{11,10},{13,12},{15,14},{17,16},{19,... | collective-permute-start | bytes 6291464 | tf_op jit(solution)/shard_map/ppermute | solution.py:343
  442.7 7.5 %copy-start.4 = (f32[1,512,1024]{2,1,0:T(8,128)S(1)}, f32[1,512,1024]{2,1,0:T(8,128)}, u32[]{:S(2)}) copy-start(f32[1,512,1024]{2,1,0:T(8,128)} %copy-done.3) | copy-start | bytes 6291460
  461.4 121.0 %all-reduce.6.cloned.1.call-start = ((), (), s32[]{:S(2)}) async-start(), calls=%async_computation.4 | async-start | bytes 1671168 | tf_op jit(solution)/shard_map/psum | solution.py:210
  461.5 35.7 %collective-permute-start.5 = (bf16[1,128,5632]{2,1,0:T(8,128)(2,1)}, bf16[1,128,5632]{2,1,0:T(8,128)(2,1)S(1)}, u32[]{:S(2)}, u32[]{:S(2)}) collective-permute-start(bf16[1,128,5632]{2,1,0:T(8,128)(2,1)} %reduce-scatter.8.cloned.1.call-done), channel_id=1, source_target_pairs={{0,8},{24,16},{1,9},{25,17},{2,10},{26,18},{3,11},{27,19},{4,12},{... | collective-permute-start | bytes 4325384 | tf_op jit(solution)/shard_map/ppermute | solution.py:199
  465.0 52.0 %copy-start.35 = (bf16[1,480,1024]{2,1,0:T(8,128)(2,1)S(1)}, bf16[1,480,1024]{2,1,0:T(8,128)(2,1)}, u32[]{:S(2)}) copy-start(bf16[1,480,1024]{2,1,0:T(8,128)(2,1)} %reduce-scatter.6.cloned.1.call-done) | copy-start | bytes 2949124
  465.0 52.0 %collective-permute-start.2 = (bf16[1,480,1024]{2,1,0:T(8,128)(2,1)}, bf16[1,480,1024]{2,1,0:T(8,128)(2,1)S(1)}, u32[]{:S(2)}, u32[]{:S(2)}) collective-permute-start(bf16[1,480,1024]{2,1,0:T(8,128)(2,1)} %reduce-scatter.6.cloned.1.call-done), channel_id=1, source_target_pairs={{0,8},{24,16},{1,9},{25,17},{2,10},{26,18},{3,11},{27,19},{4,12},{... | collective-permute-start | bytes 2949128 | tf_op jit(solution)/shard_map/ppermute | solution.py:199
  498.9 29.1 %collective-permute-start.6 = (bf16[1,128,5632]{2,1,0:T(8,128)(2,1)S(1)}, bf16[1,128,5632]{2,1,0:T(8,128)(2,1)}, u32[]{:S(2)}, u32[]{:S(2)}) collective-permute-start(bf16[1,128,5632]{2,1,0:T(8,128)(2,1)S(1)} %add_convert_fusion.1), channel_id=1, source_target_pairs={{8,16},{16,8},{9,17},{17,9},{10,18},{18,10},{11,19},{19,11},{12,20... | collective-permute-start | bytes 4325384 | tf_op jit(solution)/shard_map/ppermute | solution.py:201
  517.4 7.9 %collective-permute-start.3 = (bf16[1,480,1024]{2,1,0:T(8,128)(2,1)S(1)}, bf16[1,480,1024]{2,1,0:T(8,128)(2,1)S(1)}, u32[]{:S(2)}, u32[]{:S(2)}) collective-permute-start(bf16[1,480,1024]{2,1,0:T(8,128)(2,1)S(1)} %add_convert_fusion.3), channel_id=1, source_target_pairs={{8,16},{16,8},{9,17},{17,9},{10,18},{18,10},{11,19},{19,11},{12,20... | collective-permute-start | bytes 2949128 | tf_op jit(solution)/shard_map/ppermute | solution.py:201
  525.3 6.0 copy-start.17
  526.6 80.0 %collective-permute-start.4 = (bf16[1,480,1024]{2,1,0:T(8,128)(2,1)}, bf16[1,480,1024]{2,1,0:T(8,128)(2,1)}, u32[]{:S(2)}, u32[]{:S(2)}) collective-permute-start(bf16[1,480,1024]{2,1,0:T(8,128)(2,1)} %add_convert_fusion.2), channel_id=1, source_target_pairs={{8,0},{16,24},{9,1},{17,25},{10,2},{18,26},{11,3},{19,27},{12,4},{... | collective-permute-start | bytes 2949128 | tf_op jit(solution)/shard_map/ppermute | solution.py:203
  529.7 101.4 %collective-permute-start.7 = (bf16[1,128,5632]{2,1,0:T(8,128)(2,1)S(1)}, bf16[1,128,5632]{2,1,0:T(8,128)(2,1)S(1)}, u32[]{:S(2)}, u32[]{:S(2)}) collective-permute-start(bf16[1,128,5632]{2,1,0:T(8,128)(2,1)S(1)} %add_convert_fusion), channel_id=1, source_target_pairs={{8,0},{16,24},{9,1},{17,25},{10,2},{18,26},{11,3},{19,27},{12,4},{... | collective-permute-start | bytes 4325384 | tf_op jit(solution)/shard_map/ppermute | solution.py:203
  (41 other events, 152.0 us)
Sparse Core Ops, SparseCore 0:
  10.5 49.7 all-gather.6
  62.7 69.1 all-gather.8
  134.4 76.3 all-gather.10
  282.6 87.1 reduce-scatter.7
  373.1 82.9 reduce-scatter.5
  461.5 63.6 reduce-scatter.3
  527.6 54.7 all-reduce.5

commit v3 on v2

--- a/solution.py
+++ b/solution.py
@@ -253,11 +253,12 @@
     full_qkv = qkv_blocks.reshape(n_group * own_rows, qkv_width)
     full_gain_attn = gain_rows[:, 0, :own_rows].reshape(-1)
     full_gain_mlp = gain_rows[:, 0, own_rows : 2 * own_rows].reshape(-1)
-    out_blocks, down_blocks = gather_blocks([w_out, w_down])
-    full_out = out_blocks.reshape(-1, model_width)
+    (ogu_blocks,) = gather_blocks([jnp.concatenate([w_out, w_gate, w_up], axis=1)])
+    full_ogu = ogu_blocks.reshape(n_group * own_rows, model_width + 2 * ff_width)
+    full_out = full_ogu[:, :model_width]
+    full_gu = full_ogu[:, model_width:]
+    (down_blocks,) = gather_blocks([w_down])
     full_down = down_blocks.reshape(-1, model_width)
-    (gu_blocks,) = gather_blocks([jnp.concatenate([w_gate, w_up], axis=1)])
-    full_gu = gu_blocks.reshape(n_group * own_rows, 2 * ff_width)
     ctx_index = lax.axis_index("ctx")
     q_pos = ctx_index * slot_rows + jnp.arange(slot_rows)
     live_rows = q_pos[None, :] < lengths[:, None]
@@ -308,6 +309,9 @@
     output_gradient = jnp.where(live_rows[..., None], cotangent.astype(jnp.float32), 0.0)
     g_low = output_gradient.astype(jnp.bfloat16)
     grad_down = jnp.einsum("srf,srd->fd", hidden, g_low, preferred_element_type=jnp.float32)
+    (part_down,) = scatter_blocks(
+        [grad_down.reshape(n_group, -1, model_width).astype(jnp.bfloat16)], True
+    )
     g_hidden = jnp.einsum("srd,fd->srf", g_low, full_down, preferred_element_type=jnp.float32)
     gate_gradient = (
         g_hidden * up_proj * sigmoid_gate * (1.0 + gate_proj * (1.0 - sigmoid_gate))
@@ -321,30 +325,41 @@
     g_mlp_in, grad_gain_mlp = normalize_back(residual, inv_mlp, mlp_scale, g_normed_mlp)
     g_residual = output_gradient + g_mlp_in
     g_branch = g_residual.astype(jnp.bfloat16)
-    grad_out = jnp.einsum("sre,srd->ed", att_flat, g_branch, preferred_element_type=jnp.float32)
-    gu_block = grad_gu.reshape(n_group, own_rows, 2 * ff_width).astype(jnp.bfloat16)
-    od_blocks = [
-        grad_out.reshape(n_group, -1, model_width).astype(jnp.bfloat16),
-        grad_down.reshape(n_group, -1, model_width).astype(jnp.bfloat16),
-    ]
+    grad_out = jnp.einsum(
+        "sre,srd->ed", att_flat, g_branch, preferred_element_type=jnp.float32
+    )
+    ogu_block = (
+        jnp.concatenate([grad_out, grad_gu], axis=1)
+        .reshape(n_group, own_rows, model_width + 2 * ff_width)
+        .astype(jnp.bfloat16)
+    )
     g_attended = (
         jnp.einsum("srd,ed->sre", g_branch, full_out, preferred_element_type=jnp.float32)
         .astype(jnp.bfloat16)
         .reshape(head_shape)
     )
-    gu_block, od_blocks, g_attended = lax.optimization_barrier((gu_block, od_blocks, g_attended))
-    (part_gu,) = scatter_blocks([gu_block], True)
-    part_out, part_down = scatter_blocks(od_blocks, True)
+    (part_ogu,) = scatter_blocks([ogu_block], True)
     row_dots = jnp.sum(g_attended.astype(jnp.float32) * attended.astype(jnp.float32), axis=-1)
     g_queries, slot_dk, slot_dv = attend_backward(
         queries, slot_k, slot_v, g_attended, row_dots, attn_lse, q_pos, k_pos, lengths
     )
+    flat_shape = (n_slots, slot_rows, model_width)
     if n_ctx == 2:
         later = lax.ppermute(
             jnp.stack([slot_dk[:, :slot_rows], slot_dv[:, :slot_rows]]).astype(jnp.bfloat16),
             "ctx",
             [(1, 0)],
-        ).astype(jnp.float32)
+        )
+    gq_low = rotate(g_queries, q_pos, -1.0).reshape(flat_shape).astype(jnp.bfloat16)
+    grad_q = jnp.einsum("srd,sre->de", normed_low, gq_low, preferred_element_type=jnp.float32)
+    g_normed_q = jnp.einsum(
+        "sre,de->srd", gq_low, full_qkv[:, :attn_width], preferred_element_type=jnp.float32
+    )
+    (part_q,) = scatter_blocks(
+        [grad_q.reshape(n_group, own_rows, attn_width).astype(jnp.bfloat16)], True
+    )
+    if n_ctx == 2:
+        later = later.astype(jnp.float32)
         g_keys = slot_dk[:, slot_rows:] + later[0]
         g_values = slot_dv[:, slot_rows:] + later[1]
     else:
@@ -356,25 +371,25 @@
                 slot_dv.astype(jnp.bfloat16), "ctx", scatter_dimension=1, tiled=True
             ).astype(jnp.float32),
         )
-    flat_shape = (n_slots, slot_rows, model_width)
-    gq_low = rotate(g_queries, q_pos, -1.0).reshape(flat_shape).astype(jnp.bfloat16)
     gk_low = rotate(g_keys, q_pos, -1.0).reshape(flat_shape).astype(jnp.bfloat16)
     gv_rounded = g_values.reshape(flat_shape).astype(jnp.bfloat16).astype(jnp.float32)
     d_first = 0.5 * gv_rounded
     gv_half = d_first.astype(jnp.bfloat16)
-    g_qkv = jnp.concatenate([gq_low, gk_low, gv_half], axis=-1)
-    grad_qkv = jnp.einsum("srd,sre->de", normed_low, g_qkv, preferred_element_type=jnp.float32)
-    g_normed = jnp.einsum("sre,de->srd", g_qkv, full_qkv, preferred_element_type=jnp.float32)
+    g_kv = jnp.concatenate([gk_low, gv_half], axis=-1)
+    grad_kv = jnp.einsum("srd,sre->de", normed_low, g_kv, preferred_element_type=jnp.float32)
+    g_normed = g_normed_q + jnp.einsum(
+        "sre,de->srd", g_kv, full_qkv[:, attn_width:], preferred_element_type=jnp.float32
+    )
     g_attn_in, grad_gain_attn = normalize_back(inputs, inv_attn, attn_scale, g_normed)
     d_tokens = g_residual + g_attn_in
-    part_qkv, part_gains = scatter_blocks(
+    part_kv, part_gains = scatter_blocks(
         [
-            grad_qkv.reshape(n_group, own_rows, qkv_width),
+            grad_kv.reshape(n_group, own_rows, 2 * attn_width).astype(jnp.bfloat16),
             gain_block(
                 grad_gain_attn.reshape(n_group, own_rows),
                 grad_gain_mlp.reshape(n_group, own_rows),
-                qkv_width,
-            ),
+                2 * attn_width,
+            ).astype(jnp.bfloat16),
         ],
         False,
     )
@@ -382,12 +397,12 @@
         output,
         d_tokens,
         d_first,
-        part_qkv[:, :attn_width],
-        part_qkv[:, attn_width : 2 * attn_width],
-        part_qkv[:, 2 * attn_width :],
-        part_out,
-        part_gu[:, :ff_width],
-        part_gu[:, ff_width:],
+        part_q,
+        part_kv[:, :attn_width],
+        part_kv[:, attn_width:],
+        part_ogu[:, :model_width],
+        part_ogu[:, model_width : model_width + ff_width],
+        part_ogu[:, model_width + ff_width :],
         part_down,
         part_gains[0, :own_rows],
         part_gains[0, own_rows : 2 * own_rows],

time: 648 us -> 653 us (level)
  waiting for transfers between devices: 323 us -> 300 us
  starting transfers between devices: 17.1 us -> 28 us
  other arithmetic: 69 us -> 78.8 us
  matrix products: 150 us -> 158 us
    ppermute x1, waiting for transfers between devices: 19.2 us -> 78.1 us  [shards(): earlier = lax.ppermute(jnp.stack([keys, values]), 'ctx', [(0, 1)])]
    all_gather x3, waiting for transfers between devices: 100 us -> 48.1 us  [gather_blocks(): gathered = lax.all_gather(packed, GROUP, axis=0, tiled=False)]
    psum x1, waiting for transfers between devices: 44.3 us -> 0.01 us  [scatter_blocks(): lax.psum(summed, 'rep')]
    ppermute x2 -> x3, waiting for transfers between devices: 42.2 us -> 56.3 us  [rep_sum(): sent_out = lax.ppermute(total, 'rep', [(1, 0), (2, 3)])]
    concatenate x1 -> x2, other arithmetic: 1.19 us -> 13.4 us  [the longest x1 12.1 us: shards(): jnp.concatenate([grad_out, grad_gu], axis=1)]
    concatenate x2 -> x1, other arithmetic: 11.4 us -> 2.36 us  [scatter_blocks(): packed = jnp.concatenate(blocks, axis=1).astype(jnp.bfloat16)]
    slice x3 -> x1, local copies, waits for them, and re-layouts: 12.1 us -> 3.23 us  [gather_blocks(): fulls.append(gathered[:, offset:offset + piece.shape[0], :])]
    ppermute x2 -> x3, starting transfers between devices: 5 us -> 12.3 us  [rep_sum(): lax.ppermute(x, 'rep', [(0, 1), (3, 2)]).astype(jnp.float32)]
  transfers between devices with their start and end apart: 15 -> 19, of which waited for: 11 -> 9; matrix products, arithmetic and copies ran while one was open for 29% -> 32% of each run, Pallas kernels for 0% -> 0%
where the time goes in v3:
time: 653 us; the launch traced here: 646 us
  waiting for transfers between devices  300 us (46%)
  matrix products  158 us (24%)
  other arithmetic  78.8 us (12%)
  local copies, waits for them, and re-layouts  64.8 us (10%)
  starting transfers between devices  28 us (4%)
  between operations  15.9 us (2%)
    ppermute x1, waiting for transfers between devices, shards(): earlier = lax.ppermute(jnp.stack([keys, values]), 'ctx', [(0, 1)])  78.1 us
    ppermute x1, waiting for transfers between devices, shards(): lax.ppermute(jnp.stack([slot_dk[:, :slot_rows], slot_dv[:, :slot_rows]])....  58.2 us
    ppermute x3, waiting for transfers between devices, rep_sum(): sent_out = lax.ppermute(total, 'rep', [(1, 0), (2, 3)])  56.3 us
    ppermute x3, waiting for transfers between devices, rep_sum(): lax.ppermute(x, 'rep', [(0, 1), (3, 2)]).astype(jnp.float32)  49.6 us
    all_gather x3, waiting for transfers between devices, gather_blocks(): gathered = lax.all_gather(packed, GROUP, axis=0, tiled=False)  48.1 us
    dot_general x2, matrix products, one_block(): jnp.einsum('sqhe,skhe->shqk', g_rows, v_group, preferred_element_type=jnp...  19.2 us
    while x32, local copies, waits for them, and re-layouts  18.6 us
    dot_general x1, matrix products, shards(): jnp.einsum('srf,df->srd', gu_gradient, full_gu, preferred_element_type=jn...  14.7 us
  transfers between devices with their start and end apart: 19, of which 9 were waited for; matrix products, arithmetic and copies ran while one was open for 32% of the time, Pallas kernels for 0%

profile of v3, /device:TPU:0, one launch (start us, length us, event | category | flops | bytes accessed | tf_op | source)
XLA Modules:
  0.0 646.1 jit_solution(10322214479629295119)
XLA Ops:
  12.9 47.3 %all-gather.7.cloned.1.call-done = bf16[1088,3072]{1,0:T(8,128)(2,1)} async-done(((bf16[136,3072]{1,0:T(8,128)(2,1)}), bf16[1088,3072]{1,0:T(8,128)(2,1)}) %all-gather.7.cloned.1.call-update) | async-done | bytes 6684688 | tf_op jit(solution)/shard_map/all_gather | solution.py:186
  83.4 4.5 collective-permute-start
  90.7 78.1 %collective-permute-done = bf16[2,1,512,16,64]{2,4,3,1,0:T(8,128)(2,1)} collective-permute-done((bf16[2,1,512,16,64]{2,4,3,1,0:T(8,128)(2,1)}, bf16[2,1,512,16,64]{2,4,3,1,0:T(8,128)(2,1)}, u32[]{:S(2)}, u32[]{:S(2)}) %collective-permute-start) | collective-permute-done | bytes 2097184 | tf_op jit(solution)/shard_map/ppermute | solution.py:283
  172.4 29.3 %while.30 = (s32[]{:T(128)}, bf16[2,1,512,8,64]{2,4,3,1,0:T(8,128)(2,1)}, f32[2,1,1,8,512]{4,3,2,1,0:T(8,128)S(1)}, bf16[2,1,1024,8,64]{2,4,3,1,0:T(8,128)(2,1)}...) while((s32[]{:T(128)}, ...), condition=%wide.region_4.5_spmd.clone.clone, body=%wide.region_1.4_spmd.clone.sunk.clone | while | flops 1125644800 | bytes 73025728 | solution.py:113
  181.1 5.0 fusion.198
  195.7 5.0 fusion.198
  207.0 13.3 %fusion.54 = f32[1,512,5632]{2,1,0:T(8,128)} fusion(bf16[1024,6656]{1,0:T(8,128)(2,1)} %all-gather.9.cloned.1.call-done, f32[1,512,1024]{2,1,0:T(8,128)S(1)} %get-tuple-element.372, f32[1024]{0:T(1024)S(1)} %bitcast.391, f32[512]{0:T(512)S(1)} %add_rsqrt_fusion), kind=kOutput, calls=%fused_computation.70 | convolution fusion | flops 5907152896 | bytes 25171968 | tf_op jit(solution)/shard_map/srd,df->srf/dot_general | solution.py:300
  221.1 12.7 %fusion.60 = (bf16[1,512,2816]{2,1,0:T(8,128)(2,1)S(1)}, bf16[1,512,2816]{2,1,0:T(8,128)(2,1)S(1)}, bf16[1,512,2816]{2,1,0:T(8,128)(2,1)}) fusion(f32[1,512,5632]{2,1,0:T(8,128)} %fusion.54, bf16[2816,1024]{1,0:T(8,128)(2,1)} %all-gather.11.cloned.1.call-done, bf16[1,512,1024]{2,1,0:T(8,128)(2,1)} %param.19, pred[512]{0:T(512)(128)(4,1)S(1)} %copy-done.46), kind=kOutput, calls=%fused_computation.78 | convolution fusion | flops 2977431552 | bytes 27001344 | tf_op jit(solution)/shard_map/srd,fd->srf/dot_general | solution.py:315
  236.3 9.2 %convolution_convert_fusion = bf16[1024,5632]{1,0:T(8,128)(2,1)} fusion(bf16[1,512,2816]{2,1,0:T(8,128)(2,1)S(1)} %get-tuple-element.339, bf16[1,512,2816]{2,1,0:T(8,128)(2,1)S(1)} %get-tuple-element.338, f32[1,512,1024]{2,1,0:T(8,128)S(1)} %copy-done.19, f32[1024]{0:T(1024)S(1)} %bitcast.392, f32[512]{0:T(512)S(1)} %add_rsqrt_fusion), kind=kOutput, calls=%fused_computation.65 | convolution fusion | flops 5924454400 | bytes 19404800 | tf_op jit(solution)/shard_map/srd,srf->df/dot_general | solution.py:321
  245.6 14.7 %fusion.87 = (bf16[1024]{0:T(1024)(128)(2,1)}, f32[512]{0:T(512)S(1)}, f32[512,1024]{1,0:T(8,128)}) fusion(f32[1,512,1024]{2,1,0:T(8,128)} %copy-done.18, f32[512]{0:T(512)S(1)} %add_rsqrt_fusion, f32[1024]{0:T(1024)S(1)} %bitcast.393, bf16[1024,6656]{1,0:T(8,128)(2,1)} %all-gather.9.cloned.1.call-done, bf16[1,512,2816]{2,1,0:T(8,128)(2,1)} %copy-done.49, ...), kind=kOutput, calls=%fused_computation.128 | convolution fusion | flops 5920258560 | bytes 21506048 | tf_op jit(solution)/shard_map/srf,df->srd/dot_general | solution.py:322
  260.3 4.6 fusion.92
  273.0 12.1 %pad_maximum_fusion = bf16[1024,6656]{1,0:T(8,128)(2,1)} fusion(bf16[1024,5632]{1,0:T(8,128)(2,1)} %convolution_convert_fusion, bf16[1024,1024]{1,0:T(8,128)(2,1)} %copy.64), kind=kLoop, calls=%fused_computation.64 | loop fusion | flops 27262976 | bytes 27262976 | tf_op jit(solution)/shard_map/concatenate | solution.py:332
  285.2 4.5 fusion.110
  294.7 4.9 copy.65
  304.0 6.5 %convolution_convert_fusion.2 = bf16[8,352,1024]{2,1,0:T(8,128)(2,1)} fusion(bf16[8,352,512]{2,1,0:T(8,128)(2,1)S(1)} %bitcast.373, bf16[1,512,1024]{2,1,0:T(8,128)(2,1)} %param.19, pred[512]{0:T(512)(128)(4,1)S(1)} %copy-done.46), kind=kOutput, calls=%fused_computation.90 | convolution fusion | flops 2957246464 | bytes 9699840 | tf_op jit(solution)/shard_map/srf,srd->fd/dot_general | solution.py:311
  310.6 65.5 %while.31 = (s32[]{:T(128)}, f32[2,1,512,8,64]{2,4,3,1,0:T(8,128)}, f32[2,1,1024,8,64]{2,4,3,1,0:T(8,128)}, f32[2,1,1024,8,64]{2,4,3,1,0:T(8,128)}, bf16[2,1,102...) while((s32[]{:T(128)}, f32[2,1,512,8,64]{2,4,3,1,0:T(8,128)}, ...), condition=%wide.region_9.10_spmd.clone.clone, body=%wide.region_8.9_spmd.clone.sunk.clone | while | flops 2728659456 | bytes 200938768 | solution.py:177
  314.2 6.7 %copy-done = f32[8,512,1024]{2,1,0:T(8,128)} copy-done((f32[8,512,1024]{2,1,0:T(8,128)}, f32[8,512,1024]{2,1,0:T(8,128)S(1)}, u32[]{:S(2)}) %copy-start) | copy-done | bytes 16777240 | tf_op jit(solution)/shard_map/while
  320.8 5.9 bitcast_dynamic-update-slice_fusion.11
  326.7 9.5 %multiply_convert_fusion.5 = bf16[8,512,1024]{2,1,0:T(8,128)(2,1)S(1)} fusion(f32[8,512,1024]{2,1,0:T(8,128)} %copy-done, f32[8,512]{1,0:T(8,128)S(1)} %dynamic-slice_bitcast_fusion.6, f32[8,512]{1,0:T(8,128)S(1)} %dynamic-slice_bitcast_fusion.7, pred[512,1024]{1,0:T(8,128)(4,1)S(1)} %and_and_fusion.7, ...), kind=kOutput, calls=%fused_computation.26.clone.1.clone | convolution fusion | flops 562036736 | bytes 27296768 | tf_op jit(solution)/shard_map/while/body/eval_jaxpr/while/body/eval_jaxpr/sqhe,skhe->shqk/dot_general | solution.py:143
  347.2 5.8 copy-done
  353.1 5.9 bitcast_dynamic-update-slice_fusion.11
  359.0 9.7 %multiply_convert_fusion.5 = bf16[8,512,1024]{2,1,0:T(8,128)(2,1)S(1)} fusion(f32[8,512,1024]{2,1,0:T(8,128)} %copy-done, f32[8,512]{1,0:T(8,128)S(1)} %dynamic-slice_bitcast_fusion.6, f32[8,512]{1,0:T(8,128)S(1)} %dynamic-slice_bitcast_fusion.7, pred[512,1024]{1,0:T(8,128)(4,1)S(1)} %and_and_fusion.7, ...), kind=kOutput, calls=%fused_computation.26.clone.1.clone | convolution fusion | flops 562036736 | bytes 27296768 | tf_op jit(solution)/shard_map/while/body/eval_jaxpr/while/body/eval_jaxpr/sqhe,skhe->shqk/dot_general | solution.py:143
  387.1 58.2 %collective-permute-done.1 = bf16[2,1,512,16,64]{2,4,3,1,0:T(8,128)(2,1)S(1)} collective-permute-done((bf16[2,1,512,16,64]{2,4,3,1,0:T(8,128)(2,1)S(1)}, bf16[2,1,512,16,64]{2,4,3,1,0:T(8,128)(2,1)S(1)}, u32[]{:S(2)}, u32[]{:S(2)}) %collective-permute-start.1) | collective-permute-done | bytes 2097184 | tf_op jit(solution)/shard_map/ppermute | solution.py:348
  455.9 5.7 fusion.77
  470.5 5.0 collective-permute-start.5
  480.4 30.7 %collective-permute-done.5 = bf16[1,128,6656]{2,1,0:T(8,128)(2,1)} collective-permute-done((bf16[1,128,6656]{2,1,0:T(8,128)(2,1)}, bf16[1,128,6656]{2,1,0:T(8,128)(2,1)}, u32[]{:S(2)}, u32[]{:S(2)}) %collective-permute-start.5) | collective-permute-done | bytes 1703968 | tf_op jit(solution)/shard_map/ppermute | solution.py:199
  514.9 5.9 collective-permute-start.8
  522.2 18.9 %collective-permute-done.2 = bf16[1,128,1024]{2,1,0:T(8,128)(2,1)S(1)} collective-permute-done((bf16[1,128,1024]{2,1,0:T(8,128)(2,1)}, bf16[1,128,1024]{2,1,0:T(8,128)(2,1)S(1)}, u32[]{:S(2)}, u32[]{:S(2)}) %collective-permute-start.2) | collective-permute-done | bytes 262176 | tf_op jit(solution)/shard_map/ppermute | solution.py:199
  551.5 6.8 %fusion.94 = bf16[1,512,1024]{2,1,0:T(8,128)(2,1)} fusion(f32[1,512,1024]{2,1,0:T(8,128)S(1)} %copy-done.20, bf16[2816,1024]{1,0:T(8,128)(2,1)} %all-gather.11.cloned.1.call-done, bf16[1,512,2816]{2,1,0:T(8,128)(2,1)S(1)} %copy-done.13, pred[512]{0:T(512)(128)(4,1)S(1)} %copy-done.47), kind=kOutput, calls=%fused_computation.138 | convolution fusion | flops 2954362880 | bytes 11796992 | tf_op jit(solution)/shard_map/srf,fd->srd/dot_general | solution.py:305
  558.4 9.6 %reduce-scatter.7.cloned.1.call-done = bf16[1,136,2048]{2,1,0:T(8,128)(2,1)} async-done(((bf16[8,136,2048]{2,1,0:T(8,128)(2,1)}), bf16[1,136,2048]{2,1,0:T(8,128)(2,1)}) %reduce-scatter.7.cloned.1.call-update) | async-done | bytes 557072 | tf_op jit(solution)/shard_map/reduce_scatter | solution.py:209
  573.3 48.9 %collective-permute-done.4 = bf16[1,128,1024]{2,1,0:T(8,128)(2,1)S(1)} collective-permute-done((bf16[1,128,1024]{2,1,0:T(8,128)(2,1)S(1)}, bf16[1,128,1024]{2,1,0:T(8,128)(2,1)S(1)}, u32[]{:S(2)}, u32[]{:S(2)}) %collective-permute-start.4) | collective-permute-done | bytes 262176 | tf_op jit(solution)/shard_map/ppermute | solution.py:203
  625.9 7.4 %collective-permute-done.10 = bf16[1,352,1024]{2,1,0:T(8,128)(2,1)S(1)} collective-permute-done((bf16[1,352,1024]{2,1,0:T(8,128)(2,1)S(1)}, bf16[1,352,1024]{2,1,0:T(8,128)(2,1)S(1)}, u32[]{:S(2)}, u32[]{:S(2)}) %collective-permute-start.10) | collective-permute-done | bytes 720928 | tf_op jit(solution)/shard_map/ppermute | solution.py:203
  (250 shorter events, 166.4 us)
Async XLA Ops:
  7.2 53.1 %all-gather.7.cloned.1.call-start = ((), (), s32[]{:S(2)}) async-start(), calls=%async_computation.9 | async-start | bytes 7520256 | tf_op jit(solution)/shard_map/all_gather | solution.py:186
  10.2 191.5 %all-gather.9.cloned.1.call-start = ((), (), s32[]{:S(2)}) async-start(), calls=%async_computation.10 | async-start | bytes 15335424 | tf_op jit(solution)/shard_map/all_gather | solution.py:186
  11.6 209.5 %all-gather.11.cloned.1.call-start = ((), (), s32[]{:S(2)}) async-start(), calls=%async_computation.11 | async-start | bytes 6488064 | tf_op jit(solution)/shard_map/all_gather | solution.py:186
  12.0 53.4 %copy-start.43 = (f32[512]{0:T(512)}, f32[512]{0:T(512)S(1)}, u32[]{:S(2)}) copy-start(f32[512]{0:T(512)S(1)} %add_rsqrt_fusion.1) | copy-start | bytes 6148
  12.9 65.7 %copy-start.27 = (f32[512,32]{0,1:T(8,128)}, f32[512,32]{0,1:T(8,128)S(1)}, u32[]{:S(2)}) copy-start(f32[512,32]{0,1:T(8,128)S(1)} %get-tuple-element.370) | copy-start | bytes 196612
  81.8 8.8 %copy-start.24 = (bf16[1,512,16,32]{1,3,2,0:T(8,128)(2,1)S(1)}, bf16[1,512,16,32]{1,3,2,0:T(8,128)(2,1)}, u32[]{:S(2)}) copy-start(bf16[1,512,16,32]{1,3,2,0:T(8,128)(2,1)} %get-tuple-element.354) | copy-start | bytes 1572868
  81.8 8.8 %copy-start.25 = (bf16[1,512,16,32]{1,3,2,0:T(8,128)(2,1)S(1)}, bf16[1,512,16,32]{1,3,2,0:T(8,128)(2,1)}, u32[]{:S(2)}) copy-start(bf16[1,512,16,32]{1,3,2,0:T(8,128)(2,1)} %get-tuple-element.355) | copy-start | bytes 1572868
  83.4 85.4 %collective-permute-start = (bf16[2,1,512,16,64]{2,4,3,1,0:T(8,128)(2,1)}, bf16[2,1,512,16,64]{2,4,3,1,0:T(8,128)(2,1)}, u32[]{:S(2)}, u32[]{:S(2)}) collective-permute-start(bf16[2,1,512,16,64]{2,4,3,1,0:T(8,128)(2,1)} %pad_maximum_fusion.1), channel_id=1, source_target_pairs={{0,1},{2,3},{4,5},{6,7},{8,9},{10,11},{12,13},{14,15},{16,17},{18,... | collective-permute-start | bytes 6291464 | tf_op jit(solution)/shard_map/ppermute | solution.py:283
  88.0 382.5 %reduce-scatter.9.cloned.1.call-start = ((), (), s32[]{:S(2)}) async-start(), calls=%async_computation.7 | async-start | bytes 15335424 | tf_op jit(solution)/shard_map/reduce_scatter | solution.py:209
  207.0 14.1 %copy-start.46 = (pred[512]{0:T(512)(128)(4,1)S(1)}, pred[512]{0:T(512)(128)(4,1)}, u32[]{:S(2)}) copy-start(pred[512]{0:T(512)(128)(4,1)} %fusion.138) | copy-start | bytes 1540
  221.1 15.2 %copy-start.19 = (f32[1,512,1024]{2,1,0:T(8,128)S(1)}, f32[1,512,1024]{2,1,0:T(8,128)}, u32[]{:S(2)}) copy-start(f32[1,512,1024]{2,1,0:T(8,128)} %copy-done.18) | copy-start | bytes 6291460
  285.1 229.8 %reduce-scatter.11.cloned.1.call-start = ((), (), s32[]{:S(2)}) async-start(), calls=%async_computation.8 | async-start | bytes 6488064 | tf_op jit(solution)/shard_map/reduce_scatter | solution.py:209
  310.5 210.3 %reduce-scatter.5.cloned.1.call-start = ((), (), s32[]{:S(2)}) async-start(), calls=%async_computation.4 | async-start | bytes 2359296 | tf_op jit(solution)/shard_map/reduce_scatter | solution.py:209
  311.8 9.1 %copy-start.30 = (bf16[2,1,512,8,64]{2,4,3,1,0:T(8,128)(2,1)S(1)}, bf16[2,1,512,8,64]{2,4,3,1,0:T(8,128)(2,1)}, u32[]{:S(2)}) copy-start(bf16[2,1,512,8,64]{2,4,3,1,0:T(8,128)(2,1)} %get-tuple-element.639) | copy-start | bytes 3145732 | tf_op jit(solution)/shard_map/while
  314.2 6.7 %copy-start = (f32[8,512,1024]{2,1,0:T(8,128)}, f32[8,512,1024]{2,1,0:T(8,128)S(1)}, u32[]{:S(2)}) copy-start(f32[8,512,1024]{2,1,0:T(8,128)S(1)} %fusion.209) | copy-start | bytes 50331652 | tf_op jit(solution)/shard_map/while
  344.8 8.2 %copy-start.30 = (bf16[2,1,512,8,64]{2,4,3,1,0:T(8,128)(2,1)S(1)}, bf16[2,1,512,8,64]{2,4,3,1,0:T(8,128)(2,1)}, u32[]{:S(2)}) copy-start(bf16[2,1,512,8,64]{2,4,3,1,0:T(8,128)(2,1)} %get-tuple-element.639) | copy-start | bytes 3145732 | tf_op jit(solution)/shard_map/while
  353.1 5.9 copy-start.22
  379.8 65.5 %collective-permute-start.1 = (bf16[2,1,512,16,64]{2,4,3,1,0:T(8,128)(2,1)S(1)}, bf16[2,1,512,16,64]{2,4,3,1,0:T(8,128)(2,1)S(1)}, u32[]{:S(2)}, u32[]{:S(2)}) collective-permute-start(bf16[2,1,512,16,64]{2,4,3,1,0:T(8,128)(2,1)S(1)} %pad_maximum_fusion.2), channel_id=1, source_target_pairs={{1,0},{3,2},{5,4},{7,6},{9,8},{11,10},{13,12},{15,14},{17,16},{19,... | collective-permute-start | bytes 6291464 | tf_op jit(solution)/shard_map/ppermute | solution.py:348
  387.1 58.8 %copy-start.17 = (f32[2,1,1024,8,64]{2,4,3,1,0:T(8,128)S(1)}, f32[2,1,1024,8,64]{2,4,3,1,0:T(8,128)}, u32[]{:S(2)}) copy-start(f32[2,1,1024,8,64]{2,4,3,1,0:T(8,128)} %get-tuple-element.198) | copy-start | bytes 12582916
  453.6 8.0 %copy-start.1 = (f32[1,512,1024]{2,1,0:T(8,128)}, f32[1,512,1024]{2,1,0:T(8,128)S(1)}, u32[]{:S(2)}) copy-start(f32[1,512,1024]{2,1,0:T(8,128)S(1)} %copy.58) | copy-start | bytes 6291460
  470.4 97.6 %reduce-scatter.7.cloned.1.call-start = ((), (), s32[]{:S(2)}) async-start(), calls=%async_computation.5 | async-start | bytes 5013504 | tf_op jit(solution)/shard_map/reduce_scatter | solution.py:209
  470.5 40.6 %collective-permute-start.5 = (bf16[1,128,6656]{2,1,0:T(8,128)(2,1)}, bf16[1,128,6656]{2,1,0:T(8,128)(2,1)}, u32[]{:S(2)}, u32[]{:S(2)}) collective-permute-start(bf16[1,128,6656]{2,1,0:T(8,128)(2,1)} %reduce-scatter.9.cloned.1.call-done), channel_id=1, source_target_pairs={{0,8},{24,16},{1,9},{25,17},{2,10},{26,18},{3,11},{27,19},{4,12},{... | collective-permute-start | bytes 5111816 | tf_op jit(solution)/shard_map/ppermute | solution.py:199
  480.3 30.8 %copy-start.26 = (bf16[1,128,6656]{2,1,0:T(8,128)(2,1)S(1)}, bf16[1,128,6656]{2,1,0:T(8,128)(2,1)}, u32[]{:S(2)}) copy-start(bf16[1,128,6656]{2,1,0:T(8,128)(2,1)} %reduce-scatter.9.cloned.1.call-done) | copy-start | bytes 5111812
  480.3 142.7 %all-reduce.6.cloned.1.call-start = ((), (), s32[]{:S(2)}) async-start(), calls=%async_computation.6 | async-start | bytes 1114112 | tf_op jit(solution)/shard_map/psum | solution.py:210
  513.0 35.3 %collective-permute-start.6 = (bf16[1,128,6656]{2,1,0:T(8,128)(2,1)S(1)}, bf16[1,128,6656]{2,1,0:T(8,128)(2,1)}, u32[]{:S(2)}, u32[]{:S(2)}) collective-permute-start(bf16[1,128,6656]{2,1,0:T(8,128)(2,1)S(1)} %add_convert_fusion.1), channel_id=1, source_target_pairs={{8,16},{16,8},{9,17},{17,9},{10,18},{18,10},{11,19},{19,11},{12,20... | collective-permute-start | bytes 5111816 | tf_op jit(solution)/shard_map/ppermute | solution.py:201
  514.9 29.3 %collective-permute-start.8 = (bf16[1,352,1024]{2,1,0:T(8,128)(2,1)}, bf16[1,352,1024]{2,1,0:T(8,128)(2,1)S(1)}, u32[]{:S(2)}, u32[]{:S(2)}) collective-permute-start(bf16[1,352,1024]{2,1,0:T(8,128)(2,1)} %reduce-scatter.11.cloned.1.call-done), channel_id=1, source_target_pairs={{0,8},{24,16},{1,9},{25,17},{2,10},{26,18},{3,11},{27,19},{4,12},{... | collective-permute-start | bytes 2162696 | tf_op jit(solution)/shard_map/ppermute | solution.py:199
  520.9 20.2 %collective-permute-start.2 = (bf16[1,128,1024]{2,1,0:T(8,128)(2,1)}, bf16[1,128,1024]{2,1,0:T(8,128)(2,1)S(1)}, u32[]{:S(2)}, u32[]{:S(2)}) collective-permute-start(bf16[1,128,1024]{2,1,0:T(8,128)(2,1)} %reduce-scatter.5.cloned.1.call-done), channel_id=1, source_target_pairs={{0,8},{24,16},{1,9},{25,17},{2,10},{26,18},{3,11},{27,19},{4,12},{... | collective-permute-start | bytes 786440 | tf_op jit(solution)/shard_map/ppermute | solution.py:199
  542.8 25.2 %collective-permute-start.3 = (bf16[1,128,1024]{2,1,0:T(8,128)(2,1)}, bf16[1,128,1024]{2,1,0:T(8,128)(2,1)}, u32[]{:S(2)}, u32[]{:S(2)}) collective-permute-start(bf16[1,128,1024]{2,1,0:T(8,128)(2,1)} %add_convert_fusion.8), channel_id=1, source_target_pairs={{8,16},{16,8},{9,17},{17,9},{10,18},{18,10},{11,19},{19,11},{12,20... | collective-permute-start | bytes 786440 | tf_op jit(solution)/shard_map/ppermute | solution.py:201
  546.4 24.0 %collective-permute-start.9 = (bf16[1,352,1024]{2,1,0:T(8,128)(2,1)}, bf16[1,352,1024]{2,1,0:T(8,128)(2,1)}, u32[]{:S(2)}, u32[]{:S(2)}) collective-permute-start(bf16[1,352,1024]{2,1,0:T(8,128)(2,1)} %add_convert_fusion.3), channel_id=1, source_target_pairs={{8,16},{16,8},{9,17},{17,9},{10,18},{18,10},{11,19},{19,11},{12,20... | collective-permute-start | bytes 2162696 | tf_op jit(solution)/shard_map/ppermute | solution.py:201
  550.2 84.3 %collective-permute-start.7 = (bf16[1,128,6656]{2,1,0:T(8,128)(2,1)S(1)}, bf16[1,128,6656]{2,1,0:T(8,128)(2,1)}, u32[]{:S(2)}, u32[]{:S(2)}) collective-permute-start(bf16[1,128,6656]{2,1,0:T(8,128)(2,1)S(1)} %add_convert_fusion), channel_id=1, source_target_pairs={{8,0},{16,24},{9,1},{17,25},{10,2},{18,26},{11,3},{19,27},{12,4},{... | collective-permute-start | bytes 5111816 | tf_op jit(solution)/shard_map/ppermute | solution.py:203
  569.1 53.1 %collective-permute-start.4 = (bf16[1,128,1024]{2,1,0:T(8,128)(2,1)S(1)}, bf16[1,128,1024]{2,1,0:T(8,128)(2,1)S(1)}, u32[]{:S(2)}, u32[]{:S(2)}) collective-permute-start(bf16[1,128,1024]{2,1,0:T(8,128)(2,1)S(1)} %add_convert_fusion.7), channel_id=1, source_target_pairs={{8,0},{16,24},{9,1},{17,25},{10,2},{18,26},{11,3},{19,27},{12,4},{... | collective-permute-start | bytes 786440 | tf_op jit(solution)/shard_map/ppermute | solution.py:203
  572.0 61.3 %collective-permute-start.10 = (bf16[1,352,1024]{2,1,0:T(8,128)(2,1)S(1)}, bf16[1,352,1024]{2,1,0:T(8,128)(2,1)S(1)}, u32[]{:S(2)}, u32[]{:S(2)}) collective-permute-start(bf16[1,352,1024]{2,1,0:T(8,128)(2,1)S(1)} %add_convert_fusion.2), channel_id=1, source_target_pairs={{8,0},{16,24},{9,1},{17,25},{10,2},{18,26},{11,3},{19,27},{12,4},{... | collective-permute-start | bytes 2162696 | tf_op jit(solution)/shard_map/ppermute | solution.py:203
  (45 other events, 141.6 us)
Sparse Core Ops, SparseCore 0:
  10.5 49.7 all-gather.6
  62.2 109.4 all-gather.8
  173.5 47.5 all-gather.10
  285.3 99.5 reduce-scatter.8
  388.2 74.5 reduce-scatter.10
  470.5 41.3 reduce-scatter.4
  515.4 52.5 reduce-scatter.6
  570.3 44.2 all-reduce.5

commit v4 on v2

--- a/solution.py
+++ b/solution.py
@@ -176,6 +176,20 @@
     )
     q_grads, k_grads, v_grads = lax.map(one_group, grouped)
     return (join_heads(q_grads), join_heads(k_grads), join_heads(v_grads))
+
+
+def sums_to_rows(log_sums):
+    n_groups, n_blocks, n_slots, per_group, q_block = log_sums.shape
+    return jnp.transpose(log_sums, (2, 0, 3, 1, 4)).reshape(
+        n_slots, n_groups * per_group, n_blocks * q_block
+    )
+
+
+def rows_to_sums(rows, k_len):
+    n_slots, n_heads, q_len = rows.shape
+    q_block, per_group = head_groups(n_slots, q_len, n_heads, k_len)
+    grouped = rows.reshape(n_slots, n_heads // per_group, per_group, q_len // q_block, q_block)
+    return jnp.transpose(grouped, (1, 3, 0, 2, 4))
 
 
 GROUP = ("fsdp", "ctx")
@@ -262,27 +276,39 @@
     q_pos = ctx_index * slot_rows + jnp.arange(slot_rows)
     live_rows = q_pos[None, :] < lengths[:, None]
     head_shape = (n_slots, slot_rows, HEADS, HEAD_DIM)
+    paired = n_ctx == 2
+    if paired:
+        other_tokens = lax.ppermute(tokens, "ctx", [(0, 1), (1, 0)])
+        other_first = lax.ppermute(initial_layer_values, "ctx", [(0, 1)])
+        other_pos = (1 - ctx_index) * slot_rows + jnp.arange(slot_rows)
     inputs = tokens.astype(jnp.float32)
     attn_scale = full_gain_attn.astype(jnp.float32)
     mlp_scale = full_gain_mlp.astype(jnp.float32)
-    normed, inv_attn = normalize(inputs, attn_scale)
-    normed_low = normed.astype(jnp.bfloat16)
-    qkv_pre = jnp.einsum("srd,de->sre", normed_low, full_qkv, preferred_element_type=jnp.float32)
-    q_pre = qkv_pre[..., :attn_width]
-    k_pre = qkv_pre[..., attn_width : 2 * attn_width]
-    v_pre = qkv_pre[..., 2 * attn_width :]
-    queries = rotate(q_pre.reshape(head_shape), q_pos, 1.0).astype(jnp.bfloat16)
-    keys = rotate(k_pre.reshape(head_shape), q_pos, 1.0).astype(jnp.bfloat16)
-    values = (
-        (0.5 * v_pre + 0.5 * initial_layer_values.astype(jnp.float32))
-        .astype(jnp.bfloat16)
-        .reshape(head_shape)
-    )
-    if n_ctx == 2:
-        earlier = lax.ppermute(jnp.stack([keys, values]), "ctx", [(0, 1)])
-        slot_k = jnp.concatenate([earlier[0], keys], axis=1)
-        slot_v = jnp.concatenate([earlier[1], values], axis=1)
-        k_pos = jnp.concatenate([q_pos - slot_rows, q_pos])
+
+    def project(chunk_tokens, chunk_first, chunk_pos):
+        chunk_normed, chunk_inv = normalize(chunk_tokens.astype(jnp.float32), attn_scale)
+        chunk_low = chunk_normed.astype(jnp.bfloat16)
+        qkv_pre = jnp.einsum(
+            "srd,de->sre", chunk_low, full_qkv, preferred_element_type=jnp.float32
+        )
+        q_pre = qkv_pre[..., :attn_width]
+        k_pre = qkv_pre[..., attn_width : 2 * attn_width]
+        v_pre = qkv_pre[..., 2 * attn_width :]
+        chunk_q = rotate(q_pre.reshape(head_shape), chunk_pos, 1.0).astype(jnp.bfloat16)
+        chunk_k = rotate(k_pre.reshape(head_shape), chunk_pos, 1.0).astype(jnp.bfloat16)
+        chunk_v = (
+            (0.5 * v_pre + 0.5 * chunk_first.astype(jnp.float32))
+            .astype(jnp.bfloat16)
+            .reshape(head_shape)
+        )
+        return chunk_low, chunk_inv, chunk_q, chunk_k, chunk_v
+
+    normed_low, inv_attn, queries, keys, values = project(tokens, initial_layer_values, q_pos)
+    if paired:
+        _, _, other_q, other_k, other_v = project(other_tokens, other_first, other_pos)
+        slot_k = jnp.concatenate([other_k, keys], axis=1)
+        slot_v = jnp.concatenate([other_v, values], axis=1)
+        k_pos = jnp.concatenate([other_pos, q_pos])
     else:
         slot_k, slot_v = (
             lax.all_gather(keys, "ctx", axis=1, tiled=True),
@@ -336,18 +362,36 @@
     (part_gu,) = scatter_blocks([gu_block], True)
     part_out, part_down = scatter_blocks(od_blocks, True)
     row_dots = jnp.sum(g_attended.astype(jnp.float32) * attended.astype(jnp.float32), axis=-1)
-    g_queries, slot_dk, slot_dv = attend_backward(
-        queries, slot_k, slot_v, g_attended, row_dots, attn_lse, q_pos, k_pos, lengths
-    )
-    if n_ctx == 2:
-        later = lax.ppermute(
-            jnp.stack([slot_dk[:, :slot_rows], slot_dv[:, :slot_rows]]).astype(jnp.bfloat16),
-            "ctx",
-            [(1, 0)],
-        ).astype(jnp.float32)
-        g_keys = slot_dk[:, slot_rows:] + later[0]
-        g_values = slot_dv[:, slot_rows:] + later[1]
+    if paired:
+        lse_rows = sums_to_rows(attn_lse)
+        later_g, later_dots, later_lse = lax.ppermute(
+            (g_attended, row_dots, lse_rows), "ctx", [(1, 0)]
+        )
+        g_queries, g_keys, g_values = attend_backward(
+            queries, keys, values, g_attended, row_dots,
+            rows_to_sums(lse_rows, slot_rows), q_pos, q_pos, lengths,
+        )
+        later = ctx_index == 1
+        pick = lambda mine, theirs: jnp.where(later, mine, theirs)
+        cross_q, cross_dq_k, cross_dq_v = (
+            pick(queries, other_q), pick(other_k, keys), pick(other_v, values)
+        )
+        cross_g = pick(g_attended, later_g)
+        cross_dots = pick(row_dots, later_dots)
+        cross_lse = pick(lse_rows, later_lse)
+        cross_qpos = pick(q_pos, other_pos)
+        cross_kpos = pick(other_pos, q_pos)
+        x_dq, x_dk, x_dv = attend_backward(
+            cross_q, cross_dq_k, cross_dq_v, cross_g, cross_dots,
+            rows_to_sums(cross_lse, slot_rows), cross_qpos, cross_kpos, lengths,
+        )
+        g_queries = g_queries + jnp.where(later, x_dq, 0.0)
+        g_keys = g_keys + jnp.where(later, 0.0, x_dk)
+        g_values = g_values + jnp.where(later, 0.0, x_dv)
     else:
+        g_queries, slot_dk, slot_dv = attend_backward(
+            queries, slot_k, slot_v, g_attended, row_dots, attn_lse, q_pos, k_pos, lengths
+        )
         g_keys, g_values = (
             lax.psum_scatter(
                 slot_dk.astype(jnp.bfloat16), "ctx", scatter_dimension=1, tiled=True

time: 648 us -> 629 us (0.971)
  waiting for transfers between devices: 323 us -> 288 us
  matrix products: 150 us -> 176 us
  local copies, waits for them, and re-layouts: 65 us -> 54.1 us
  other arithmetic: 69 us -> 62 us
    reduce_scatter x3, waiting for transfers between devices: 7.14 us -> 89.1 us  [scatter_blocks(): summed = lax.psum_scatter(packed, GROUP, scatter_dimension=0, tiled=True)]
    all_gather x3, waiting for transfers between devices: 100 us -> 37.3 us  [gather_blocks(): gathered = lax.all_gather(packed, GROUP, axis=0, tiled=False)]
    ppermute x2, waiting for transfers between devices: 47 us -> 17.6 us  [rep_sum(): lax.ppermute(x, 'rep', [(0, 1), (3, 2)]).astype(jnp.float32)]
    ppermute x2, waiting for transfers between devices: 42.2 us -> 17.8 us  [rep_sum(): sent_out = lax.ppermute(total, 'rep', [(1, 0), (2, 3)])]
    dot_general x4, matrix products: 10.8 us -> 26.3 us  [score_block(): jnp.einsum('sqhe,skhe->shqk', q_rows, k_rows, preferred_element_type=jnp....]
    while x24 -> x12, local copies, waits for them, and re-layouts: 17.2 us -> 1.91 us
    dot_general x2, matrix products: 11.7 us -> 20.2 us  [one_block(): jnp.einsum('shqk,sqhe->skhe', probabilities.astype(jnp.bfloat16), g_rows,...]
    ppermute x2 -> x5, waiting for transfers between devices: 81.8 us -> 78.4 us  [the longest x1 67.8 us: shards(): other_tokens = lax.ppermute(tokens, 'ctx', [(0, 1), (1, 0)])]
  transfers between devices with their start and end apart: 15 -> 18, of which waited for: 11 -> 8; matrix products, arithmetic and copies ran while one was open for 29% -> 34% of each run, Pallas kernels for 0% -> 0%
where the time goes in v4:
time: 629 us; the launch traced here: 620 us
  waiting for transfers between devices  288 us (46%)
  matrix products  176 us (28%)
  other arithmetic  62 us (10%)
  local copies, waits for them, and re-layouts  54.1 us (9%)
  starting transfers between devices  22.8 us (4%)
  between operations  15.9 us (3%)
    reduce_scatter x3, waiting for transfers between devices, scatter_blocks(): summed = lax.psum_scatter(packed, GROUP, scatter_dimension=0, tiled=True)  89.1 us
    ppermute x1, waiting for transfers between devices, shards(): other_tokens = lax.ppermute(tokens, 'ctx', [(0, 1), (1, 0)])  67.8 us
    psum x1, waiting for transfers between devices, scatter_blocks(): lax.psum(summed, 'rep')  47.8 us
    all_gather x3, waiting for transfers between devices, gather_blocks(): gathered = lax.all_gather(packed, GROUP, axis=0, tiled=False)  37.3 us
    dot_general x4, matrix products, score_block(): jnp.einsum('sqhe,skhe->shqk', q_rows, k_rows, preferred_element_type=jnp....  26.3 us
    dot_general x2, matrix products, one_block(): jnp.einsum('sqhe,skhe->shqk', g_rows, v_group, preferred_element_type=jnp...  20.9 us
    dot_general x2, matrix products, one_block(): jnp.einsum('shqk,sqhe->skhe', probabilities.astype(jnp.bfloat16), g_rows,...  20.2 us
    ppermute x2, waiting for transfers between devices, rep_sum(): sent_out = lax.ppermute(total, 'rep', [(1, 0), (2, 3)])  17.8 us
  transfers between devices with their start and end apart: 18, of which 8 were waited for; matrix products, arithmetic and copies ran while one was open for 34% of the time, Pallas kernels for 0%

profile of v4, /device:TPU:0, one launch (start us, length us, event | category | flops | bytes accessed | tf_op | source)
XLA Modules:
  0.0 619.5 jit_solution(7100975019816440096)
XLA Ops:
  13.0 5.9 collective-permute-start.1
  21.9 67.8 %collective-permute-done = bf16[1,512,1024]{2,1,0:T(8,128)(2,1)S(1)} collective-permute-done((bf16[1,512,1024]{2,1,0:T(8,128)(2,1)S(1)}, bf16[1,512,1024]{2,1,0:T(8,128)(2,1)S(1)}, u32[]{:S(2)}, u32[]{:S(2)}) %collective-permute-start) | collective-permute-done | bytes 1048608 | tf_op jit(solution)/shard_map/ppermute | solution.py:281
  109.5 5.8 convolution_bitcast_fusion.1
  134.5 29.7 %while.27 = (s32[]{:T(128)}, bf16[2,1,512,8,64]{2,4,3,1,0:T(8,128)(2,1)}, f32[2,1,1,8,512]{4,3,2,1,0:T(8,128)S(1)}, bf16[2,1,1024,8,64]{2,4,3,1,0:T(8,128)(2,1)}...) while((s32[]{:T(128)}, ...), condition=%wide.region_5.6_spmd.clone, body=%wide.region_2.5_spmd.clone.sunk | while | flops 1125644800 | bytes 73025736 | solution.py:113
  143.6 5.0 fusion.161
  153.8 4.4 fusion.160
  158.2 5.0 fusion.161
  166.1 6.6 %slice.171 = bf16[8,352,1024]{2,1,0:T(8,128)(2,1)} slice(bf16[8,480,1024]{2,1,0:T(8,128)(2,1)} %bitcast.316), slice={[0:8], [128:480], [0:1024]} | slice | bytes 11534336 | tf_op jit(solution)/shard_map/slice | solution.py:203
  174.1 37.2 %all-gather.11.cloned.1.call-done = bf16[1024,5632]{1,0:T(8,128)(2,1)} async-done(((bf16[128,5632]{1,0:T(8,128)(2,1)}), bf16[1024,5632]{1,0:T(8,128)(2,1)}) %all-gather.11.cloned.1.call-update) | async-done | bytes 11534352 | tf_op jit(solution)/shard_map/all_gather | solution.py:200
  211.3 13.4 %convolution_bitcast_fusion = f32[1,512,5632]{2,1,0:T(8,128)} fusion(bf16[1024,5632]{1,0:T(8,128)(2,1)} %all-gather.11.cloned.1.call-done, f32[1,512,1024]{2,1,0:T(8,128)S(1)} %get-tuple-element.407, f32[1024]{0:T(1024)S(1)} %bitcast.347, f32[512]{0:T(512)S(1)} %add_rsqrt_fusion), kind=kOutput, calls=%fused_computation.34 | convolution fusion | flops 5907152896 | bytes 25171968 | tf_op jit(solution)/shard_map/srd,df->srf/dot_general | solution.py:325
  224.8 10.5 %fusion.33 = (bf16[1,512,2816]{2,1,0:T(8,128)(2,1)}, bf16[1,512,2816]{2,1,0:T(8,128)(2,1)}, bf16[1,512,2816]{2,1,0:T(8,128)(2,1)}) fusion(f32[1,512,5632]{2,1,0:T(8,128)} %convolution_bitcast_fusion, bf16[2816,1024]{1,0:T(8,128)(2,1)S(1)} %bitcast.323, bf16[1,512,1024]{2,1,0:T(8,128)(2,1)S(1)} %copy-done.43, pred[512]{0:T(512)(128)(4,1)S(1)} %copy-done.64), kind=kOutput, calls=%fused_computation.49 | convolution fusion | flops 2977431552 | bytes 27001344 | tf_op jit(solution)/shard_map/srd,fd->srf/dot_general | solution.py:337
  235.2 4.6 copy.68
  239.9 11.8 %fusion.60 = (bf16[1024]{0:T(1024)(128)(2,1)S(1)}, f32[512]{0:T(512)S(1)}, f32[512,1024]{1,0:T(8,128)S(1)}) fusion(f32[1,512,1024]{2,1,0:T(8,128)S(1)} %get-tuple-element.407, f32[512]{0:T(512)S(1)} %add_rsqrt_fusion, f32[1024]{0:T(1024)S(1)} %bitcast.348, bf16[1024,5632]{1,0:T(8,128)(2,1)} %all-gather.11.cloned.1.call-done, ...), kind=kOutput, calls=%fused_computation.96 | convolution fusion | flops 5920258560 | bytes 21506048 | tf_op jit(solution)/shard_map/srf,df->srd/dot_general | solution.py:344
  262.9 5.2 convolution_convert_fusion.2
  268.1 9.3 %convolution_convert_fusion = bf16[8,128,5632]{2,1,0:T(8,128)(2,1)} fusion(bf16[8,128,512]{2,1,0:T(8,128)(2,1)S(1)} %bitcast.338, bf16[1,512,2816]{2,1,0:T(8,128)(2,1)S(1)} %copy-done.68, bf16[1,512,2816]{2,1,0:T(8,128)(2,1)S(1)} %copy-done.67), kind=kOutput, calls=%fused_computation.33 | convolution fusion | flops 5922881536 | bytes 18350080 | tf_op jit(solution)/shard_map/srd,srf->df/dot_general | solution.py:343
  280.0 11.5 %fusion.99 = f32[16,512,512]{2,1,0:T(8,128)} fusion(bf16[512,16,32]{0,2,1:T(8,128)(2,1)S(1)} %bitcast.284, bf16[512,16,32]{0,2,1:T(8,128)(2,1)S(1)} %bitcast.289, bf16[512,16,32]{0,2,1:T(8,128)(2,1)S(1)} %bitcast.299, bf16[512,16,32]{0,2,1:T(8,128)(2,1)S(1)} %bitcast.294), kind=kOutput, calls=%fused_computation.169 | convolution fusion | flops 541065216 | bytes 18874368 | tf_op jit(solution)/shard_map/while/body/eval_jaxpr/while/body/eval_jaxpr/sqhe,skhe->shqk/dot_general | solution.py:67
  291.5 8.8 %fusion.130 = f32[16,512,512]{2,1,0:T(8,128)} fusion(bf16[512,16,32]{0,2,1:T(8,128)(2,1)S(1)} %copy-done.29, bf16[512,16,32]{0,2,1:T(8,128)(2,1)S(1)} %copy-done.27, pred[]{:T(512)S(6)} %eq.11, bf16[512,16,32]{0,2,1:T(8,128)(2,1)S(1)} %bitcast.285, bf16[512,16,32]{0,2,1:T(8,128)(2,1)S(1)} %bitcast.290, bf16[512,16,32]{0,2,1:T(8,128)(2,1)S(1)} %bitcast.310, ...), kind=kOutput, calls=%fused_computation.225 | convolution fusion | flops 546308096 | bytes 20971520 | tf_op jit(solution)/shard_map/while/body/eval_jaxpr/while/body/eval_jaxpr/sqhe,skhe->shqk/dot_general | solution.py:67
  301.6 7.3 %pad_maximum_fusion = bf16[8,480,1024]{2,1,0:T(8,128)(2,1)} fusion(bf16[8,352,1024]{2,1,0:T(8,128)(2,1)} %convolution_convert_fusion.2, bf16[8,128,1024]{2,1,0:T(8,128)(2,1)} %convolution_convert_fusion.3), kind=kLoop, calls=%fused_computation.39 | loop fusion | flops 15728640 | bytes 15728640 | tf_op jit(solution)/shard_map/concatenate | solution.py:222
  312.1 10.4 %fusion.23 = f32[16,64,512]{2,1,0:T(8,128)} fusion(f32[16,512,512]{2,1,0:T(8,128)} %fusion.99, f32[16,512]{1,0:T(8,128)S(1)} %bitcast.351, pred[512,512]{1,0:T(8,128)(4,1)S(1)} %and_and_fusion.2, bf16[1,512,16,64]{1,3,2,0:T(8,128)(2,1)} %bitcast.60), kind=kOutput, calls=%fused_computation.36 | convolution fusion | flops 553648128 | bytes 20217856 | tf_op jit(solution)/shard_map/while/body/eval_jaxpr/while/body/eval_jaxpr/shqk,sqhe->skhe/dot_general | solution.py:137
  322.5 10.0 %multiply_convert_fusion.1 = bf16[16,512,512]{2,1,0:T(8,128)(2,1)S(1)} fusion(f32[16,512,512]{2,1,0:T(8,128)} %fusion.99, bf16[512,16,64]{0,2,1:T(8,128)(2,1)S(1)} %bitcast.330, f32[16,512]{1,0:T(8,128)S(1)} %bitcast.342, f32[16,512]{1,0:T(8,128)S(1)} %bitcast.352, pred[512,512]{1,0:T(8,128)(4,1)S(1)} %and_and_fusion.2, bf16[1,512,16,64]{1,3,2,0:T(8,128)(2,1)} %bitcast.60), kind=kOutput, calls=%fused_computation.27 | convolution fusion | flops 562036736 | bytes 27590656 | tf_op jit(solution)/shard_map/while/body/eval_jaxpr/while/body/eval_jaxpr/sqhe,skhe->shqk/dot_general | solution.py:143
  339.4 10.5 %collective-permute-done.4 = f32[1,512,16]{1,2,0:T(8,128)S(1)} collective-permute-done((f32[1,512,16]{1,2,0:T(8,128)S(1)}, f32[1,512,16]{1,2,0:T(8,128)S(1)}, u32[]{:S(2)}, u32[]{:S(2)}) %collective-permute-start.4) | collective-permute-done | bytes 32800 | tf_op jit(solution)/shard_map/ppermute | solution.py:367
  350.0 9.9 %convert_multiply_fusion.5 = f32[16,64,512]{2,1,0:T(8,128)} fusion(f32[16,64,512]{2,1,0:T(8,128)S(1)} %copy-done.66, f32[16,512,512]{2,1,0:T(8,128)} %fusion.130, f32[16,512]{1,0:T(8,128)S(1)} %select_bitcast_fusion.1, pred[512,512]{1,0:T(8,128)(4,1)S(1)} %and_and_fusion.1, pred[]{:T(512)S(6)} %eq.11, bf16[1,512,16,64]{1,3,2,0:T(8,128)(2,1)} %bitcast.60, ...), kind=kOutput, calls=%fused_computation.105 | convolution fusion | flops 556793856 | bytes 23363584 | tf_op jit(solution)/shard_map/while/body/eval_jaxpr/while/body/eval_jaxpr/shqk,sqhe->skhe/dot_general | solution.py:137
  365.5 11.0 %multiply_convert_fusion = bf16[16,512,512]{2,1,0:T(8,128)(2,1)S(1)} fusion(f32[16,512,512]{2,1,0:T(8,128)} %fusion.130, f32[16,512]{1,0:T(8,128)S(1)} %select_bitcast_fusion, f32[16,512]{1,0:T(8,128)S(1)} %select_bitcast_fusion.1, pred[512,512]{1,0:T(8,128)(4,1)S(1)} %and_and_fusion.1, bf16[512,16,64]{0,2,1:T(8,128)(2,1)} %bitcast.326, ...), kind=kOutput, calls=%fused_computation.25 | convolution fusion | flops 563085312 | bytes 29687808 | tf_op jit(solution)/shard_map/while/body/eval_jaxpr/while/body/eval_jaxpr/sqhe,skhe->shqk/dot_general | solution.py:143
  376.5 4.6 add_bitcast_fusion.1
  387.0 7.3 %fusion.53 = (bf16[1024]{0:T(1024)(128)(2,1)S(1)}, f32[512]{0:T(512)S(1)}, f32[512,1024]{1,0:T(8,128)S(1)}) fusion(bf16[1,512,1024]{2,1,0:T(8,128)(2,1)S(1)} %copy-done.11, f32[512]{0:T(512)S(1)} %copy-done.63, f32[1024]{0:T(1024)S(1)} %bitcast.345, bf16[1024,3072]{1,0:T(8,128)(2,1)} %bitcast.319, bf16[1,512,1024]{2,1,0:T(8,128)(2,1)S(1)} %copy-done.46, ...), kind=kOutput, calls=%fused_computation.83 | convolution fusion | flops 3234331136 | bytes 12593152 | tf_op jit(solution)/shard_map/sre,de->srd/dot_general | solution.py:411
  397.9 5.4 convolution_convert_fusion.1
  410.7 47.9 %reduce-scatter.6.cloned.1.call-done = bf16[1,480,1024]{2,1,0:T(8,128)(2,1)} async-done(((bf16[8,480,1024]{2,1,0:T(8,128)(2,1)}), bf16[1,480,1024]{2,1,0:T(8,128)(2,1)}) %reduce-scatter.6.cloned.1.call-update) | async-done | bytes 983056 | tf_op jit(solution)/shard_map/reduce_scatter | solution.py:223
  465.7 17.6 %collective-permute-done.5 = bf16[1,480,1024]{2,1,0:T(8,128)(2,1)S(1)} collective-permute-done((bf16[1,480,1024]{2,1,0:T(8,128)(2,1)}, bf16[1,480,1024]{2,1,0:T(8,128)(2,1)S(1)}, u32[]{:S(2)}, u32[]{:S(2)}) %collective-permute-start.5) | collective-permute-done | bytes 983072 | tf_op jit(solution)/shard_map/ppermute | solution.py:213
  484.4 41.2 %reduce-scatter.4.cloned.1.call-done = bf16[1,136,3072]{2,1,0:T(8,128)(2,1)} async-done(((bf16[8,136,3072]{2,1,0:T(8,128)(2,1)}), bf16[1,136,3072]{2,1,0:T(8,128)(2,1)}) %reduce-scatter.4.cloned.1.call-update) | async-done | bytes 835600 | tf_op jit(solution)/shard_map/reduce_scatter | solution.py:223
  531.4 6.9 %fusion.65 = bf16[1,512,1024]{2,1,0:T(8,128)(2,1)} fusion(f32[1,512,1024]{2,1,0:T(8,128)S(1)} %copy-done.15, bf16[2816,1024]{1,0:T(8,128)(2,1)} %bitcast.322, bf16[1,512,2816]{2,1,0:T(8,128)(2,1)S(1)} %copy-done.38, pred[512]{0:T(512)(128)(4,1)S(1)} %copy-done.64), kind=kOutput, calls=%fused_computation.104 | convolution fusion | flops 2954362880 | bytes 11796992 | tf_op jit(solution)/shard_map/srf,fd->srd/dot_general | solution.py:330
  538.3 47.8 %all-reduce.6.cloned.1.call-done = bf16[136,3072]{1,0:T(8,128)(2,1)} async-done(((bf16[136,3072]{1,0:T(8,128)(2,1)}), bf16[136,3072]{1,0:T(8,128)(2,1)}) %all-reduce.6.cloned.1.call-update) | async-done | bytes 835600 | tf_op jit(solution)/shard_map/psum | solution.py:224
  592.7 17.8 %collective-permute-done.10 = bf16[1,128,5632]{2,1,0:T(8,128)(2,1)S(1)} collective-permute-done((bf16[1,128,5632]{2,1,0:T(8,128)(2,1)S(1)}, bf16[1,128,5632]{2,1,0:T(8,128)(2,1)S(1)}, u32[]{:S(2)}, u32[]{:S(2)}) %collective-permute-start.10) | collective-permute-done | bytes 1441824 | tf_op jit(solution)/shard_map/ppermute | solution.py:217
  (266 shorter events, 134.6 us)
Async XLA Ops:
  7.2 82.8 %all-gather.7.cloned.1.call-start = ((), (), s32[]{:S(2)}) async-start(), calls=%async_computation.7 | async-start | bytes 7520256 | tf_op jit(solution)/shard_map/all_gather | solution.py:200
  10.1 154.1 %all-gather.9.cloned.1.call-start = ((), (), s32[]{:S(2)}) async-start(), calls=%async_computation.8 | async-start | bytes 8847360 | tf_op jit(solution)/shard_map/all_gather | solution.py:200
  11.3 200.0 %all-gather.11.cloned.1.call-start = ((), (), s32[]{:S(2)}) async-start(), calls=%async_computation.9 | async-start | bytes 12976128 | tf_op jit(solution)/shard_map/all_gather | solution.py:200
  13.0 393.8 %reduce-scatter.8.cloned.1.call-start = ((), (), s32[]{:S(2)}) async-start(), calls=%async_computation.6 | async-start | bytes 12976128 | tf_op jit(solution)/shard_map/reduce_scatter | solution.py:223
  13.0 85.7 %collective-permute-start.1 = (bf16[1,512,1024]{2,1,0:T(8,128)(2,1)S(1)}, bf16[1,512,1024]{2,1,0:T(8,128)(2,1)}, u32[]{:S(2)}, u32[]{:S(2)}) collective-permute-start(bf16[1,512,1024]{2,1,0:T(8,128)(2,1)S(1)} %copy-done.41), channel_id=1, source_target_pairs={{0,1},{2,3},{4,5},{6,7},{8,9},{10,11},{12,13},{14,15},{16,17},{18,... | collective-permute-start | bytes 3145736 | tf_op jit(solution)/shard_map/ppermute | solution.py:282
  18.9 70.7 %collective-permute-start = (bf16[1,512,1024]{2,1,0:T(8,128)(2,1)S(1)}, bf16[1,512,1024]{2,1,0:T(8,128)(2,1)S(1)}, u32[]{:S(2)}, u32[]{:S(2)}) collective-permute-start(bf16[1,512,1024]{2,1,0:T(8,128)(2,1)S(1)} %copy-done.9), channel_id=1, source_target_pairs={{0,1},{1,0},{2,3},{3,2},{4,5},{5,4},{6,7},{7,6},{8,9},{9,8},{10,11... | collective-permute-start | bytes 3145736 | tf_op jit(solution)/shard_map/ppermute | solution.py:281
  20.5 89.0 %copy-start.62 = (f32[512]{0:T(512)}, f32[512]{0:T(512)S(1)}, u32[]{:S(2)}) copy-start(f32[512]{0:T(512)S(1)} %add_rsqrt_fusion.1) | copy-start | bytes 6148
  21.9 102.5 %copy-start.53 = (f32[512,32]{0,1:T(8,128)}, f32[512,32]{0,1:T(8,128)S(1)}, u32[]{:S(2)}) copy-start(f32[512,32]{0,1:T(8,128)S(1)} %get-tuple-element.401) | copy-start | bytes 196612
  95.1 14.3 %copy-start.57 = (f32[8,1,128]{2,1,0:T(1,128)}, f32[8,1,128]{2,1,0:T(1,128)S(1)}, u32[]{:S(2)}) copy-start(f32[8,1,128]{2,1,0:T(1,128)S(1)} %get-tuple-element.363) | copy-start | bytes 12292
  172.7 38.7 %copy-start.59 = (f32[8,1,128]{2,1,0:T(1,128)S(1)}, f32[8,1,128]{2,1,0:T(1,128)}, u32[]{:S(2)}) copy-start(f32[8,1,128]{2,1,0:T(1,128)} %get-tuple-element.362) | copy-start | bytes 12292
  174.1 65.8 %copy-start.14 = (f32[1,512,1024]{2,1,0:T(8,128)}, f32[1,512,1024]{2,1,0:T(8,128)S(1)}, u32[]{:S(2)}) copy-start(f32[1,512,1024]{2,1,0:T(8,128)S(1)} %get-tuple-element.407) | copy-start | bytes 6291460
  211.3 13.4 %copy-start.26 = (bf16[8,352,1024]{2,1,0:T(8,128)(2,1)S(1)}, bf16[8,352,1024]{2,1,0:T(8,128)(2,1)}, u32[]{:S(2)}) copy-start(bf16[8,352,1024]{2,1,0:T(8,128)(2,1)} %slice.171) | copy-start | bytes 17301508
  211.3 13.4 %copy-start.43 = (bf16[1,512,1024]{2,1,0:T(8,128)(2,1)S(1)}, bf16[1,512,1024]{2,1,0:T(8,128)(2,1)}, u32[]{:S(2)}) copy-start(bf16[1,512,1024]{2,1,0:T(8,128)(2,1)} %param.17) | copy-start | bytes 3145732
  211.3 13.4 %copy-start.64 = (pred[512]{0:T(512)(128)(4,1)S(1)}, pred[512]{0:T(512)(128)(4,1)}, u32[]{:S(2)}) copy-start(pred[512]{0:T(512)(128)(4,1)} %get-tuple-element.415) | copy-start | bytes 1540
  239.9 11.8 %copy-start.44 = (bf16[1,512,1024]{2,1,0:T(8,128)(2,1)S(1)}, bf16[1,512,1024]{2,1,0:T(8,128)(2,1)}, u32[]{:S(2)}) copy-start(bf16[1,512,1024]{2,1,0:T(8,128)(2,1)} %param.17) | copy-start | bytes 3145732
  277.4 181.2 %reduce-scatter.6.cloned.1.call-start = ((), (), s32[]{:S(2)}) async-start(), calls=%async_computation.5 | async-start | bytes 8847360 | tf_op jit(solution)/shard_map/reduce_scatter | solution.py:223
  278.6 21.6 %collective-permute-start.2 = (f32[1,16,512]{2,1,0:T(8,128)S(1)}, f32[1,16,512]{2,1,0:T(8,128)S(1)}, u32[]{:S(2)}, u32[]{:S(2)}) collective-permute-start(f32[1,16,512]{2,1,0:T(8,128)S(1)} %bitcast.350), channel_id=1, source_target_pairs={{1,0},{3,2},{5,4},{7,6},{9,8},{11,10},{13,12},{15,14},{17,16},{19,... | collective-permute-start | bytes 98312 | tf_op jit(solution)/shard_map/ppermute | solution.py:367
  279.9 11.5 %copy-start.21 = (bf16[1,512,16,32]{1,3,2,0:T(8,128)(2,1)S(1)}, bf16[1,512,16,32]{1,3,2,0:T(8,128)(2,1)}, u32[]{:S(2)}) copy-start(bf16[1,512,16,32]{1,3,2,0:T(8,128)(2,1)} %copy-done.20) | copy-start | bytes 1572868
  280.0 11.5 %copy-start.23 = (bf16[1,512,16,32]{1,3,2,0:T(8,128)(2,1)S(1)}, bf16[1,512,16,32]{1,3,2,0:T(8,128)(2,1)}, u32[]{:S(2)}) copy-start(bf16[1,512,16,32]{1,3,2,0:T(8,128)(2,1)} %copy-done.22) | copy-start | bytes 1572868
  280.0 11.5 %copy-start.27 = (bf16[512,16,32]{0,2,1:T(8,128)(2,1)S(1)}, bf16[512,16,32]{0,2,1:T(8,128)(2,1)}, u32[]{:S(2)}) copy-start(bf16[512,16,32]{0,2,1:T(8,128)(2,1)} %get-tuple-element.376) | copy-start | bytes 1572868
  300.3 49.7 %collective-permute-start.3 = (bf16[1,512,16,64]{1,3,2,0:T(8,128)(2,1)}, bf16[1,512,16,64]{1,3,2,0:T(8,128)(2,1)}, u32[]{:S(2)}, u32[]{:S(2)}) collective-permute-start(bf16[1,512,16,64]{1,3,2,0:T(8,128)(2,1)} %bitcast.60), channel_id=1, source_target_pairs={{1,0},{3,2},{5,4},{7,6},{9,8},{11,10},{13,12},{15,14},{17,16},{19,... | collective-permute-start | bytes 3145736 | tf_op jit(solution)/shard_map/ppermute | solution.py:367
  308.9 216.7 %reduce-scatter.4.cloned.1.call-start = ((), (), s32[]{:S(2)}) async-start(), calls=%async_computation.3 | async-start | bytes 7520256 | tf_op jit(solution)/shard_map/reduce_scatter | solution.py:223
  310.8 39.1 %collective-permute-start.4 = (f32[1,512,16]{1,2,0:T(8,128)S(1)}, f32[1,512,16]{1,2,0:T(8,128)S(1)}, u32[]{:S(2)}, u32[]{:S(2)}) collective-permute-start(f32[1,512,16]{1,2,0:T(8,128)S(1)} %bitcast.341), channel_id=1, source_target_pairs={{1,0},{3,2},{5,4},{7,6},{9,8},{11,10},{13,12},{15,14},{17,16},{19,... | collective-permute-start | bytes 98312 | tf_op jit(solution)/shard_map/ppermute | solution.py:367
  335.4 14.5 %copy-start.66 = (f32[16,64,512]{2,1,0:T(8,128)S(1)}, f32[16,64,512]{2,1,0:T(8,128)}, u32[]{:S(2)}) copy-start(f32[16,64,512]{2,1,0:T(8,128)} %fusion.23) | copy-start | bytes 6291460
  406.7 179.4 %all-reduce.6.cloned.1.call-start = ((), (), s32[]{:S(2)}) async-start(), calls=%async_computation.4 | async-start | bytes 1671168 | tf_op jit(solution)/shard_map/psum | solution.py:224
  406.8 55.4 %collective-permute-start.8 = (bf16[1,128,5632]{2,1,0:T(8,128)(2,1)}, bf16[1,128,5632]{2,1,0:T(8,128)(2,1)S(1)}, u32[]{:S(2)}, u32[]{:S(2)}) collective-permute-start(bf16[1,128,5632]{2,1,0:T(8,128)(2,1)} %reduce-scatter.8.cloned.1.call-done), channel_id=1, source_target_pairs={{0,8},{24,16},{1,9},{25,17},{2,10},{26,18},{3,11},{27,19},{4,12},{... | collective-permute-start | bytes 4325384 | tf_op jit(solution)/shard_map/ppermute | solution.py:213
  458.6 24.7 %copy-start.49 = (bf16[1,480,1024]{2,1,0:T(8,128)(2,1)S(1)}, bf16[1,480,1024]{2,1,0:T(8,128)(2,1)}, u32[]{:S(2)}) copy-start(bf16[1,480,1024]{2,1,0:T(8,128)(2,1)} %reduce-scatter.6.cloned.1.call-done) | copy-start | bytes 2949124
  458.6 24.7 %collective-permute-start.5 = (bf16[1,480,1024]{2,1,0:T(8,128)(2,1)}, bf16[1,480,1024]{2,1,0:T(8,128)(2,1)S(1)}, u32[]{:S(2)}, u32[]{:S(2)}) collective-permute-start(bf16[1,480,1024]{2,1,0:T(8,128)(2,1)} %reduce-scatter.6.cloned.1.call-done), channel_id=1, source_target_pairs={{0,8},{24,16},{1,9},{25,17},{2,10},{26,18},{3,11},{27,19},{4,12},{... | collective-permute-start | bytes 2949128 | tf_op jit(solution)/shard_map/ppermute | solution.py:213
  463.9 64.5 %collective-permute-start.9 = (bf16[1,128,5632]{2,1,0:T(8,128)(2,1)S(1)}, bf16[1,128,5632]{2,1,0:T(8,128)(2,1)}, u32[]{:S(2)}, u32[]{:S(2)}) collective-permute-start(bf16[1,128,5632]{2,1,0:T(8,128)(2,1)S(1)} %add_convert_fusion.1), channel_id=1, source_target_pairs={{8,16},{16,8},{9,17},{17,9},{10,18},{18,10},{11,19},{19,11},{12,20... | collective-permute-start | bytes 4325384 | tf_op jit(solution)/shard_map/ppermute | solution.py:215
  483.7 42.0 %collective-permute-start.6 = (bf16[1,480,1024]{2,1,0:T(8,128)(2,1)S(1)}, bf16[1,480,1024]{2,1,0:T(8,128)(2,1)S(1)}, u32[]{:S(2)}, u32[]{:S(2)}) collective-permute-start(bf16[1,480,1024]{2,1,0:T(8,128)(2,1)S(1)} %add_convert_fusion.4), channel_id=1, source_target_pairs={{8,16},{16,8},{9,17},{17,9},{10,18},{18,10},{11,19},{19,11},{12,20... | collective-permute-start | bytes 2949128 | tf_op jit(solution)/shard_map/ppermute | solution.py:215
  527.0 62.3 %collective-permute-start.7 = (bf16[1,480,1024]{2,1,0:T(8,128)(2,1)}, bf16[1,480,1024]{2,1,0:T(8,128)(2,1)}, u32[]{:S(2)}, u32[]{:S(2)}) collective-permute-start(bf16[1,480,1024]{2,1,0:T(8,128)(2,1)} %add_convert_fusion.3), channel_id=1, source_target_pairs={{8,0},{16,24},{9,1},{17,25},{10,2},{18,26},{11,3},{19,27},{12,4},{... | collective-permute-start | bytes 2949128 | tf_op jit(solution)/shard_map/ppermute | solution.py:217
  530.1 80.4 %collective-permute-start.10 = (bf16[1,128,5632]{2,1,0:T(8,128)(2,1)S(1)}, bf16[1,128,5632]{2,1,0:T(8,128)(2,1)S(1)}, u32[]{:S(2)}, u32[]{:S(2)}) collective-permute-start(bf16[1,128,5632]{2,1,0:T(8,128)(2,1)S(1)} %add_convert_fusion), channel_id=1, source_target_pairs={{8,0},{16,24},{9,1},{17,25},{10,2},{18,26},{11,3},{19,27},{12,4},{... | collective-permute-start | bytes 4325384 | tf_op jit(solution)/shard_map/ppermute | solution.py:217
  (58 other events, 206.2 us)
Sparse Core Ops, SparseCore 0:
  10.5 72.8 all-gather.6
  85.3 55.9 all-gather.8
  143.7 67.5 all-gather.10
  277.6 108.2 reduce-scatter.7
  389.1 69.4 reduce-scatter.5
  461.9 63.6 reduce-scatter.3
  528.0 58.1 all-reduce.5

commit v5 on v4

--- a/solution.py
+++ b/solution.py
@@ -334,6 +334,9 @@
     output_gradient = jnp.where(live_rows[..., None], cotangent.astype(jnp.float32), 0.0)
     g_low = output_gradient.astype(jnp.bfloat16)
     grad_down = jnp.einsum("srf,srd->fd", hidden, g_low, preferred_element_type=jnp.float32)
+    (part_down,) = scatter_blocks(
+        [grad_down.reshape(n_group, -1, model_width).astype(jnp.bfloat16)], True
+    )
     g_hidden = jnp.einsum("srd,fd->srf", g_low, full_down, preferred_element_type=jnp.float32)
     gate_gradient = (
         g_hidden * up_proj * sigmoid_gate * (1.0 + gate_proj * (1.0 - sigmoid_gate))
@@ -347,20 +350,20 @@
     g_mlp_in, grad_gain_mlp = normalize_back(residual, inv_mlp, mlp_scale, g_normed_mlp)
     g_residual = output_gradient + g_mlp_in
     g_branch = g_residual.astype(jnp.bfloat16)
-    grad_out = jnp.einsum("sre,srd->ed", att_flat, g_branch, preferred_element_type=jnp.float32)
-    gu_block = grad_gu.reshape(n_group, own_rows, 2 * ff_width).astype(jnp.bfloat16)
-    od_blocks = [
-        grad_out.reshape(n_group, -1, model_width).astype(jnp.bfloat16),
-        grad_down.reshape(n_group, -1, model_width).astype(jnp.bfloat16),
-    ]
+    grad_out = jnp.einsum(
+        "sre,srd->ed", att_flat, g_branch, preferred_element_type=jnp.float32
+    )
+    ogu_block = (
+        jnp.concatenate([grad_out, grad_gu], axis=1)
+        .reshape(n_group, own_rows, model_width + 2 * ff_width)
+        .astype(jnp.bfloat16)
+    )
     g_attended = (
         jnp.einsum("srd,ed->sre", g_branch, full_out, preferred_element_type=jnp.float32)
         .astype(jnp.bfloat16)
         .reshape(head_shape)
     )
-    gu_block, od_blocks, g_attended = lax.optimization_barrier((gu_block, od_blocks, g_attended))
-    (part_gu,) = scatter_blocks([gu_block], True)
-    part_out, part_down = scatter_blocks(od_blocks, True)
+    (part_ogu,) = scatter_blocks([ogu_block], True)
     row_dots = jnp.sum(g_attended.astype(jnp.float32) * attended.astype(jnp.float32), axis=-1)
     if paired:
         lse_rows = sums_to_rows(attn_lse)
@@ -429,9 +432,9 @@
         part_qkv[:, :attn_width],
         part_qkv[:, attn_width : 2 * attn_width],
         part_qkv[:, 2 * attn_width :],
-        part_out,
-        part_gu[:, :ff_width],
-        part_gu[:, ff_width:],
+        part_ogu[:, :model_width],
+        part_ogu[:, model_width : model_width + ff_width],
+        part_ogu[:, model_width + ff_width :],
         part_down,
         part_gains[0, :own_rows],
         part_gains[0, own_rows : 2 * own_rows],

time: 629 us -> 625 us (level)
  waiting for transfers between devices: 288 us -> 268 us
  other arithmetic: 62 us -> 69.2 us
    psum x1, waiting for transfers between devices: 47.8 us -> 32.2 us  [scatter_blocks(): lax.psum(summed, 'rep')]
    concatenate x0 -> x1, other arithmetic: none -> 11.5 us  [shards(): jnp.concatenate([grad_out, grad_gu], axis=1)]
    reduce_scatter x3, waiting for transfers between devices: 89.1 us -> 77.7 us  [scatter_blocks(): summed = lax.psum_scatter(packed, GROUP, scatter_dimension=0, tiled=True)]
    ppermute x2, waiting for transfers between devices: 17.8 us -> 27.6 us  [rep_sum(): sent_out = lax.ppermute(total, 'rep', [(1, 0), (2, 3)])]
    concatenate x2 -> x1, other arithmetic: 10.7 us -> 3.46 us  [scatter_blocks(): packed = jnp.concatenate(blocks, axis=1).astype(jnp.bfloat16)]
  transfers between devices with their start and end apart: 18 -> 18, of which waited for: 8 -> 9; matrix products, arithmetic and copies ran while one was open for 34% -> 37% of each run, Pallas kernels for 0% -> 0%
where the time goes in v5:
time: 625 us; the launch traced here: 615 us
  waiting for transfers between devices  268 us (43%)
  matrix products  182 us (29%)
  other arithmetic  69.2 us (11%)
  local copies, waits for them, and re-layouts  56.2 us (9%)
  starting transfers between devices  23.3 us (4%)
  between operations  16.1 us (3%)
    reduce_scatter x3, waiting for transfers between devices, scatter_blocks(): summed = lax.psum_scatter(packed, GROUP, scatter_dimension=0, tiled=True)  77.7 us
    ppermute x1, waiting for transfers between devices, shards(): other_tokens = lax.ppermute(tokens, 'ctx', [(0, 1), (1, 0)])  67.8 us
    all_gather x3, waiting for transfers between devices, gather_blocks(): gathered = lax.all_gather(packed, GROUP, axis=0, tiled=False)  37.5 us
    psum x1, waiting for transfers between devices, scatter_blocks(): lax.psum(summed, 'rep')  32.2 us
    ppermute x2, waiting for transfers between devices, rep_sum(): sent_out = lax.ppermute(total, 'rep', [(1, 0), (2, 3)])  27.6 us
    dot_general x4, matrix products, score_block(): jnp.einsum('sqhe,skhe->shqk', q_rows, k_rows, preferred_element_type=jnp....  27 us
    dot_general x2, matrix products, one_block(): jnp.einsum('shqk,sqhe->skhe', probabilities.astype(jnp.bfloat16), g_rows,...  20.1 us
    dot_general x2, matrix products, one_block(): jnp.einsum('sqhe,skhe->shqk', g_rows, v_group, preferred_element_type=jnp...  19.6 us
  transfers between devices with their start and end apart: 18, of which 9 were waited for; matrix products, arithmetic and copies ran while one was open for 37% of the time, Pallas kernels for 0%

profile of v5, /device:TPU:0, one launch (start us, length us, event | category | flops | bytes accessed | tf_op | source)
XLA Modules:
  0.0 615.4 jit_solution(12913084785980001606)
XLA Ops:
  13.0 5.9 collective-permute-start.1
  21.9 67.8 %collective-permute-done = bf16[1,512,1024]{2,1,0:T(8,128)(2,1)S(1)} collective-permute-done((bf16[1,512,1024]{2,1,0:T(8,128)(2,1)S(1)}, bf16[1,512,1024]{2,1,0:T(8,128)(2,1)S(1)}, u32[]{:S(2)}, u32[]{:S(2)}) %collective-permute-start) | collective-permute-done | bytes 1048608 | tf_op jit(solution)/shard_map/ppermute | solution.py:281
  109.5 5.8 convolution_bitcast_fusion.1
  134.5 29.5 %while.27 = (s32[]{:T(128)}, bf16[2,1,512,8,64]{2,4,3,1,0:T(8,128)(2,1)}, f32[2,1,1,8,512]{4,3,2,1,0:T(8,128)S(1)}, bf16[2,1,1024,8,64]{2,4,3,1,0:T(8,128)(2,1)}...) while((s32[]{:T(128)}, ...), condition=%wide.region_5.6_spmd.clone, body=%wide.region_2.5_spmd.clone.sunk | while | flops 1125644800 | bytes 73025736 | solution.py:113
  143.4 5.0 fusion.159
  158.0 5.0 fusion.159
  165.9 6.5 %slice.159 = bf16[8,352,1024]{2,1,0:T(8,128)(2,1)} slice(bf16[8,480,1024]{2,1,0:T(8,128)(2,1)} %bitcast.304), slice={[0:8], [128:480], [0:1024]} | slice | bytes 11534336 | tf_op jit(solution)/shard_map/slice | solution.py:203
  173.8 37.5 %all-gather.11.cloned.1.call-done = bf16[1024,5632]{1,0:T(8,128)(2,1)} async-done(((bf16[128,5632]{1,0:T(8,128)(2,1)}), bf16[1024,5632]{1,0:T(8,128)(2,1)}) %all-gather.11.cloned.1.call-update) | async-done | bytes 11534352 | tf_op jit(solution)/shard_map/all_gather | solution.py:200
  211.3 13.4 %convolution_bitcast_fusion = f32[1,512,5632]{2,1,0:T(8,128)} fusion(bf16[1024,5632]{1,0:T(8,128)(2,1)} %all-gather.11.cloned.1.call-done, f32[1,512,1024]{2,1,0:T(8,128)S(1)} %get-tuple-element.397, f32[1024]{0:T(1024)S(1)} %bitcast.343, f32[512]{0:T(512)S(1)} %add_rsqrt_fusion), kind=kOutput, calls=%fused_computation.35 | convolution fusion | flops 5907152896 | bytes 25171968 | tf_op jit(solution)/shard_map/srd,df->srf/dot_general | solution.py:325
  224.7 10.2 %fusion.30 = (bf16[1,512,2816]{2,1,0:T(8,128)(2,1)S(1)}, bf16[1,512,2816]{2,1,0:T(8,128)(2,1)}, bf16[1,512,2816]{2,1,0:T(8,128)(2,1)}) fusion(f32[1,512,5632]{2,1,0:T(8,128)} %convolution_bitcast_fusion, bf16[2816,1024]{1,0:T(8,128)(2,1)S(1)} %bitcast.311, bf16[1,512,1024]{2,1,0:T(8,128)(2,1)S(1)} %copy-done.41, pred[512]{0:T(512)(128)(4,1)S(1)} %copy-done.58), kind=kOutput, calls=%fused_computation.46 | convolution fusion | flops 2977431552 | bytes 27001344 | tf_op jit(solution)/shard_map/srd,fd->srf/dot_general | solution.py:340
  236.5 10.9 %convolution_convert_fusion = bf16[1024,5632]{1,0:T(8,128)(2,1)} fusion(bf16[1,512,2816]{2,1,0:T(8,128)(2,1)} %get-tuple-element.352, bf16[1,512,2816]{2,1,0:T(8,128)(2,1)S(1)} %get-tuple-element.351, f32[1,512,1024]{2,1,0:T(8,128)S(1)} %get-tuple-element.397, f32[1024]{0:T(1024)S(1)} %bitcast.344, f32[512]{0:T(512)S(1)} %add_rsqrt_fusion), kind=kOutput, calls=%fused_computation.34 | convolution fusion | flops 5924454400 | bytes 19404800 | tf_op jit(solution)/shard_map/srd,srf->df/dot_general | solution.py:346
  247.4 11.8 %fusion.58 = (bf16[1024]{0:T(1024)(128)(2,1)S(1)}, f32[512]{0:T(512)S(1)}, f32[512,1024]{1,0:T(8,128)S(1)}) fusion(f32[1,512,1024]{2,1,0:T(8,128)S(1)} %get-tuple-element.397, f32[512]{0:T(512)S(1)} %add_rsqrt_fusion, f32[1024]{0:T(1024)S(1)} %bitcast.345, bf16[1024,5632]{1,0:T(8,128)(2,1)} %all-gather.11.cloned.1.call-done, ...), kind=kOutput, calls=%fused_computation.94 | convolution fusion | flops 5920258560 | bytes 21506048 | tf_op jit(solution)/shard_map/srf,df->srd/dot_general | solution.py:347
  268.2 11.5 %pad_maximum_fusion = bf16[1024,6656]{1,0:T(8,128)(2,1)} fusion(bf16[1024,5632]{1,0:T(8,128)(2,1)} %convolution_convert_fusion, bf16[1024,1024]{1,0:T(8,128)(2,1)S(1)} %copy.78), kind=kLoop, calls=%fused_computation.29 | loop fusion | flops 27262976 | bytes 27262976 | tf_op jit(solution)/shard_map/concatenate | solution.py:357
  282.5 11.6 %fusion.95 = f32[16,512,512]{2,1,0:T(8,128)} fusion(bf16[512,16,32]{0,2,1:T(8,128)(2,1)S(1)} %bitcast.272, bf16[512,16,32]{0,2,1:T(8,128)(2,1)S(1)} %bitcast.277, bf16[512,16,32]{0,2,1:T(8,128)(2,1)S(1)} %bitcast.287, bf16[512,16,32]{0,2,1:T(8,128)(2,1)S(1)} %bitcast.282), kind=kOutput, calls=%fused_computation.163 | convolution fusion | flops 541065216 | bytes 18874368 | tf_op jit(solution)/shard_map/while/body/eval_jaxpr/while/body/eval_jaxpr/sqhe,skhe->shqk/dot_general | solution.py:67
  294.2 9.3 %fusion.127 = f32[16,512,512]{2,1,0:T(8,128)} fusion(bf16[512,16,32]{0,2,1:T(8,128)(2,1)S(1)} %copy-done.26, bf16[512,16,32]{0,2,1:T(8,128)(2,1)S(1)} %copy-done.24, pred[]{:T(512)S(6)} %eq.11, bf16[512,16,32]{0,2,1:T(8,128)(2,1)S(1)} %bitcast.273, bf16[512,16,32]{0,2,1:T(8,128)(2,1)S(1)} %bitcast.278, bf16[512,16,32]{0,2,1:T(8,128)(2,1)S(1)} %bitcast.298, ...), kind=kOutput, calls=%fused_computation.218 | convolution fusion | flops 546308096 | bytes 20971520 | tf_op jit(solution)/shard_map/while/body/eval_jaxpr/while/body/eval_jaxpr/sqhe,skhe->shqk/dot_general | solution.py:67
  303.5 4.6 copy.79
  308.2 5.3 convolution_convert_fusion.4
  320.8 6.9 %convolution_convert_fusion.2 = bf16[8,352,1024]{2,1,0:T(8,128)(2,1)} fusion(bf16[8,352,512]{2,1,0:T(8,128)(2,1)} %bitcast.329, bf16[1,512,1024]{2,1,0:T(8,128)(2,1)S(1)} %copy-done.42, pred[512]{0:T(512)(128)(4,1)S(1)} %copy-done.58), kind=kOutput, calls=%fused_computation.57 | convolution fusion | flops 2957246464 | bytes 9699840 | tf_op jit(solution)/shard_map/srf,srd->fd/dot_general | solution.py:336
  328.0 10.2 %fusion.23 = f32[16,64,512]{2,1,0:T(8,128)} fusion(bf16[512,16,64]{0,2,1:T(8,128)(2,1)} %bitcast.314, f32[16,512,512]{2,1,0:T(8,128)} %fusion.95, f32[16,512]{1,0:T(8,128)S(1)} %bitcast.341, pred[512,512]{1,0:T(8,128)(4,1)S(1)} %and_and_fusion.2), kind=kOutput, calls=%fused_computation.37 | convolution fusion | flops 553648128 | bytes 20217856 | tf_op jit(solution)/shard_map/while/body/eval_jaxpr/while/body/eval_jaxpr/shqk,sqhe->skhe/dot_general | solution.py:137
  338.2 9.3 %multiply_convert_fusion.1 = bf16[16,512,512]{2,1,0:T(8,128)(2,1)S(1)} fusion(f32[16,512,512]{2,1,0:T(8,128)} %fusion.95, bf16[512,16,64]{0,2,1:T(8,128)(2,1)S(1)} %bitcast.316, bf16[512,16,64]{0,2,1:T(8,128)(2,1)S(1)} %bitcast.324, f32[16,512]{1,0:T(8,128)S(1)} %bitcast.335, f32[16,512]{1,0:T(8,128)S(1)} %bitcast.342, pred[512,512]{1,0:T(8,128)(4,1)S(1)} %and_and_fusion.2), kind=kOutput, calls=%fused_computation.27 | convolution fusion | flops 562036736 | bytes 27590656 | tf_op jit(solution)/shard_map/while/body/eval_jaxpr/while/body/eval_jaxpr/sqhe,skhe->shqk/dot_general | solution.py:143
  354.4 13.3 %collective-permute-done.4 = f32[1,512,16]{1,2,0:T(8,128)S(1)} collective-permute-done((f32[1,512,16]{1,2,0:T(8,128)S(1)}, f32[1,512,16]{1,2,0:T(8,128)S(1)}, u32[]{:S(2)}, u32[]{:S(2)}) %collective-permute-start.4) | collective-permute-done | bytes 32800 | tf_op jit(solution)/shard_map/ppermute | solution.py:370
  367.8 10.0 %convert_multiply_fusion.5 = f32[16,64,512]{2,1,0:T(8,128)} fusion(f32[16,64,512]{2,1,0:T(8,128)S(1)} %copy-done.59, f32[16,512,512]{2,1,0:T(8,128)} %fusion.127, f32[16,512]{1,0:T(8,128)S(1)} %select_bitcast_fusion.1, pred[512,512]{1,0:T(8,128)(4,1)S(1)} %and_and_fusion.1, pred[]{:T(512)S(6)} %eq.11, bf16[1,512,16,64]{1,3,2,0:T(8,128)(2,1)S(1)} %bitcast.317, ...), kind=kOutput, calls=%fused_computation.103 | convolution fusion | flops 556793856 | bytes 23363584 | tf_op jit(solution)/shard_map/while/body/eval_jaxpr/while/body/eval_jaxpr/shqk,sqhe->skhe/dot_general | solution.py:137
  383.9 10.3 %multiply_convert_fusion = bf16[16,512,512]{2,1,0:T(8,128)(2,1)S(1)} fusion(f32[16,512,512]{2,1,0:T(8,128)} %fusion.127, f32[16,512]{1,0:T(8,128)S(1)} %select_bitcast_fusion, f32[16,512]{1,0:T(8,128)S(1)} %select_bitcast_fusion.1, pred[512,512]{1,0:T(8,128)(4,1)S(1)} %and_and_fusion.1, bf16[512,16,64]{0,2,1:T(8,128)(2,1)} %bitcast.320, ...), kind=kOutput, calls=%fused_computation.25 | convolution fusion | flops 563085312 | bytes 29687808 | tf_op jit(solution)/shard_map/while/body/eval_jaxpr/while/body/eval_jaxpr/sqhe,skhe->shqk/dot_general | solution.py:143
  404.7 7.2 %fusion.51 = (bf16[1024]{0:T(1024)(128)(2,1)S(1)}, f32[512]{0:T(512)S(1)}, f32[512,1024]{1,0:T(8,128)S(1)}) fusion(bf16[1,512,1024]{2,1,0:T(8,128)(2,1)S(1)} %copy-done.11, f32[512]{0:T(512)S(1)} %copy-done.57, f32[1024]{0:T(1024)S(1)} %bitcast.338, bf16[1024,3072]{1,0:T(8,128)(2,1)} %bitcast.307, bf16[1,512,1024]{2,1,0:T(8,128)(2,1)S(1)} %copy-done.39, ...), kind=kOutput, calls=%fused_computation.81 | convolution fusion | flops 3234331136 | bytes 12593152 | tf_op jit(solution)/shard_map/sre,de->srd/dot_general | solution.py:414
  417.3 5.1 convolution_convert_fusion.1
  429.7 33.1 %reduce-scatter.8.cloned.1.call-done = bf16[1,352,1024]{2,1,0:T(8,128)(2,1)} async-done(((bf16[8,352,1024]{2,1,0:T(8,128)(2,1)}), bf16[1,352,1024]{2,1,0:T(8,128)(2,1)}) %reduce-scatter.8.cloned.1.call-update) | async-done | bytes 720912 | tf_op jit(solution)/shard_map/reduce_scatter | solution.py:223
  470.4 11.5 %collective-permute-done.8 = bf16[1,352,1024]{2,1,0:T(8,128)(2,1)S(1)} collective-permute-done((bf16[1,352,1024]{2,1,0:T(8,128)(2,1)}, bf16[1,352,1024]{2,1,0:T(8,128)(2,1)S(1)}, u32[]{:S(2)}, u32[]{:S(2)}) %collective-permute-start.8) | collective-permute-done | bytes 720928 | tf_op jit(solution)/shard_map/ppermute | solution.py:213
  485.4 44.5 %reduce-scatter.4.cloned.1.call-done = bf16[1,136,3072]{2,1,0:T(8,128)(2,1)} async-done(((bf16[8,136,3072]{2,1,0:T(8,128)(2,1)}), bf16[1,136,3072]{2,1,0:T(8,128)(2,1)}) %reduce-scatter.4.cloned.1.call-update) | async-done | bytes 835600 | tf_op jit(solution)/shard_map/reduce_scatter | solution.py:223
  533.2 6.8 %fusion.63 = bf16[1,512,1024]{2,1,0:T(8,128)(2,1)} fusion(f32[1,512,1024]{2,1,0:T(8,128)S(1)} %copy-done.13, bf16[2816,1024]{1,0:T(8,128)(2,1)} %bitcast.310, bf16[1,512,2816]{2,1,0:T(8,128)(2,1)S(1)} %copy-done.35, pred[512]{0:T(512)(128)(4,1)S(1)} %copy-done.58), kind=kOutput, calls=%fused_computation.102 | convolution fusion | flops 2954362880 | bytes 11796992 | tf_op jit(solution)/shard_map/srf,fd->srd/dot_general | solution.py:330
  540.0 15.9 %collective-permute-done.10 = bf16[1,352,1024]{2,1,0:T(8,128)(2,1)} collective-permute-done((bf16[1,352,1024]{2,1,0:T(8,128)(2,1)}, bf16[1,352,1024]{2,1,0:T(8,128)(2,1)}, u32[]{:S(2)}, u32[]{:S(2)}) %collective-permute-start.10) | collective-permute-done | bytes 720928 | tf_op jit(solution)/shard_map/ppermute | solution.py:217
  558.2 32.2 %all-reduce.6.cloned.1.call-done = bf16[136,3072]{1,0:T(8,128)(2,1)} async-done(((bf16[136,3072]{1,0:T(8,128)(2,1)}), bf16[136,3072]{1,0:T(8,128)(2,1)}) %all-reduce.6.cloned.1.call-update) | async-done | bytes 835600 | tf_op jit(solution)/shard_map/psum | solution.py:224
  593.5 11.7 %collective-permute-done.7 = bf16[1,128,6656]{2,1,0:T(8,128)(2,1)S(1)} collective-permute-done((bf16[1,128,6656]{2,1,0:T(8,128)(2,1)S(1)}, bf16[1,128,6656]{2,1,0:T(8,128)(2,1)S(1)}, u32[]{:S(2)}, u32[]{:S(2)}) %collective-permute-start.7) | collective-permute-done | bytes 1703968 | tf_op jit(solution)/shard_map/ppermute | solution.py:217
  (250 shorter events, 148.7 us)
Async XLA Ops:
  7.2 82.8 %all-gather.7.cloned.1.call-start = ((), (), s32[]{:S(2)}) async-start(), calls=%async_computation.7 | async-start | bytes 7520256 | tf_op jit(solution)/shard_map/all_gather | solution.py:200
  10.1 153.9 %all-gather.9.cloned.1.call-start = ((), (), s32[]{:S(2)}) async-start(), calls=%async_computation.8 | async-start | bytes 8847360 | tf_op jit(solution)/shard_map/all_gather | solution.py:200
  11.3 200.1 %all-gather.11.cloned.1.call-start = ((), (), s32[]{:S(2)}) async-start(), calls=%async_computation.9 | async-start | bytes 12976128 | tf_op jit(solution)/shard_map/all_gather | solution.py:200
  13.0 412.9 %reduce-scatter.6.cloned.1.call-start = ((), (), s32[]{:S(2)}) async-start(), calls=%async_computation.5 | async-start | bytes 15335424 | tf_op jit(solution)/shard_map/reduce_scatter | solution.py:223
  13.0 85.7 %collective-permute-start.1 = (bf16[1,512,1024]{2,1,0:T(8,128)(2,1)S(1)}, bf16[1,512,1024]{2,1,0:T(8,128)(2,1)}, u32[]{:S(2)}, u32[]{:S(2)}) collective-permute-start(bf16[1,512,1024]{2,1,0:T(8,128)(2,1)S(1)} %copy-done.37), channel_id=1, source_target_pairs={{0,1},{2,3},{4,5},{6,7},{8,9},{10,11},{12,13},{14,15},{16,17},{18,... | collective-permute-start | bytes 3145736 | tf_op jit(solution)/shard_map/ppermute | solution.py:282
  18.9 70.8 %collective-permute-start = (bf16[1,512,1024]{2,1,0:T(8,128)(2,1)S(1)}, bf16[1,512,1024]{2,1,0:T(8,128)(2,1)S(1)}, u32[]{:S(2)}, u32[]{:S(2)}) collective-permute-start(bf16[1,512,1024]{2,1,0:T(8,128)(2,1)S(1)} %copy-done.9), channel_id=1, source_target_pairs={{0,1},{1,0},{2,3},{3,2},{4,5},{5,4},{6,7},{7,6},{8,9},{9,8},{10,11... | collective-permute-start | bytes 3145736 | tf_op jit(solution)/shard_map/ppermute | solution.py:281
  20.5 89.0 %copy-start.56 = (f32[512]{0:T(512)}, f32[512]{0:T(512)S(1)}, u32[]{:S(2)}) copy-start(f32[512]{0:T(512)S(1)} %add_rsqrt_fusion.1) | copy-start | bytes 6148
  21.9 102.4 %copy-start.47 = (f32[512,32]{0,1:T(8,128)}, f32[512,32]{0,1:T(8,128)S(1)}, u32[]{:S(2)}) copy-start(f32[512,32]{0,1:T(8,128)S(1)} %get-tuple-element.391) | copy-start | bytes 196612
  95.1 14.3 %copy-start.51 = (f32[8,1,128]{2,1,0:T(1,128)}, f32[8,1,128]{2,1,0:T(1,128)S(1)}, u32[]{:S(2)}) copy-start(f32[8,1,128]{2,1,0:T(1,128)S(1)} %get-tuple-element.355) | copy-start | bytes 12292
  172.4 38.9 %copy-start.55 = (f32[8,1,128]{2,1,0:T(1,128)S(1)}, f32[8,1,128]{2,1,0:T(1,128)}, u32[]{:S(2)}) copy-start(f32[8,1,128]{2,1,0:T(1,128)} %get-tuple-element.354) | copy-start | bytes 12292
  173.8 85.4 %copy-start.12 = (f32[1,512,1024]{2,1,0:T(8,128)}, f32[1,512,1024]{2,1,0:T(8,128)S(1)}, u32[]{:S(2)}) copy-start(f32[1,512,1024]{2,1,0:T(8,128)S(1)} %get-tuple-element.397) | copy-start | bytes 6291460
  211.3 13.4 %copy-start.23 = (bf16[8,352,1024]{2,1,0:T(8,128)(2,1)S(1)}, bf16[8,352,1024]{2,1,0:T(8,128)(2,1)}, u32[]{:S(2)}) copy-start(bf16[8,352,1024]{2,1,0:T(8,128)(2,1)} %slice.159) | copy-start | bytes 17301508
  211.3 13.4 %copy-start.41 = (bf16[1,512,1024]{2,1,0:T(8,128)(2,1)S(1)}, bf16[1,512,1024]{2,1,0:T(8,128)(2,1)}, u32[]{:S(2)}) copy-start(bf16[1,512,1024]{2,1,0:T(8,128)(2,1)} %param.17) | copy-start | bytes 3145732
  211.3 13.4 %copy-start.58 = (pred[512]{0:T(512)(128)(4,1)S(1)}, pred[512]{0:T(512)(128)(4,1)}, u32[]{:S(2)}) copy-start(pred[512]{0:T(512)(128)(4,1)} %fusion.111) | copy-start | bytes 1540
  279.8 183.1 %reduce-scatter.8.cloned.1.call-start = ((), (), s32[]{:S(2)}) async-start(), calls=%async_computation.6 | async-start | bytes 6488064 | tf_op jit(solution)/shard_map/reduce_scatter | solution.py:223
  281.0 22.5 %collective-permute-start.2 = (f32[1,16,512]{2,1,0:T(8,128)S(1)}, f32[1,16,512]{2,1,0:T(8,128)S(1)}, u32[]{:S(2)}, u32[]{:S(2)}) collective-permute-start(f32[1,16,512]{2,1,0:T(8,128)S(1)} %bitcast.340), channel_id=1, source_target_pairs={{1,0},{3,2},{5,4},{7,6},{9,8},{11,10},{13,12},{15,14},{17,16},{19,... | collective-permute-start | bytes 98312 | tf_op jit(solution)/shard_map/ppermute | solution.py:370
  282.5 11.7 %copy-start.18 = (bf16[1,512,16,32]{1,3,2,0:T(8,128)(2,1)S(1)}, bf16[1,512,16,32]{1,3,2,0:T(8,128)(2,1)}, u32[]{:S(2)}) copy-start(bf16[1,512,16,32]{1,3,2,0:T(8,128)(2,1)} %copy-done.17) | copy-start | bytes 1572868
  282.5 11.7 %copy-start.20 = (bf16[1,512,16,32]{1,3,2,0:T(8,128)(2,1)S(1)}, bf16[1,512,16,32]{1,3,2,0:T(8,128)(2,1)}, u32[]{:S(2)}) copy-start(bf16[1,512,16,32]{1,3,2,0:T(8,128)(2,1)} %copy-done.19) | copy-start | bytes 1572868
  282.5 11.6 %copy-start.24 = (bf16[512,16,32]{0,2,1:T(8,128)(2,1)S(1)}, bf16[512,16,32]{0,2,1:T(8,128)(2,1)}, u32[]{:S(2)}) copy-start(bf16[512,16,32]{0,2,1:T(8,128)(2,1)} %get-tuple-element.368) | copy-start | bytes 1572868
  282.5 11.6 %copy-start.26 = (bf16[512,16,32]{0,2,1:T(8,128)(2,1)S(1)}, bf16[512,16,32]{0,2,1:T(8,128)(2,1)}, u32[]{:S(2)}) copy-start(bf16[512,16,32]{0,2,1:T(8,128)(2,1)} %get-tuple-element.369) | copy-start | bytes 1572868
  315.8 52.0 %collective-permute-start.3 = (bf16[1,512,16,64]{1,3,2,0:T(8,128)(2,1)}, bf16[1,512,16,64]{1,3,2,0:T(8,128)(2,1)}, u32[]{:S(2)}, u32[]{:S(2)}) collective-permute-start(bf16[1,512,16,64]{1,3,2,0:T(8,128)(2,1)} %bitcast.312), channel_id=1, source_target_pairs={{1,0},{3,2},{5,4},{7,6},{9,8},{11,10},{13,12},{15,14},{17,16},{19,... | collective-permute-start | bytes 3145736 | tf_op jit(solution)/shard_map/ppermute | solution.py:370
  319.5 48.3 %collective-permute-start.4 = (f32[1,512,16]{1,2,0:T(8,128)S(1)}, f32[1,512,16]{1,2,0:T(8,128)S(1)}, u32[]{:S(2)}, u32[]{:S(2)}) collective-permute-start(f32[1,512,16]{1,2,0:T(8,128)S(1)} %bitcast.334), channel_id=1, source_target_pairs={{1,0},{3,2},{5,4},{7,6},{9,8},{11,10},{13,12},{15,14},{17,16},{19,... | collective-permute-start | bytes 98312 | tf_op jit(solution)/shard_map/ppermute | solution.py:370
  327.7 202.1 %reduce-scatter.4.cloned.1.call-start = ((), (), s32[]{:S(2)}) async-start(), calls=%async_computation.3 | async-start | bytes 7520256 | tf_op jit(solution)/shard_map/reduce_scatter | solution.py:223
  350.4 17.3 %copy-start.59 = (f32[16,64,512]{2,1,0:T(8,128)S(1)}, f32[16,64,512]{2,1,0:T(8,128)}, u32[]{:S(2)}) copy-start(f32[16,64,512]{2,1,0:T(8,128)} %fusion.23) | copy-start | bytes 6291460
  425.8 164.6 %all-reduce.6.cloned.1.call-start = ((), (), s32[]{:S(2)}) async-start(), calls=%async_computation.4 | async-start | bytes 1671168 | tf_op jit(solution)/shard_map/psum | solution.py:224
  425.9 40.5 %collective-permute-start.5 = (bf16[1,128,6656]{2,1,0:T(8,128)(2,1)}, bf16[1,128,6656]{2,1,0:T(8,128)(2,1)S(1)}, u32[]{:S(2)}, u32[]{:S(2)}) collective-permute-start(bf16[1,128,6656]{2,1,0:T(8,128)(2,1)} %reduce-scatter.6.cloned.1.call-done), channel_id=1, source_target_pairs={{0,8},{24,16},{1,9},{25,17},{2,10},{26,18},{3,11},{27,19},{4,12},{... | collective-permute-start | bytes 5111816 | tf_op jit(solution)/shard_map/ppermute | solution.py:213
  462.9 19.1 %copy-start.43 = (bf16[1,352,1024]{2,1,0:T(8,128)(2,1)S(1)}, bf16[1,352,1024]{2,1,0:T(8,128)(2,1)}, u32[]{:S(2)}) copy-start(bf16[1,352,1024]{2,1,0:T(8,128)(2,1)} %reduce-scatter.8.cloned.1.call-done) | copy-start | bytes 2162692
  462.9 19.1 %collective-permute-start.8 = (bf16[1,352,1024]{2,1,0:T(8,128)(2,1)}, bf16[1,352,1024]{2,1,0:T(8,128)(2,1)S(1)}, u32[]{:S(2)}, u32[]{:S(2)}) collective-permute-start(bf16[1,352,1024]{2,1,0:T(8,128)(2,1)} %reduce-scatter.8.cloned.1.call-done), channel_id=1, source_target_pairs={{0,8},{24,16},{1,9},{25,17},{2,10},{26,18},{3,11},{27,19},{4,12},{... | collective-permute-start | bytes 2162696 | tf_op jit(solution)/shard_map/ppermute | solution.py:213
  468.3 61.6 %collective-permute-start.6 = (bf16[1,128,6656]{2,1,0:T(8,128)(2,1)S(1)}, bf16[1,128,6656]{2,1,0:T(8,128)(2,1)}, u32[]{:S(2)}, u32[]{:S(2)}) collective-permute-start(bf16[1,128,6656]{2,1,0:T(8,128)(2,1)S(1)} %add_convert_fusion.1), channel_id=1, source_target_pairs={{8,16},{16,8},{9,17},{17,9},{10,18},{18,10},{11,19},{19,11},{12,20... | collective-permute-start | bytes 5111816 | tf_op jit(solution)/shard_map/ppermute | solution.py:215
  482.2 0.7 collective-permute-start.9
  484.1 71.8 %collective-permute-start.10 = (bf16[1,352,1024]{2,1,0:T(8,128)(2,1)}, bf16[1,352,1024]{2,1,0:T(8,128)(2,1)}, u32[]{:S(2)}, u32[]{:S(2)}) collective-permute-start(bf16[1,352,1024]{2,1,0:T(8,128)(2,1)} %add_convert_fusion.3), channel_id=1, source_target_pairs={{8,0},{16,24},{9,1},{17,25},{10,2},{18,26},{11,3},{19,27},{12,4},{... | collective-permute-start | bytes 2162696 | tf_op jit(solution)/shard_map/ppermute | solution.py:217
  531.9 73.3 %collective-permute-start.7 = (bf16[1,128,6656]{2,1,0:T(8,128)(2,1)S(1)}, bf16[1,128,6656]{2,1,0:T(8,128)(2,1)S(1)}, u32[]{:S(2)}, u32[]{:S(2)}) collective-permute-start(bf16[1,128,6656]{2,1,0:T(8,128)(2,1)S(1)} %add_convert_fusion), channel_id=1, source_target_pairs={{8,0},{16,24},{9,1},{17,25},{10,2},{18,26},{11,3},{19,27},{12,4},{... | collective-permute-start | bytes 5111816 | tf_op jit(solution)/shard_map/ppermute | solution.py:217
  (50 other events, 168.3 us)
Sparse Core Ops, SparseCore 0:
  10.5 72.8 all-gather.6
  85.2 55.9 all-gather.8
  143.7 67.5 all-gather.10
  279.9 120.6 reduce-scatter.5
  403.9 58.9 reduce-scatter.7
  466.2 63.6 reduce-scatter.3
  532.2 58.0 all-reduce.5

commit v6 on v5

--- a/solution.py
+++ b/solution.py
@@ -210,10 +210,10 @@
     if n_rep != 4:
         return lax.psum(x, "rep")
     me = lax.axis_index("rep")
-    folded = (x.astype(jnp.float32) + lax.ppermute(x, "rep", [(0, 1), (3, 2)]).astype(jnp.float32)).astype(x.dtype)
-    total = (
-        folded.astype(jnp.float32) + lax.ppermute(folded, "rep", [(1, 2), (2, 1)]).astype(jnp.float32)
-    ).astype(x.dtype)
+    arrived = lax.ppermute(x, "rep", [(0, 1), (3, 2)])
+    folded = (x.astype(jnp.float32) + arrived.astype(jnp.float32)).astype(x.dtype)
+    arrived = lax.ppermute(folded, "rep", [(1, 2), (2, 1)])
+    total = (folded.astype(jnp.float32) + arrived.astype(jnp.float32)).astype(x.dtype)
     sent_out = lax.ppermute(total, "rep", [(1, 0), (2, 3)])
     return jnp.where((me == 0) | (me == 3), sent_out, total)
 

time: 625 us -> 625 us (level)
  no operation moved by 1% of the time
where the time goes in v6:
time: 625 us; the launch traced here: 615 us
  waiting for transfers between devices  268 us (43%)
  matrix products  182 us (29%)
  other arithmetic  69.2 us (11%)
  local copies, waits for them, and re-layouts  56.2 us (9%)
  starting transfers between devices  23.3 us (4%)
  between operations  16.1 us (3%)
    reduce_scatter x3, waiting for transfers between devices, scatter_blocks(): summed = lax.psum_scatter(packed, GROUP, scatter_dimension=0, tiled=True)  77.7 us
    ppermute x1, waiting for transfers between devices, shards(): other_tokens = lax.ppermute(tokens, 'ctx', [(0, 1), (1, 0)])  67.8 us
    all_gather x3, waiting for transfers between devices, gather_blocks(): gathered = lax.all_gather(packed, GROUP, axis=0, tiled=False)  37.5 us
    psum x1, waiting for transfers between devices, scatter_blocks(): lax.psum(summed, 'rep')  32.2 us
    ppermute x2, waiting for transfers between devices, rep_sum(): sent_out = lax.ppermute(total, 'rep', [(1, 0), (2, 3)])  27.6 us
    dot_general x4, matrix products, score_block(): jnp.einsum('sqhe,skhe->shqk', q_rows, k_rows, preferred_element_type=jnp....  27 us
    dot_general x2, matrix products, one_block(): jnp.einsum('shqk,sqhe->skhe', probabilities.astype(jnp.bfloat16), g_rows,...  20.1 us
    dot_general x2, matrix products, one_block(): jnp.einsum('sqhe,skhe->shqk', g_rows, v_group, preferred_element_type=jnp...  19.6 us
  transfers between devices with their start and end apart: 18, of which 9 were waited for; matrix products, arithmetic and copies ran while one was open for 37% of the time, Pallas kernels for 0%

profile of v6, /device:TPU:0, one launch (start us, length us, event | category | flops | bytes accessed | tf_op | source)
XLA Modules:
  0.0 615.4 jit_solution(12913084785980001606)
XLA Ops:
  13.0 5.9 collective-permute-start.1
  21.9 67.8 %collective-permute-done = bf16[1,512,1024]{2,1,0:T(8,128)(2,1)S(1)} collective-permute-done((bf16[1,512,1024]{2,1,0:T(8,128)(2,1)S(1)}, bf16[1,512,1024]{2,1,0:T(8,128)(2,1)S(1)}, u32[]{:S(2)}, u32[]{:S(2)}) %collective-permute-start) | collective-permute-done | bytes 1048608 | tf_op jit(solution)/shard_map/ppermute | solution.py:281
  109.5 5.8 convolution_bitcast_fusion.1
  134.5 29.5 %while.27 = (s32[]{:T(128)}, bf16[2,1,512,8,64]{2,4,3,1,0:T(8,128)(2,1)}, f32[2,1,1,8,512]{4,3,2,1,0:T(8,128)S(1)}, bf16[2,1,1024,8,64]{2,4,3,1,0:T(8,128)(2,1)}...) while((s32[]{:T(128)}, ...), condition=%wide.region_5.6_spmd.clone, body=%wide.region_2.5_spmd.clone.sunk | while | flops 1125644800 | bytes 73025736 | solution.py:113
  143.4 5.0 fusion.159
  158.0 5.0 fusion.159
  165.9 6.5 %slice.159 = bf16[8,352,1024]{2,1,0:T(8,128)(2,1)} slice(bf16[8,480,1024]{2,1,0:T(8,128)(2,1)} %bitcast.304), slice={[0:8], [128:480], [0:1024]} | slice | bytes 11534336 | tf_op jit(solution)/shard_map/slice | solution.py:203
  173.8 37.5 %all-gather.11.cloned.1.call-done = bf16[1024,5632]{1,0:T(8,128)(2,1)} async-done(((bf16[128,5632]{1,0:T(8,128)(2,1)}), bf16[1024,5632]{1,0:T(8,128)(2,1)}) %all-gather.11.cloned.1.call-update) | async-done | bytes 11534352 | tf_op jit(solution)/shard_map/all_gather | solution.py:200
  211.3 13.4 %convolution_bitcast_fusion = f32[1,512,5632]{2,1,0:T(8,128)} fusion(bf16[1024,5632]{1,0:T(8,128)(2,1)} %all-gather.11.cloned.1.call-done, f32[1,512,1024]{2,1,0:T(8,128)S(1)} %get-tuple-element.397, f32[1024]{0:T(1024)S(1)} %bitcast.343, f32[512]{0:T(512)S(1)} %add_rsqrt_fusion), kind=kOutput, calls=%fused_computation.35 | convolution fusion | flops 5907152896 | bytes 25171968 | tf_op jit(solution)/shard_map/srd,df->srf/dot_general | solution.py:325
  224.7 10.2 %fusion.30 = (bf16[1,512,2816]{2,1,0:T(8,128)(2,1)S(1)}, bf16[1,512,2816]{2,1,0:T(8,128)(2,1)}, bf16[1,512,2816]{2,1,0:T(8,128)(2,1)}) fusion(f32[1,512,5632]{2,1,0:T(8,128)} %convolution_bitcast_fusion, bf16[2816,1024]{1,0:T(8,128)(2,1)S(1)} %bitcast.311, bf16[1,512,1024]{2,1,0:T(8,128)(2,1)S(1)} %copy-done.41, pred[512]{0:T(512)(128)(4,1)S(1)} %copy-done.58), kind=kOutput, calls=%fused_computation.46 | convolution fusion | flops 2977431552 | bytes 27001344 | tf_op jit(solution)/shard_map/srd,fd->srf/dot_general | solution.py:340
  236.5 10.9 %convolution_convert_fusion = bf16[1024,5632]{1,0:T(8,128)(2,1)} fusion(bf16[1,512,2816]{2,1,0:T(8,128)(2,1)} %get-tuple-element.352, bf16[1,512,2816]{2,1,0:T(8,128)(2,1)S(1)} %get-tuple-element.351, f32[1,512,1024]{2,1,0:T(8,128)S(1)} %get-tuple-element.397, f32[1024]{0:T(1024)S(1)} %bitcast.344, f32[512]{0:T(512)S(1)} %add_rsqrt_fusion), kind=kOutput, calls=%fused_computation.34 | convolution fusion | flops 5924454400 | bytes 19404800 | tf_op jit(solution)/shard_map/srd,srf->df/dot_general | solution.py:346
  247.4 11.8 %fusion.58 = (bf16[1024]{0:T(1024)(128)(2,1)S(1)}, f32[512]{0:T(512)S(1)}, f32[512,1024]{1,0:T(8,128)S(1)}) fusion(f32[1,512,1024]{2,1,0:T(8,128)S(1)} %get-tuple-element.397, f32[512]{0:T(512)S(1)} %add_rsqrt_fusion, f32[1024]{0:T(1024)S(1)} %bitcast.345, bf16[1024,5632]{1,0:T(8,128)(2,1)} %all-gather.11.cloned.1.call-done, ...), kind=kOutput, calls=%fused_computation.94 | convolution fusion | flops 5920258560 | bytes 21506048 | tf_op jit(solution)/shard_map/srf,df->srd/dot_general | solution.py:347
  268.2 11.5 %pad_maximum_fusion = bf16[1024,6656]{1,0:T(8,128)(2,1)} fusion(bf16[1024,5632]{1,0:T(8,128)(2,1)} %convolution_convert_fusion, bf16[1024,1024]{1,0:T(8,128)(2,1)S(1)} %copy.78), kind=kLoop, calls=%fused_computation.29 | loop fusion | flops 27262976 | bytes 27262976 | tf_op jit(solution)/shard_map/concatenate | solution.py:357
  282.5 11.6 %fusion.95 = f32[16,512,512]{2,1,0:T(8,128)} fusion(bf16[512,16,32]{0,2,1:T(8,128)(2,1)S(1)} %bitcast.272, bf16[512,16,32]{0,2,1:T(8,128)(2,1)S(1)} %bitcast.277, bf16[512,16,32]{0,2,1:T(8,128)(2,1)S(1)} %bitcast.287, bf16[512,16,32]{0,2,1:T(8,128)(2,1)S(1)} %bitcast.282), kind=kOutput, calls=%fused_computation.163 | convolution fusion | flops 541065216 | bytes 18874368 | tf_op jit(solution)/shard_map/while/body/eval_jaxpr/while/body/eval_jaxpr/sqhe,skhe->shqk/dot_general | solution.py:67
  294.2 9.3 %fusion.127 = f32[16,512,512]{2,1,0:T(8,128)} fusion(bf16[512,16,32]{0,2,1:T(8,128)(2,1)S(1)} %copy-done.26, bf16[512,16,32]{0,2,1:T(8,128)(2,1)S(1)} %copy-done.24, pred[]{:T(512)S(6)} %eq.11, bf16[512,16,32]{0,2,1:T(8,128)(2,1)S(1)} %bitcast.273, bf16[512,16,32]{0,2,1:T(8,128)(2,1)S(1)} %bitcast.278, bf16[512,16,32]{0,2,1:T(8,128)(2,1)S(1)} %bitcast.298, ...), kind=kOutput, calls=%fused_computation.218 | convolution fusion | flops 546308096 | bytes 20971520 | tf_op jit(solution)/shard_map/while/body/eval_jaxpr/while/body/eval_jaxpr/sqhe,skhe->shqk/dot_general | solution.py:67
  303.5 4.6 copy.79
  308.2 5.3 convolution_convert_fusion.4
  320.8 6.9 %convolution_convert_fusion.2 = bf16[8,352,1024]{2,1,0:T(8,128)(2,1)} fusion(bf16[8,352,512]{2,1,0:T(8,128)(2,1)} %bitcast.329, bf16[1,512,1024]{2,1,0:T(8,128)(2,1)S(1)} %copy-done.42, pred[512]{0:T(512)(128)(4,1)S(1)} %copy-done.58), kind=kOutput, calls=%fused_computation.57 | convolution fusion | flops 2957246464 | bytes 9699840 | tf_op jit(solution)/shard_map/srf,srd->fd/dot_general | solution.py:336
  328.0 10.2 %fusion.23 = f32[16,64,512]{2,1,0:T(8,128)} fusion(bf16[512,16,64]{0,2,1:T(8,128)(2,1)} %bitcast.314, f32[16,512,512]{2,1,0:T(8,128)} %fusion.95, f32[16,512]{1,0:T(8,128)S(1)} %bitcast.341, pred[512,512]{1,0:T(8,128)(4,1)S(1)} %and_and_fusion.2), kind=kOutput, calls=%fused_computation.37 | convolution fusion | flops 553648128 | bytes 20217856 | tf_op jit(solution)/shard_map/while/body/eval_jaxpr/while/body/eval_jaxpr/shqk,sqhe->skhe/dot_general | solution.py:137
  338.2 9.3 %multiply_convert_fusion.1 = bf16[16,512,512]{2,1,0:T(8,128)(2,1)S(1)} fusion(f32[16,512,512]{2,1,0:T(8,128)} %fusion.95, bf16[512,16,64]{0,2,1:T(8,128)(2,1)S(1)} %bitcast.316, bf16[512,16,64]{0,2,1:T(8,128)(2,1)S(1)} %bitcast.324, f32[16,512]{1,0:T(8,128)S(1)} %bitcast.335, f32[16,512]{1,0:T(8,128)S(1)} %bitcast.342, pred[512,512]{1,0:T(8,128)(4,1)S(1)} %and_and_fusion.2), kind=kOutput, calls=%fused_computation.27 | convolution fusion | flops 562036736 | bytes 27590656 | tf_op jit(solution)/shard_map/while/body/eval_jaxpr/while/body/eval_jaxpr/sqhe,skhe->shqk/dot_general | solution.py:143
  354.4 13.3 %collective-permute-done.4 = f32[1,512,16]{1,2,0:T(8,128)S(1)} collective-permute-done((f32[1,512,16]{1,2,0:T(8,128)S(1)}, f32[1,512,16]{1,2,0:T(8,128)S(1)}, u32[]{:S(2)}, u32[]{:S(2)}) %collective-permute-start.4) | collective-permute-done | bytes 32800 | tf_op jit(solution)/shard_map/ppermute | solution.py:370
  367.8 10.0 %convert_multiply_fusion.5 = f32[16,64,512]{2,1,0:T(8,128)} fusion(f32[16,64,512]{2,1,0:T(8,128)S(1)} %copy-done.59, f32[16,512,512]{2,1,0:T(8,128)} %fusion.127, f32[16,512]{1,0:T(8,128)S(1)} %select_bitcast_fusion.1, pred[512,512]{1,0:T(8,128)(4,1)S(1)} %and_and_fusion.1, pred[]{:T(512)S(6)} %eq.11, bf16[1,512,16,64]{1,3,2,0:T(8,128)(2,1)S(1)} %bitcast.317, ...), kind=kOutput, calls=%fused_computation.103 | convolution fusion | flops 556793856 | bytes 23363584 | tf_op jit(solution)/shard_map/while/body/eval_jaxpr/while/body/eval_jaxpr/shqk,sqhe->skhe/dot_general | solution.py:137
  383.9 10.3 %multiply_convert_fusion = bf16[16,512,512]{2,1,0:T(8,128)(2,1)S(1)} fusion(f32[16,512,512]{2,1,0:T(8,128)} %fusion.127, f32[16,512]{1,0:T(8,128)S(1)} %select_bitcast_fusion, f32[16,512]{1,0:T(8,128)S(1)} %select_bitcast_fusion.1, pred[512,512]{1,0:T(8,128)(4,1)S(1)} %and_and_fusion.1, bf16[512,16,64]{0,2,1:T(8,128)(2,1)} %bitcast.320, ...), kind=kOutput, calls=%fused_computation.25 | convolution fusion | flops 563085312 | bytes 29687808 | tf_op jit(solution)/shard_map/while/body/eval_jaxpr/while/body/eval_jaxpr/sqhe,skhe->shqk/dot_general | solution.py:143
  404.7 7.2 %fusion.51 = (bf16[1024]{0:T(1024)(128)(2,1)S(1)}, f32[512]{0:T(512)S(1)}, f32[512,1024]{1,0:T(8,128)S(1)}) fusion(bf16[1,512,1024]{2,1,0:T(8,128)(2,1)S(1)} %copy-done.11, f32[512]{0:T(512)S(1)} %copy-done.57, f32[1024]{0:T(1024)S(1)} %bitcast.338, bf16[1024,3072]{1,0:T(8,128)(2,1)} %bitcast.307, bf16[1,512,1024]{2,1,0:T(8,128)(2,1)S(1)} %copy-done.39, ...), kind=kOutput, calls=%fused_computation.81 | convolution fusion | flops 3234331136 | bytes 12593152 | tf_op jit(solution)/shard_map/sre,de->srd/dot_general | solution.py:414
  417.3 5.1 convolution_convert_fusion.1
  429.7 33.1 %reduce-scatter.8.cloned.1.call-done = bf16[1,352,1024]{2,1,0:T(8,128)(2,1)} async-done(((bf16[8,352,1024]{2,1,0:T(8,128)(2,1)}), bf16[1,352,1024]{2,1,0:T(8,128)(2,1)}) %reduce-scatter.8.cloned.1.call-update) | async-done | bytes 720912 | tf_op jit(solution)/shard_map/reduce_scatter | solution.py:223
  470.4 11.5 %collective-permute-done.8 = bf16[1,352,1024]{2,1,0:T(8,128)(2,1)S(1)} collective-permute-done((bf16[1,352,1024]{2,1,0:T(8,128)(2,1)}, bf16[1,352,1024]{2,1,0:T(8,128)(2,1)S(1)}, u32[]{:S(2)}, u32[]{:S(2)}) %collective-permute-start.8) | collective-permute-done | bytes 720928 | tf_op jit(solution)/shard_map/ppermute | solution.py:213
  485.4 44.5 %reduce-scatter.4.cloned.1.call-done = bf16[1,136,3072]{2,1,0:T(8,128)(2,1)} async-done(((bf16[8,136,3072]{2,1,0:T(8,128)(2,1)}), bf16[1,136,3072]{2,1,0:T(8,128)(2,1)}) %reduce-scatter.4.cloned.1.call-update) | async-done | bytes 835600 | tf_op jit(solution)/shard_map/reduce_scatter | solution.py:223
  533.2 6.8 %fusion.63 = bf16[1,512,1024]{2,1,0:T(8,128)(2,1)} fusion(f32[1,512,1024]{2,1,0:T(8,128)S(1)} %copy-done.13, bf16[2816,1024]{1,0:T(8,128)(2,1)} %bitcast.310, bf16[1,512,2816]{2,1,0:T(8,128)(2,1)S(1)} %copy-done.35, pred[512]{0:T(512)(128)(4,1)S(1)} %copy-done.58), kind=kOutput, calls=%fused_computation.102 | convolution fusion | flops 2954362880 | bytes 11796992 | tf_op jit(solution)/shard_map/srf,fd->srd/dot_general | solution.py:330
  540.0 15.9 %collective-permute-done.10 = bf16[1,352,1024]{2,1,0:T(8,128)(2,1)} collective-permute-done((bf16[1,352,1024]{2,1,0:T(8,128)(2,1)}, bf16[1,352,1024]{2,1,0:T(8,128)(2,1)}, u32[]{:S(2)}, u32[]{:S(2)}) %collective-permute-start.10) | collective-permute-done | bytes 720928 | tf_op jit(solution)/shard_map/ppermute | solution.py:217
  558.2 32.2 %all-reduce.6.cloned.1.call-done = bf16[136,3072]{1,0:T(8,128)(2,1)} async-done(((bf16[136,3072]{1,0:T(8,128)(2,1)}), bf16[136,3072]{1,0:T(8,128)(2,1)}) %all-reduce.6.cloned.1.call-update) | async-done | bytes 835600 | tf_op jit(solution)/shard_map/psum | solution.py:224
  593.5 11.7 %collective-permute-done.7 = bf16[1,128,6656]{2,1,0:T(8,128)(2,1)S(1)} collective-permute-done((bf16[1,128,6656]{2,1,0:T(8,128)(2,1)S(1)}, bf16[1,128,6656]{2,1,0:T(8,128)(2,1)S(1)}, u32[]{:S(2)}, u32[]{:S(2)}) %collective-permute-start.7) | collective-permute-done | bytes 1703968 | tf_op jit(solution)/shard_map/ppermute | solution.py:217
  (250 shorter events, 148.7 us)
Async XLA Ops:
  7.2 82.8 %all-gather.7.cloned.1.call-start = ((), (), s32[]{:S(2)}) async-start(), calls=%async_computation.7 | async-start | bytes 7520256 | tf_op jit(solution)/shard_map/all_gather | solution.py:200
  10.1 153.9 %all-gather.9.cloned.1.call-start = ((), (), s32[]{:S(2)}) async-start(), calls=%async_computation.8 | async-start | bytes 8847360 | tf_op jit(solution)/shard_map/all_gather | solution.py:200
  11.3 200.1 %all-gather.11.cloned.1.call-start = ((), (), s32[]{:S(2)}) async-start(), calls=%async_computation.9 | async-start | bytes 12976128 | tf_op jit(solution)/shard_map/all_gather | solution.py:200
  13.0 412.9 %reduce-scatter.6.cloned.1.call-start = ((), (), s32[]{:S(2)}) async-start(), calls=%async_computation.5 | async-start | bytes 15335424 | tf_op jit(solution)/shard_map/reduce_scatter | solution.py:223
  13.0 85.7 %collective-permute-start.1 = (bf16[1,512,1024]{2,1,0:T(8,128)(2,1)S(1)}, bf16[1,512,1024]{2,1,0:T(8,128)(2,1)}, u32[]{:S(2)}, u32[]{:S(2)}) collective-permute-start(bf16[1,512,1024]{2,1,0:T(8,128)(2,1)S(1)} %copy-done.37), channel_id=1, source_target_pairs={{0,1},{2,3},{4,5},{6,7},{8,9},{10,11},{12,13},{14,15},{16,17},{18,... | collective-permute-start | bytes 3145736 | tf_op jit(solution)/shard_map/ppermute | solution.py:282
  18.9 70.8 %collective-permute-start = (bf16[1,512,1024]{2,1,0:T(8,128)(2,1)S(1)}, bf16[1,512,1024]{2,1,0:T(8,128)(2,1)S(1)}, u32[]{:S(2)}, u32[]{:S(2)}) collective-permute-start(bf16[1,512,1024]{2,1,0:T(8,128)(2,1)S(1)} %copy-done.9), channel_id=1, source_target_pairs={{0,1},{1,0},{2,3},{3,2},{4,5},{5,4},{6,7},{7,6},{8,9},{9,8},{10,11... | collective-permute-start | bytes 3145736 | tf_op jit(solution)/shard_map/ppermute | solution.py:281
  20.5 89.0 %copy-start.56 = (f32[512]{0:T(512)}, f32[512]{0:T(512)S(1)}, u32[]{:S(2)}) copy-start(f32[512]{0:T(512)S(1)} %add_rsqrt_fusion.1) | copy-start | bytes 6148
  21.9 102.4 %copy-start.47 = (f32[512,32]{0,1:T(8,128)}, f32[512,32]{0,1:T(8,128)S(1)}, u32[]{:S(2)}) copy-start(f32[512,32]{0,1:T(8,128)S(1)} %get-tuple-element.391) | copy-start | bytes 196612
  95.1 14.3 %copy-start.51 = (f32[8,1,128]{2,1,0:T(1,128)}, f32[8,1,128]{2,1,0:T(1,128)S(1)}, u32[]{:S(2)}) copy-start(f32[8,1,128]{2,1,0:T(1,128)S(1)} %get-tuple-element.355) | copy-start | bytes 12292
  172.4 38.9 %copy-start.55 = (f32[8,1,128]{2,1,0:T(1,128)S(1)}, f32[8,1,128]{2,1,0:T(1,128)}, u32[]{:S(2)}) copy-start(f32[8,1,128]{2,1,0:T(1,128)} %get-tuple-element.354) | copy-start | bytes 12292
  173.8 85.4 %copy-start.12 = (f32[1,512,1024]{2,1,0:T(8,128)}, f32[1,512,1024]{2,1,0:T(8,128)S(1)}, u32[]{:S(2)}) copy-start(f32[1,512,1024]{2,1,0:T(8,128)S(1)} %get-tuple-element.397) | copy-start | bytes 6291460
  211.3 13.4 %copy-start.23 = (bf16[8,352,1024]{2,1,0:T(8,128)(2,1)S(1)}, bf16[8,352,1024]{2,1,0:T(8,128)(2,1)}, u32[]{:S(2)}) copy-start(bf16[8,352,1024]{2,1,0:T(8,128)(2,1)} %slice.159) | copy-start | bytes 17301508
  211.3 13.4 %copy-start.41 = (bf16[1,512,1024]{2,1,0:T(8,128)(2,1)S(1)}, bf16[1,512,1024]{2,1,0:T(8,128)(2,1)}, u32[]{:S(2)}) copy-start(bf16[1,512,1024]{2,1,0:T(8,128)(2,1)} %param.17) | copy-start | bytes 3145732
  211.3 13.4 %copy-start.58 = (pred[512]{0:T(512)(128)(4,1)S(1)}, pred[512]{0:T(512)(128)(4,1)}, u32[]{:S(2)}) copy-start(pred[512]{0:T(512)(128)(4,1)} %fusion.111) | copy-start | bytes 1540
  279.8 183.1 %reduce-scatter.8.cloned.1.call-start = ((), (), s32[]{:S(2)}) async-start(), calls=%async_computation.6 | async-start | bytes 6488064 | tf_op jit(solution)/shard_map/reduce_scatter | solution.py:223
  281.0 22.5 %collective-permute-start.2 = (f32[1,16,512]{2,1,0:T(8,128)S(1)}, f32[1,16,512]{2,1,0:T(8,128)S(1)}, u32[]{:S(2)}, u32[]{:S(2)}) collective-permute-start(f32[1,16,512]{2,1,0:T(8,128)S(1)} %bitcast.340), channel_id=1, source_target_pairs={{1,0},{3,2},{5,4},{7,6},{9,8},{11,10},{13,12},{15,14},{17,16},{19,... | collective-permute-start | bytes 98312 | tf_op jit(solution)/shard_map/ppermute | solution.py:370
  282.5 11.7 %copy-start.18 = (bf16[1,512,16,32]{1,3,2,0:T(8,128)(2,1)S(1)}, bf16[1,512,16,32]{1,3,2,0:T(8,128)(2,1)}, u32[]{:S(2)}) copy-start(bf16[1,512,16,32]{1,3,2,0:T(8,128)(2,1)} %copy-done.17) | copy-start | bytes 1572868
  282.5 11.7 %copy-start.20 = (bf16[1,512,16,32]{1,3,2,0:T(8,128)(2,1)S(1)}, bf16[1,512,16,32]{1,3,2,0:T(8,128)(2,1)}, u32[]{:S(2)}) copy-start(bf16[1,512,16,32]{1,3,2,0:T(8,128)(2,1)} %copy-done.19) | copy-start | bytes 1572868
  282.5 11.6 %copy-start.24 = (bf16[512,16,32]{0,2,1:T(8,128)(2,1)S(1)}, bf16[512,16,32]{0,2,1:T(8,128)(2,1)}, u32[]{:S(2)}) copy-start(bf16[512,16,32]{0,2,1:T(8,128)(2,1)} %get-tuple-element.368) | copy-start | bytes 1572868
  282.5 11.6 %copy-start.26 = (bf16[512,16,32]{0,2,1:T(8,128)(2,1)S(1)}, bf16[512,16,32]{0,2,1:T(8,128)(2,1)}, u32[]{:S(2)}) copy-start(bf16[512,16,32]{0,2,1:T(8,128)(2,1)} %get-tuple-element.369) | copy-start | bytes 1572868
  315.8 52.0 %collective-permute-start.3 = (bf16[1,512,16,64]{1,3,2,0:T(8,128)(2,1)}, bf16[1,512,16,64]{1,3,2,0:T(8,128)(2,1)}, u32[]{:S(2)}, u32[]{:S(2)}) collective-permute-start(bf16[1,512,16,64]{1,3,2,0:T(8,128)(2,1)} %bitcast.312), channel_id=1, source_target_pairs={{1,0},{3,2},{5,4},{7,6},{9,8},{11,10},{13,12},{15,14},{17,16},{19,... | collective-permute-start | bytes 3145736 | tf_op jit(solution)/shard_map/ppermute | solution.py:370
  319.5 48.3 %collective-permute-start.4 = (f32[1,512,16]{1,2,0:T(8,128)S(1)}, f32[1,512,16]{1,2,0:T(8,128)S(1)}, u32[]{:S(2)}, u32[]{:S(2)}) collective-permute-start(f32[1,512,16]{1,2,0:T(8,128)S(1)} %bitcast.334), channel_id=1, source_target_pairs={{1,0},{3,2},{5,4},{7,6},{9,8},{11,10},{13,12},{15,14},{17,16},{19,... | collective-permute-start | bytes 98312 | tf_op jit(solution)/shard_map/ppermute | solution.py:370
  327.7 202.1 %reduce-scatter.4.cloned.1.call-start = ((), (), s32[]{:S(2)}) async-start(), calls=%async_computation.3 | async-start | bytes 7520256 | tf_op jit(solution)/shard_map/reduce_scatter | solution.py:223
  350.4 17.3 %copy-start.59 = (f32[16,64,512]{2,1,0:T(8,128)S(1)}, f32[16,64,512]{2,1,0:T(8,128)}, u32[]{:S(2)}) copy-start(f32[16,64,512]{2,1,0:T(8,128)} %fusion.23) | copy-start | bytes 6291460
  425.8 164.6 %all-reduce.6.cloned.1.call-start = ((), (), s32[]{:S(2)}) async-start(), calls=%async_computation.4 | async-start | bytes 1671168 | tf_op jit(solution)/shard_map/psum | solution.py:224
  425.9 40.5 %collective-permute-start.5 = (bf16[1,128,6656]{2,1,0:T(8,128)(2,1)}, bf16[1,128,6656]{2,1,0:T(8,128)(2,1)S(1)}, u32[]{:S(2)}, u32[]{:S(2)}) collective-permute-start(bf16[1,128,6656]{2,1,0:T(8,128)(2,1)} %reduce-scatter.6.cloned.1.call-done), channel_id=1, source_target_pairs={{0,8},{24,16},{1,9},{25,17},{2,10},{26,18},{3,11},{27,19},{4,12},{... | collective-permute-start | bytes 5111816 | tf_op jit(solution)/shard_map/ppermute | solution.py:213
  462.9 19.1 %copy-start.43 = (bf16[1,352,1024]{2,1,0:T(8,128)(2,1)S(1)}, bf16[1,352,1024]{2,1,0:T(8,128)(2,1)}, u32[]{:S(2)}) copy-start(bf16[1,352,1024]{2,1,0:T(8,128)(2,1)} %reduce-scatter.8.cloned.1.call-done) | copy-start | bytes 2162692
  462.9 19.1 %collective-permute-start.8 = (bf16[1,352,1024]{2,1,0:T(8,128)(2,1)}, bf16[1,352,1024]{2,1,0:T(8,128)(2,1)S(1)}, u32[]{:S(2)}, u32[]{:S(2)}) collective-permute-start(bf16[1,352,1024]{2,1,0:T(8,128)(2,1)} %reduce-scatter.8.cloned.1.call-done), channel_id=1, source_target_pairs={{0,8},{24,16},{1,9},{25,17},{2,10},{26,18},{3,11},{27,19},{4,12},{... | collective-permute-start | bytes 2162696 | tf_op jit(solution)/shard_map/ppermute | solution.py:213
  468.3 61.6 %collective-permute-start.6 = (bf16[1,128,6656]{2,1,0:T(8,128)(2,1)S(1)}, bf16[1,128,6656]{2,1,0:T(8,128)(2,1)}, u32[]{:S(2)}, u32[]{:S(2)}) collective-permute-start(bf16[1,128,6656]{2,1,0:T(8,128)(2,1)S(1)} %add_convert_fusion.1), channel_id=1, source_target_pairs={{8,16},{16,8},{9,17},{17,9},{10,18},{18,10},{11,19},{19,11},{12,20... | collective-permute-start | bytes 5111816 | tf_op jit(solution)/shard_map/ppermute | solution.py:215
  482.2 0.7 collective-permute-start.9
  484.1 71.8 %collective-permute-start.10 = (bf16[1,352,1024]{2,1,0:T(8,128)(2,1)}, bf16[1,352,1024]{2,1,0:T(8,128)(2,1)}, u32[]{:S(2)}, u32[]{:S(2)}) collective-permute-start(bf16[1,352,1024]{2,1,0:T(8,128)(2,1)} %add_convert_fusion.3), channel_id=1, source_target_pairs={{8,0},{16,24},{9,1},{17,25},{10,2},{18,26},{11,3},{19,27},{12,4},{... | collective-permute-start | bytes 2162696 | tf_op jit(solution)/shard_map/ppermute | solution.py:217
  531.9 73.3 %collective-permute-start.7 = (bf16[1,128,6656]{2,1,0:T(8,128)(2,1)S(1)}, bf16[1,128,6656]{2,1,0:T(8,128)(2,1)S(1)}, u32[]{:S(2)}, u32[]{:S(2)}) collective-permute-start(bf16[1,128,6656]{2,1,0:T(8,128)(2,1)S(1)} %add_convert_fusion), channel_id=1, source_target_pairs={{8,0},{16,24},{9,1},{17,25},{10,2},{18,26},{11,3},{19,27},{12,4},{... | collective-permute-start | bytes 5111816 | tf_op jit(solution)/shard_map/ppermute | solution.py:217
  (50 other events, 168.3 us)
Sparse Core Ops, SparseCore 0:
  10.5 72.8 all-gather.6
  85.2 55.9 all-gather.8
  143.7 67.5 all-gather.10
  279.9 120.6 reduce-scatter.5
  403.9 58.9 reduce-scatter.7
  466.2 63.6 reduce-scatter.3
  532.2 58.0 all-reduce.5

commit v7 on v6

--- a/solution.py
+++ b/solution.py
@@ -1,6 +1,9 @@
+import functools
+
 import jax
 import jax.numpy as jnp
 from jax import lax
+from jax.experimental import pallas as pl
 from jax.sharding import PartitionSpec as P
 
 
@@ -185,11 +188,72 @@
     )
 
 
-def rows_to_sums(rows, k_len):
-    n_slots, n_heads, q_len = rows.shape
-    q_block, per_group = head_groups(n_slots, q_len, n_heads, k_len)
-    grouped = rows.reshape(n_slots, n_heads // per_group, per_group, q_len // q_block, q_block)
-    return jnp.transpose(grouped, (1, 3, 0, 2, 4))
+FAR = 1 << 30
+
+
+def _block_backward_kernel(q_ref, k_ref, v_ref, g_ref, lse_ref, dots_ref, qpos_ref, kpos_ref,
+                           dq_ref, dk_ref, dv_ref, *, head_width, scale):
+    pair = pl.program_id(1)
+    allowed = kpos_ref[0] <= qpos_ref[...]
+    for j in range(2):
+        cols = slice(j * head_width, (j + 1) * head_width)
+        q = q_ref[0, :, cols]
+        k = k_ref[0, :, cols]
+        v = v_ref[0, :, cols]
+        g = g_ref[0, :, cols]
+        head = 2 * pair + j
+        lse = lse_ref[0, pl.ds(head, 1), :]
+        dots = dots_ref[0, pl.ds(head, 1), :]
+        nt = (((1,), (1,)), ((), ()))
+        scores = lax.dot_general(k, q, nt, preferred_element_type=jnp.float32) * scale
+        scores = jnp.where(allowed, scores, -1e30)
+        probs = jnp.exp(scores - lse)
+        dv_ref[0, :, cols] = jnp.dot(probs.astype(jnp.bfloat16), g, preferred_element_type=jnp.float32)
+        dprobs = lax.dot_general(v, g, nt, preferred_element_type=jnp.float32)
+        dscores = (probs * (dprobs - dots)).astype(jnp.bfloat16)
+        dk_ref[0, :, cols] = jnp.dot(dscores, q, preferred_element_type=jnp.float32) * scale
+        tn = (((0,), (0,)), ((), ()))
+        dq_ref[0, :, cols] = lax.dot_general(dscores, k, tn, preferred_element_type=jnp.float32) * scale
+
+
+def block_backward(queries, keys, values, upstream, lse_rows, dot_rows, q_pos, k_pos, lengths):
+    n_slots, q_len, n_heads, head_width = queries.shape
+    k_len = keys.shape[1]
+    width = n_heads * head_width
+    pair_width = 2 * head_width
+    flat = lambda a: a.reshape(a.shape[0], a.shape[1], width)
+    kpos = jnp.where(
+        (k_pos[None, :] < lengths[:, None]) & (k_pos[None, :] >= 0), k_pos[None, :], FAR
+    ).astype(jnp.int32)[..., None]
+    qpos = q_pos.astype(jnp.int32)[None, :]
+    kernel = functools.partial(_block_backward_kernel, head_width=head_width, scale=head_width ** (-0.5))
+    q_spec = pl.BlockSpec((1, q_len, pair_width), lambda s, p: (s, 0, p))
+    k_spec = pl.BlockSpec((1, k_len, pair_width), lambda s, p: (s, 0, p))
+    row_spec = pl.BlockSpec((1, n_heads, q_len), lambda s, p: (s, 0, 0))
+    flops = n_slots * n_heads * 10 * q_len * k_len * head_width
+    dq, dk, dv = pl.pallas_call(
+        kernel,
+        grid=(n_slots, n_heads // 2),
+        in_specs=[
+            q_spec, k_spec, k_spec, q_spec, row_spec, row_spec,
+            pl.BlockSpec((1, q_len), lambda s, p: (0, 0)),
+            pl.BlockSpec((1, k_len, 1), lambda s, p: (s, 0, 0)),
+        ],
+        out_specs=[q_spec, k_spec, k_spec],
+        out_shape=[
+            jax.ShapeDtypeStruct((n_slots, q_len, width), jnp.float32),
+            jax.ShapeDtypeStruct((n_slots, k_len, width), jnp.float32),
+            jax.ShapeDtypeStruct((n_slots, k_len, width), jnp.float32),
+        ],
+        cost_estimate=pl.CostEstimate(
+            flops=flops,
+            transcendentals=n_slots * n_heads * q_len * k_len,
+            bytes_accessed=2 * (2 * q_len + 2 * k_len) * width * n_slots + 4 * (q_len + 2 * k_len) * width * n_slots,
+        ),
+    )(flat(queries), flat(keys), flat(values), flat(upstream), lse_rows, dot_rows, qpos, kpos)
+    shape_q = (n_slots, q_len, n_heads, head_width)
+    shape_k = (n_slots, k_len, n_heads, head_width)
+    return dq.reshape(shape_q), dk.reshape(shape_k), dv.reshape(shape_k)
 
 
 GROUP = ("fsdp", "ctx")
@@ -367,26 +431,25 @@
     row_dots = jnp.sum(g_attended.astype(jnp.float32) * attended.astype(jnp.float32), axis=-1)
     if paired:
         lse_rows = sums_to_rows(attn_lse)
+        dot_rows = jnp.transpose(row_dots, (0, 2, 1))
         later_g, later_dots, later_lse = lax.ppermute(
-            (g_attended, row_dots, lse_rows), "ctx", [(1, 0)]
-        )
-        g_queries, g_keys, g_values = attend_backward(
-            queries, keys, values, g_attended, row_dots,
-            rows_to_sums(lse_rows, slot_rows), q_pos, q_pos, lengths,
+            (g_attended, dot_rows, lse_rows), "ctx", [(1, 0)]
+        )
+        g_queries, g_keys, g_values = block_backward(
+            queries, keys, values, g_attended, lse_rows, dot_rows, q_pos, q_pos, lengths
         )
         later = ctx_index == 1
         pick = lambda mine, theirs: jnp.where(later, mine, theirs)
-        cross_q, cross_dq_k, cross_dq_v = (
-            pick(queries, other_q), pick(other_k, keys), pick(other_v, values)
-        )
-        cross_g = pick(g_attended, later_g)
-        cross_dots = pick(row_dots, later_dots)
-        cross_lse = pick(lse_rows, later_lse)
-        cross_qpos = pick(q_pos, other_pos)
-        cross_kpos = pick(other_pos, q_pos)
-        x_dq, x_dk, x_dv = attend_backward(
-            cross_q, cross_dq_k, cross_dq_v, cross_g, cross_dots,
-            rows_to_sums(cross_lse, slot_rows), cross_qpos, cross_kpos, lengths,
+        x_dq, x_dk, x_dv = block_backward(
+            pick(queries, other_q),
+            pick(other_k, keys),
+            pick(other_v, values),
+            pick(g_attended, later_g),
+            pick(lse_rows, later_lse),
+            pick(dot_rows, later_dots),
+            pick(q_pos, other_pos),
+            pick(other_pos, q_pos),
+            lengths,
         )
         g_queries = g_queries + jnp.where(later, x_dq, 0.0)
         g_keys = g_keys + jnp.where(later, 0.0, x_dk)

time: 625 us -> 634 us (1.014)
  matrix products: 182 us -> 105 us
  Pallas kernels: 0 us -> 33.4 us
  other arithmetic: 69.2 us -> 94.2 us
  local copies, waits for them, and re-layouts: 56.2 us -> 74.8 us
  waiting for transfers between devices: 268 us -> 279 us
    dot_general x8 -> x0, matrix products: 52.8 us -> none  [the longest x2 20.1 us: one_block(): jnp.einsum('shqk,sqhe->skhe', probabilities.astype(jnp.bfloat16), g_rows,...]
    pallas_call x0 -> x2, Pallas kernels: none -> 33.4 us  [block_backward(): pl.pallas_call(kernel, grid=(n_slots, n_heads // 2), in_specs=[q_spec, k_...]
    dot_general x4 -> x2, matrix products: 27 us -> 6.08 us  [score_block(): jnp.einsum('sqhe,skhe->shqk', q_rows, k_rows, preferred_element_type=jnp....]
    ppermute x2, waiting for transfers between devices: 27.6 us -> 47.9 us  [rep_sum(): sent_out = lax.ppermute(total, 'rep', [(1, 0), (2, 3)])]
    reduce_scatter x3, waiting for transfers between devices: 77.7 us -> 57.5 us  [scatter_blocks(): summed = lax.psum_scatter(packed, GROUP, scatter_dimension=0, tiled=True)]
    ppermute x3, waiting for transfers between devices: 13.3 us -> 27.4 us  [shards(): lax.ppermute((g_attended, dot_rows, lse_rows), 'ctx', [(1, 0)])]
    select_n x1 -> x7, other arithmetic: 0.01 us -> 11.4 us  [shards(): pick = lambda mine, theirs: jnp.where(later, mine, theirs)]
    ppermute x2, waiting for transfers between devices: 11.5 us -> 21.7 us  [rep_sum(): arrived = lax.ppermute(x, 'rep', [(0, 1), (3, 2)])]
  transfers between devices with their start and end apart: 18 -> 18, of which waited for: 9 -> 10; matrix products, arithmetic and copies ran while one was open for 37% -> 31% of each run, Pallas kernels for 0% -> 5%
where the time goes in v7:
time: 634 us; the launch traced here: 626 us
  waiting for transfers between devices  279 us (44%)
  matrix products  105 us (17%)
  other arithmetic  94.2 us (15%)
  local copies, waits for them, and re-layouts  74.8 us (12%)
  Pallas kernels  33.4 us (5%)
  starting transfers between devices  22.8 us (4%)
  between operations  16 us (3%)
    ppermute x1, waiting for transfers between devices, shards(): other_tokens = lax.ppermute(tokens, 'ctx', [(0, 1), (1, 0)])  68 us
    reduce_scatter x3, waiting for transfers between devices, scatter_blocks(): summed = lax.psum_scatter(packed, GROUP, scatter_dimension=0, tiled=True)  57.5 us
    ppermute x2, waiting for transfers between devices, rep_sum(): sent_out = lax.ppermute(total, 'rep', [(1, 0), (2, 3)])  47.9 us
    pallas_call x2, Pallas kernels, block_backward(): pl.pallas_call(kernel, grid=(n_slots, n_heads // 2), in_specs=[q_spec, k_...  33.4 us
    all_gather x3, waiting for transfers between devices, gather_blocks(): gathered = lax.all_gather(packed, GROUP, axis=0, tiled=False)  32.9 us
    ppermute x3, waiting for transfers between devices, shards(): lax.ppermute((g_attended, dot_rows, lse_rows), 'ctx', [(1, 0)])  27.4 us
    psum x1, waiting for transfers between devices, scatter_blocks(): lax.psum(summed, 'rep')  23.4 us
    ppermute x2, waiting for transfers between devices, rep_sum(): arrived = lax.ppermute(x, 'rep', [(0, 1), (3, 2)])  21.7 us
  transfers between devices with their start and end apart: 18, of which 10 were waited for; matrix products, arithmetic and copies ran while one was open for 31% of the time, Pallas kernels for 5%

profile of v7, /device:TPU:0, one launch (start us, length us, event | category | flops | bytes accessed | tf_op | source)
XLA Modules:
  0.0 625.6 jit_solution(18332262760012300614)
XLA Ops:
  13.8 5.9 collective-permute-start.1
  22.5 68.0 %collective-permute-done = bf16[1,512,1024]{2,1,0:T(8,128)(2,1)S(1)} collective-permute-done((bf16[1,512,1024]{2,1,0:T(8,128)(2,1)S(1)}, bf16[1,512,1024]{2,1,0:T(8,128)(2,1)S(1)}, u32[]{:S(2)}, u32[]{:S(2)}) %collective-permute-start) | collective-permute-done | bytes 1048608 | tf_op jit(solution)/shard_map/ppermute | solution.py:345
  118.7 4.8 fusion.107
  138.7 29.7 %while.13 = (s32[]{:T(128)}, bf16[2,1,512,8,64]{2,4,3,1,0:T(8,128)(2,1)}, f32[2,1,1,8,512]{4,3,2,1,0:T(8,128)S(1)}, bf16[2,1,1024,8,64]{2,4,3,1,0:T(8,128)(2,1)}...) while((s32[]{:T(128)}, ...), condition=%wide.region_5.6_spmd.clone, body=%wide.region_2.5_spmd.clone.sunk | while | flops 1125644800 | bytes 73025736 | solution.py:116
  142.9 4.4 fusion.130
  147.3 5.0 fusion.131
  157.5 4.4 fusion.130
  161.9 5.0 fusion.131
  170.3 6.8 %slice.159 = bf16[8,352,1024]{2,1,0:T(8,128)(2,1)} slice(bf16[8,480,1024]{2,1,0:T(8,128)(2,1)} %bitcast.245), slice={[0:8], [128:480], [0:1024]} | slice | bytes 11534336 | tf_op jit(solution)/shard_map/slice | solution.py:267
  178.5 32.8 %all-gather.11.cloned.1.call-done = bf16[1024,5632]{1,0:T(8,128)(2,1)} async-done(((bf16[128,5632]{1,0:T(8,128)(2,1)}), bf16[1024,5632]{1,0:T(8,128)(2,1)}) %all-gather.11.cloned.1.call-update) | async-done | bytes 11534352 | tf_op jit(solution)/shard_map/all_gather | solution.py:264
  211.3 13.5 %convolution_bitcast_fusion = f32[1,512,5632]{2,1,0:T(8,128)} fusion(bf16[1024,5632]{1,0:T(8,128)(2,1)} %all-gather.11.cloned.1.call-done, f32[1,512,1024]{2,1,0:T(8,128)S(1)} %get-tuple-element.206, f32[1024]{0:T(1024)S(1)} %bitcast.285, f32[512]{0:T(512)S(1)} %add_rsqrt_fusion), kind=kOutput, calls=%fused_computation.29 | convolution fusion | flops 5907152896 | bytes 25171968 | tf_op jit(solution)/shard_map/srd,df->srf/dot_general | solution.py:389
  224.8 9.8 %fusion.22 = (bf16[1,512,2816]{2,1,0:T(8,128)(2,1)S(1)}, bf16[1,512,2816]{2,1,0:T(8,128)(2,1)}, bf16[1,512,2816]{2,1,0:T(8,128)(2,1)}) fusion(f32[1,512,5632]{2,1,0:T(8,128)} %convolution_bitcast_fusion, bf16[2816,1024]{1,0:T(8,128)(2,1)S(1)} %bitcast.252, bf16[1,512,1024]{2,1,0:T(8,128)(2,1)S(1)} %copy-done.38, pred[512]{0:T(512)(128)(4,1)S(1)} %copy-done.53), kind=kOutput, calls=%fused_computation.36 | convolution fusion | flops 2977431552 | bytes 27001344 | tf_op jit(solution)/shard_map/srd,fd->srf/dot_general | solution.py:404
  236.2 10.9 %convolution_convert_fusion = bf16[1024,5632]{1,0:T(8,128)(2,1)} fusion(bf16[1,512,2816]{2,1,0:T(8,128)(2,1)} %get-tuple-element.163, bf16[1,512,2816]{2,1,0:T(8,128)(2,1)S(1)} %get-tuple-element.162, f32[1,512,1024]{2,1,0:T(8,128)S(1)} %get-tuple-element.206, f32[1024]{0:T(1024)S(1)} %bitcast.286, f32[512]{0:T(512)S(1)} %add_rsqrt_fusion), kind=kOutput, calls=%fused_computation.28 | convolution fusion | flops 5924454400 | bytes 19404800 | tf_op jit(solution)/shard_map/srd,srf->df/dot_general | solution.py:410
  247.1 11.9 %fusion.50 = (bf16[1024]{0:T(1024)(128)(2,1)S(1)}, f32[512]{0:T(512)S(1)}, f32[512,1024]{1,0:T(8,128)S(1)}) fusion(f32[1,512,1024]{2,1,0:T(8,128)S(1)} %get-tuple-element.206, f32[512]{0:T(512)S(1)} %add_rsqrt_fusion, f32[1024]{0:T(1024)S(1)} %bitcast.287, bf16[1024,5632]{1,0:T(8,128)(2,1)} %all-gather.11.cloned.1.call-done, ...), kind=kOutput, calls=%fused_computation.84 | convolution fusion | flops 5920258560 | bytes 21506048 | tf_op jit(solution)/shard_map/srf,df->srd/dot_general | solution.py:411
  268.0 12.0 %pad_maximum_fusion = bf16[1024,6656]{1,0:T(8,128)(2,1)} fusion(bf16[1024,5632]{1,0:T(8,128)(2,1)} %convolution_convert_fusion, bf16[1024,1024]{1,0:T(8,128)(2,1)} %copy.64), kind=kLoop, calls=%fused_computation.25 | loop fusion | flops 27262976 | bytes 27262976 | tf_op jit(solution)/shard_map/concatenate | solution.py:421
  280.0 4.6 copy.65
  284.6 10.0 %convolution_convert_fusion.2 = bf16[8,352,1024]{2,1,0:T(8,128)(2,1)} fusion(bf16[8,352,512]{2,1,0:T(8,128)(2,1)} %bitcast.272, bf16[1,512,1024]{2,1,0:T(8,128)(2,1)} %param.17, pred[512]{0:T(512)(128)(4,1)S(1)} %copy-done.53), kind=kOutput, calls=%fused_computation.47 | convolution fusion | flops 2957246464 | bytes 9699840 | tf_op jit(solution)/shard_map/srf,srd->fd/dot_general | solution.py:400
  328.6 16.5 %shard_map.220 = (f32[1,512,1024]{2,1,0:T(8,128)}, f32[1,512,1024]{2,1,0:T(8,128)}, f32[1,512,1024]{2,1,0:T(8,128)}) custom-call(bf16[1,512,1024]{2,1,0:T(8,128)(2,1)} %copy.50.q_ref, bf16[1,512,1024]{2,1,0:T(8,128)(2,1)} %copy.51.k_ref, bf16[1,512,1024]{2,1,0:T(8,128)(2,1)} %copy-done.20, bf16[1,512,1024]{2,1,0:T(8,128)(2,1)} %bitcast.273, ...), custom_call_target="tpu_custom_call" | custom-call | flops 2684354560 | bytes 10485760 | tf_op jit(solution)/shard_map/pallas_call | solution.py:234
  345.1 27.4 %collective-permute-done.4 = f32[1,16,512]{2,1,0:T(8,128)S(1)} collective-permute-done((f32[1,16,512]{2,1,0:T(8,128)S(1)}, f32[1,16,512]{2,1,0:T(8,128)S(1)}, u32[]{:S(2)}, u32[]{:S(2)}) %collective-permute-start.4) | collective-permute-done | bytes 32800 | tf_op jit(solution)/shard_map/ppermute | solution.py:435
  376.5 16.9 %shard_map.221 = (f32[1,512,1024]{2,1,0:T(8,128)}, f32[1,512,1024]{2,1,0:T(8,128)}, f32[1,512,1024]{2,1,0:T(8,128)}) custom-call(bf16[1,512,1024]{2,1,0:T(8,128)(2,1)} %broadcast_select_fusion.3.q_ref, bf16[1,512,1024]{2,1,0:T(8,128)(2,1)} %broadcast_select_fusion.2.k_ref, bf16[1,512,1024]{2,1,0:T(8,128)(2,1)} %get-tuple-element.155.v_ref, ...), custom_call_target="tpu_custom_call" | custom-call | flops 2684354560 | bytes 10485760 | tf_op jit(solution)/shard_map/pallas_call | solution.py:234
  393.4 5.6 select_add_fusion
  409.9 5.0 fusion.104
  415.0 7.3 %fusion.43 = (bf16[1024]{0:T(1024)(128)(2,1)S(1)}, f32[512]{0:T(512)S(1)}, f32[512,1024]{1,0:T(8,128)S(1)}) fusion(bf16[1,512,1024]{2,1,0:T(8,128)(2,1)S(1)} %copy-done.1, f32[512]{0:T(512)S(1)} %copy-done.52, f32[1024]{0:T(1024)S(1)} %bitcast.281, bf16[1024,3072]{1,0:T(8,128)(2,1)} %bitcast.248, bf16[1,512,1024]{2,1,0:T(8,128)(2,1)S(1)} %get-tuple-element.153, ...), kind=kOutput, calls=%fused_computation.71 | convolution fusion | flops 3234331136 | bytes 12593152 | tf_op jit(solution)/shard_map/sre,de->srd/dot_general | solution.py:477
  426.0 5.3 convolution_convert_fusion.1
  438.6 23.1 %reduce-scatter.8.cloned.1.call-done = bf16[1,352,1024]{2,1,0:T(8,128)(2,1)} async-done(((bf16[8,352,1024]{2,1,0:T(8,128)(2,1)}), bf16[1,352,1024]{2,1,0:T(8,128)(2,1)}) %reduce-scatter.8.cloned.1.call-update) | async-done | bytes 720912 | tf_op jit(solution)/shard_map/reduce_scatter | solution.py:287
  465.2 11.1 %collective-permute-done.5 = bf16[1,128,6656]{2,1,0:T(8,128)(2,1)S(1)} collective-permute-done((bf16[1,128,6656]{2,1,0:T(8,128)(2,1)}, bf16[1,128,6656]{2,1,0:T(8,128)(2,1)S(1)}, u32[]{:S(2)}, u32[]{:S(2)}) %collective-permute-start.5) | collective-permute-done | bytes 1703968 | tf_op jit(solution)/shard_map/ppermute | solution.py:277
  480.3 10.6 %collective-permute-done.8 = bf16[1,352,1024]{2,1,0:T(8,128)(2,1)S(1)} collective-permute-done((bf16[1,352,1024]{2,1,0:T(8,128)(2,1)}, bf16[1,352,1024]{2,1,0:T(8,128)(2,1)S(1)}, u32[]{:S(2)}, u32[]{:S(2)}) %collective-permute-start.8) | collective-permute-done | bytes 720928 | tf_op jit(solution)/shard_map/ppermute | solution.py:277
  494.3 34.3 %reduce-scatter.4.cloned.1.call-done = bf16[1,136,3072]{2,1,0:T(8,128)(2,1)} async-done(((bf16[8,136,3072]{2,1,0:T(8,128)(2,1)}), bf16[1,136,3072]{2,1,0:T(8,128)(2,1)}) %reduce-scatter.4.cloned.1.call-update) | async-done | bytes 835600 | tf_op jit(solution)/shard_map/reduce_scatter | solution.py:287
  532.0 6.8 %fusion.55 = bf16[1,512,1024]{2,1,0:T(8,128)(2,1)} fusion(f32[1,512,1024]{2,1,0:T(8,128)S(1)} %copy-done.5, bf16[2816,1024]{1,0:T(8,128)(2,1)} %bitcast.251, bf16[1,512,2816]{2,1,0:T(8,128)(2,1)S(1)} %copy-done.29, pred[512]{0:T(512)(128)(4,1)S(1)} %copy-done.53), kind=kOutput, calls=%fused_computation.92 | convolution fusion | flops 2954362880 | bytes 11796992 | tf_op jit(solution)/shard_map/srf,fd->srd/dot_general | solution.py:394
  538.8 30.2 %collective-permute-done.10 = bf16[1,352,1024]{2,1,0:T(8,128)(2,1)} collective-permute-done((bf16[1,352,1024]{2,1,0:T(8,128)(2,1)}, bf16[1,352,1024]{2,1,0:T(8,128)(2,1)}, u32[]{:S(2)}, u32[]{:S(2)}) %collective-permute-start.10) | collective-permute-done | bytes 720928 | tf_op jit(solution)/shard_map/ppermute | solution.py:281
  571.3 23.4 %all-reduce.6.cloned.1.call-done = bf16[136,3072]{1,0:T(8,128)(2,1)} async-done(((bf16[136,3072]{1,0:T(8,128)(2,1)}), bf16[136,3072]{1,0:T(8,128)(2,1)}) %all-reduce.6.cloned.1.call-update) | async-done | bytes 835600 | tf_op jit(solution)/shard_map/psum | solution.py:288
  597.8 17.7 %collective-permute-done.7 = bf16[1,128,6656]{2,1,0:T(8,128)(2,1)S(1)} collective-permute-done((bf16[1,128,6656]{2,1,0:T(8,128)(2,1)S(1)}, bf16[1,128,6656]{2,1,0:T(8,128)(2,1)S(1)}, u32[]{:S(2)}, u32[]{:S(2)}) %collective-permute-start.7) | collective-permute-done | bytes 1703968 | tf_op jit(solution)/shard_map/ppermute | solution.py:281
  (246 shorter events, 158.1 us)
Async XLA Ops:
  7.2 83.6 %all-gather.7.cloned.1.call-start = ((), (), s32[]{:S(2)}) async-start(), calls=%async_computation.7 | async-start | bytes 7520256 | tf_op jit(solution)/shard_map/all_gather | solution.py:264
  10.1 158.3 %all-gather.9.cloned.1.call-start = ((), (), s32[]{:S(2)}) async-start(), calls=%async_computation.8 | async-start | bytes 8847360 | tf_op jit(solution)/shard_map/all_gather | solution.py:264
  11.2 8.5 %copy-start = (bf16[1,512,1024]{2,1,0:T(8,128)(2,1)S(1)}, bf16[1,512,1024]{2,1,0:T(8,128)(2,1)}, u32[]{:S(2)}) copy-start(bf16[1,512,1024]{2,1,0:T(8,128)(2,1)} %param.15) | copy-start | bytes 3145732
  11.3 200.1 %all-gather.11.cloned.1.call-start = ((), (), s32[]{:S(2)}) async-start(), calls=%async_computation.9 | async-start | bytes 12976128 | tf_op jit(solution)/shard_map/all_gather | solution.py:264
  13.8 421.0 %reduce-scatter.6.cloned.1.call-start = ((), (), s32[]{:S(2)}) async-start(), calls=%async_computation.5 | async-start | bytes 15335424 | tf_op jit(solution)/shard_map/reduce_scatter | solution.py:287
  13.8 89.2 %collective-permute-start.1 = (bf16[1,512,1024]{2,1,0:T(8,128)(2,1)S(1)}, bf16[1,512,1024]{2,1,0:T(8,128)(2,1)}, u32[]{:S(2)}, u32[]{:S(2)}) collective-permute-start(bf16[1,512,1024]{2,1,0:T(8,128)(2,1)S(1)} %copy-done.34), channel_id=1, source_target_pairs={{0,1},{2,3},{4,5},{6,7},{8,9},{10,11},{12,13},{14,15},{16,17},{18,... | collective-permute-start | bytes 3145736 | tf_op jit(solution)/shard_map/ppermute | solution.py:346
  19.7 70.7 %collective-permute-start = (bf16[1,512,1024]{2,1,0:T(8,128)(2,1)S(1)}, bf16[1,512,1024]{2,1,0:T(8,128)(2,1)S(1)}, u32[]{:S(2)}, u32[]{:S(2)}) collective-permute-start(bf16[1,512,1024]{2,1,0:T(8,128)(2,1)S(1)} %copy-done), channel_id=1, source_target_pairs={{0,1},{1,0},{2,3},{3,2},{4,5},{5,4},{6,7},{7,6},{8,9},{9,8},{10,11... | collective-permute-start | bytes 3145736 | tf_op jit(solution)/shard_map/ppermute | solution.py:345
  21.3 74.5 %copy-start.51 = (f32[512]{0:T(512)}, f32[512]{0:T(512)S(1)}, u32[]{:S(2)}) copy-start(f32[512]{0:T(512)S(1)} %add_rsqrt_fusion.1) | copy-start | bytes 6148
  22.5 105.9 %copy-start.43 = (f32[512,32]{0,1:T(8,128)}, f32[512,32]{0,1:T(8,128)S(1)}, u32[]{:S(2)}) copy-start(f32[512,32]{0,1:T(8,128)S(1)} %get-tuple-element.200) | copy-start | bytes 196612
  170.2 6.9 %copy-start.7 = (bf16[8,128,1024]{2,1,0:T(8,128)(2,1)}, bf16[8,128,1024]{2,1,0:T(8,128)(2,1)S(1)}, u32[]{:S(2)}) copy-start(bf16[8,128,1024]{2,1,0:T(8,128)(2,1)S(1)} %slice.155) | copy-start | bytes 6291460
  177.1 34.2 %copy-start.50 = (f32[8,1,128]{2,1,0:T(1,128)S(1)}, f32[8,1,128]{2,1,0:T(1,128)}, u32[]{:S(2)}) copy-start(f32[8,1,128]{2,1,0:T(1,128)} %get-tuple-element.165) | copy-start | bytes 12292
  178.5 68.6 %copy-start.4 = (f32[1,512,1024]{2,1,0:T(8,128)}, f32[1,512,1024]{2,1,0:T(8,128)S(1)}, u32[]{:S(2)}) copy-start(f32[1,512,1024]{2,1,0:T(8,128)S(1)} %get-tuple-element.206) | copy-start | bytes 6291460
  211.3 13.5 %copy-start.13 = (bf16[8,352,1024]{2,1,0:T(8,128)(2,1)S(1)}, bf16[8,352,1024]{2,1,0:T(8,128)(2,1)}, u32[]{:S(2)}) copy-start(bf16[8,352,1024]{2,1,0:T(8,128)(2,1)} %slice.159) | copy-start | bytes 17301508
  211.3 13.5 %copy-start.38 = (bf16[1,512,1024]{2,1,0:T(8,128)(2,1)S(1)}, bf16[1,512,1024]{2,1,0:T(8,128)(2,1)}, u32[]{:S(2)}) copy-start(bf16[1,512,1024]{2,1,0:T(8,128)(2,1)} %param.17) | copy-start | bytes 3145732
  211.3 13.5 %copy-start.53 = (pred[512]{0:T(512)(128)(4,1)S(1)}, pred[512]{0:T(512)(128)(4,1)}, u32[]{:S(2)}) copy-start(pred[512]{0:T(512)(128)(4,1)} %fusion.94) | copy-start | bytes 1540
  261.4 58.5 %copy-start.2 = (f32[1,512,1024]{2,1,0:T(8,128)}, f32[1,512,1024]{2,1,0:T(8,128)S(1)}, u32[]{:S(2)}) copy-start(f32[1,512,1024]{2,1,0:T(8,128)S(1)} %fusion.53) | copy-start | bytes 6291460
  280.0 181.7 %reduce-scatter.8.cloned.1.call-start = ((), (), s32[]{:S(2)}) async-start(), calls=%async_computation.6 | async-start | bytes 6488064 | tf_op jit(solution)/shard_map/reduce_scatter | solution.py:287
  294.6 234.1 %reduce-scatter.4.cloned.1.call-start = ((), (), s32[]{:S(2)}) async-start(), calls=%async_computation.3 | async-start | bytes 7520256 | tf_op jit(solution)/shard_map/reduce_scatter | solution.py:287
  316.1 10.2 %collective-permute-start.3 = (f32[1,16,512]{2,1,0:T(8,128)S(1)}, f32[1,16,512]{2,1,0:T(8,128)S(1)}, u32[]{:S(2)}, u32[]{:S(2)}) collective-permute-start(f32[1,16,512]{2,1,0:T(8,128)S(1)} %bitcast.283), channel_id=1, source_target_pairs={{1,0},{3,2},{5,4},{7,6},{9,8},{11,10},{13,12},{15,14},{17,16},{19,... | collective-permute-start | bytes 98312 | tf_op jit(solution)/shard_map/ppermute | solution.py:435
  323.8 50.0 %collective-permute-start.2 = (bf16[1,512,16,64]{1,3,2,0:T(8,128)(2,1)S(1)}, bf16[1,512,16,64]{1,3,2,0:T(8,128)(2,1)}, u32[]{:S(2)}, u32[]{:S(2)}) collective-permute-start(bf16[1,512,16,64]{1,3,2,0:T(8,128)(2,1)S(1)} %bitcast.234), channel_id=1, source_target_pairs={{1,0},{3,2},{5,4},{7,6},{9,8},{11,10},{13,12},{15,14},{17,16},{19,... | collective-permute-start | bytes 3145736 | tf_op jit(solution)/shard_map/ppermute | solution.py:435
  327.3 45.2 %collective-permute-start.4 = (f32[1,16,512]{2,1,0:T(8,128)S(1)}, f32[1,16,512]{2,1,0:T(8,128)S(1)}, u32[]{:S(2)}, u32[]{:S(2)}) collective-permute-start(f32[1,16,512]{2,1,0:T(8,128)S(1)} %bitcast.277), channel_id=1, source_target_pairs={{1,0},{3,2},{5,4},{7,6},{9,8},{11,10},{13,12},{15,14},{17,16},{19,... | collective-permute-start | bytes 98312 | tf_op jit(solution)/shard_map/ppermute | solution.py:435
  376.5 16.9 %copy-start.30 = (f32[1,512,1024]{2,1,0:T(8,128)S(1)}, f32[1,512,1024]{2,1,0:T(8,128)}, u32[]{:S(2)}) copy-start(f32[1,512,1024]{2,1,0:T(8,128)} %get-tuple-element.95) | copy-start | bytes 6291460
  414.9 7.4 %copy-start.39 = (bf16[1,512,1024]{2,1,0:T(8,128)(2,1)}, bf16[1,512,1024]{2,1,0:T(8,128)(2,1)S(1)}, u32[]{:S(2)}) copy-start(bf16[1,512,1024]{2,1,0:T(8,128)(2,1)S(1)} %get-tuple-element.153) | copy-start | bytes 3145732
  415.0 7.5 %copy-start.3 = (f32[1,512,1024]{2,1,0:T(8,128)S(1)}, f32[1,512,1024]{2,1,0:T(8,128)}, u32[]{:S(2)}) copy-start(f32[1,512,1024]{2,1,0:T(8,128)} %copy-done.2) | copy-start | bytes 6291460
  434.7 160.1 %all-reduce.6.cloned.1.call-start = ((), (), s32[]{:S(2)}) async-start(), calls=%async_computation.4 | async-start | bytes 1671168 | tf_op jit(solution)/shard_map/psum | solution.py:288
  434.8 41.6 %collective-permute-start.5 = (bf16[1,128,6656]{2,1,0:T(8,128)(2,1)}, bf16[1,128,6656]{2,1,0:T(8,128)(2,1)S(1)}, u32[]{:S(2)}, u32[]{:S(2)}) collective-permute-start(bf16[1,128,6656]{2,1,0:T(8,128)(2,1)} %reduce-scatter.6.cloned.1.call-done), channel_id=1, source_target_pairs={{0,8},{24,16},{1,9},{25,17},{2,10},{26,18},{3,11},{27,19},{4,12},{... | collective-permute-start | bytes 5111816 | tf_op jit(solution)/shard_map/ppermute | solution.py:277
  461.7 29.2 %copy-start.40 = (bf16[1,352,1024]{2,1,0:T(8,128)(2,1)S(1)}, bf16[1,352,1024]{2,1,0:T(8,128)(2,1)}, u32[]{:S(2)}) copy-start(bf16[1,352,1024]{2,1,0:T(8,128)(2,1)} %reduce-scatter.8.cloned.1.call-done) | copy-start | bytes 2162692
  461.7 29.2 %collective-permute-start.8 = (bf16[1,352,1024]{2,1,0:T(8,128)(2,1)}, bf16[1,352,1024]{2,1,0:T(8,128)(2,1)S(1)}, u32[]{:S(2)}, u32[]{:S(2)}) collective-permute-start(bf16[1,352,1024]{2,1,0:T(8,128)(2,1)} %reduce-scatter.8.cloned.1.call-done), channel_id=1, source_target_pairs={{0,8},{24,16},{1,9},{25,17},{2,10},{26,18},{3,11},{27,19},{4,12},{... | collective-permute-start | bytes 2162696 | tf_op jit(solution)/shard_map/ppermute | solution.py:277
  478.5 50.3 %collective-permute-start.6 = (bf16[1,128,6656]{2,1,0:T(8,128)(2,1)S(1)}, bf16[1,128,6656]{2,1,0:T(8,128)(2,1)}, u32[]{:S(2)}, u32[]{:S(2)}) collective-permute-start(bf16[1,128,6656]{2,1,0:T(8,128)(2,1)S(1)} %add_convert_fusion.1), channel_id=1, source_target_pairs={{8,16},{16,8},{9,17},{17,9},{10,18},{18,10},{11,19},{19,11},{12,20... | collective-permute-start | bytes 5111816 | tf_op jit(solution)/shard_map/ppermute | solution.py:279
  491.2 0.7 collective-permute-start.9
  493.0 75.9 %collective-permute-start.10 = (bf16[1,352,1024]{2,1,0:T(8,128)(2,1)}, bf16[1,352,1024]{2,1,0:T(8,128)(2,1)}, u32[]{:S(2)}, u32[]{:S(2)}) collective-permute-start(bf16[1,352,1024]{2,1,0:T(8,128)(2,1)} %add_convert_fusion.3), channel_id=1, source_target_pairs={{8,0},{16,24},{9,1},{17,25},{10,2},{18,26},{11,3},{19,27},{12,4},{... | collective-permute-start | bytes 2162696 | tf_op jit(solution)/shard_map/ppermute | solution.py:281
  530.7 84.8 %collective-permute-start.7 = (bf16[1,128,6656]{2,1,0:T(8,128)(2,1)S(1)}, bf16[1,128,6656]{2,1,0:T(8,128)(2,1)S(1)}, u32[]{:S(2)}, u32[]{:S(2)}) collective-permute-start(bf16[1,128,6656]{2,1,0:T(8,128)(2,1)S(1)} %add_convert_fusion), channel_id=1, source_target_pairs={{8,0},{16,24},{9,1},{17,25},{10,2},{18,26},{11,3},{19,27},{12,4},{... | collective-permute-start | bytes 5111816 | tf_op jit(solution)/shard_map/ppermute | solution.py:281
  (44 other events, 138.4 us)
Sparse Core Ops, SparseCore 0:
  10.5 72.8 all-gather.6
  85.2 55.9 all-gather.8
  143.7 67.5 all-gather.10
  280.1 119.2 reduce-scatter.5
  402.6 59.0 reduce-scatter.7
  465.0 63.6 reduce-scatter.3
  531.1 63.6 all-reduce.5

commit v8 on v7

--- a/solution.py
+++ b/solution.py
@@ -322,20 +322,22 @@
     ff_width = w_gate.shape[1]
     attn_width = w_query.shape[1]
     qkv_width = 3 * attn_width
-    (qkv_blocks, gain_rows) = gather_blocks(
+    qkvo_width = qkv_width + model_width
+    (qkvo_blocks, gain_rows) = gather_blocks(
         [
-            jnp.concatenate([w_query, w_key, w_value], axis=1),
-            gain_block(gain_attn, gain_mlp, qkv_width),
+            jnp.concatenate([w_query, w_key, w_value, w_out], axis=1),
+            gain_block(gain_attn, gain_mlp, qkvo_width),
         ]
     )
-    full_qkv = qkv_blocks.reshape(n_group * own_rows, qkv_width)
+    full_qkvo = qkvo_blocks.reshape(n_group * own_rows, qkvo_width)
+    full_qkv = full_qkvo[:, :qkv_width]
+    full_out = full_qkvo[:, qkv_width:]
     full_gain_attn = gain_rows[:, 0, :own_rows].reshape(-1)
     full_gain_mlp = gain_rows[:, 0, own_rows : 2 * own_rows].reshape(-1)
-    out_blocks, down_blocks = gather_blocks([w_out, w_down])
-    full_out = out_blocks.reshape(-1, model_width)
-    full_down = down_blocks.reshape(-1, model_width)
     (gu_blocks,) = gather_blocks([jnp.concatenate([w_gate, w_up], axis=1)])
     full_gu = gu_blocks.reshape(n_group * own_rows, 2 * ff_width)
+    (down_blocks,) = gather_blocks([w_down])
+    full_down = down_blocks.reshape(-1, model_width)
     ctx_index = lax.axis_index("ctx")
     q_pos = ctx_index * slot_rows + jnp.arange(slot_rows)
     live_rows = q_pos[None, :] < lengths[:, None]
@@ -391,6 +393,9 @@
     up_proj = gu_proj[..., ff_width:]
     sigmoid_gate = jax.nn.sigmoid(gate_proj)
     hidden = (gate_proj * sigmoid_gate * up_proj).astype(jnp.bfloat16)
+    hidden, gate_proj, up_proj, sigmoid_gate = lax.optimization_barrier(
+        (hidden, gate_proj, up_proj, sigmoid_gate)
+    )
     final = residual + jnp.einsum(
         "srf,fd->srd", hidden, full_down, preferred_element_type=jnp.float32
     )

time: 634 us -> 646 us (1.019)
  waiting for transfers between devices: 279 us -> 256 us
  other arithmetic: 94.2 us -> 116 us
  matrix products: 105 us -> 117 us
    ppermute x1, waiting for transfers between devices: 68 us -> 29.8 us  [shards(): other_tokens = lax.ppermute(tokens, 'ctx', [(0, 1), (1, 0)])]
    reduce_scatter x3, waiting for transfers between devices: 57.5 us -> 33 us  [scatter_blocks(): summed = lax.psum_scatter(packed, GROUP, scatter_dimension=0, tiled=True)]
    all_gather x3, waiting for transfers between devices: 32.9 us -> 56.5 us  [gather_blocks(): gathered = lax.all_gather(packed, GROUP, axis=0, tiled=False)]
    ppermute x2, waiting for transfers between devices: 47.9 us -> 57.5 us  [rep_sum(): sent_out = lax.ppermute(total, 'rep', [(1, 0), (2, 3)])]
    ppermute x2, waiting for transfers between devices: 21.7 us -> 30.2 us  [rep_sum(): arrived = lax.ppermute(x, 'rep', [(0, 1), (3, 2)])]
    div x0 -> x1, other arithmetic: none -> 7.74 us  [shards(): sigmoid_gate = jax.nn.sigmoid(gate_proj)]
  transfers between devices with their start and end apart: 18 -> 18, of which waited for: 10 -> 11; matrix products, arithmetic and copies ran while one was open for 31% -> 36% of each run, Pallas kernels for 5% -> 5%
where the time goes in v8:
time: 646 us; the launch traced here: 637 us
  waiting for transfers between devices  256 us (40%)
  matrix products  117 us (18%)
  other arithmetic  116 us (18%)
  local copies, waits for them, and re-layouts  74.8 us (12%)
  Pallas kernels  32.9 us (5%)
  starting transfers between devices  24.2 us (4%)
  between operations  15.8 us (2%)
    ppermute x2, waiting for transfers between devices, rep_sum(): sent_out = lax.ppermute(total, 'rep', [(1, 0), (2, 3)])  57.5 us
    all_gather x3, waiting for transfers between devices, gather_blocks(): gathered = lax.all_gather(packed, GROUP, axis=0, tiled=False)  56.5 us
    reduce_scatter x3, waiting for transfers between devices, scatter_blocks(): summed = lax.psum_scatter(packed, GROUP, scatter_dimension=0, tiled=True)  33 us
    pallas_call x2, Pallas kernels, block_backward(): pl.pallas_call(kernel, grid=(n_slots, n_heads // 2), in_specs=[q_spec, k_...  32.9 us
    ppermute x2, waiting for transfers between devices, rep_sum(): arrived = lax.ppermute(x, 'rep', [(0, 1), (3, 2)])  30.2 us
    ppermute x1, waiting for transfers between devices, shards(): other_tokens = lax.ppermute(tokens, 'ctx', [(0, 1), (1, 0)])  29.8 us
    ppermute x3, waiting for transfers between devices, shards(): lax.ppermute((g_attended, dot_rows, lse_rows), 'ctx', [(1, 0)])  24.8 us
    psum x1, waiting for transfers between devices, scatter_blocks(): lax.psum(summed, 'rep')  24.1 us
  transfers between devices with their start and end apart: 18, of which 11 were waited for; matrix products, arithmetic and copies ran while one was open for 36% of the time, Pallas kernels for 5%

profile of v8, /device:TPU:0, one launch (start us, length us, event | category | flops | bytes accessed | tf_op | source)
XLA Modules:
  0.0 636.8 jit_solution(11786548970799796945)
XLA Ops:
  20.6 29.8 %collective-permute-done = bf16[1,512,1024]{2,1,0:T(8,128)(2,1)S(1)} collective-permute-done((bf16[1,512,1024]{2,1,0:T(8,128)(2,1)S(1)}, bf16[1,512,1024]{2,1,0:T(8,128)(2,1)S(1)}, u32[]{:S(2)}, u32[]{:S(2)}) %collective-permute-start) | collective-permute-done | bytes 1048608 | tf_op jit(solution)/shard_map/ppermute | solution.py:347
  50.7 45.1 %all-gather.7.cloned.1.call-done = bf16[1088,4096]{1,0:T(8,128)(2,1)} async-done(((bf16[136,4096]{1,0:T(8,128)(2,1)}), bf16[1088,4096]{1,0:T(8,128)(2,1)}) %all-gather.7.cloned.1.call-update) | async-done | bytes 8912912 | tf_op jit(solution)/shard_map/all_gather | solution.py:264
  95.7 7.8 %slice.143 = bf16[8,128,4096]{2,1,0:T(8,128)(2,1)} slice(bf16[8,136,4096]{2,1,0:T(8,128)(2,1)} %bitcast.240), slice={[0:8], [0:128], [0:4096]} | slice | bytes 16777216 | tf_op jit(solution)/shard_map/slice | solution.py:267
  104.9 5.7 convolution_bitcast_fusion.1
  118.6 5.7 convolution_bitcast_fusion.2
  133.1 6.1 broadcast_select_fusion.1
  153.0 28.9 %while.13 = (s32[]{:T(128)}, bf16[2,1,512,8,64]{2,4,3,1,0:T(8,128)(2,1)}, f32[2,1,1,8,512]{4,3,2,1,0:T(8,128)S(1)}, bf16[2,1,1024,8,64]{2,4,3,1,0:T(8,128)(2,1)}...) while((s32[]{:T(128)}, ...), condition=%wide.region_5.6_spmd.clone, body=%wide.region_2.5_spmd.clone.sunk | while | flops 1125644800 | bytes 64637068 | solution.py:116
  161.8 5.7 fusion.138
  176.2 5.7 fusion.138
  186.8 9.1 %convolution_bitcast_fusion = f32[1,512,5632]{2,1,0:T(8,128)S(1)} fusion(bf16[1024,5632]{1,0:T(8,128)(2,1)} %all-gather.9.cloned.1.call-done, f32[1,512,1024]{2,1,0:T(8,128)S(1)} %get-tuple-element.217, f32[1024]{0:T(1024)S(1)} %bitcast.270, f32[512]{0:T(512)S(1)} %add_rsqrt_fusion), kind=kOutput, calls=%fused_computation.29 | convolution fusion | flops 5907152896 | bytes 25171968 | tf_op jit(solution)/shard_map/srd,df->srf/dot_general | solution.py:391
  195.9 7.7 %add_divide_fusion = (f32[1,512,2816]{2,1,0:T(8,128)}, bf16[1,512,2816]{2,1,0:T(8,128)(2,1)S(1)}, f32[1,512,2816]{2,1,0:T(8,128)}, f32[1,512,2816]{2,1,0:T(8,128)}) fusion(f32[1,512,5632]{2,1,0:T(8,128)S(1)} %convolution_bitcast_fusion), kind=kLoop, calls=%fused_computation.40 | loop fusion | flops 8650752 | bytes 31719424 | tf_op jit(solution)/shard_map/div | solution.py:394
  203.6 11.4 %all-gather.11.cloned.1.call-done = bf16[2816,1024]{1,0:T(8,128)(2,1)} async-done(((bf16[352,1024]{1,0:T(8,128)(2,1)}), bf16[2816,1024]{1,0:T(8,128)(2,1)}) %all-gather.11.cloned.1.call-update) | async-done | bytes 5767184 | tf_op jit(solution)/shard_map/all_gather | solution.py:264
  215.0 13.6 %fusion.22 = (bf16[1,512,2816]{2,1,0:T(8,128)(2,1)S(1)}, bf16[1,512,2816]{2,1,0:T(8,128)(2,1)}) fusion(f32[1,512,2816]{2,1,0:T(8,128)} %get-tuple-element.100, f32[1,512,2816]{2,1,0:T(8,128)} %get-tuple-element.99, f32[1,512,2816]{2,1,0:T(8,128)} %get-tuple-element.101, bf16[2816,1024]{1,0:T(8,128)(2,1)} %all-gather.11.cloned.1.call-done, ...), kind=kOutput, calls=%fused_computation.36 | convolution fusion | flops 2968780800 | bytes 29884928 | tf_op jit(solution)/shard_map/srd,fd->srf/dot_general | solution.py:409
  230.2 11.0 %convolution_convert_fusion = bf16[1024,5632]{1,0:T(8,128)(2,1)} fusion(bf16[1,512,2816]{2,1,0:T(8,128)(2,1)} %get-tuple-element.171, bf16[1,512,2816]{2,1,0:T(8,128)(2,1)S(1)} %get-tuple-element.170, f32[1,512,1024]{2,1,0:T(8,128)} %copy-done.23, f32[1024]{0:T(1024)S(1)} %bitcast.271, f32[512]{0:T(512)S(1)} %add_rsqrt_fusion), kind=kOutput, calls=%fused_computation.28 | convolution fusion | flops 5924454400 | bytes 19404800 | tf_op jit(solution)/shard_map/srd,srf->df/dot_general | solution.py:415
  241.2 13.1 %fusion.54 = (bf16[1024]{0:T(1024)(128)(2,1)S(1)}, f32[512]{0:T(512)S(1)}, f32[512,1024]{1,0:T(8,128)}) fusion(f32[1,512,1024]{2,1,0:T(8,128)} %copy-done.23, f32[512]{0:T(512)S(1)} %add_rsqrt_fusion, f32[1024]{0:T(1024)S(1)} %bitcast.272, bf16[1024,5632]{1,0:T(8,128)(2,1)} %all-gather.9.cloned.1.call-done, bf16[1,512,2816]{2,1,0:T(8,128)(2,1)} %get-tuple-element.171, ...), kind=kOutput, calls=%fused_computation.89 | convolution fusion | flops 5920258560 | bytes 21506048 | tf_op jit(solution)/shard_map/srf,df->srd/dot_general | solution.py:416
  265.7 11.9 %pad_maximum_fusion = bf16[1024,6656]{1,0:T(8,128)(2,1)} fusion(bf16[1024,5632]{1,0:T(8,128)(2,1)} %convolution_convert_fusion, bf16[1024,1024]{1,0:T(8,128)(2,1)} %copy.64), kind=kLoop, calls=%fused_computation.25 | loop fusion | flops 27262976 | bytes 27262976 | tf_op jit(solution)/shard_map/concatenate | solution.py:426
  280.8 9.3 %convolution_convert_fusion.2 = bf16[8,352,1024]{2,1,0:T(8,128)(2,1)} fusion(bf16[8,352,512]{2,1,0:T(8,128)(2,1)} %bitcast.257, bf16[1,512,1024]{2,1,0:T(8,128)(2,1)} %param.17, pred[512]{0:T(512)(128)(4,1)S(1)} %copy-done.43), kind=kOutput, calls=%fused_computation.51 | convolution fusion | flops 2957246464 | bytes 9699840 | tf_op jit(solution)/shard_map/srf,srd->fd/dot_general | solution.py:405
  328.9 16.5 %shard_map.220 = (f32[1,512,1024]{2,1,0:T(8,128)}, f32[1,512,1024]{2,1,0:T(8,128)}, f32[1,512,1024]{2,1,0:T(8,128)}) custom-call(bf16[1,512,1024]{2,1,0:T(8,128)(2,1)} %copy.50.q_ref, bf16[1,512,1024]{2,1,0:T(8,128)(2,1)} %copy.51.k_ref, bf16[1,512,1024]{2,1,0:T(8,128)(2,1)} %copy-done.18, bf16[1,512,1024]{2,1,0:T(8,128)(2,1)} %bitcast.258, ...), custom_call_target="tpu_custom_call" | custom-call | flops 2684354560 | bytes 10485760 | tf_op jit(solution)/shard_map/pallas_call | solution.py:234
  345.4 24.8 %collective-permute-done.4 = f32[1,16,512]{2,1,0:T(8,128)S(1)} collective-permute-done((f32[1,16,512]{2,1,0:T(8,128)S(1)}, f32[1,16,512]{2,1,0:T(8,128)S(1)}, u32[]{:S(2)}, u32[]{:S(2)}) %collective-permute-start.4) | collective-permute-done | bytes 32800 | tf_op jit(solution)/shard_map/ppermute | solution.py:440
  376.7 16.4 %shard_map.221 = (f32[1,512,1024]{2,1,0:T(8,128)}, f32[1,512,1024]{2,1,0:T(8,128)}, f32[1,512,1024]{2,1,0:T(8,128)}) custom-call(bf16[1,512,1024]{2,1,0:T(8,128)(2,1)} %broadcast_select_fusion.3.q_ref, bf16[1,512,1024]{2,1,0:T(8,128)(2,1)} %broadcast_select_fusion.2.k_ref, bf16[1,512,1024]{2,1,0:T(8,128)(2,1)} %get-tuple-element.163.v_ref, ...), custom_call_target="tpu_custom_call" | custom-call | flops 2684354560 | bytes 10485760 | tf_op jit(solution)/shard_map/pallas_call | solution.py:234
  393.1 6.3 select_add_fusion
  416.9 4.4 fusion.116
  421.4 7.8 %fusion.47 = (bf16[1024]{0:T(1024)(128)(2,1)S(1)}, f32[512]{0:T(512)S(1)}, f32[512,1024]{1,0:T(8,128)S(1)}) fusion(bf16[1,512,1024]{2,1,0:T(8,128)(2,1)S(1)} %copy-done.17, f32[512]{0:T(512)S(1)} %copy-done.42, f32[1024]{0:T(1024)S(1)} %bitcast.266, bf16[1024,4096]{1,0:T(8,128)(2,1)} %bitcast.239, bf16[1,512,1024]{2,1,0:T(8,128)(2,1)S(1)} %get-tuple-element.161, ...), kind=kOutput, calls=%fused_computation.76 | convolution fusion | flops 3234331136 | bytes 12593152 | tf_op jit(solution)/shard_map/sre,de->srd/dot_general | solution.py:482
  434.2 5.7 convolution_convert_fusion.1
  447.8 11.6 %reduce-scatter.8.cloned.1.call-done = bf16[1,352,1024]{2,1,0:T(8,128)(2,1)} async-done(((bf16[8,352,1024]{2,1,0:T(8,128)(2,1)}), bf16[1,352,1024]{2,1,0:T(8,128)(2,1)}) %reduce-scatter.8.cloned.1.call-update) | async-done | bytes 720912 | tf_op jit(solution)/shard_map/reduce_scatter | solution.py:287
  463.0 21.5 %collective-permute-done.5 = bf16[1,128,6656]{2,1,0:T(8,128)(2,1)} collective-permute-done((bf16[1,128,6656]{2,1,0:T(8,128)(2,1)}, bf16[1,128,6656]{2,1,0:T(8,128)(2,1)}, u32[]{:S(2)}, u32[]{:S(2)}) %collective-permute-start.5) | collective-permute-done | bytes 1703968 | tf_op jit(solution)/shard_map/ppermute | solution.py:277
  490.0 8.7 %collective-permute-done.8 = bf16[1,352,1024]{2,1,0:T(8,128)(2,1)S(1)} collective-permute-done((bf16[1,352,1024]{2,1,0:T(8,128)(2,1)}, bf16[1,352,1024]{2,1,0:T(8,128)(2,1)S(1)}, u32[]{:S(2)}, u32[]{:S(2)}) %collective-permute-start.8) | collective-permute-done | bytes 720928 | tf_op jit(solution)/shard_map/ppermute | solution.py:277
  505.1 21.3 %reduce-scatter.4.cloned.1.call-done = bf16[1,136,3072]{2,1,0:T(8,128)(2,1)} async-done(((bf16[8,136,3072]{2,1,0:T(8,128)(2,1)}), bf16[1,136,3072]{2,1,0:T(8,128)(2,1)}) %reduce-scatter.4.cloned.1.call-update) | async-done | bytes 835600 | tf_op jit(solution)/shard_map/reduce_scatter | solution.py:287
  531.5 6.8 %fusion.59 = bf16[1,512,1024]{2,1,0:T(8,128)(2,1)} fusion(f32[1,512,1024]{2,1,0:T(8,128)S(1)} %copy-done.25, bf16[2816,1024]{1,0:T(8,128)(2,1)} %all-gather.11.cloned.1.call-done, bf16[1,512,2816]{2,1,0:T(8,128)(2,1)S(1)} %get-tuple-element.98, pred[512]{0:T(512)(128)(4,1)S(1)} %copy-done.43), kind=kOutput, calls=%fused_computation.97 | convolution fusion | flops 2954362880 | bytes 11796992 | tf_op jit(solution)/shard_map/srf,fd->srd/dot_general | solution.py:399
  538.3 41.3 %collective-permute-done.10 = bf16[1,352,1024]{2,1,0:T(8,128)(2,1)} collective-permute-done((bf16[1,352,1024]{2,1,0:T(8,128)(2,1)}, bf16[1,352,1024]{2,1,0:T(8,128)(2,1)}, u32[]{:S(2)}, u32[]{:S(2)}) %collective-permute-start.10) | collective-permute-done | bytes 720928 | tf_op jit(solution)/shard_map/ppermute | solution.py:281
  581.9 24.1 %all-reduce.6.cloned.1.call-done = bf16[136,3072]{1,0:T(8,128)(2,1)} async-done(((bf16[136,3072]{1,0:T(8,128)(2,1)}), bf16[136,3072]{1,0:T(8,128)(2,1)}) %all-reduce.6.cloned.1.call-update) | async-done | bytes 835600 | tf_op jit(solution)/shard_map/psum | solution.py:288
  609.1 16.1 %collective-permute-done.7 = bf16[1,128,6656]{2,1,0:T(8,128)(2,1)} collective-permute-done((bf16[1,128,6656]{2,1,0:T(8,128)(2,1)}, bf16[1,128,6656]{2,1,0:T(8,128)(2,1)}, u32[]{:S(2)}, u32[]{:S(2)}) %collective-permute-start.7) | collective-permute-done | bytes 1703968 | tf_op jit(solution)/shard_map/ppermute | solution.py:281
  (218 shorter events, 188.4 us)
Async XLA Ops:
  7.2 88.5 %all-gather.7.cloned.1.call-start = ((), (), s32[]{:S(2)}) async-start(), calls=%async_computation.7 | async-start | bytes 10027008 | tf_op jit(solution)/shard_map/all_gather | solution.py:264
  10.4 175.1 %all-gather.9.cloned.1.call-start = ((), (), s32[]{:S(2)}) async-start(), calls=%async_computation.8 | async-start | bytes 12976128 | tf_op jit(solution)/shard_map/all_gather | solution.py:264
  11.7 203.3 %all-gather.11.cloned.1.call-start = ((), (), s32[]{:S(2)}) async-start(), calls=%async_computation.9 | async-start | bytes 6488064 | tf_op jit(solution)/shard_map/all_gather | solution.py:264
  11.9 38.5 %collective-permute-start = (bf16[1,512,1024]{2,1,0:T(8,128)(2,1)S(1)}, bf16[1,512,1024]{2,1,0:T(8,128)(2,1)S(1)}, u32[]{:S(2)}, u32[]{:S(2)}) collective-permute-start(bf16[1,512,1024]{2,1,0:T(8,128)(2,1)S(1)} %copy-done.16), channel_id=1, source_target_pairs={{0,1},{1,0},{2,3},{3,2},{4,5},{5,4},{6,7},{7,6},{8,9},{9,8},{10,11... | collective-permute-start | bytes 3145736 | tf_op jit(solution)/shard_map/ppermute | solution.py:347
  14.9 118.2 %collective-permute-start.1 = (bf16[1,512,1024]{2,1,0:T(8,128)(2,1)}, bf16[1,512,1024]{2,1,0:T(8,128)(2,1)}, u32[]{:S(2)}, u32[]{:S(2)}) collective-permute-start(bf16[1,512,1024]{2,1,0:T(8,128)(2,1)} %param.16), channel_id=1, source_target_pairs={{0,1},{2,3},{4,5},{6,7},{8,9},{10,11},{12,13},{14,15},{16,17},{18,... | collective-permute-start | bytes 3145736 | tf_op jit(solution)/shard_map/ppermute | solution.py:348
  17.8 425.6 %reduce-scatter.6.cloned.1.call-start = ((), (), s32[]{:S(2)}) async-start(), calls=%async_computation.5 | async-start | bytes 15335424 | tf_op jit(solution)/shard_map/reduce_scatter | solution.py:287
  19.4 85.5 %copy-start.41 = (f32[512]{0:T(512)}, f32[512]{0:T(512)S(1)}, u32[]{:S(2)}) copy-start(f32[512]{0:T(512)S(1)} %add_rsqrt_fusion.1) | copy-start | bytes 6148
  20.6 122.2 %copy-start.34 = (f32[512,32]{0,1:T(8,128)}, f32[512,32]{0,1:T(8,128)S(1)}, u32[]{:S(2)}) copy-start(f32[512,32]{0,1:T(8,128)S(1)} %get-tuple-element.211) | copy-start | bytes 196612
  104.9 13.7 %copy-start.38 = (f32[8,1,128]{2,1,0:T(1,128)}, f32[8,1,128]{2,1,0:T(1,128)S(1)}, u32[]{:S(2)}) copy-start(f32[8,1,128]{2,1,0:T(1,128)S(1)} %get-tuple-element.177) | copy-start | bytes 12292
  145.7 6.3 copy-start.11
  145.7 6.3 copy-start.13
  181.9 4.9 copy-start.40
  195.9 19.1 %copy-start.43 = (pred[512]{0:T(512)(128)(4,1)S(1)}, pred[512]{0:T(512)(128)(4,1)}, u32[]{:S(2)}) copy-start(pred[512]{0:T(512)(128)(4,1)} %fusion.106) | copy-start | bytes 1540
  241.2 13.1 %copy-start.19 = (bf16[1,512,1024]{2,1,0:T(8,128)(2,1)S(1)}, bf16[1,512,1024]{2,1,0:T(8,128)(2,1)}, u32[]{:S(2)}) copy-start(bf16[1,512,1024]{2,1,0:T(8,128)(2,1)} %param.17) | copy-start | bytes 3145732
  241.2 13.1 %copy-start.24 = (f32[1,512,1024]{2,1,0:T(8,128)S(1)}, f32[1,512,1024]{2,1,0:T(8,128)}, u32[]{:S(2)}) copy-start(f32[1,512,1024]{2,1,0:T(8,128)} %copy-done.23) | copy-start | bytes 6291460
  277.7 181.8 %reduce-scatter.8.cloned.1.call-start = ((), (), s32[]{:S(2)}) async-start(), calls=%async_computation.6 | async-start | bytes 6488064 | tf_op jit(solution)/shard_map/reduce_scatter | solution.py:287
  290.1 236.3 %reduce-scatter.4.cloned.1.call-start = ((), (), s32[]{:S(2)}) async-start(), calls=%async_computation.3 | async-start | bytes 7520256 | tf_op jit(solution)/shard_map/reduce_scatter | solution.py:287
  297.7 4.7 copy-start.9
  311.3 13.9 %collective-permute-start.3 = (f32[1,16,512]{2,1,0:T(8,128)S(1)}, f32[1,16,512]{2,1,0:T(8,128)S(1)}, u32[]{:S(2)}, u32[]{:S(2)}) collective-permute-start(f32[1,16,512]{2,1,0:T(8,128)S(1)} %bitcast.268), channel_id=1, source_target_pairs={{1,0},{3,2},{5,4},{7,6},{9,8},{11,10},{13,12},{15,14},{17,16},{19,... | collective-permute-start | bytes 98312 | tf_op jit(solution)/shard_map/ppermute | solution.py:440
  321.4 50.1 %collective-permute-start.2 = (bf16[1,512,16,64]{1,3,2,0:T(8,128)(2,1)}, bf16[1,512,16,64]{1,3,2,0:T(8,128)(2,1)}, u32[]{:S(2)}, u32[]{:S(2)}) collective-permute-start(bf16[1,512,16,64]{1,3,2,0:T(8,128)(2,1)} %bitcast.227), channel_id=1, source_target_pairs={{1,0},{3,2},{5,4},{7,6},{9,8},{11,10},{13,12},{15,14},{17,16},{19,... | collective-permute-start | bytes 3145736 | tf_op jit(solution)/shard_map/ppermute | solution.py:440
  327.6 42.6 %collective-permute-start.4 = (f32[1,16,512]{2,1,0:T(8,128)S(1)}, f32[1,16,512]{2,1,0:T(8,128)S(1)}, u32[]{:S(2)}, u32[]{:S(2)}) collective-permute-start(f32[1,16,512]{2,1,0:T(8,128)S(1)} %bitcast.262), channel_id=1, source_target_pairs={{1,0},{3,2},{5,4},{7,6},{9,8},{11,10},{13,12},{15,14},{17,16},{19,... | collective-permute-start | bytes 98312 | tf_op jit(solution)/shard_map/ppermute | solution.py:440
  421.4 7.9 %copy-start.30 = (bf16[1,512,1024]{2,1,0:T(8,128)(2,1)}, bf16[1,512,1024]{2,1,0:T(8,128)(2,1)S(1)}, u32[]{:S(2)}) copy-start(bf16[1,512,1024]{2,1,0:T(8,128)(2,1)S(1)} %get-tuple-element.161) | copy-start | bytes 3145732
  421.4 7.8 %copy-start.3 = (f32[1,512,1024]{2,1,0:T(8,128)S(1)}, f32[1,512,1024]{2,1,0:T(8,128)}, u32[]{:S(2)}) copy-start(f32[1,512,1024]{2,1,0:T(8,128)} %copy-done.1) | copy-start | bytes 6291460
  443.3 162.7 %all-reduce.6.cloned.1.call-start = ((), (), s32[]{:S(2)}) async-start(), calls=%async_computation.4 | async-start | bytes 1671168 | tf_op jit(solution)/shard_map/psum | solution.py:288
  443.4 41.1 %collective-permute-start.5 = (bf16[1,128,6656]{2,1,0:T(8,128)(2,1)}, bf16[1,128,6656]{2,1,0:T(8,128)(2,1)}, u32[]{:S(2)}, u32[]{:S(2)}) collective-permute-start(bf16[1,128,6656]{2,1,0:T(8,128)(2,1)} %reduce-scatter.6.cloned.1.call-done), channel_id=1, source_target_pairs={{0,8},{24,16},{1,9},{25,17},{2,10},{26,18},{3,11},{27,19},{4,12},{... | collective-permute-start | bytes 5111816 | tf_op jit(solution)/shard_map/ppermute | solution.py:277
  459.4 39.2 %copy-start.31 = (bf16[1,352,1024]{2,1,0:T(8,128)(2,1)S(1)}, bf16[1,352,1024]{2,1,0:T(8,128)(2,1)}, u32[]{:S(2)}) copy-start(bf16[1,352,1024]{2,1,0:T(8,128)(2,1)} %reduce-scatter.8.cloned.1.call-done) | copy-start | bytes 2162692
  459.4 39.2 %collective-permute-start.8 = (bf16[1,352,1024]{2,1,0:T(8,128)(2,1)}, bf16[1,352,1024]{2,1,0:T(8,128)(2,1)S(1)}, u32[]{:S(2)}, u32[]{:S(2)}) collective-permute-start(bf16[1,352,1024]{2,1,0:T(8,128)(2,1)} %reduce-scatter.8.cloned.1.call-done), channel_id=1, source_target_pairs={{0,8},{24,16},{1,9},{25,17},{2,10},{26,18},{3,11},{27,19},{4,12},{... | collective-permute-start | bytes 2162696 | tf_op jit(solution)/shard_map/ppermute | solution.py:277
  488.1 38.3 %collective-permute-start.6 = (bf16[1,128,6656]{2,1,0:T(8,128)(2,1)}, bf16[1,128,6656]{2,1,0:T(8,128)(2,1)}, u32[]{:S(2)}, u32[]{:S(2)}) collective-permute-start(bf16[1,128,6656]{2,1,0:T(8,128)(2,1)} %add_convert_fusion.1), channel_id=1, source_target_pairs={{8,16},{16,8},{9,17},{17,9},{10,18},{18,10},{11,19},{19,11},{12,20... | collective-permute-start | bytes 5111816 | tf_op jit(solution)/shard_map/ppermute | solution.py:279
  499.8 1.5 collective-permute-start.9
  503.8 75.8 %collective-permute-start.10 = (bf16[1,352,1024]{2,1,0:T(8,128)(2,1)}, bf16[1,352,1024]{2,1,0:T(8,128)(2,1)}, u32[]{:S(2)}, u32[]{:S(2)}) collective-permute-start(bf16[1,352,1024]{2,1,0:T(8,128)(2,1)} %add_convert_fusion.3), channel_id=1, source_target_pairs={{8,0},{16,24},{9,1},{17,25},{10,2},{18,26},{11,3},{19,27},{12,4},{... | collective-permute-start | bytes 2162696 | tf_op jit(solution)/shard_map/ppermute | solution.py:281
  526.4 5.1 copy-start.25
  530.2 95.1 %collective-permute-start.7 = (bf16[1,128,6656]{2,1,0:T(8,128)(2,1)}, bf16[1,128,6656]{2,1,0:T(8,128)(2,1)}, u32[]{:S(2)}, u32[]{:S(2)}) collective-permute-start(bf16[1,128,6656]{2,1,0:T(8,128)(2,1)} %add_convert_fusion), channel_id=1, source_target_pairs={{8,0},{16,24},{9,1},{17,25},{10,2},{18,26},{11,3},{19,27},{12,4},{... | collective-permute-start | bytes 5111816 | tf_op jit(solution)/shard_map/ppermute | solution.py:281
  (31 other events, 86.7 us)
Sparse Core Ops, SparseCore 0:
  10.5 85.2 all-gather.6
  98.2 71.6 all-gather.8
  171.8 43.1 all-gather.10
  277.8 119.2 reduce-scatter.5
  400.4 59.0 reduce-scatter.7
  462.8 63.5 reduce-scatter.3
  528.8 77.1 all-reduce.5

commit v9 on v7

--- a/solution.py
+++ b/solution.py
@@ -331,11 +331,12 @@
     full_qkv = qkv_blocks.reshape(n_group * own_rows, qkv_width)
     full_gain_attn = gain_rows[:, 0, :own_rows].reshape(-1)
     full_gain_mlp = gain_rows[:, 0, own_rows : 2 * own_rows].reshape(-1)
-    out_blocks, down_blocks = gather_blocks([w_out, w_down])
+    (out_blocks,) = gather_blocks([w_out])
     full_out = out_blocks.reshape(-1, model_width)
-    full_down = down_blocks.reshape(-1, model_width)
     (gu_blocks,) = gather_blocks([jnp.concatenate([w_gate, w_up], axis=1)])
     full_gu = gu_blocks.reshape(n_group * own_rows, 2 * ff_width)
+    (down_blocks,) = gather_blocks([w_down])
+    full_down = down_blocks.reshape(-1, model_width)
     ctx_index = lax.axis_index("ctx")
     q_pos = ctx_index * slot_rows + jnp.arange(slot_rows)
     live_rows = q_pos[None, :] < lengths[:, None]
@@ -397,7 +398,12 @@
     output = jnp.where(live_rows[..., None], final, 0.0).astype(jnp.bfloat16)
     output_gradient = jnp.where(live_rows[..., None], cotangent.astype(jnp.float32), 0.0)
     g_low = output_gradient.astype(jnp.bfloat16)
-    grad_down = jnp.einsum("srf,srd->fd", hidden, g_low, preferred_element_type=jnp.float32)
+    gu_alone = lax.optimization_barrier(gu_proj)
+    gate_alone = gu_alone[..., :ff_width]
+    hidden_alone = (gate_alone * jax.nn.sigmoid(gate_alone) * gu_alone[..., ff_width:]).astype(
+        jnp.bfloat16
+    )
+    grad_down = jnp.einsum("srf,srd->fd", hidden_alone, g_low, preferred_element_type=jnp.float32)
     (part_down,) = scatter_blocks(
         [grad_down.reshape(n_group, -1, model_width).astype(jnp.bfloat16)], True
     )

time: 634 us -> 640 us (level)
  waiting for transfers between devices: 279 us -> 297 us
  local copies, waits for them, and re-layouts: 74.8 us -> 59.9 us
    all_gather x3 -> x4, waiting for transfers between devices: 32.9 us -> 52.2 us  [gather_blocks(): gathered = lax.all_gather(packed, GROUP, axis=0, tiled=False)]
    slice x3 -> x1, local copies, waits for them, and re-layouts: 11.9 us -> 3.28 us  [gather_blocks(): fulls.append(gathered[:, offset:offset + piece.shape[0], :])]
  transfers between devices with their start and end apart: 18 -> 19, of which waited for: 10 -> 11; matrix products, arithmetic and copies ran while one was open for 31% -> 32% of each run, Pallas kernels for 5% -> 5%
where the time goes in v9:
time: 640 us; the launch traced here: 632 us
  waiting for transfers between devices  297 us (46%)
  matrix products  111 us (17%)
  other arithmetic  93.2 us (15%)
  local copies, waits for them, and re-layouts  59.9 us (9%)
  Pallas kernels  32.9 us (5%)
  starting transfers between devices  22.6 us (4%)
  between operations  16 us (2%)
    ppermute x1, waiting for transfers between devices, shards(): other_tokens = lax.ppermute(tokens, 'ctx', [(0, 1), (1, 0)])  67.9 us
    reduce_scatter x3, waiting for transfers between devices, scatter_blocks(): summed = lax.psum_scatter(packed, GROUP, scatter_dimension=0, tiled=True)  57.3 us
    all_gather x4, waiting for transfers between devices, gather_blocks(): gathered = lax.all_gather(packed, GROUP, axis=0, tiled=False)  52.2 us
    ppermute x2, waiting for transfers between devices, rep_sum(): sent_out = lax.ppermute(total, 'rep', [(1, 0), (2, 3)])  43.9 us
    pallas_call x2, Pallas kernels, block_backward(): pl.pallas_call(kernel, grid=(n_slots, n_heads // 2), in_specs=[q_spec, k_...  32.9 us
    ppermute x3, waiting for transfers between devices, shards(): lax.ppermute((g_attended, dot_rows, lse_rows), 'ctx', [(1, 0)])  29.2 us
    psum x1, waiting for transfers between devices, scatter_blocks(): lax.psum(summed, 'rep')  23.4 us
    ppermute x2, waiting for transfers between devices, rep_sum(): arrived = lax.ppermute(x, 'rep', [(0, 1), (3, 2)])  21.8 us
  transfers between devices with their start and end apart: 19, of which 11 were waited for; matrix products, arithmetic and copies ran while one was open for 32% of the time, Pallas kernels for 5%

profile of v9, /device:TPU:0, one launch (start us, length us, event | category | flops | bytes accessed | tf_op | source)
XLA Modules:
  0.0 631.8 jit_solution(15660598719133682825)
XLA Ops:
  13.4 5.9 collective-permute-start.1
  22.2 67.9 %collective-permute-done = bf16[1,512,1024]{2,1,0:T(8,128)(2,1)S(1)} collective-permute-done((bf16[1,512,1024]{2,1,0:T(8,128)(2,1)S(1)}, bf16[1,512,1024]{2,1,0:T(8,128)(2,1)S(1)}, u32[]{:S(2)}, u32[]{:S(2)}) %collective-permute-start) | collective-permute-done | bytes 1048608 | tf_op jit(solution)/shard_map/ppermute | solution.py:346
  133.2 29.3 %while.13 = (s32[]{:T(128)}, bf16[2,1,512,8,64]{2,4,3,1,0:T(8,128)(2,1)}, f32[2,1,1,8,512]{4,3,2,1,0:T(8,128)S(1)}, bf16[2,1,1024,8,64]{2,4,3,1,0:T(8,128)(2,1)}...) while((s32[]{:T(128)}, ...), condition=%wide.region_5.6_spmd.clone, body=%wide.region_2.5_spmd.clone.sunk | while | flops 1125644800 | bytes 73025736 | solution.py:116
  137.4 4.4 fusion.133
  141.9 5.0 fusion.134
  152.1 4.4 fusion.133
  156.5 5.0 fusion.134
  166.2 20.9 %all-gather.13.cloned.1.call-done = bf16[1024,5632]{1,0:T(8,128)(2,1)} async-done(((bf16[128,5632]{1,0:T(8,128)(2,1)}), bf16[1024,5632]{1,0:T(8,128)(2,1)}) %all-gather.13.cloned.1.call-update) | async-done | bytes 11534352 | tf_op jit(solution)/shard_map/all_gather | solution.py:264
  187.1 13.7 %convolution_bitcast_fusion = f32[1,512,5632]{2,1,0:T(8,128)} fusion(bf16[1024,5632]{1,0:T(8,128)(2,1)} %all-gather.13.cloned.1.call-done, f32[1,512,1024]{2,1,0:T(8,128)S(1)} %get-tuple-element.205, f32[1024]{0:T(1024)S(1)} %bitcast.277, f32[512]{0:T(512)S(1)} %add_rsqrt_fusion), kind=kOutput, calls=%fused_computation.29 | convolution fusion | flops 5907152896 | bytes 25171968 | tf_op jit(solution)/shard_map/srd,df->srf/dot_general | solution.py:390
  200.7 31.3 %all-gather.15.cloned.1.call-done = bf16[2816,1024]{1,0:T(8,128)(2,1)} async-done(((bf16[352,1024]{1,0:T(8,128)(2,1)}), bf16[2816,1024]{1,0:T(8,128)(2,1)}) %all-gather.15.cloned.1.call-update) | async-done | bytes 5767184 | tf_op jit(solution)/shard_map/all_gather | solution.py:264
  232.0 9.5 %fusion.23 = (bf16[1,512,2816]{2,1,0:T(8,128)(2,1)S(1)}, bf16[1,512,2816]{2,1,0:T(8,128)(2,1)S(1)}) fusion(f32[1,512,5632]{2,1,0:T(8,128)} %convolution_bitcast_fusion, bf16[2816,1024]{1,0:T(8,128)(2,1)} %all-gather.15.cloned.1.call-done, bf16[1,512,1024]{2,1,0:T(8,128)(2,1)S(1)} %copy-done.39, pred[512]{0:T(512)(128)(4,1)S(1)} %copy-done.52), kind=kOutput, calls=%fused_computation.38 | convolution fusion | flops 2973106176 | bytes 24117760 | tf_op jit(solution)/shard_map/srd,fd->srf/dot_general | solution.py:410
  243.9 9.3 %convolution_convert_fusion = bf16[1024,5632]{1,0:T(8,128)(2,1)} fusion(bf16[1,512,2816]{2,1,0:T(8,128)(2,1)S(1)} %get-tuple-element.163, bf16[1,512,2816]{2,1,0:T(8,128)(2,1)S(1)} %get-tuple-element.162, f32[1,512,1024]{2,1,0:T(8,128)S(1)} %get-tuple-element.205, f32[1024]{0:T(1024)S(1)} %bitcast.278, f32[512]{0:T(512)S(1)} %add_rsqrt_fusion), kind=kOutput, calls=%fused_computation.28 | convolution fusion | flops 5924454400 | bytes 19404800 | tf_op jit(solution)/shard_map/srd,srf->df/dot_general | solution.py:416
  253.2 11.9 %fusion.52 = (bf16[1024]{0:T(1024)(128)(2,1)S(1)}, f32[512]{0:T(512)S(1)}, f32[512,1024]{1,0:T(8,128)S(1)}) fusion(f32[1,512,1024]{2,1,0:T(8,128)S(1)} %get-tuple-element.205, f32[512]{0:T(512)S(1)} %add_rsqrt_fusion, f32[1024]{0:T(1024)S(1)} %bitcast.279, bf16[1024,5632]{1,0:T(8,128)(2,1)} %all-gather.13.cloned.1.call-done, ...), kind=kOutput, calls=%fused_computation.87 | convolution fusion | flops 5920258560 | bytes 21506048 | tf_op jit(solution)/shard_map/srf,df->srd/dot_general | solution.py:417
  272.7 11.5 %pad_maximum_fusion = bf16[1024,6656]{1,0:T(8,128)(2,1)} fusion(bf16[1024,5632]{1,0:T(8,128)(2,1)} %convolution_convert_fusion, bf16[1024,1024]{1,0:T(8,128)(2,1)S(1)} %copy.64), kind=kLoop, calls=%fused_computation.25 | loop fusion | flops 27262976 | bytes 27262976 | tf_op jit(solution)/shard_map/concatenate | solution.py:427
  284.2 5.2 fusion.36
  292.3 10.2 %convolution_convert_fusion.2 = bf16[8,352,1024]{2,1,0:T(8,128)(2,1)} fusion(bf16[8,352,512]{2,1,0:T(8,128)(2,1)} %bitcast.264, bf16[1,512,1024]{2,1,0:T(8,128)(2,1)} %param.17, pred[512]{0:T(512)(128)(4,1)S(1)} %copy-done.52), kind=kOutput, calls=%fused_computation.49 | convolution fusion | flops 2957246464 | bytes 9699840 | tf_op jit(solution)/shard_map/srf,srd->fd/dot_general | solution.py:406
  317.3 3.9 convolution_convert_fusion.4
  328.8 16.5 %shard_map.220 = (f32[1,512,1024]{2,1,0:T(8,128)}, f32[1,512,1024]{2,1,0:T(8,128)}, f32[1,512,1024]{2,1,0:T(8,128)}) custom-call(bf16[1,512,1024]{2,1,0:T(8,128)(2,1)} %copy-done.24, bf16[1,512,1024]{2,1,0:T(8,128)(2,1)} %copy.51.k_ref, bf16[1,512,1024]{2,1,0:T(8,128)(2,1)} %copy-done.23, bf16[1,512,1024]{2,1,0:T(8,128)(2,1)} %bitcast.265, ...), custom_call_target="tpu_custom_call" | custom-call | flops 2684354560 | bytes 10485760 | tf_op jit(solution)/shard_map/pallas_call | solution.py:234
  345.2 29.2 %collective-permute-done.4 = f32[1,16,512]{2,1,0:T(8,128)S(1)} collective-permute-done((f32[1,16,512]{2,1,0:T(8,128)S(1)}, f32[1,16,512]{2,1,0:T(8,128)S(1)}, u32[]{:S(2)}, u32[]{:S(2)}) %collective-permute-start.4) | collective-permute-done | bytes 32800 | tf_op jit(solution)/shard_map/ppermute | solution.py:441
  380.4 16.4 %shard_map.221 = (f32[1,512,1024]{2,1,0:T(8,128)}, f32[1,512,1024]{2,1,0:T(8,128)}, f32[1,512,1024]{2,1,0:T(8,128)}) custom-call(bf16[1,512,1024]{2,1,0:T(8,128)(2,1)} %broadcast_select_fusion.3.q_ref, bf16[1,512,1024]{2,1,0:T(8,128)(2,1)} %broadcast_select_fusion.2.k_ref, bf16[1,512,1024]{2,1,0:T(8,128)(2,1)} %get-tuple-element.155.v_ref, ...), custom_call_target="tpu_custom_call" | custom-call | flops 2684354560 | bytes 10485760 | tf_op jit(solution)/shard_map/pallas_call | solution.py:234
  396.8 6.3 select_add_fusion
  416.9 5.0 fusion.107
  421.9 7.3 %fusion.45 = (bf16[1024]{0:T(1024)(128)(2,1)S(1)}, f32[512]{0:T(512)S(1)}, f32[512,1024]{1,0:T(8,128)S(1)}) fusion(bf16[1,512,1024]{2,1,0:T(8,128)(2,1)S(1)} %copy-done.1, f32[512]{0:T(512)S(1)} %copy-done.51, f32[1024]{0:T(1024)S(1)} %bitcast.273, bf16[1024,3072]{1,0:T(8,128)(2,1)} %bitcast.243, bf16[1,512,1024]{2,1,0:T(8,128)(2,1)S(1)} %get-tuple-element.153, ...), kind=kOutput, calls=%fused_computation.74 | convolution fusion | flops 3234331136 | bytes 12593152 | tf_op jit(solution)/shard_map/sre,de->srd/dot_general | solution.py:483
  433.5 5.0 convolution_convert_fusion.1
  445.4 22.9 %reduce-scatter.8.cloned.1.call-done = bf16[1,352,1024]{2,1,0:T(8,128)(2,1)} async-done(((bf16[8,352,1024]{2,1,0:T(8,128)(2,1)}), bf16[1,352,1024]{2,1,0:T(8,128)(2,1)}) %reduce-scatter.8.cloned.1.call-update) | async-done | bytes 720912 | tf_op jit(solution)/shard_map/reduce_scatter | solution.py:287
  471.8 11.4 %collective-permute-done.5 = bf16[1,128,6656]{2,1,0:T(8,128)(2,1)S(1)} collective-permute-done((bf16[1,128,6656]{2,1,0:T(8,128)(2,1)}, bf16[1,128,6656]{2,1,0:T(8,128)(2,1)S(1)}, u32[]{:S(2)}, u32[]{:S(2)}) %collective-permute-start.5) | collective-permute-done | bytes 1703968 | tf_op jit(solution)/shard_map/ppermute | solution.py:277
  487.2 10.4 %collective-permute-done.8 = bf16[1,352,1024]{2,1,0:T(8,128)(2,1)S(1)} collective-permute-done((bf16[1,352,1024]{2,1,0:T(8,128)(2,1)}, bf16[1,352,1024]{2,1,0:T(8,128)(2,1)S(1)}, u32[]{:S(2)}, u32[]{:S(2)}) %collective-permute-start.8) | collective-permute-done | bytes 720928 | tf_op jit(solution)/shard_map/ppermute | solution.py:277
  501.0 34.4 %reduce-scatter.4.cloned.1.call-done = bf16[1,136,3072]{2,1,0:T(8,128)(2,1)} async-done(((bf16[8,136,3072]{2,1,0:T(8,128)(2,1)}), bf16[1,136,3072]{2,1,0:T(8,128)(2,1)}) %reduce-scatter.4.cloned.1.call-update) | async-done | bytes 835600 | tf_op jit(solution)/shard_map/reduce_scatter | solution.py:287
  538.8 10.2 %fusion.57 = bf16[1,512,1024]{2,1,0:T(8,128)(2,1)} fusion(f32[1,512,1024]{2,1,0:T(8,128)S(1)} %copy-done.5, bf16[2816,1024]{1,0:T(8,128)(2,1)} %all-gather.15.cloned.1.call-done, f32[1,512,5632]{2,1,0:T(8,128)} %convolution_bitcast_fusion, pred[512]{0:T(512)(128)(4,1)S(1)} %copy-done.52), kind=kOutput, calls=%fused_computation.95 | convolution fusion | flops 2963013632 | bytes 20447744 | tf_op jit(solution)/shard_map/srf,fd->srd/dot_general | solution.py:395
  549.0 26.6 %collective-permute-done.10 = bf16[1,352,1024]{2,1,0:T(8,128)(2,1)} collective-permute-done((bf16[1,352,1024]{2,1,0:T(8,128)(2,1)}, bf16[1,352,1024]{2,1,0:T(8,128)(2,1)}, u32[]{:S(2)}, u32[]{:S(2)}) %collective-permute-start.10) | collective-permute-done | bytes 720928 | tf_op jit(solution)/shard_map/ppermute | solution.py:281
  577.8 23.4 %all-reduce.6.cloned.1.call-done = bf16[136,3072]{1,0:T(8,128)(2,1)} async-done(((bf16[136,3072]{1,0:T(8,128)(2,1)}), bf16[136,3072]{1,0:T(8,128)(2,1)}) %all-reduce.6.cloned.1.call-update) | async-done | bytes 835600 | tf_op jit(solution)/shard_map/psum | solution.py:288
  604.4 17.3 %collective-permute-done.7 = bf16[1,128,6656]{2,1,0:T(8,128)(2,1)S(1)} collective-permute-done((bf16[1,128,6656]{2,1,0:T(8,128)(2,1)S(1)}, bf16[1,128,6656]{2,1,0:T(8,128)(2,1)S(1)}, u32[]{:S(2)}, u32[]{:S(2)}) %collective-permute-start.7) | collective-permute-done | bytes 1703968 | tf_op jit(solution)/shard_map/ppermute | solution.py:281
  (247 shorter events, 153.5 us)
Async XLA Ops:
  7.2 83.2 %all-gather.9.cloned.1.call-start = ((), (), s32[]{:S(2)}) async-start(), calls=%async_computation.7 | async-start | bytes 7520256 | tf_op jit(solution)/shard_map/all_gather | solution.py:264
  10.1 152.4 %all-gather.11.cloned.1.call-start = ((), (), s32[]{:S(2)}) async-start(), calls=%async_computation.8 | async-start | bytes 2359296 | tf_op jit(solution)/shard_map/all_gather | solution.py:264
  10.9 8.5 %copy-start = (bf16[1,512,1024]{2,1,0:T(8,128)(2,1)S(1)}, bf16[1,512,1024]{2,1,0:T(8,128)(2,1)}, u32[]{:S(2)}) copy-start(bf16[1,512,1024]{2,1,0:T(8,128)(2,1)} %param.15) | copy-start | bytes 3145732
  10.9 176.2 %all-gather.13.cloned.1.call-start = ((), (), s32[]{:S(2)}) async-start(), calls=%async_computation.9 | async-start | bytes 12976128 | tf_op jit(solution)/shard_map/all_gather | solution.py:264
  13.4 218.6 %all-gather.15.cloned.1.call-start = ((), (), s32[]{:S(2)}) async-start(), calls=%async_computation.10 | async-start | bytes 6488064 | tf_op jit(solution)/shard_map/all_gather | solution.py:264
  13.4 93.4 %collective-permute-start.1 = (bf16[1,512,1024]{2,1,0:T(8,128)(2,1)S(1)}, bf16[1,512,1024]{2,1,0:T(8,128)(2,1)}, u32[]{:S(2)}, u32[]{:S(2)}) collective-permute-start(bf16[1,512,1024]{2,1,0:T(8,128)(2,1)S(1)} %copy-done.31), channel_id=1, source_target_pairs={{0,1},{2,3},{4,5},{6,7},{8,9},{10,11},{12,13},{14,15},{16,17},{18,... | collective-permute-start | bytes 3145736 | tf_op jit(solution)/shard_map/ppermute | solution.py:347
  19.3 70.7 %collective-permute-start = (bf16[1,512,1024]{2,1,0:T(8,128)(2,1)S(1)}, bf16[1,512,1024]{2,1,0:T(8,128)(2,1)S(1)}, u32[]{:S(2)}, u32[]{:S(2)}) collective-permute-start(bf16[1,512,1024]{2,1,0:T(8,128)(2,1)S(1)} %copy-done), channel_id=1, source_target_pairs={{0,1},{1,0},{2,3},{3,2},{4,5},{5,4},{6,7},{7,6},{8,9},{9,8},{10,11... | collective-permute-start | bytes 3145736 | tf_op jit(solution)/shard_map/ppermute | solution.py:346
  19.4 422.6 %reduce-scatter.6.cloned.1.call-start = ((), (), s32[]{:S(2)}) async-start(), calls=%async_computation.5 | async-start | bytes 15335424 | tf_op jit(solution)/shard_map/reduce_scatter | solution.py:287
  21.0 74.5 %copy-start.50 = (f32[512]{0:T(512)}, f32[512]{0:T(512)S(1)}, u32[]{:S(2)}) copy-start(f32[512]{0:T(512)S(1)} %add_rsqrt_fusion.1) | copy-start | bytes 6148
  22.2 104.8 %copy-start.43 = (f32[512,32]{0,1:T(8,128)}, f32[512,32]{0,1:T(8,128)S(1)}, u32[]{:S(2)}) copy-start(f32[512,32]{0,1:T(8,128)S(1)} %get-tuple-element.199) | copy-start | bytes 196612
  93.7 7.1 %copy-start.10 = (bf16[8,128,3072]{2,1,0:T(8,128)(2,1)}, bf16[8,128,3072]{2,1,0:T(8,128)(2,1)S(1)}, u32[]{:S(2)}) copy-start(bf16[8,128,3072]{2,1,0:T(8,128)(2,1)S(1)} %slice.143) | copy-start | bytes 18874372
  95.6 5.2 copy-start.47
  162.5 24.6 %copy-start.49 = (f32[8,1,128]{2,1,0:T(1,128)S(1)}, f32[8,1,128]{2,1,0:T(1,128)}, u32[]{:S(2)}) copy-start(f32[8,1,128]{2,1,0:T(1,128)} %get-tuple-element.164) | copy-start | bytes 12292
  166.2 99.0 %copy-start.4 = (f32[1,512,1024]{2,1,0:T(8,128)}, f32[1,512,1024]{2,1,0:T(8,128)S(1)}, u32[]{:S(2)}) copy-start(f32[1,512,1024]{2,1,0:T(8,128)S(1)} %get-tuple-element.205) | copy-start | bytes 6291460
  187.1 45.0 %copy-start.39 = (bf16[1,512,1024]{2,1,0:T(8,128)(2,1)S(1)}, bf16[1,512,1024]{2,1,0:T(8,128)(2,1)}, u32[]{:S(2)}) copy-start(bf16[1,512,1024]{2,1,0:T(8,128)(2,1)} %param.17) | copy-start | bytes 3145732
  187.1 45.0 %copy-start.52 = (pred[512]{0:T(512)(128)(4,1)S(1)}, pred[512]{0:T(512)(128)(4,1)}, u32[]{:S(2)}) copy-start(pred[512]{0:T(512)(128)(4,1)} %fusion.96) | copy-start | bytes 1540
  284.2 184.1 %reduce-scatter.8.cloned.1.call-start = ((), (), s32[]{:S(2)}) async-start(), calls=%async_computation.6 | async-start | bytes 6488064 | tf_op jit(solution)/shard_map/reduce_scatter | solution.py:287
  302.5 232.9 %reduce-scatter.4.cloned.1.call-start = ((), (), s32[]{:S(2)}) async-start(), calls=%async_computation.3 | async-start | bytes 7520256 | tf_op jit(solution)/shard_map/reduce_scatter | solution.py:287
  307.8 7.1 %copy-start.24 = (bf16[1,512,1024]{2,1,0:T(8,128)(2,1)}, bf16[1,512,1024]{2,1,0:T(8,128)(2,1)S(1)}, u32[]{:S(2)}) copy-start(bf16[1,512,1024]{2,1,0:T(8,128)(2,1)S(1)} %copy.50.q_ref) | copy-start | bytes 3145732
  313.3 13.2 %collective-permute-start.3 = (f32[1,16,512]{2,1,0:T(8,128)S(1)}, f32[1,16,512]{2,1,0:T(8,128)S(1)}, u32[]{:S(2)}, u32[]{:S(2)}) collective-permute-start(f32[1,16,512]{2,1,0:T(8,128)S(1)} %bitcast.275), channel_id=1, source_target_pairs={{1,0},{3,2},{5,4},{7,6},{9,8},{11,10},{13,12},{15,14},{17,16},{19,... | collective-permute-start | bytes 98312 | tf_op jit(solution)/shard_map/ppermute | solution.py:441
  322.7 53.1 %collective-permute-start.2 = (bf16[1,512,16,64]{1,3,2,0:T(8,128)(2,1)S(1)}, bf16[1,512,16,64]{1,3,2,0:T(8,128)(2,1)}, u32[]{:S(2)}, u32[]{:S(2)}) collective-permute-start(bf16[1,512,16,64]{1,3,2,0:T(8,128)(2,1)S(1)} %bitcast.233), channel_id=1, source_target_pairs={{1,0},{3,2},{5,4},{7,6},{9,8},{11,10},{13,12},{15,14},{17,16},{19,... | collective-permute-start | bytes 3145736 | tf_op jit(solution)/shard_map/ppermute | solution.py:441
  327.5 47.0 %collective-permute-start.4 = (f32[1,16,512]{2,1,0:T(8,128)S(1)}, f32[1,16,512]{2,1,0:T(8,128)S(1)}, u32[]{:S(2)}, u32[]{:S(2)}) collective-permute-start(f32[1,16,512]{2,1,0:T(8,128)S(1)} %bitcast.269), channel_id=1, source_target_pairs={{1,0},{3,2},{5,4},{7,6},{9,8},{11,10},{13,12},{15,14},{17,16},{19,... | collective-permute-start | bytes 98312 | tf_op jit(solution)/shard_map/ppermute | solution.py:441
  416.9 5.1 copy-start.51
  421.9 7.4 %copy-start.40 = (bf16[1,512,1024]{2,1,0:T(8,128)(2,1)}, bf16[1,512,1024]{2,1,0:T(8,128)(2,1)S(1)}, u32[]{:S(2)}) copy-start(bf16[1,512,1024]{2,1,0:T(8,128)(2,1)S(1)} %get-tuple-element.153) | copy-start | bytes 3145732
  441.9 159.4 %all-reduce.6.cloned.1.call-start = ((), (), s32[]{:S(2)}) async-start(), calls=%async_computation.4 | async-start | bytes 1671168 | tf_op jit(solution)/shard_map/psum | solution.py:288
  442.0 41.2 %collective-permute-start.5 = (bf16[1,128,6656]{2,1,0:T(8,128)(2,1)}, bf16[1,128,6656]{2,1,0:T(8,128)(2,1)S(1)}, u32[]{:S(2)}, u32[]{:S(2)}) collective-permute-start(bf16[1,128,6656]{2,1,0:T(8,128)(2,1)} %reduce-scatter.6.cloned.1.call-done), channel_id=1, source_target_pairs={{0,8},{24,16},{1,9},{25,17},{2,10},{26,18},{3,11},{27,19},{4,12},{... | collective-permute-start | bytes 5111816 | tf_op jit(solution)/shard_map/ppermute | solution.py:277
  468.3 29.3 %copy-start.41 = (bf16[1,352,1024]{2,1,0:T(8,128)(2,1)S(1)}, bf16[1,352,1024]{2,1,0:T(8,128)(2,1)}, u32[]{:S(2)}) copy-start(bf16[1,352,1024]{2,1,0:T(8,128)(2,1)} %reduce-scatter.8.cloned.1.call-done) | copy-start | bytes 2162692
  468.3 29.3 %collective-permute-start.8 = (bf16[1,352,1024]{2,1,0:T(8,128)(2,1)}, bf16[1,352,1024]{2,1,0:T(8,128)(2,1)S(1)}, u32[]{:S(2)}, u32[]{:S(2)}) collective-permute-start(bf16[1,352,1024]{2,1,0:T(8,128)(2,1)} %reduce-scatter.8.cloned.1.call-done), channel_id=1, source_target_pairs={{0,8},{24,16},{1,9},{25,17},{2,10},{26,18},{3,11},{27,19},{4,12},{... | collective-permute-start | bytes 2162696 | tf_op jit(solution)/shard_map/ppermute | solution.py:277
  485.3 50.1 %collective-permute-start.6 = (bf16[1,128,6656]{2,1,0:T(8,128)(2,1)S(1)}, bf16[1,128,6656]{2,1,0:T(8,128)(2,1)}, u32[]{:S(2)}, u32[]{:S(2)}) collective-permute-start(bf16[1,128,6656]{2,1,0:T(8,128)(2,1)S(1)} %add_convert_fusion.1), channel_id=1, source_target_pairs={{8,16},{16,8},{9,17},{17,9},{10,18},{18,10},{11,19},{19,11},{12,20... | collective-permute-start | bytes 5111816 | tf_op jit(solution)/shard_map/ppermute | solution.py:279
  497.9 0.7 collective-permute-start.9
  499.7 75.8 %collective-permute-start.10 = (bf16[1,352,1024]{2,1,0:T(8,128)(2,1)}, bf16[1,352,1024]{2,1,0:T(8,128)(2,1)}, u32[]{:S(2)}, u32[]{:S(2)}) collective-permute-start(bf16[1,352,1024]{2,1,0:T(8,128)(2,1)} %add_convert_fusion.3), channel_id=1, source_target_pairs={{8,0},{16,24},{9,1},{17,25},{10,2},{18,26},{11,3},{19,27},{12,4},{... | collective-permute-start | bytes 2162696 | tf_op jit(solution)/shard_map/ppermute | solution.py:281
  537.4 84.3 %collective-permute-start.7 = (bf16[1,128,6656]{2,1,0:T(8,128)(2,1)S(1)}, bf16[1,128,6656]{2,1,0:T(8,128)(2,1)S(1)}, u32[]{:S(2)}, u32[]{:S(2)}) collective-permute-start(bf16[1,128,6656]{2,1,0:T(8,128)(2,1)S(1)} %add_convert_fusion), channel_id=1, source_target_pairs={{8,0},{16,24},{9,1},{17,25},{10,2},{18,26},{11,3},{19,27},{12,4},{... | collective-permute-start | bytes 5111816 | tf_op jit(solution)/shard_map/ppermute | solution.py:281
  (45 other events, 136.1 us)
Sparse Core Ops, SparseCore 0:
  10.5 72.8 all-gather.8
  85.2 31.7 all-gather.10
  119.5 67.5 all-gather.12
  188.8 43.1 all-gather.14
  284.3 121.5 reduce-scatter.5
  409.2 59.0 reduce-scatter.7
  471.8 63.5 reduce-scatter.3
  537.8 63.4 all-reduce.5

commit v10 on v9

--- a/solution.py
+++ b/solution.py
@@ -4,6 +4,7 @@
 import jax.numpy as jnp
 from jax import lax
 from jax.experimental import pallas as pl
+from jax.experimental.pallas import tpu as pltpu
 from jax.sharding import PartitionSpec as P
 
 
@@ -181,13 +182,6 @@
     return (join_heads(q_grads), join_heads(k_grads), join_heads(v_grads))
 
 
-def sums_to_rows(log_sums):
-    n_groups, n_blocks, n_slots, per_group, q_block = log_sums.shape
-    return jnp.transpose(log_sums, (2, 0, 3, 1, 4)).reshape(
-        n_slots, n_groups * per_group, n_blocks * q_block
-    )
-
-
 FAR = 1 << 30
 
 
@@ -214,6 +208,63 @@
         dk_ref[0, :, cols] = jnp.dot(dscores, q, preferred_element_type=jnp.float32) * scale
         tn = (((0,), (0,)), ((), ()))
         dq_ref[0, :, cols] = lax.dot_general(dscores, k, tn, preferred_element_type=jnp.float32) * scale
+
+
+def _block_forward_kernel(q_ref, k_ref, v_ref, qpos_ref, kpos_ref, out_ref, lse_ref, *, head_width, scale):
+    pair = pl.program_id(1)
+    allowed = kpos_ref[0] <= qpos_ref[...]
+    nt = (((1,), (1,)), ((), ()))
+    tn = (((0,), (0,)), ((), ()))
+    for j in range(2):
+        cols = slice(j * head_width, (j + 1) * head_width)
+        q = q_ref[0, :, cols]
+        k = k_ref[0, :, cols]
+        v = v_ref[0, :, cols]
+        scores = lax.dot_general(k, q, nt, preferred_element_type=jnp.float32) * scale
+        scores = jnp.where(allowed, scores, -1e30)
+        highest = jnp.max(scores, axis=0, keepdims=True)
+        exponent = jnp.exp(scores - highest)
+        totals = jnp.sum(exponent, axis=0, keepdims=True)
+        probs = (exponent / totals).astype(jnp.bfloat16)
+        mixture = lax.dot_general(probs, v, tn, preferred_element_type=jnp.float32)
+        out_ref[0, :, cols] = mixture.astype(out_ref.dtype)
+        lse_ref[0, pl.ds(2 * pair + j, 1), :] = highest + jnp.log(totals)
+
+
+def block_forward(queries, keys, values, q_pos, k_pos, lengths):
+    n_slots, q_len, n_heads, head_width = queries.shape
+    k_len = keys.shape[1]
+    width = n_heads * head_width
+    pair_width = 2 * head_width
+    flat = lambda a: a.reshape(a.shape[0], a.shape[1], width)
+    kpos = jnp.where(
+        (k_pos[None, :] < lengths[:, None]) & (k_pos[None, :] >= 0), k_pos[None, :], FAR
+    ).astype(jnp.int32)[..., None]
+    qpos = q_pos.astype(jnp.int32)[None, :]
+    kernel = functools.partial(_block_forward_kernel, head_width=head_width, scale=head_width ** (-0.5))
+    q_spec = pl.BlockSpec((1, q_len, pair_width), lambda s, p: (s, 0, p))
+    k_spec = pl.BlockSpec((1, k_len, pair_width), lambda s, p: (s, 0, p))
+    out, lse = pl.pallas_call(
+        kernel,
+        grid=(n_slots, n_heads // 2),
+        in_specs=[
+            q_spec, k_spec, k_spec,
+            pl.BlockSpec((1, q_len), lambda s, p: (0, 0)),
+            pl.BlockSpec((1, k_len, 1), lambda s, p: (s, 0, 0)),
+        ],
+        out_specs=[q_spec, pl.BlockSpec((1, n_heads, q_len), lambda s, p: (s, 0, 0))],
+        out_shape=[
+            jax.ShapeDtypeStruct((n_slots, q_len, width), jnp.bfloat16),
+            jax.ShapeDtypeStruct((n_slots, n_heads, q_len), jnp.float32),
+        ],
+        compiler_params=pltpu.CompilerParams(dimension_semantics=("arbitrary", "arbitrary")),
+        cost_estimate=pl.CostEstimate(
+            flops=n_slots * n_heads * 4 * q_len * k_len * head_width,
+            transcendentals=n_slots * n_heads * q_len * k_len,
+            bytes_accessed=2 * (2 * q_len + 2 * k_len) * width * n_slots,
+        ),
+    )(flat(queries), flat(keys), flat(values), qpos, kpos)
+    return out.reshape(n_slots, q_len, n_heads, head_width), lse
 
 
 def block_backward(queries, keys, values, upstream, lse_rows, dot_rows, q_pos, k_pos, lengths):
@@ -380,8 +431,11 @@
             lax.all_gather(values, "ctx", axis=1, tiled=True),
         )
         k_pos = jnp.arange(n_ctx * slot_rows)
-    attn_raw, attn_lse = attend_forward(queries, slot_k, slot_v, q_pos, k_pos, lengths)
-    attended = attn_raw.astype(jnp.bfloat16)
+    if paired:
+        attended, lse_rows = block_forward(queries, slot_k, slot_v, q_pos, k_pos, lengths)
+    else:
+        attn_raw, attn_lse = attend_forward(queries, slot_k, slot_v, q_pos, k_pos, lengths)
+        attended = attn_raw.astype(jnp.bfloat16)
     att_flat = attended.reshape(n_slots, slot_rows, model_width)
     branch = jnp.einsum("sre,ed->srd", att_flat, full_out, preferred_element_type=jnp.float32)
     residual = inputs + branch
@@ -403,17 +457,19 @@
     hidden_alone = (gate_alone * jax.nn.sigmoid(gate_alone) * gu_alone[..., ff_width:]).astype(
         jnp.bfloat16
     )
-    grad_down = jnp.einsum("srf,srd->fd", hidden_alone, g_low, preferred_element_type=jnp.float32)
+    grad_down = jnp.einsum(
+        "srf,srd->fd", hidden_alone, g_low, preferred_element_type=jnp.float32
+    )
     (part_down,) = scatter_blocks(
         [grad_down.reshape(n_group, -1, model_width).astype(jnp.bfloat16)], True
     )
     g_hidden = jnp.einsum("srd,fd->srf", g_low, full_down, preferred_element_type=jnp.float32)
-    gate_gradient = (
-        g_hidden * up_proj * sigmoid_gate * (1.0 + gate_proj * (1.0 - sigmoid_gate))
-    ).astype(jnp.bfloat16)
+    gate_gradient = (g_hidden * up_proj * sigmoid_gate * (1.0 + gate_proj * (1.0 - sigmoid_gate))).astype(jnp.bfloat16)
     up_gradient = (g_hidden * gate_proj * sigmoid_gate).astype(jnp.bfloat16)
     gu_gradient = jnp.concatenate([gate_gradient, up_gradient], axis=-1)
-    grad_gu = jnp.einsum("srd,srf->df", mlp_low, gu_gradient, preferred_element_type=jnp.float32)
+    grad_gu = jnp.einsum(
+        "srd,srf->df", mlp_low, gu_gradient, preferred_element_type=jnp.float32
+    )
     g_normed_mlp = jnp.einsum(
         "srf,df->srd", gu_gradient, full_gu, preferred_element_type=jnp.float32
     )
@@ -436,7 +492,6 @@
     (part_ogu,) = scatter_blocks([ogu_block], True)
     row_dots = jnp.sum(g_attended.astype(jnp.float32) * attended.astype(jnp.float32), axis=-1)
     if paired:
-        lse_rows = sums_to_rows(attn_lse)
         dot_rows = jnp.transpose(row_dots, (0, 2, 1))
         later_g, later_dots, later_lse = lax.ppermute(
             (g_attended, dot_rows, lse_rows), "ctx", [(1, 0)]
@@ -486,11 +541,7 @@
     part_qkv, part_gains = scatter_blocks(
         [
             grad_qkv.reshape(n_group, own_rows, qkv_width),
-            gain_block(
-                grad_gain_attn.reshape(n_group, own_rows),
-                grad_gain_mlp.reshape(n_group, own_rows),
-                qkv_width,
-            ),
+            gain_block(grad_gain_attn.reshape(n_group, own_rows), grad_gain_mlp.reshape(n_group, own_rows), qkv_width),
         ],
         False,
     )

time: 640 us -> 627 us (0.980)
  Pallas kernels: 32.9 us -> 55.7 us
  other arithmetic: 93.2 us -> 74.3 us
  matrix products: 111 us -> 99 us
    ppermute x1, waiting for transfers between devices: 67.9 us -> 26.6 us  [shards(): other_tokens = lax.ppermute(tokens, 'ctx', [(0, 1), (1, 0)])]
    all_gather x4, waiting for transfers between devices: 52.2 us -> 90.8 us  [gather_blocks(): gathered = lax.all_gather(packed, GROUP, axis=0, tiled=False)]
    reduce_scatter x3, waiting for transfers between devices: 57.3 us -> 82.1 us  [scatter_blocks(): summed = lax.psum_scatter(packed, GROUP, scatter_dimension=0, tiled=True)]
    ppermute x2, waiting for transfers between devices: 43.9 us -> 19.4 us  [rep_sum(): sent_out = lax.ppermute(total, 'rep', [(1, 0), (2, 3)])]
    pallas_call x0 -> x1, Pallas kernels: none -> 22.6 us  [block_forward(): pl.pallas_call(kernel, grid=(n_slots, n_heads // 2), in_specs=[q_spec, k_...]
    dot_general x4 -> x0, matrix products: 16.1 us -> none  [the longest x2 10.1 us: one_block(): jnp.einsum('shqk,skhe->sqhe', probabilities, v_group, preferred_element_t...]
    psum x1, waiting for transfers between devices: 23.4 us -> 36.6 us  [scatter_blocks(): lax.psum(summed, 'rep')]
    ppermute x2, waiting for transfers between devices: 21.8 us -> 11.8 us  [rep_sum(): arrived = lax.ppermute(x, 'rep', [(0, 1), (3, 2)])]
  transfers between devices with their start and end apart: 19 -> 19, of which waited for: 11 -> 11; matrix products, arithmetic and copies ran while one was open for 32% -> 27% of each run, Pallas kernels for 5% -> 9%
where the time goes in v10:
time: 627 us; the launch traced here: 621 us
  waiting for transfers between devices  298 us (48%)
  matrix products  99 us (16%)
  other arithmetic  74.3 us (12%)
  local copies, waits for them, and re-layouts  56.6 us (9%)
  Pallas kernels  55.7 us (9%)
  starting transfers between devices  21.9 us (3%)
  between operations  16 us (3%)
    all_gather x4, waiting for transfers between devices, gather_blocks(): gathered = lax.all_gather(packed, GROUP, axis=0, tiled=False)  90.8 us
    reduce_scatter x3, waiting for transfers between devices, scatter_blocks(): summed = lax.psum_scatter(packed, GROUP, scatter_dimension=0, tiled=True)  82.1 us
    psum x1, waiting for transfers between devices, scatter_blocks(): lax.psum(summed, 'rep')  36.6 us
    pallas_call x2, Pallas kernels, block_backward(): pl.pallas_call(kernel, grid=(n_slots, n_heads // 2), in_specs=[q_spec, k_...  33 us
    ppermute x3, waiting for transfers between devices, shards(): lax.ppermute((g_attended, dot_rows, lse_rows), 'ctx', [(1, 0)])  29.1 us
    ppermute x1, waiting for transfers between devices, shards(): other_tokens = lax.ppermute(tokens, 'ctx', [(0, 1), (1, 0)])  26.6 us
    pallas_call x1, Pallas kernels, block_forward(): pl.pallas_call(kernel, grid=(n_slots, n_heads // 2), in_specs=[q_spec, k_...  22.6 us
    ppermute x2, waiting for transfers between devices, rep_sum(): sent_out = lax.ppermute(total, 'rep', [(1, 0), (2, 3)])  19.4 us
  transfers between devices with their start and end apart: 19, of which 11 were waited for; matrix products, arithmetic and copies ran while one was open for 27% of the time, Pallas kernels for 9%

profile of v10, /device:TPU:0, one launch (start us, length us, event | category | flops | bytes accessed | tf_op | source)
XLA Modules:
  0.0 621.0 jit_solution(9231494964156220254)
XLA Ops:
  22.7 26.6 %collective-permute-done = bf16[1,512,1024]{2,1,0:T(8,128)(2,1)S(1)} collective-permute-done((bf16[1,512,1024]{2,1,0:T(8,128)(2,1)S(1)}, bf16[1,512,1024]{2,1,0:T(8,128)(2,1)S(1)}, u32[]{:S(2)}, u32[]{:S(2)}) %collective-permute-start) | collective-permute-done | bytes 1048608 | tf_op jit(solution)/shard_map/ppermute | solution.py:397
  49.5 33.9 %all-gather.9.cloned.1.call-done = bf16[1088,3072]{1,0:T(8,128)(2,1)} async-done(((bf16[136,3072]{1,0:T(8,128)(2,1)}), bf16[1088,3072]{1,0:T(8,128)(2,1)}) %all-gather.9.cloned.1.call-update) | async-done | bytes 6684688 | tf_op jit(solution)/shard_map/all_gather | solution.py:315
  87.5 3.6 convolution_bitcast_fusion.2
  102.3 8.2 %convolution_bitcast_fusion.1 = f32[1,512,3072]{2,1,0:T(8,128)} fusion(bf16[1024,3072]{1,0:T(8,128)(2,1)} %bitcast.177, bf16[1,512,1024]{2,1,0:T(8,128)(2,1)S(1)} %collective-permute-done, f32[512]{0:T(512)S(1)} %add_rsqrt_fusion.1, f32[1024]{0:T(1024)S(1)} %bitcast.195), kind=kOutput, calls=%fused_computation.19 | convolution fusion | flops 3223322624 | bytes 13637632 | tf_op jit(solution)/shard_map/srd,de->sre/dot_general | solution.py:407
  112.5 5.2 fusion.93
  128.0 5.2 broadcast_select_fusion.1
  135.6 22.6 %shard_map.220 = (bf16[1,512,1024]{2,1,0:T(8,128)(2,1)}, f32[1,16,512]{2,1,0:T(8,128)}) custom-call(bf16[1,512,1024]{2,1,0:T(8,128)(2,1)} %copy.91.q_ref, bf16[1,1024,1024]{2,1,0:T(8,128)(2,1)} %pad_maximum_fusion.2.k_ref, bf16[1,1024,1024]{2,1,0:T(8,128)(2,1)} %pad_maximum_fusion.3.v_ref, s32[1,512]{1,0:T(1,128)} %iota_add_fusion.1.qpos_ref, ...), custom_call_target="tpu_custom_call" | custom-call | flops 2147483648 | bytes 6291456 | tf_op jit(solution)/shard_map/pallas_call | solution.py:247
  161.6 25.6 %all-gather.13.cloned.1.call-done = bf16[1024,5632]{1,0:T(8,128)(2,1)} async-done(((bf16[128,5632]{1,0:T(8,128)(2,1)}), bf16[1024,5632]{1,0:T(8,128)(2,1)}) %all-gather.13.cloned.1.call-update) | async-done | bytes 11534352 | tf_op jit(solution)/shard_map/all_gather | solution.py:315
  187.2 13.6 %convolution_bitcast_fusion = f32[1,512,5632]{2,1,0:T(8,128)} fusion(bf16[1024,5632]{1,0:T(8,128)(2,1)} %all-gather.13.cloned.1.call-done, f32[1,512,1024]{2,1,0:T(8,128)S(1)} %get-tuple-element.82, f32[1024]{0:T(1024)S(1)} %bitcast.198, f32[512]{0:T(512)S(1)} %add_rsqrt_fusion), kind=kOutput, calls=%fused_computation.4 | convolution fusion | flops 5907152896 | bytes 25171968 | tf_op jit(solution)/shard_map/srd,df->srf/dot_general | solution.py:444
  200.8 31.3 %all-gather.15.cloned.1.call-done = bf16[2816,1024]{1,0:T(8,128)(2,1)} async-done(((bf16[352,1024]{1,0:T(8,128)(2,1)}), bf16[2816,1024]{1,0:T(8,128)(2,1)}) %all-gather.15.cloned.1.call-update) | async-done | bytes 5767184 | tf_op jit(solution)/shard_map/all_gather | solution.py:315
  232.1 9.5 %fusion.5 = (bf16[1,512,2816]{2,1,0:T(8,128)(2,1)S(1)}, bf16[1,512,2816]{2,1,0:T(8,128)(2,1)S(1)}) fusion(f32[1,512,5632]{2,1,0:T(8,128)} %convolution_bitcast_fusion, bf16[2816,1024]{1,0:T(8,128)(2,1)} %all-gather.15.cloned.1.call-done, bf16[1,512,1024]{2,1,0:T(8,128)(2,1)S(1)} %copy-done.26, pred[512]{0:T(512)(128)(4,1)S(1)} %fusion.79), kind=kOutput, calls=%fused_computation.13 | convolution fusion | flops 2973106176 | bytes 24117760 | tf_op jit(solution)/shard_map/srd,fd->srf/dot_general | solution.py:466
  244.0 9.3 %convolution_convert_fusion = bf16[1024,5632]{1,0:T(8,128)(2,1)} fusion(bf16[1,512,2816]{2,1,0:T(8,128)(2,1)S(1)} %get-tuple-element.40, bf16[1,512,2816]{2,1,0:T(8,128)(2,1)S(1)} %get-tuple-element.39, f32[1,512,1024]{2,1,0:T(8,128)S(1)} %get-tuple-element.82, f32[1024]{0:T(1024)S(1)} %bitcast.199, f32[512]{0:T(512)S(1)} %add_rsqrt_fusion), kind=kOutput, calls=%fused_computation.3 | convolution fusion | flops 5924454400 | bytes 19404800 | tf_op jit(solution)/shard_map/srd,srf->df/dot_general | solution.py:470
  253.4 11.9 %fusion.33 = (bf16[1024]{0:T(1024)(128)(2,1)S(1)}, f32[512]{0:T(512)S(1)}, f32[512,1024]{1,0:T(8,128)S(1)}) fusion(f32[1,512,1024]{2,1,0:T(8,128)S(1)} %get-tuple-element.82, f32[512]{0:T(512)S(1)} %add_rsqrt_fusion, f32[1024]{0:T(1024)S(1)} %bitcast.200, bf16[1024,5632]{1,0:T(8,128)(2,1)} %all-gather.13.cloned.1.call-done, ...), kind=kOutput, calls=%fused_computation.60 | convolution fusion | flops 5920258560 | bytes 21506048 | tf_op jit(solution)/shard_map/srf,df->srd/dot_general | solution.py:473
  272.9 11.4 %pad_maximum_fusion = bf16[1024,6656]{1,0:T(8,128)(2,1)} fusion(bf16[1024,5632]{1,0:T(8,128)(2,1)} %convolution_convert_fusion, bf16[1024,1024]{1,0:T(8,128)(2,1)S(1)} %copy.108), kind=kLoop, calls=%fused_computation | loop fusion | flops 27262976 | bytes 27262976 | tf_op jit(solution)/shard_map/concatenate | solution.py:483
  284.4 5.2 fusion.18
  292.5 10.3 %convolution_convert_fusion.2 = bf16[8,352,1024]{2,1,0:T(8,128)(2,1)} fusion(bf16[8,352,512]{2,1,0:T(8,128)(2,1)} %bitcast.188, bf16[1,512,1024]{2,1,0:T(8,128)(2,1)} %param.15, pred[512]{0:T(512)(128)(4,1)S(1)} %fusion.79), kind=kOutput, calls=%fused_computation.24 | convolution fusion | flops 2957246464 | bytes 9699840 | tf_op jit(solution)/shard_map/srf,srd->fd/dot_general | solution.py:460
  310.1 3.9 convolution_convert_fusion.4
  321.8 16.5 %shard_map.221 = (f32[1,512,1024]{2,1,0:T(8,128)}, f32[1,512,1024]{2,1,0:T(8,128)}, f32[1,512,1024]{2,1,0:T(8,128)}) custom-call(bf16[1,512,1024]{2,1,0:T(8,128)(2,1)} %copy.91.q_ref, bf16[1,512,1024]{2,1,0:T(8,128)(2,1)} %copy-done, bf16[1,512,1024]{2,1,0:T(8,128)(2,1)} %copy-done.14, bf16[1,512,1024]{2,1,0:T(8,128)(2,1)} %bitcast.189, ...), custom_call_target="tpu_custom_call" | custom-call | flops 2684354560 | bytes 10485760 | tf_op jit(solution)/shard_map/pallas_call | solution.py:285
  338.3 29.1 %collective-permute-done.4 = f32[1,16,512]{2,1,0:T(8,128)S(1)} collective-permute-done((f32[1,16,512]{2,1,0:T(8,128)S(1)}, f32[1,16,512]{2,1,0:T(8,128)S(1)}, u32[]{:S(2)}, u32[]{:S(2)}) %collective-permute-start.4) | collective-permute-done | bytes 32800 | tf_op jit(solution)/shard_map/ppermute | solution.py:496
  371.4 16.5 %shard_map.222 = (f32[1,512,1024]{2,1,0:T(8,128)}, f32[1,512,1024]{2,1,0:T(8,128)}, f32[1,512,1024]{2,1,0:T(8,128)}) custom-call(bf16[1,512,1024]{2,1,0:T(8,128)(2,1)} %broadcast_select_fusion.3.q_ref, bf16[1,512,1024]{2,1,0:T(8,128)(2,1)} %broadcast_select_fusion.2.k_ref, bf16[1,512,1024]{2,1,0:T(8,128)(2,1)} %get-tuple-element.34.v_ref, ...), custom_call_target="tpu_custom_call" | custom-call | flops 2684354560 | bytes 10485760 | tf_op jit(solution)/shard_map/pallas_call | solution.py:285
  391.6 4.3 select_add_fusion
  404.6 3.6 fusion.90
  408.2 7.1 %fusion.27 = (bf16[1024]{0:T(1024)(128)(2,1)S(1)}, f32[512]{0:T(512)S(1)}, f32[512,1024]{1,0:T(8,128)S(1)}) fusion(bf16[1,512,1024]{2,1,0:T(8,128)(2,1)S(1)} %copy-done.12, f32[512]{0:T(512)S(1)} %add_rsqrt_fusion.2, f32[1024]{0:T(1024)S(1)} %bitcast.196, bf16[1024,3072]{1,0:T(8,128)(2,1)} %bitcast.178, bf16[1,512,1024]{2,1,0:T(8,128)(2,1)S(1)} %get-tuple-element.32, ...), kind=kOutput, calls=%fused_computation.49 | convolution fusion | flops 3234331136 | bytes 12593152 | tf_op jit(solution)/shard_map/sre,de->srd/dot_general | solution.py:538
  419.6 5.3 convolution_convert_fusion.1
  431.3 37.4 %reduce-scatter.8.cloned.1.call-done = bf16[1,352,1024]{2,1,0:T(8,128)(2,1)} async-done(((bf16[8,352,1024]{2,1,0:T(8,128)(2,1)}), bf16[1,352,1024]{2,1,0:T(8,128)(2,1)}) %reduce-scatter.8.cloned.1.call-update) | async-done | bytes 720912 | tf_op jit(solution)/shard_map/reduce_scatter | solution.py:338
  468.7 3.6 collective-permute-start.8
  476.0 11.8 %collective-permute-done.8 = bf16[1,352,1024]{2,1,0:T(8,128)(2,1)S(1)} collective-permute-done((bf16[1,352,1024]{2,1,0:T(8,128)(2,1)}, bf16[1,352,1024]{2,1,0:T(8,128)(2,1)S(1)}, u32[]{:S(2)}, u32[]{:S(2)}) %collective-permute-start.8) | collective-permute-done | bytes 720928 | tf_op jit(solution)/shard_map/ppermute | solution.py:328
  491.2 44.6 %reduce-scatter.4.cloned.1.call-done = bf16[1,136,3072]{2,1,0:T(8,128)(2,1)} async-done(((bf16[8,136,3072]{2,1,0:T(8,128)(2,1)}), bf16[1,136,3072]{2,1,0:T(8,128)(2,1)}) %reduce-scatter.4.cloned.1.call-update) | async-done | bytes 835600 | tf_op jit(solution)/shard_map/reduce_scatter | solution.py:338
  539.1 10.4 %fusion.38 = bf16[1,512,1024]{2,1,0:T(8,128)(2,1)} fusion(f32[1,512,1024]{2,1,0:T(8,128)S(1)} %copy-done.16, bf16[2816,1024]{1,0:T(8,128)(2,1)} %all-gather.15.cloned.1.call-done, f32[1,512,5632]{2,1,0:T(8,128)} %convolution_bitcast_fusion, pred[512]{0:T(512)(128)(4,1)S(1)} %fusion.79), kind=kOutput, calls=%fused_computation.68 | convolution fusion | flops 2963013632 | bytes 20447744 | tf_op jit(solution)/shard_map/srf,fd->srd/dot_general | solution.py:449
  549.5 7.9 %collective-permute-done.10 = bf16[1,352,1024]{2,1,0:T(8,128)(2,1)} collective-permute-done((bf16[1,352,1024]{2,1,0:T(8,128)(2,1)}, bf16[1,352,1024]{2,1,0:T(8,128)(2,1)}, u32[]{:S(2)}, u32[]{:S(2)}) %collective-permute-start.10) | collective-permute-done | bytes 720928 | tf_op jit(solution)/shard_map/ppermute | solution.py:332
  559.7 36.6 %all-reduce.6.cloned.1.call-done = bf16[136,3072]{1,0:T(8,128)(2,1)} async-done(((bf16[136,3072]{1,0:T(8,128)(2,1)}), bf16[136,3072]{1,0:T(8,128)(2,1)}) %all-reduce.6.cloned.1.call-update) | async-done | bytes 835600 | tf_op jit(solution)/shard_map/psum | solution.py:339
  599.4 11.5 %collective-permute-done.7 = bf16[1,128,6656]{2,1,0:T(8,128)(2,1)S(1)} collective-permute-done((bf16[1,128,6656]{2,1,0:T(8,128)(2,1)S(1)}, bf16[1,128,6656]{2,1,0:T(8,128)(2,1)S(1)}, u32[]{:S(2)}, u32[]{:S(2)}) %collective-permute-start.7) | collective-permute-done | bytes 1703968 | tf_op jit(solution)/shard_map/ppermute | solution.py:332
  (187 shorter events, 121.6 us)
Async XLA Ops:
  7.2 3.8 copy-start.29
  7.2 76.3 %all-gather.9.cloned.1.call-start = ((), (), s32[]{:S(2)}) async-start(), calls=%async_computation.7 | async-start | bytes 7520256 | tf_op jit(solution)/shard_map/all_gather | solution.py:315
  10.1 148.1 %all-gather.11.cloned.1.call-start = ((), (), s32[]{:S(2)}) async-start(), calls=%async_computation.8 | async-start | bytes 2359296 | tf_op jit(solution)/shard_map/all_gather | solution.py:315
  10.9 176.3 %all-gather.13.cloned.1.call-start = ((), (), s32[]{:S(2)}) async-start(), calls=%async_computation.9 | async-start | bytes 12976128 | tf_op jit(solution)/shard_map/all_gather | solution.py:315
  12.2 219.9 %all-gather.15.cloned.1.call-start = ((), (), s32[]{:S(2)}) async-start(), calls=%async_computation.10 | async-start | bytes 6488064 | tf_op jit(solution)/shard_map/all_gather | solution.py:315
  12.8 415.6 %reduce-scatter.6.cloned.1.call-start = ((), (), s32[]{:S(2)}) async-start(), calls=%async_computation.5 | async-start | bytes 15335424 | tf_op jit(solution)/shard_map/reduce_scatter | solution.py:338
  12.8 36.4 %collective-permute-start = (bf16[1,512,1024]{2,1,0:T(8,128)(2,1)S(1)}, bf16[1,512,1024]{2,1,0:T(8,128)(2,1)S(1)}, u32[]{:S(2)}, u32[]{:S(2)}) collective-permute-start(bf16[1,512,1024]{2,1,0:T(8,128)(2,1)S(1)} %copy-done.10), channel_id=1, source_target_pairs={{0,1},{1,0},{2,3},{3,2},{4,5},{5,4},{6,7},{7,6},{8,9},{9,8},{10,11... | collective-permute-start | bytes 3145736 | tf_op jit(solution)/shard_map/ppermute | solution.py:397
  15.9 112.1 %collective-permute-start.1 = (bf16[1,512,1024]{2,1,0:T(8,128)(2,1)}, bf16[1,512,1024]{2,1,0:T(8,128)(2,1)}, u32[]{:S(2)}, u32[]{:S(2)}) collective-permute-start(bf16[1,512,1024]{2,1,0:T(8,128)(2,1)} %param.14), channel_id=1, source_target_pairs={{0,1},{2,3},{4,5},{6,7},{8,9},{10,11},{12,13},{14,15},{16,17},{18,... | collective-permute-start | bytes 3145736 | tf_op jit(solution)/shard_map/ppermute | solution.py:398
  86.7 4.4 copy-start.8
  91.1 3.9 copy-start.9
  112.5 13.8 %copy-start = (bf16[1,512,1024]{2,1,0:T(8,128)(2,1)}, bf16[1,512,1024]{2,1,0:T(8,128)(2,1)S(1)}, u32[]{:S(2)}) copy-start(bf16[1,512,1024]{2,1,0:T(8,128)(2,1)S(1)} %copy.87.k_ref) | copy-start | bytes 3145732
  135.6 22.6 %copy-start.11 = (bf16[1,512,1024]{2,1,0:T(8,128)(2,1)S(1)}, bf16[1,512,1024]{2,1,0:T(8,128)(2,1)}, u32[]{:S(2)}) copy-start(bf16[1,512,1024]{2,1,0:T(8,128)(2,1)} %param.13) | copy-start | bytes 3145732
  161.6 103.7 %copy-start.15 = (f32[1,512,1024]{2,1,0:T(8,128)}, f32[1,512,1024]{2,1,0:T(8,128)S(1)}, u32[]{:S(2)}) copy-start(f32[1,512,1024]{2,1,0:T(8,128)S(1)} %get-tuple-element.82) | copy-start | bytes 6291460
  187.2 45.0 %copy-start.26 = (bf16[1,512,1024]{2,1,0:T(8,128)(2,1)S(1)}, bf16[1,512,1024]{2,1,0:T(8,128)(2,1)}, u32[]{:S(2)}) copy-start(bf16[1,512,1024]{2,1,0:T(8,128)(2,1)} %param.15) | copy-start | bytes 3145732
  284.3 184.4 %reduce-scatter.8.cloned.1.call-start = ((), (), s32[]{:S(2)}) async-start(), calls=%async_computation.6 | async-start | bytes 6488064 | tf_op jit(solution)/shard_map/reduce_scatter | solution.py:338
  302.8 233.0 %reduce-scatter.4.cloned.1.call-start = ((), (), s32[]{:S(2)}) async-start(), calls=%async_computation.3 | async-start | bytes 7520256 | tf_op jit(solution)/shard_map/reduce_scatter | solution.py:338
  304.9 4.1 copy-start.1
  304.9 4.1 copy-start.3
  307.6 11.9 %collective-permute-start.3 = (f32[1,16,512]{2,1,0:T(8,128)S(1)}, f32[1,16,512]{2,1,0:T(8,128)S(1)}, u32[]{:S(2)}, u32[]{:S(2)}) collective-permute-start(f32[1,16,512]{2,1,0:T(8,128)S(1)} %copy-done.32), channel_id=1, source_target_pairs={{1,0},{3,2},{5,4},{7,6},{9,8},{11,10},{13,12},{15,14},{17,16},{19,... | collective-permute-start | bytes 98312 | tf_op jit(solution)/shard_map/ppermute | solution.py:496
  315.6 53.2 %collective-permute-start.2 = (bf16[1,512,16,64]{1,3,2,0:T(8,128)(2,1)S(1)}, bf16[1,512,16,64]{1,3,2,0:T(8,128)(2,1)}, u32[]{:S(2)}, u32[]{:S(2)}) collective-permute-start(bf16[1,512,16,64]{1,3,2,0:T(8,128)(2,1)S(1)} %bitcast.167), channel_id=1, source_target_pairs={{1,0},{3,2},{5,4},{7,6},{9,8},{11,10},{13,12},{15,14},{17,16},{19,... | collective-permute-start | bytes 3145736 | tf_op jit(solution)/shard_map/ppermute | solution.py:496
  320.5 46.9 %collective-permute-start.4 = (f32[1,16,512]{2,1,0:T(8,128)S(1)}, f32[1,16,512]{2,1,0:T(8,128)S(1)}, u32[]{:S(2)}, u32[]{:S(2)}) collective-permute-start(f32[1,16,512]{2,1,0:T(8,128)S(1)} %bitcast.192), channel_id=1, source_target_pairs={{1,0},{3,2},{5,4},{7,6},{9,8},{11,10},{13,12},{15,14},{17,16},{19,... | collective-permute-start | bytes 98312 | tf_op jit(solution)/shard_map/ppermute | solution.py:496
  371.4 16.5 %copy-start.17 = (f32[1,512,1024]{2,1,0:T(8,128)S(1)}, f32[1,512,1024]{2,1,0:T(8,128)}, u32[]{:S(2)}) copy-start(f32[1,512,1024]{2,1,0:T(8,128)} %get-tuple-element.22) | copy-start | bytes 6291460
  408.2 7.1 %copy-start.27 = (bf16[1,512,1024]{2,1,0:T(8,128)(2,1)}, bf16[1,512,1024]{2,1,0:T(8,128)(2,1)S(1)}, u32[]{:S(2)}) copy-start(bf16[1,512,1024]{2,1,0:T(8,128)(2,1)S(1)} %get-tuple-element.32) | copy-start | bytes 3145732
  408.2 7.2 %copy-start.6 = (f32[1,512,1024]{2,1,0:T(8,128)S(1)}, f32[1,512,1024]{2,1,0:T(8,128)}, u32[]{:S(2)}) copy-start(f32[1,512,1024]{2,1,0:T(8,128)} %copy-done.4) | copy-start | bytes 6291460
  428.3 168.0 %all-reduce.6.cloned.1.call-start = ((), (), s32[]{:S(2)}) async-start(), calls=%async_computation.4 | async-start | bytes 1671168 | tf_op jit(solution)/shard_map/psum | solution.py:339
  428.4 43.9 %collective-permute-start.5 = (bf16[1,128,6656]{2,1,0:T(8,128)(2,1)}, bf16[1,128,6656]{2,1,0:T(8,128)(2,1)S(1)}, u32[]{:S(2)}, u32[]{:S(2)}) collective-permute-start(bf16[1,128,6656]{2,1,0:T(8,128)(2,1)} %reduce-scatter.6.cloned.1.call-done), channel_id=1, source_target_pairs={{0,8},{24,16},{1,9},{25,17},{2,10},{26,18},{3,11},{27,19},{4,12},{... | collective-permute-start | bytes 5111816 | tf_op jit(solution)/shard_map/ppermute | solution.py:328
  468.7 19.0 %copy-start.28 = (bf16[1,352,1024]{2,1,0:T(8,128)(2,1)S(1)}, bf16[1,352,1024]{2,1,0:T(8,128)(2,1)}, u32[]{:S(2)}) copy-start(bf16[1,352,1024]{2,1,0:T(8,128)(2,1)} %reduce-scatter.8.cloned.1.call-done) | copy-start | bytes 2162692
  468.7 19.0 %collective-permute-start.8 = (bf16[1,352,1024]{2,1,0:T(8,128)(2,1)}, bf16[1,352,1024]{2,1,0:T(8,128)(2,1)S(1)}, u32[]{:S(2)}, u32[]{:S(2)}) collective-permute-start(bf16[1,352,1024]{2,1,0:T(8,128)(2,1)} %reduce-scatter.8.cloned.1.call-done), channel_id=1, source_target_pairs={{0,8},{24,16},{1,9},{25,17},{2,10},{26,18},{3,11},{27,19},{4,12},{... | collective-permute-start | bytes 2162696 | tf_op jit(solution)/shard_map/ppermute | solution.py:328
  474.1 61.7 %collective-permute-start.6 = (bf16[1,128,6656]{2,1,0:T(8,128)(2,1)S(1)}, bf16[1,128,6656]{2,1,0:T(8,128)(2,1)}, u32[]{:S(2)}, u32[]{:S(2)}) collective-permute-start(bf16[1,128,6656]{2,1,0:T(8,128)(2,1)S(1)} %add_convert_fusion.1), channel_id=1, source_target_pairs={{8,16},{16,8},{9,17},{17,9},{10,18},{18,10},{11,19},{19,11},{12,20... | collective-permute-start | bytes 5111816 | tf_op jit(solution)/shard_map/ppermute | solution.py:330
  488.0 0.7 collective-permute-start.9
  489.9 67.5 %collective-permute-start.10 = (bf16[1,352,1024]{2,1,0:T(8,128)(2,1)}, bf16[1,352,1024]{2,1,0:T(8,128)(2,1)}, u32[]{:S(2)}, u32[]{:S(2)}) collective-permute-start(bf16[1,352,1024]{2,1,0:T(8,128)(2,1)} %add_convert_fusion.3), channel_id=1, source_target_pairs={{8,0},{16,24},{9,1},{17,25},{10,2},{18,26},{11,3},{19,27},{12,4},{... | collective-permute-start | bytes 2162696 | tf_op jit(solution)/shard_map/ppermute | solution.py:332
  537.8 73.1 %collective-permute-start.7 = (bf16[1,128,6656]{2,1,0:T(8,128)(2,1)S(1)}, bf16[1,128,6656]{2,1,0:T(8,128)(2,1)S(1)}, u32[]{:S(2)}, u32[]{:S(2)}) collective-permute-start(bf16[1,128,6656]{2,1,0:T(8,128)(2,1)S(1)} %add_convert_fusion), channel_id=1, source_target_pairs={{8,0},{16,24},{9,1},{17,25},{10,2},{18,26},{11,3},{19,27},{12,4},{... | collective-permute-start | bytes 5111816 | tf_op jit(solution)/shard_map/ppermute | solution.py:332
  (22 other events, 51.3 us)
Sparse Core Ops, SparseCore 0:
  10.5 72.9 all-gather.8
  85.3 31.7 all-gather.10
  119.6 67.5 all-gather.12
  188.9 43.1 all-gather.14
  284.5 121.8 reduce-scatter.5
  409.6 59.0 reduce-scatter.7
  472.2 63.5 reduce-scatter.3
  538.2 58.1 all-reduce.5

commit v11 on v10

--- a/solution.py
+++ b/solution.py
@@ -479,17 +479,13 @@
     grad_out = jnp.einsum(
         "sre,srd->ed", att_flat, g_branch, preferred_element_type=jnp.float32
     )
-    ogu_block = (
-        jnp.concatenate([grad_out, grad_gu], axis=1)
-        .reshape(n_group, own_rows, model_width + 2 * ff_width)
-        .astype(jnp.bfloat16)
-    )
+    gu_block = grad_gu.reshape(n_group, own_rows, 2 * ff_width).astype(jnp.bfloat16)
     g_attended = (
         jnp.einsum("srd,ed->sre", g_branch, full_out, preferred_element_type=jnp.float32)
         .astype(jnp.bfloat16)
         .reshape(head_shape)
     )
-    (part_ogu,) = scatter_blocks([ogu_block], True)
+    (part_gu,) = scatter_blocks([gu_block], True)
     row_dots = jnp.sum(g_attended.astype(jnp.float32) * attended.astype(jnp.float32), axis=-1)
     if paired:
         dot_rows = jnp.transpose(row_dots, (0, 2, 1))
@@ -538,13 +534,20 @@
     g_normed = jnp.einsum("sre,de->srd", g_qkv, full_qkv, preferred_element_type=jnp.float32)
     g_attn_in, grad_gain_attn = normalize_back(inputs, inv_attn, attn_scale, g_normed)
     d_tokens = g_residual + g_attn_in
-    part_qkv, part_gains = scatter_blocks(
+    part_qkvo, part_gains = scatter_blocks(
         [
-            grad_qkv.reshape(n_group, own_rows, qkv_width),
-            gain_block(grad_gain_attn.reshape(n_group, own_rows), grad_gain_mlp.reshape(n_group, own_rows), qkv_width),
+            jnp.concatenate([grad_qkv, grad_out], axis=1).reshape(
+                n_group, own_rows, qkv_width + model_width
+            ),
+            gain_block(
+                grad_gain_attn.reshape(n_group, own_rows),
+                grad_gain_mlp.reshape(n_group, own_rows),
+                qkv_width + model_width,
+            ),
         ],
         False,
     )
+    part_qkv = part_qkvo[:, :qkv_width]
     return (
         output,
         d_tokens,
@@ -552,9 +555,9 @@
         part_qkv[:, :attn_width],
         part_qkv[:, attn_width : 2 * attn_width],
         part_qkv[:, 2 * attn_width :],
-        part_ogu[:, :model_width],
-        part_ogu[:, model_width : model_width + ff_width],
-        part_ogu[:, model_width + ff_width :],
+        part_qkvo[:, qkv_width:],
+        part_gu[:, :ff_width],
+        part_gu[:, ff_width:],
         part_down,
         part_gains[0, :own_rows],
         part_gains[0, own_rows : 2 * own_rows],

time: 627 us -> 610 us (0.973)
  waiting for transfers between devices: 298 us -> 282 us
  local copies, waits for them, and re-layouts: 56.6 us -> 47.2 us
    reduce_scatter x3, waiting for transfers between devices: 82.1 us -> 53.4 us  [scatter_blocks(): summed = lax.psum_scatter(packed, GROUP, scatter_dimension=0, tiled=True)]
    ppermute x2, waiting for transfers between devices: 11.8 us -> 26.5 us  [rep_sum(): arrived = lax.ppermute(x, 'rep', [(0, 1), (3, 2)])]
    ppermute x2, waiting for transfers between devices: 19.4 us -> 8.48 us  [rep_sum(): sent_out = lax.ppermute(total, 'rep', [(1, 0), (2, 3)])]
    psum x1, waiting for transfers between devices: 36.6 us -> 47.1 us  [scatter_blocks(): lax.psum(summed, 'rep')]
  transfers between devices with their start and end apart: 19 -> 19, of which waited for: 11 -> 12; matrix products, arithmetic and copies ran while one was open for 27% -> 30% of each run, Pallas kernels for 9% -> 9%
where the time goes in v11:
time: 610 us; the launch traced here: 604 us
  waiting for transfers between devices  282 us (46%)
  matrix products  104 us (17%)
  other arithmetic  75.9 us (12%)
  Pallas kernels  55.6 us (9%)
  local copies, waits for them, and re-layouts  47.2 us (8%)
  starting transfers between devices  23 us (4%)
  between operations  15.7 us (3%)
    all_gather x4, waiting for transfers between devices, gather_blocks(): gathered = lax.all_gather(packed, GROUP, axis=0, tiled=False)  90.7 us
    reduce_scatter x3, waiting for transfers between devices, scatter_blocks(): summed = lax.psum_scatter(packed, GROUP, scatter_dimension=0, tiled=True)  53.4 us
    psum x1, waiting for transfers between devices, scatter_blocks(): lax.psum(summed, 'rep')  47.1 us
    pallas_call x2, Pallas kernels, block_backward(): pl.pallas_call(kernel, grid=(n_slots, n_heads // 2), in_specs=[q_spec, k_...  33 us
    ppermute x3, waiting for transfers between devices, shards(): lax.ppermute((g_attended, dot_rows, lse_rows), 'ctx', [(1, 0)])  27.6 us
    ppermute x1, waiting for transfers between devices, shards(): other_tokens = lax.ppermute(tokens, 'ctx', [(0, 1), (1, 0)])  26.7 us
    ppermute x2, waiting for transfers between devices, rep_sum(): arrived = lax.ppermute(x, 'rep', [(0, 1), (3, 2)])  26.5 us
    pallas_call x1, Pallas kernels, block_forward(): pl.pallas_call(kernel, grid=(n_slots, n_heads // 2), in_specs=[q_spec, k_...  22.6 us
  transfers between devices with their start and end apart: 19, of which 12 were waited for; matrix products, arithmetic and copies ran while one was open for 30% of the time, Pallas kernels for 9%

profile of v11, /device:TPU:0, one launch (start us, length us, event | category | flops | bytes accessed | tf_op | source)
XLA Modules:
  0.0 603.7 jit_solution(15407613356793030930)
XLA Ops:
  22.7 26.7 %collective-permute-done = bf16[1,512,1024]{2,1,0:T(8,128)(2,1)S(1)} collective-permute-done((bf16[1,512,1024]{2,1,0:T(8,128)(2,1)S(1)}, bf16[1,512,1024]{2,1,0:T(8,128)(2,1)S(1)}, u32[]{:S(2)}, u32[]{:S(2)}) %collective-permute-start) | collective-permute-done | bytes 1048608 | tf_op jit(solution)/shard_map/ppermute | solution.py:397
  49.6 33.7 %all-gather.9.cloned.1.call-done = bf16[1088,3072]{1,0:T(8,128)(2,1)} async-done(((bf16[136,3072]{1,0:T(8,128)(2,1)}), bf16[1088,3072]{1,0:T(8,128)(2,1)}) %all-gather.9.cloned.1.call-update) | async-done | bytes 6684688 | tf_op jit(solution)/shard_map/all_gather | solution.py:315
  87.4 3.6 convolution_bitcast_fusion.2
  102.2 8.2 %convolution_bitcast_fusion.1 = f32[1,512,3072]{2,1,0:T(8,128)} fusion(bf16[1024,3072]{1,0:T(8,128)(2,1)} %bitcast.177, bf16[1,512,1024]{2,1,0:T(8,128)(2,1)S(1)} %collective-permute-done, f32[512]{0:T(512)S(1)} %add_rsqrt_fusion.1, f32[1024]{0:T(1024)S(1)} %bitcast.198), kind=kOutput, calls=%fused_computation.22 | convolution fusion | flops 3223322624 | bytes 13637632 | tf_op jit(solution)/shard_map/srd,de->sre/dot_general | solution.py:407
  112.4 5.2 fusion.92
  127.8 5.2 broadcast_select_fusion.1
  135.5 22.6 %shard_map.220 = (bf16[1,512,1024]{2,1,0:T(8,128)(2,1)}, f32[1,16,512]{2,1,0:T(8,128)}) custom-call(bf16[1,512,1024]{2,1,0:T(8,128)(2,1)} %copy.91.q_ref, bf16[1,1024,1024]{2,1,0:T(8,128)(2,1)} %pad_maximum_fusion.4.k_ref, bf16[1,1024,1024]{2,1,0:T(8,128)(2,1)} %pad_maximum_fusion.5.v_ref, s32[1,512]{1,0:T(1,128)} %iota_add_fusion.1.qpos_ref, ...), custom_call_target="tpu_custom_call" | custom-call | flops 2147483648 | bytes 6291456 | tf_op jit(solution)/shard_map/pallas_call | solution.py:247
  161.5 25.6 %all-gather.13.cloned.1.call-done = bf16[1024,5632]{1,0:T(8,128)(2,1)} async-done(((bf16[128,5632]{1,0:T(8,128)(2,1)}), bf16[1024,5632]{1,0:T(8,128)(2,1)}) %all-gather.13.cloned.1.call-update) | async-done | bytes 11534352 | tf_op jit(solution)/shard_map/all_gather | solution.py:315
  187.1 13.5 %convolution_bitcast_fusion = f32[1,512,5632]{2,1,0:T(8,128)} fusion(bf16[1024,5632]{1,0:T(8,128)(2,1)} %all-gather.13.cloned.1.call-done, f32[1,512,1024]{2,1,0:T(8,128)S(1)} %get-tuple-element.83, f32[1024]{0:T(1024)S(1)} %bitcast.194, f32[512]{0:T(512)S(1)} %add_rsqrt_fusion), kind=kOutput, calls=%fused_computation.3 | convolution fusion | flops 5907152896 | bytes 25171968 | tf_op jit(solution)/shard_map/srd,df->srf/dot_general | solution.py:444
  200.6 31.4 %all-gather.15.cloned.1.call-done = bf16[2816,1024]{1,0:T(8,128)(2,1)} async-done(((bf16[352,1024]{1,0:T(8,128)(2,1)}), bf16[2816,1024]{1,0:T(8,128)(2,1)}) %all-gather.15.cloned.1.call-update) | async-done | bytes 5767184 | tf_op jit(solution)/shard_map/all_gather | solution.py:315
  232.0 11.0 %fusion.8 = (bf16[1,512,2816]{2,1,0:T(8,128)(2,1)}, bf16[1,512,2816]{2,1,0:T(8,128)(2,1)}) fusion(f32[1,512,5632]{2,1,0:T(8,128)} %convolution_bitcast_fusion, bf16[2816,1024]{1,0:T(8,128)(2,1)} %all-gather.15.cloned.1.call-done, bf16[1,512,1024]{2,1,0:T(8,128)(2,1)S(1)} %copy-done.23, pred[512]{0:T(512)(128)(4,1)S(1)} %fusion.79), kind=kOutput, calls=%fused_computation.16 | convolution fusion | flops 2973106176 | bytes 24117760 | tf_op jit(solution)/shard_map/srd,fd->srf/dot_general | solution.py:466
  243.0 11.8 %fusion.32 = (bf16[1024]{0:T(1024)(128)(2,1)S(1)}, f32[512]{0:T(512)S(1)}, f32[512,1024]{1,0:T(8,128)S(1)}) fusion(f32[1,512,1024]{2,1,0:T(8,128)S(1)} %get-tuple-element.83, f32[512]{0:T(512)S(1)} %add_rsqrt_fusion, f32[1024]{0:T(1024)S(1)} %bitcast.195, bf16[1024,5632]{1,0:T(8,128)(2,1)} %all-gather.13.cloned.1.call-done, ...), kind=kOutput, calls=%fused_computation.59 | convolution fusion | flops 5920258560 | bytes 21506048 | tf_op jit(solution)/shard_map/srf,df->srd/dot_general | solution.py:473
  257.6 11.5 %convolution_convert_fusion = bf16[8,128,5632]{2,1,0:T(8,128)(2,1)} fusion(bf16[8,128,512]{2,1,0:T(8,128)(2,1)S(1)} %bitcast.191, bf16[1,512,2816]{2,1,0:T(8,128)(2,1)} %get-tuple-element.40, bf16[1,512,2816]{2,1,0:T(8,128)(2,1)} %get-tuple-element.39), kind=kOutput, calls=%fused_computation.2 | convolution fusion | flops 5922881536 | bytes 18350080 | tf_op jit(solution)/shard_map/srd,srf->df/dot_general | solution.py:470
  269.2 5.6 fusion.17
  277.6 9.6 %convolution_convert_fusion.2 = bf16[8,352,1024]{2,1,0:T(8,128)(2,1)} fusion(bf16[8,352,512]{2,1,0:T(8,128)(2,1)} %bitcast.188, bf16[1,512,1024]{2,1,0:T(8,128)(2,1)} %param.15, pred[512]{0:T(512)(128)(4,1)S(1)} %fusion.79), kind=kOutput, calls=%fused_computation.24 | convolution fusion | flops 2957246464 | bytes 9699840 | tf_op jit(solution)/shard_map/srf,srd->fd/dot_general | solution.py:460
  298.6 4.5 convolution_convert_fusion.4
  310.5 16.5 %shard_map.221 = (f32[1,512,1024]{2,1,0:T(8,128)}, f32[1,512,1024]{2,1,0:T(8,128)}, f32[1,512,1024]{2,1,0:T(8,128)}) custom-call(bf16[1,512,1024]{2,1,0:T(8,128)(2,1)} %copy.91.q_ref, bf16[1,512,1024]{2,1,0:T(8,128)(2,1)} %copy-done, bf16[1,512,1024]{2,1,0:T(8,128)(2,1)} %copy-done.10, bf16[1,512,1024]{2,1,0:T(8,128)(2,1)} %bitcast.190, ...), custom_call_target="tpu_custom_call" | custom-call | flops 2684354560 | bytes 10485760 | tf_op jit(solution)/shard_map/pallas_call | solution.py:285
  326.9 26.4 %collective-permute-done.4 = f32[1,16,512]{2,1,0:T(8,128)S(1)} collective-permute-done((f32[1,16,512]{2,1,0:T(8,128)S(1)}, f32[1,16,512]{2,1,0:T(8,128)S(1)}, u32[]{:S(2)}, u32[]{:S(2)}) %collective-permute-start.4) | collective-permute-done | bytes 32800 | tf_op jit(solution)/shard_map/ppermute | solution.py:492
  356.6 16.5 %shard_map.222 = (f32[1,512,1024]{2,1,0:T(8,128)}, f32[1,512,1024]{2,1,0:T(8,128)}, f32[1,512,1024]{2,1,0:T(8,128)}) custom-call(bf16[1,512,1024]{2,1,0:T(8,128)(2,1)} %broadcast_select_fusion.3.q_ref, bf16[1,512,1024]{2,1,0:T(8,128)(2,1)} %broadcast_select_fusion.2.k_ref, bf16[1,512,1024]{2,1,0:T(8,128)(2,1)} %get-tuple-element.34.v_ref, ...), custom_call_target="tpu_custom_call" | custom-call | flops 2684354560 | bytes 10485760 | tf_op jit(solution)/shard_map/pallas_call | solution.py:285
  376.8 4.2 select_add_fusion
  389.9 3.9 fusion.89
  393.8 8.2 %fusion.26 = (bf16[1024]{0:T(1024)(128)(2,1)S(1)}, f32[512]{0:T(512)S(1)}, f32[512,1024]{1,0:T(8,128)}) fusion(bf16[1,512,1024]{2,1,0:T(8,128)(2,1)S(1)} %copy-done.13, f32[512]{0:T(512)S(1)} %add_rsqrt_fusion.2, f32[1024]{0:T(1024)S(1)} %bitcast.199, bf16[1024,3072]{1,0:T(8,128)(2,1)} %bitcast.178, bf16[1,512,1024]{2,1,0:T(8,128)(2,1)S(1)} %get-tuple-element.32, ...), kind=kOutput, calls=%fused_computation.48 | convolution fusion | flops 3234331136 | bytes 12593152 | tf_op jit(solution)/shard_map/sre,de->srd/dot_general | solution.py:534
  402.1 6.2 %convolution_convert_fusion.1 = bf16[1024,3072]{1,0:T(8,128)(2,1)} fusion(bf16[1,512,1024]{2,1,0:T(8,128)(2,1)S(1)} %get-tuple-element.32, bf16[1,512,1024]{2,1,0:T(8,128)(2,1)S(1)} %copy-done.27, bf16[1,512,1024]{2,1,0:T(8,128)(2,1)S(1)} %copy-done.28, bf16[1,512,1024]{2,1,0:T(8,128)(2,1)S(1)} %copy-done.13, f32[1024]{0:T(1024)S(1)} %bitcast.200, ...), kind=kOutput, calls=%fused_computation.21 | convolution fusion | flops 3235905536 | bytes 10491904 | tf_op jit(solution)/shard_map/srd,sre->de/dot_general | solution.py:533
  408.3 6.8 %pad_maximum_fusion = bf16[1024,4096]{1,0:T(8,128)(2,1)} fusion(bf16[1024,1024]{1,0:T(8,128)(2,1)S(1)} %copy-done.22, bf16[1024,3072]{1,0:T(8,128)(2,1)} %convolution_convert_fusion.1), kind=kLoop, calls=%fused_computation.5 | loop fusion | flops 16777216 | bytes 16777216 | tf_op jit(solution)/shard_map/concatenate | solution.py:539
  415.1 8.4 %fusion.1 = bf16[8,136,4096]{2,1,0:T(8,128)(2,1)} fusion(bf16[8,1,4096]{2,1,0:T(2,128)(2,1)S(1)} %copy.112, bf16[8,128,4096]{2,1,0:T(8,128)(2,1)} %bitcast.166), kind=kLoop, calls=%fused_computation.4 | loop fusion | flops 26738688 | bytes 17367040 | tf_op jit(solution)/shard_map/concatenate | solution.py:337
  427.1 12.7 %reduce-scatter.8.cloned.1.call-done = bf16[1,352,1024]{2,1,0:T(8,128)(2,1)} async-done(((bf16[8,352,1024]{2,1,0:T(8,128)(2,1)}), bf16[1,352,1024]{2,1,0:T(8,128)(2,1)}) %reduce-scatter.8.cloned.1.call-update) | async-done | bytes 720912 | tf_op jit(solution)/shard_map/reduce_scatter | solution.py:338
  443.4 15.9 %collective-permute-done.5 = bf16[1,128,5632]{2,1,0:T(8,128)(2,1)S(1)} collective-permute-done((bf16[1,128,5632]{2,1,0:T(8,128)(2,1)}, bf16[1,128,5632]{2,1,0:T(8,128)(2,1)S(1)}, u32[]{:S(2)}, u32[]{:S(2)}) %collective-permute-start.5) | collective-permute-done | bytes 1441824 | tf_op jit(solution)/shard_map/ppermute | solution.py:328
  462.9 10.6 %collective-permute-done.8 = bf16[1,352,1024]{2,1,0:T(8,128)(2,1)S(1)} collective-permute-done((bf16[1,352,1024]{2,1,0:T(8,128)(2,1)}, bf16[1,352,1024]{2,1,0:T(8,128)(2,1)S(1)}, u32[]{:S(2)}, u32[]{:S(2)}) %collective-permute-start.8) | collective-permute-done | bytes 720928 | tf_op jit(solution)/shard_map/ppermute | solution.py:328
  476.9 40.7 %reduce-scatter.4.cloned.1.call-done = bf16[1,136,4096]{2,1,0:T(8,128)(2,1)} async-done(((bf16[8,136,4096]{2,1,0:T(8,128)(2,1)}), bf16[1,136,4096]{2,1,0:T(8,128)(2,1)}) %reduce-scatter.4.cloned.1.call-update) | async-done | bytes 1114128 | tf_op jit(solution)/shard_map/reduce_scatter | solution.py:338
  521.0 10.4 %fusion.37 = bf16[1,512,1024]{2,1,0:T(8,128)(2,1)} fusion(f32[1,512,1024]{2,1,0:T(8,128)S(1)} %copy-done.16, bf16[2816,1024]{1,0:T(8,128)(2,1)} %all-gather.15.cloned.1.call-done, f32[1,512,5632]{2,1,0:T(8,128)} %convolution_bitcast_fusion, pred[512]{0:T(512)(128)(4,1)S(1)} %fusion.79), kind=kOutput, calls=%fused_computation.67 | convolution fusion | flops 2963013632 | bytes 20447744 | tf_op jit(solution)/shard_map/srf,fd->srd/dot_general | solution.py:449
  533.3 8.5 %collective-permute-done.10 = bf16[1,352,1024]{2,1,0:T(8,128)(2,1)} collective-permute-done((bf16[1,352,1024]{2,1,0:T(8,128)(2,1)}, bf16[1,352,1024]{2,1,0:T(8,128)(2,1)}, u32[]{:S(2)}, u32[]{:S(2)}) %collective-permute-start.10) | collective-permute-done | bytes 720928 | tf_op jit(solution)/shard_map/ppermute | solution.py:332
  544.1 47.1 %all-reduce.6.cloned.1.call-done = bf16[136,4096]{1,0:T(8,128)(2,1)} async-done(((bf16[136,4096]{1,0:T(8,128)(2,1)}), bf16[136,4096]{1,0:T(8,128)(2,1)}) %all-reduce.6.cloned.1.call-update) | async-done | bytes 1114128 | tf_op jit(solution)/shard_map/psum | solution.py:339
  (185 shorter events, 115.3 us)
Async XLA Ops:
  7.2 76.2 %all-gather.9.cloned.1.call-start = ((), (), s32[]{:S(2)}) async-start(), calls=%async_computation.7 | async-start | bytes 7520256 | tf_op jit(solution)/shard_map/all_gather | solution.py:315
  10.1 148.0 %all-gather.11.cloned.1.call-start = ((), (), s32[]{:S(2)}) async-start(), calls=%async_computation.8 | async-start | bytes 2359296 | tf_op jit(solution)/shard_map/all_gather | solution.py:315
  10.9 176.2 %all-gather.13.cloned.1.call-start = ((), (), s32[]{:S(2)}) async-start(), calls=%async_computation.9 | async-start | bytes 12976128 | tf_op jit(solution)/shard_map/all_gather | solution.py:315
  12.2 219.8 %all-gather.15.cloned.1.call-start = ((), (), s32[]{:S(2)}) async-start(), calls=%async_computation.10 | async-start | bytes 6488064 | tf_op jit(solution)/shard_map/all_gather | solution.py:315
  12.8 410.8 %reduce-scatter.6.cloned.1.call-start = ((), (), s32[]{:S(2)}) async-start(), calls=%async_computation.5 | async-start | bytes 12976128 | tf_op jit(solution)/shard_map/reduce_scatter | solution.py:338
  12.8 36.5 %collective-permute-start = (bf16[1,512,1024]{2,1,0:T(8,128)(2,1)S(1)}, bf16[1,512,1024]{2,1,0:T(8,128)(2,1)S(1)}, u32[]{:S(2)}, u32[]{:S(2)}) collective-permute-start(bf16[1,512,1024]{2,1,0:T(8,128)(2,1)S(1)} %copy-done.11), channel_id=1, source_target_pairs={{0,1},{1,0},{2,3},{3,2},{4,5},{5,4},{6,7},{7,6},{8,9},{9,8},{10,11... | collective-permute-start | bytes 3145736 | tf_op jit(solution)/shard_map/ppermute | solution.py:397
  15.9 112.0 %collective-permute-start.1 = (bf16[1,512,1024]{2,1,0:T(8,128)(2,1)}, bf16[1,512,1024]{2,1,0:T(8,128)(2,1)}, u32[]{:S(2)}, u32[]{:S(2)}) collective-permute-start(bf16[1,512,1024]{2,1,0:T(8,128)(2,1)} %param.14), channel_id=1, source_target_pairs={{0,1},{2,3},{4,5},{6,7},{8,9},{10,11},{12,13},{14,15},{16,17},{18,... | collective-permute-start | bytes 3145736 | tf_op jit(solution)/shard_map/ppermute | solution.py:398
  86.6 4.4 copy-start.7
  112.4 13.8 %copy-start = (bf16[1,512,1024]{2,1,0:T(8,128)(2,1)}, bf16[1,512,1024]{2,1,0:T(8,128)(2,1)S(1)}, u32[]{:S(2)}) copy-start(bf16[1,512,1024]{2,1,0:T(8,128)(2,1)S(1)} %copy.87.k_ref) | copy-start | bytes 3145732
  135.5 22.6 %copy-start.12 = (bf16[1,512,1024]{2,1,0:T(8,128)(2,1)S(1)}, bf16[1,512,1024]{2,1,0:T(8,128)(2,1)}, u32[]{:S(2)}) copy-start(bf16[1,512,1024]{2,1,0:T(8,128)(2,1)} %param.13) | copy-start | bytes 3145732
  161.4 93.4 %copy-start.15 = (f32[1,512,1024]{2,1,0:T(8,128)}, f32[1,512,1024]{2,1,0:T(8,128)S(1)}, u32[]{:S(2)}) copy-start(f32[1,512,1024]{2,1,0:T(8,128)S(1)} %get-tuple-element.83) | copy-start | bytes 6291460
  187.1 45.0 %copy-start.23 = (bf16[1,512,1024]{2,1,0:T(8,128)(2,1)S(1)}, bf16[1,512,1024]{2,1,0:T(8,128)(2,1)}, u32[]{:S(2)}) copy-start(bf16[1,512,1024]{2,1,0:T(8,128)(2,1)} %param.15) | copy-start | bytes 3145732
  243.0 11.9 %copy-start.24 = (bf16[1,512,1024]{2,1,0:T(8,128)(2,1)S(1)}, bf16[1,512,1024]{2,1,0:T(8,128)(2,1)}, u32[]{:S(2)}) copy-start(bf16[1,512,1024]{2,1,0:T(8,128)(2,1)} %param.15) | copy-start | bytes 3145732
  269.1 170.7 %reduce-scatter.8.cloned.1.call-start = ((), (), s32[]{:S(2)}) async-start(), calls=%async_computation.6 | async-start | bytes 6488064 | tf_op jit(solution)/shard_map/reduce_scatter | solution.py:338
  287.2 230.3 %reduce-scatter.4.cloned.1.call-start = ((), (), s32[]{:S(2)}) async-start(), calls=%async_computation.3 | async-start | bytes 10027008 | tf_op jit(solution)/shard_map/reduce_scatter | solution.py:338
  292.0 5.9 collective-permute-start.3
  304.6 49.4 %collective-permute-start.2 = (bf16[1,512,16,64]{1,3,2,0:T(8,128)(2,1)S(1)}, bf16[1,512,16,64]{1,3,2,0:T(8,128)(2,1)}, u32[]{:S(2)}, u32[]{:S(2)}) collective-permute-start(bf16[1,512,16,64]{1,3,2,0:T(8,128)(2,1)S(1)} %bitcast.167), channel_id=1, source_target_pairs={{1,0},{3,2},{5,4},{7,6},{9,8},{11,10},{13,12},{15,14},{17,16},{19,... | collective-permute-start | bytes 3145736 | tf_op jit(solution)/shard_map/ppermute | solution.py:492
  306.5 46.8 %collective-permute-start.4 = (f32[1,16,512]{2,1,0:T(8,128)S(1)}, f32[1,16,512]{2,1,0:T(8,128)S(1)}, u32[]{:S(2)}, u32[]{:S(2)}) collective-permute-start(f32[1,16,512]{2,1,0:T(8,128)S(1)} %bitcast.192), channel_id=1, source_target_pairs={{1,0},{3,2},{5,4},{7,6},{9,8},{11,10},{13,12},{15,14},{17,16},{19,... | collective-permute-start | bytes 98312 | tf_op jit(solution)/shard_map/ppermute | solution.py:492
  310.4 42.9 %copy-start.33 = (f32[512,16]{0,1:T(8,128)S(1)}, f32[512,16]{0,1:T(8,128)}, u32[]{:S(2)}) copy-start(f32[512,16]{0,1:T(8,128)} %copy-done.32) | copy-start | bytes 98308
  356.6 16.5 %copy-start.17 = (f32[1,512,1024]{2,1,0:T(8,128)S(1)}, f32[1,512,1024]{2,1,0:T(8,128)}, u32[]{:S(2)}) copy-start(f32[1,512,1024]{2,1,0:T(8,128)} %get-tuple-element.22) | copy-start | bytes 6291460
  402.1 6.2 %copy-start.22 = (bf16[1024,1024]{1,0:T(8,128)(2,1)S(1)}, bf16[1024,1024]{1,0:T(8,128)(2,1)}, u32[]{:S(2)}) copy-start(bf16[1024,1024]{1,0:T(8,128)(2,1)} %convolution_convert_fusion.3) | copy-start | bytes 6291460
  423.5 167.7 %all-reduce.6.cloned.1.call-start = ((), (), s32[]{:S(2)}) async-start(), calls=%async_computation.4 | async-start | bytes 2228224 | tf_op jit(solution)/shard_map/psum | solution.py:339
  423.6 35.7 %collective-permute-start.5 = (bf16[1,128,5632]{2,1,0:T(8,128)(2,1)}, bf16[1,128,5632]{2,1,0:T(8,128)(2,1)S(1)}, u32[]{:S(2)}, u32[]{:S(2)}) collective-permute-start(bf16[1,128,5632]{2,1,0:T(8,128)(2,1)} %reduce-scatter.6.cloned.1.call-done), channel_id=1, source_target_pairs={{0,8},{24,16},{1,9},{25,17},{2,10},{26,18},{3,11},{27,19},{4,12},{... | collective-permute-start | bytes 4325384 | tf_op jit(solution)/shard_map/ppermute | solution.py:328
  439.8 33.6 %copy-start.29 = (bf16[1,352,1024]{2,1,0:T(8,128)(2,1)S(1)}, bf16[1,352,1024]{2,1,0:T(8,128)(2,1)}, u32[]{:S(2)}) copy-start(bf16[1,352,1024]{2,1,0:T(8,128)(2,1)} %reduce-scatter.8.cloned.1.call-done) | copy-start | bytes 2162692
  439.8 33.6 %collective-permute-start.8 = (bf16[1,352,1024]{2,1,0:T(8,128)(2,1)}, bf16[1,352,1024]{2,1,0:T(8,128)(2,1)S(1)}, u32[]{:S(2)}, u32[]{:S(2)}) collective-permute-start(bf16[1,352,1024]{2,1,0:T(8,128)(2,1)} %reduce-scatter.8.cloned.1.call-done), channel_id=1, source_target_pairs={{0,8},{24,16},{1,9},{25,17},{2,10},{26,18},{3,11},{27,19},{4,12},{... | collective-permute-start | bytes 2162696 | tf_op jit(solution)/shard_map/ppermute | solution.py:328
  461.1 56.5 %collective-permute-start.6 = (bf16[1,128,5632]{2,1,0:T(8,128)(2,1)S(1)}, bf16[1,128,5632]{2,1,0:T(8,128)(2,1)}, u32[]{:S(2)}, u32[]{:S(2)}) collective-permute-start(bf16[1,128,5632]{2,1,0:T(8,128)(2,1)S(1)} %add_convert_fusion.1), channel_id=1, source_target_pairs={{8,16},{16,8},{9,17},{17,9},{10,18},{18,10},{11,19},{19,11},{12,20... | collective-permute-start | bytes 4325384 | tf_op jit(solution)/shard_map/ppermute | solution.py:330
  473.7 0.7 collective-permute-start.9
  475.6 66.3 %collective-permute-start.10 = (bf16[1,352,1024]{2,1,0:T(8,128)(2,1)}, bf16[1,352,1024]{2,1,0:T(8,128)(2,1)}, u32[]{:S(2)}, u32[]{:S(2)}) collective-permute-start(bf16[1,352,1024]{2,1,0:T(8,128)(2,1)} %add_convert_fusion.3), channel_id=1, source_target_pairs={{8,0},{16,24},{9,1},{17,25},{10,2},{18,26},{11,3},{19,27},{12,4},{... | collective-permute-start | bytes 2162696 | tf_op jit(solution)/shard_map/ppermute | solution.py:332
  519.4 12.0 %copy-start.6 = (f32[1,512,1024]{2,1,0:T(8,128)S(1)}, f32[1,512,1024]{2,1,0:T(8,128)}, u32[]{:S(2)}) copy-start(f32[1,512,1024]{2,1,0:T(8,128)} %get-tuple-element.64) | copy-start | bytes 6291460
  519.4 12.0 %copy-start.14 = (bf16[1,512,1024]{2,1,0:T(8,128)(2,1)S(1)}, bf16[1,512,1024]{2,1,0:T(8,128)(2,1)}, u32[]{:S(2)}) copy-start(bf16[1,512,1024]{2,1,0:T(8,128)(2,1)} %param.13) | copy-start | bytes 3145732
  519.5 12.0 %copy-start.20 = (f32[512,1024]{1,0:T(8,128)S(1)}, f32[512,1024]{1,0:T(8,128)}, u32[]{:S(2)}) copy-start(f32[512,1024]{1,0:T(8,128)} %get-tuple-element.85) | copy-start | bytes 6291460
  519.5 75.2 %collective-permute-start.7 = (bf16[1,128,5632]{2,1,0:T(8,128)(2,1)S(1)}, bf16[1,128,5632]{2,1,0:T(8,128)(2,1)S(1)}, u32[]{:S(2)}, u32[]{:S(2)}) collective-permute-start(bf16[1,128,5632]{2,1,0:T(8,128)(2,1)S(1)} %add_convert_fusion), channel_id=1, source_target_pairs={{8,0},{16,24},{9,1},{17,25},{10,2},{18,26},{11,3},{19,27},{12,4},{... | collective-permute-start | bytes 4325384 | tf_op jit(solution)/shard_map/ppermute | solution.py:332
  (22 other events, 65.3 us)
Sparse Core Ops, SparseCore 0:
  10.5 72.8 all-gather.8
  85.3 31.7 all-gather.10
  119.5 67.5 all-gather.12
  188.8 43.1 all-gather.14
  269.3 108.2 reduce-scatter.5
  380.8 58.9 reduce-scatter.7
  443.4 74.0 reduce-scatter.3
  519.9 71.2 all-reduce.5

commit v12 on v10

--- a/solution.py
+++ b/solution.py
@@ -320,10 +320,7 @@
     return fulls
 
 
-def rep_sum(x):
-    n_rep = lax.axis_size("rep")
-    if n_rep != 4:
-        return lax.psum(x, "rep")
+def rep_chain(x):
     me = lax.axis_index("rep")
     arrived = lax.ppermute(x, "rep", [(0, 1), (3, 2)])
     folded = (x.astype(jnp.float32) + arrived.astype(jnp.float32)).astype(x.dtype)
@@ -333,10 +330,25 @@
     return jnp.where((me == 0) | (me == 3), sent_out, total)
 
 
-def scatter_blocks(blocks, by_permutes):
+def rep_sum(x, pieces=1):
+    if lax.axis_size("rep") != 4:
+        return lax.psum(x, "rep")
+    rows = x.shape[1]
+    if pieces == 1 or rows % (8 * pieces):
+        return rep_chain(x)
+    step = rows // pieces
+    parts = []
+    for i in range(pieces):
+        parts.append(rep_chain(x[:, i * step : (i + 1) * step]))
+    return jnp.concatenate(parts, axis=1)
+
+
+def scatter_blocks(blocks, by_permutes, pieces=1):
     packed = jnp.concatenate(blocks, axis=1).astype(jnp.bfloat16)
     summed = lax.psum_scatter(packed, GROUP, scatter_dimension=0, tiled=True)
-    summed = (rep_sum(summed) if by_permutes else lax.psum(summed, "rep"))[0].astype(jnp.float32)
+    summed = (rep_sum(summed, pieces) if by_permutes else lax.psum(summed, "rep"))[0].astype(
+        jnp.float32
+    )
     parts, offset = [], 0
     for block in blocks:
         parts.append(summed[offset : offset + block.shape[1], :])
@@ -479,7 +491,7 @@
     grad_out = jnp.einsum(
         "sre,srd->ed", att_flat, g_branch, preferred_element_type=jnp.float32
     )
-    ogu_block = (
+    gu_block = (
         jnp.concatenate([grad_out, grad_gu], axis=1)
         .reshape(n_group, own_rows, model_width + 2 * ff_width)
         .astype(jnp.bfloat16)
@@ -489,7 +501,7 @@
         .astype(jnp.bfloat16)
         .reshape(head_shape)
     )
-    (part_ogu,) = scatter_blocks([ogu_block], True)
+    (part_gu,) = scatter_blocks([gu_block], True, 2)
     row_dots = jnp.sum(g_attended.astype(jnp.float32) * attended.astype(jnp.float32), axis=-1)
     if paired:
         dot_rows = jnp.transpose(row_dots, (0, 2, 1))
@@ -552,9 +564,9 @@
         part_qkv[:, :attn_width],
         part_qkv[:, attn_width : 2 * attn_width],
         part_qkv[:, 2 * attn_width :],
-        part_ogu[:, :model_width],
-        part_ogu[:, model_width : model_width + ff_width],
-        part_ogu[:, model_width + ff_width :],
+        part_gu[:, :model_width],
+        part_gu[:, model_width : model_width + ff_width],
+        part_gu[:, model_width + ff_width :],
         part_down,
         part_gains[0, :own_rows],
         part_gains[0, own_rows : 2 * own_rows],

time: 627 us -> 579 us (0.923)
  waiting for transfers between devices: 298 us -> 246 us
  starting transfers between devices: 21.9 us -> 29.4 us
  other arithmetic: 74.3 us -> 67 us
    reduce_scatter x3, waiting for transfers between devices: 82.1 us -> 43.9 us  [scatter_blocks(): summed = lax.psum_scatter(packed, GROUP, scatter_dimension=0, tiled=True)]
    ppermute x3, waiting for transfers between devices: 29.1 us -> 5.28 us  [shards(): lax.ppermute((g_attended, dot_rows, lse_rows), 'ctx', [(1, 0)])]
    ppermute x6 -> x9, waiting for transfers between devices: 31.1 us -> 53 us  [the longest x3 38 us: rep_chain(): sent_out = lax.ppermute(total, 'rep', [(1, 0), (2, 3)])]
    all_gather x4, waiting for transfers between devices: 90.8 us -> 78.5 us  [gather_blocks(): gathered = lax.all_gather(packed, GROUP, axis=0, tiled=False)]
    ppermute x6 -> x9, starting transfers between devices: 11.6 us -> 19 us  [the longest x3 12.2 us: rep_chain(): arrived = lax.ppermute(x, 'rep', [(0, 1), (3, 2)])]
  transfers between devices with their start and end apart: 19 -> 22, of which waited for: 11 -> 10; matrix products, arithmetic and copies ran while one was open for 27% -> 37% of each run, Pallas kernels for 9% -> 10%
where the time goes in v12:
time: 579 us; the launch traced here: 573 us
  waiting for transfers between devices  246 us (42%)
  matrix products  96.6 us (17%)
  other arithmetic  67 us (12%)
  local copies, waits for them, and re-layouts  62.6 us (11%)
  Pallas kernels  55.5 us (10%)
  starting transfers between devices  29.4 us (5%)
  between operations  15.8 us (3%)
    all_gather x4, waiting for transfers between devices, gather_blocks(): gathered = lax.all_gather(packed, GROUP, axis=0, tiled=False)  78.5 us
    reduce_scatter x3, waiting for transfers between devices, scatter_blocks(): summed = lax.psum_scatter(packed, GROUP, scatter_dimension=0, tiled=True)  43.9 us
    psum x1, waiting for transfers between devices, scatter_blocks(): lax.psum(summed, 'rep')  38.4 us
    ppermute x3, waiting for transfers between devices, rep_chain(): sent_out = lax.ppermute(total, 'rep', [(1, 0), (2, 3)])  38 us
    pallas_call x2, Pallas kernels, block_backward(): pl.pallas_call(kernel, grid=(n_slots, n_heads // 2), in_specs=[q_spec, k_...  32.8 us
    ppermute x1, waiting for transfers between devices, shards(): other_tokens = lax.ppermute(tokens, 'ctx', [(0, 1), (1, 0)])  26.2 us
    pallas_call x1, Pallas kernels, block_forward(): pl.pallas_call(kernel, grid=(n_slots, n_heads // 2), in_specs=[q_spec, k_...  22.6 us
    ppermute x3, waiting for transfers between devices, rep_chain(): arrived = lax.ppermute(x, 'rep', [(0, 1), (3, 2)])  14.9 us
  transfers between devices with their start and end apart: 22, of which 10 were waited for; matrix products, arithmetic and copies ran while one was open for 37% of the time, Pallas kernels for 10%

profile of v12, /device:TPU:0, one launch (start us, length us, event | category | flops | bytes accessed | tf_op | source)
XLA Modules:
  0.0 572.8 jit_solution(17165513802331209790)
XLA Ops:
  22.3 26.2 %collective-permute-done = bf16[1,512,1024]{2,1,0:T(8,128)(2,1)S(1)} collective-permute-done((bf16[1,512,1024]{2,1,0:T(8,128)(2,1)S(1)}, bf16[1,512,1024]{2,1,0:T(8,128)(2,1)S(1)}, u32[]{:S(2)}, u32[]{:S(2)}) %collective-permute-start) | collective-permute-done | bytes 1048608 | tf_op jit(solution)/shard_map/ppermute | solution.py:409
  48.7 34.6 %all-gather.9.cloned.1.call-done = bf16[1088,3072]{1,0:T(8,128)(2,1)} async-done(((bf16[136,3072]{1,0:T(8,128)(2,1)}), bf16[1088,3072]{1,0:T(8,128)(2,1)}) %all-gather.9.cloned.1.call-update) | async-done | bytes 6684688 | tf_op jit(solution)/shard_map/all_gather | solution.py:315
  87.4 3.6 convolution_bitcast_fusion.2
  102.2 8.2 %convolution_bitcast_fusion.1 = f32[1,512,3072]{2,1,0:T(8,128)} fusion(bf16[1024,3072]{1,0:T(8,128)(2,1)} %bitcast.179, bf16[1,512,1024]{2,1,0:T(8,128)(2,1)S(1)} %collective-permute-done, f32[512]{0:T(512)S(1)} %add_rsqrt_fusion.1, f32[1024]{0:T(1024)S(1)} %bitcast.197), kind=kOutput, calls=%fused_computation.19 | convolution fusion | flops 3223322624 | bytes 13637632 | tf_op jit(solution)/shard_map/srd,de->sre/dot_general | solution.py:419
  112.4 5.2 fusion.94
  127.9 5.2 broadcast_select_fusion.1
  135.6 22.6 %shard_map.220 = (bf16[1,512,1024]{2,1,0:T(8,128)(2,1)}, f32[1,16,512]{2,1,0:T(8,128)}) custom-call(bf16[1,512,1024]{2,1,0:T(8,128)(2,1)} %copy.91.q_ref, bf16[1,1024,1024]{2,1,0:T(8,128)(2,1)} %pad_maximum_fusion.2.k_ref, bf16[1,1024,1024]{2,1,0:T(8,128)(2,1)} %pad_maximum_fusion.3.v_ref, s32[1,512]{1,0:T(1,128)} %iota_add_fusion.1.qpos_ref, ...), custom_call_target="tpu_custom_call" | custom-call | flops 2147483648 | bytes 6291456 | tf_op jit(solution)/shard_map/pallas_call | solution.py:247
  161.5 25.6 %all-gather.13.cloned.1.call-done = bf16[1024,5632]{1,0:T(8,128)(2,1)} async-done(((bf16[128,5632]{1,0:T(8,128)(2,1)}), bf16[1024,5632]{1,0:T(8,128)(2,1)}) %all-gather.13.cloned.1.call-update) | async-done | bytes 11534352 | tf_op jit(solution)/shard_map/all_gather | solution.py:315
  187.1 9.5 %convolution_bitcast_fusion = f32[1,512,5632]{2,1,0:T(8,128)S(1)} fusion(bf16[1024,5632]{1,0:T(8,128)(2,1)} %all-gather.13.cloned.1.call-done, f32[1,512,1024]{2,1,0:T(8,128)S(1)} %get-tuple-element.86, f32[1024]{0:T(1024)S(1)} %bitcast.200, f32[512]{0:T(512)S(1)} %add_rsqrt_fusion), kind=kOutput, calls=%fused_computation.4 | convolution fusion | flops 5907152896 | bytes 25171968 | tf_op jit(solution)/shard_map/srd,df->srf/dot_general | solution.py:456
  196.6 4.2 copy-done
  205.6 8.1 %convolution_convert_fusion.2 = bf16[8,352,1024]{2,1,0:T(8,128)(2,1)} fusion(bf16[8,352,512]{2,1,0:T(8,128)(2,1)} %bitcast.190, bf16[1,512,1024]{2,1,0:T(8,128)(2,1)} %param.15, pred[512]{0:T(512)(128)(4,1)S(1)} %fusion.80), kind=kOutput, calls=%fused_computation.22 | convolution fusion | flops 2957246464 | bytes 9699840 | tf_op jit(solution)/shard_map/srf,srd->fd/dot_general | solution.py:472
  213.8 18.3 %all-gather.15.cloned.1.call-done = bf16[2816,1024]{1,0:T(8,128)(2,1)} async-done(((bf16[352,1024]{1,0:T(8,128)(2,1)}), bf16[2816,1024]{1,0:T(8,128)(2,1)}) %all-gather.15.cloned.1.call-update) | async-done | bytes 5767184 | tf_op jit(solution)/shard_map/all_gather | solution.py:315
  232.1 11.0 %fusion.5 = (bf16[1,512,2816]{2,1,0:T(8,128)(2,1)}, bf16[1,512,2816]{2,1,0:T(8,128)(2,1)}) fusion(f32[1,512,5632]{2,1,0:T(8,128)} %copy-done, bf16[2816,1024]{1,0:T(8,128)(2,1)} %all-gather.15.cloned.1.call-done, bf16[1,512,1024]{2,1,0:T(8,128)(2,1)S(1)} %copy-done.29, pred[512]{0:T(512)(128)(4,1)S(1)} %fusion.80), kind=kOutput, calls=%fused_computation.13 | convolution fusion | flops 2973106176 | bytes 24117760 | tf_op jit(solution)/shard_map/srd,fd->srf/dot_general | solution.py:478
  243.1 13.5 %fusion.33 = (bf16[1024]{0:T(1024)(128)(2,1)S(1)}, f32[512]{0:T(512)S(1)}, f32[512,1024]{1,0:T(8,128)S(1)}) fusion(f32[1,512,1024]{2,1,0:T(8,128)S(1)} %copy-done.18, f32[512]{0:T(512)S(1)} %add_rsqrt_fusion, f32[1024]{0:T(1024)S(1)} %bitcast.201, bf16[1024,5632]{1,0:T(8,128)(2,1)} %all-gather.13.cloned.1.call-done, ...), kind=kOutput, calls=%fused_computation.58 | convolution fusion | flops 5920258560 | bytes 21506048 | tf_op jit(solution)/shard_map/srf,df->srd/dot_general | solution.py:485
  264.2 9.7 %convolution_convert_fusion = bf16[1024,5632]{1,0:T(8,128)(2,1)S(1)} fusion(bf16[1,512,2816]{2,1,0:T(8,128)(2,1)} %get-tuple-element.40, bf16[1,512,2816]{2,1,0:T(8,128)(2,1)} %get-tuple-element.39, f32[1,512,1024]{2,1,0:T(8,128)} %copy-done.17, f32[1024]{0:T(1024)S(1)} %bitcast.203, f32[512]{0:T(512)S(1)} %add_rsqrt_fusion), kind=kOutput, calls=%fused_computation.3 | convolution fusion | flops 5924454400 | bytes 19404800 | tf_op jit(solution)/shard_map/srd,srf->df/dot_general | solution.py:482
  273.9 6.4 %pad_maximum_fusion = bf16[1024,6656]{1,0:T(8,128)(2,1)} fusion(bf16[1024,5632]{1,0:T(8,128)(2,1)S(1)} %convolution_convert_fusion, bf16[1024,1024]{1,0:T(8,128)(2,1)S(1)} %copy.108), kind=kLoop, calls=%fused_computation | loop fusion | flops 27262976 | bytes 27262976 | tf_op jit(solution)/shard_map/concatenate | solution.py:495
  287.8 3.9 convolution_convert_fusion.4
  299.7 16.3 %shard_map.221 = (f32[1,512,1024]{2,1,0:T(8,128)}, f32[1,512,1024]{2,1,0:T(8,128)}, f32[1,512,1024]{2,1,0:T(8,128)}) custom-call(bf16[1,512,1024]{2,1,0:T(8,128)(2,1)} %copy.91.q_ref, bf16[1,512,1024]{2,1,0:T(8,128)(2,1)} %copy-done.1, bf16[1,512,1024]{2,1,0:T(8,128)(2,1)} %copy-done.16, bf16[1,512,1024]{2,1,0:T(8,128)(2,1)} %bitcast.191, ...), custom_call_target="tpu_custom_call" | custom-call | flops 2684354560 | bytes 10485760 | tf_op jit(solution)/shard_map/pallas_call | solution.py:285
  316.0 5.3 collective-permute-done.4
  325.3 16.5 %shard_map.222 = (f32[1,512,1024]{2,1,0:T(8,128)}, f32[1,512,1024]{2,1,0:T(8,128)}, f32[1,512,1024]{2,1,0:T(8,128)}) custom-call(bf16[1,512,1024]{2,1,0:T(8,128)(2,1)} %broadcast_select_fusion.3.q_ref, bf16[1,512,1024]{2,1,0:T(8,128)(2,1)} %broadcast_select_fusion.2.k_ref, bf16[1,512,1024]{2,1,0:T(8,128)(2,1)} %get-tuple-element.34.v_ref, ...), custom_call_target="tpu_custom_call" | custom-call | flops 2684354560 | bytes 10485760 | tf_op jit(solution)/shard_map/pallas_call | solution.py:285
  345.5 4.3 select_add_fusion
  358.7 3.7 fusion.91
  362.4 7.2 %fusion.27 = (bf16[1024]{0:T(1024)(128)(2,1)S(1)}, f32[512]{0:T(512)S(1)}, f32[512,1024]{1,0:T(8,128)S(1)}) fusion(bf16[1,512,1024]{2,1,0:T(8,128)(2,1)S(1)} %copy-done.14, f32[512]{0:T(512)S(1)} %add_rsqrt_fusion.2, f32[1024]{0:T(1024)S(1)} %bitcast.198, bf16[1024,3072]{1,0:T(8,128)(2,1)} %bitcast.180, bf16[1,512,1024]{2,1,0:T(8,128)(2,1)S(1)} %get-tuple-element.32, ...), kind=kOutput, calls=%fused_computation.47 | convolution fusion | flops 3234331136 | bytes 12593152 | tf_op jit(solution)/shard_map/sre,de->srd/dot_general | solution.py:550
  373.7 5.4 convolution_convert_fusion.1
  382.7 3.6 collective-permute-start.11
  386.3 14.9 %collective-permute-done.11 = bf16[1,352,1024]{2,1,0:T(8,128)(2,1)S(1)} collective-permute-done((bf16[1,352,1024]{2,1,0:T(8,128)(2,1)}, bf16[1,352,1024]{2,1,0:T(8,128)(2,1)S(1)}, u32[]{:S(2)}, u32[]{:S(2)}) %collective-permute-start.11) | collective-permute-done | bytes 720928 | tf_op jit(solution)/shard_map/ppermute | solution.py:325
  407.2 6.3 %collective-permute-start.5 = (bf16[1,64,6656]{2,1,0:T(8,128)(2,1)}, bf16[1,64,6656]{2,1,0:T(8,128)(2,1)S(1)}, u32[]{:S(2)}, u32[]{:S(2)}) collective-permute-start(bf16[1,64,6656]{2,1,0:T(8,128)(2,1)} %get-tuple-element.63), channel_id=1, source_target_pairs={{0,8},{24,16},{1,9},{25,17},{2,10},{26,18},{3,11},{27,19},{4,12},{... | collective-permute-start | bytes 2555912 | tf_op jit(solution)/shard_map/ppermute | solution.py:325
  419.3 43.9 %reduce-scatter.4.cloned.1.call-done = bf16[1,136,3072]{2,1,0:T(8,128)(2,1)} async-done(((bf16[8,136,3072]{2,1,0:T(8,128)(2,1)}), bf16[1,136,3072]{2,1,0:T(8,128)(2,1)}) %reduce-scatter.4.cloned.1.call-update) | async-done | bytes 835600 | tf_op jit(solution)/shard_map/reduce_scatter | solution.py:348
  466.6 10.4 %fusion.38 = bf16[1,512,1024]{2,1,0:T(8,128)(2,1)} fusion(f32[1,512,1024]{2,1,0:T(8,128)S(1)} %copy-done.19, bf16[2816,1024]{1,0:T(8,128)(2,1)} %all-gather.15.cloned.1.call-done, f32[1,512,5632]{2,1,0:T(8,128)} %copy-done, pred[512]{0:T(512)(128)(4,1)S(1)} %fusion.80), kind=kOutput, calls=%fused_computation.66 | convolution fusion | flops 2963013632 | bytes 20447744 | tf_op jit(solution)/shard_map/srf,fd->srd/dot_general | solution.py:461
  479.3 38.4 %all-reduce.6.cloned.1.call-done = bf16[136,3072]{1,0:T(8,128)(2,1)} async-done(((bf16[136,3072]{1,0:T(8,128)(2,1)}), bf16[136,3072]{1,0:T(8,128)(2,1)}) %all-reduce.6.cloned.1.call-update) | async-done | bytes 835600 | tf_op jit(solution)/shard_map/psum | solution.py:349
  524.6 19.9 %collective-permute-done.10 = bf16[1,64,6656]{2,1,0:T(8,128)(2,1)S(1)} collective-permute-done((bf16[1,64,6656]{2,1,0:T(8,128)(2,1)S(1)}, bf16[1,64,6656]{2,1,0:T(8,128)(2,1)S(1)}, u32[]{:S(2)}, u32[]{:S(2)}) %collective-permute-start.10) | collective-permute-done | bytes 852000 | tf_op jit(solution)/shard_map/ppermute | solution.py:329
  544.6 18.1 %collective-permute-done.7 = bf16[1,64,6656]{2,1,0:T(8,128)(2,1)S(1)} collective-permute-done((bf16[1,64,6656]{2,1,0:T(8,128)(2,1)S(1)}, bf16[1,64,6656]{2,1,0:T(8,128)(2,1)S(1)}, u32[]{:S(2)}, u32[]{:S(2)}) %collective-permute-start.7) | collective-permute-done | bytes 852000 | tf_op jit(solution)/shard_map/ppermute | solution.py:329
  (199 shorter events, 126.7 us)
Async XLA Ops:
  7.2 76.2 %all-gather.9.cloned.1.call-start = ((), (), s32[]{:S(2)}) async-start(), calls=%async_computation.7 | async-start | bytes 7520256 | tf_op jit(solution)/shard_map/all_gather | solution.py:315
  10.1 148.0 %all-gather.11.cloned.1.call-start = ((), (), s32[]{:S(2)}) async-start(), calls=%async_computation.8 | async-start | bytes 2359296 | tf_op jit(solution)/shard_map/all_gather | solution.py:315
  10.9 176.2 %all-gather.13.cloned.1.call-start = ((), (), s32[]{:S(2)}) async-start(), calls=%async_computation.9 | async-start | bytes 12976128 | tf_op jit(solution)/shard_map/all_gather | solution.py:315
  12.2 219.9 %all-gather.15.cloned.1.call-start = ((), (), s32[]{:S(2)}) async-start(), calls=%async_computation.10 | async-start | bytes 6488064 | tf_op jit(solution)/shard_map/all_gather | solution.py:315
  12.4 36.0 %collective-permute-start = (bf16[1,512,1024]{2,1,0:T(8,128)(2,1)S(1)}, bf16[1,512,1024]{2,1,0:T(8,128)(2,1)S(1)}, u32[]{:S(2)}, u32[]{:S(2)}) collective-permute-start(bf16[1,512,1024]{2,1,0:T(8,128)(2,1)S(1)} %copy-done.12), channel_id=1, source_target_pairs={{0,1},{1,0},{2,3},{3,2},{4,5},{5,4},{6,7},{7,6},{8,9},{9,8},{10,11... | collective-permute-start | bytes 3145736 | tf_op jit(solution)/shard_map/ppermute | solution.py:409
  15.4 112.5 %collective-permute-start.1 = (bf16[1,512,1024]{2,1,0:T(8,128)(2,1)}, bf16[1,512,1024]{2,1,0:T(8,128)(2,1)}, u32[]{:S(2)}, u32[]{:S(2)}) collective-permute-start(bf16[1,512,1024]{2,1,0:T(8,128)(2,1)} %param.14), channel_id=1, source_target_pairs={{0,1},{2,3},{4,5},{6,7},{8,9},{10,11},{12,13},{14,15},{16,17},{18,... | collective-permute-start | bytes 3145736 | tf_op jit(solution)/shard_map/ppermute | solution.py:410
  18.3 364.3 %reduce-scatter.8.cloned.1.call-start = ((), (), s32[]{:S(2)}) async-start(), calls=%async_computation.6 | async-start | bytes 6488064 | tf_op jit(solution)/shard_map/reduce_scatter | solution.py:348
  86.6 4.4 copy-start.10
  112.4 13.8 %copy-start.1 = (bf16[1,512,1024]{2,1,0:T(8,128)(2,1)}, bf16[1,512,1024]{2,1,0:T(8,128)(2,1)S(1)}, u32[]{:S(2)}) copy-start(bf16[1,512,1024]{2,1,0:T(8,128)(2,1)S(1)} %copy.87.k_ref) | copy-start | bytes 3145732
  135.5 22.6 %copy-start.13 = (bf16[1,512,1024]{2,1,0:T(8,128)(2,1)S(1)}, bf16[1,512,1024]{2,1,0:T(8,128)(2,1)}, u32[]{:S(2)}) copy-start(bf16[1,512,1024]{2,1,0:T(8,128)(2,1)} %param.13) | copy-start | bytes 3145732
  161.5 25.6 %copy-start.17 = (f32[1,512,1024]{2,1,0:T(8,128)}, f32[1,512,1024]{2,1,0:T(8,128)S(1)}, u32[]{:S(2)}) copy-start(f32[1,512,1024]{2,1,0:T(8,128)S(1)} %get-tuple-element.86) | copy-start | bytes 6291460
  213.7 18.4 %copy-start.29 = (bf16[1,512,1024]{2,1,0:T(8,128)(2,1)S(1)}, bf16[1,512,1024]{2,1,0:T(8,128)(2,1)}, u32[]{:S(2)}) copy-start(bf16[1,512,1024]{2,1,0:T(8,128)(2,1)} %param.15) | copy-start | bytes 3145732
  213.7 29.4 %copy-start.18 = (f32[1,512,1024]{2,1,0:T(8,128)S(1)}, f32[1,512,1024]{2,1,0:T(8,128)}, u32[]{:S(2)}) copy-start(f32[1,512,1024]{2,1,0:T(8,128)} %copy-done.17) | copy-start | bytes 6291460
  213.7 190.5 %reduce-scatter.6.cloned.1.call-start = ((), (), s32[]{:S(2)}) async-start(), calls=%async_computation.5 | async-start | bytes 15335424 | tf_op jit(solution)/shard_map/reduce_scatter | solution.py:348
  280.3 182.8 %reduce-scatter.4.cloned.1.call-start = ((), (), s32[]{:S(2)}) async-start(), calls=%async_computation.3 | async-start | bytes 7520256 | tf_op jit(solution)/shard_map/reduce_scatter | solution.py:348
  285.2 11.9 %collective-permute-start.3 = (f32[1,16,512]{2,1,0:T(8,128)S(1)}, f32[1,16,512]{2,1,0:T(8,128)S(1)}, u32[]{:S(2)}, u32[]{:S(2)}) collective-permute-start(f32[1,16,512]{2,1,0:T(8,128)S(1)} %copy-done.35), channel_id=1, source_target_pairs={{1,0},{3,2},{5,4},{7,6},{9,8},{11,10},{13,12},{15,14},{17,16},{19,... | collective-permute-start | bytes 98312 | tf_op jit(solution)/shard_map/ppermute | solution.py:508
  293.3 29.4 %collective-permute-start.2 = (bf16[1,512,16,64]{1,3,2,0:T(8,128)(2,1)S(1)}, bf16[1,512,16,64]{1,3,2,0:T(8,128)(2,1)}, u32[]{:S(2)}, u32[]{:S(2)}) collective-permute-start(bf16[1,512,16,64]{1,3,2,0:T(8,128)(2,1)S(1)} %bitcast.169), channel_id=1, source_target_pairs={{1,0},{3,2},{5,4},{7,6},{9,8},{11,10},{13,12},{15,14},{17,16},{19,... | collective-permute-start | bytes 3145736 | tf_op jit(solution)/shard_map/ppermute | solution.py:508
  298.2 23.1 %collective-permute-start.4 = (f32[1,16,512]{2,1,0:T(8,128)S(1)}, f32[1,16,512]{2,1,0:T(8,128)S(1)}, u32[]{:S(2)}, u32[]{:S(2)}) collective-permute-start(f32[1,16,512]{2,1,0:T(8,128)S(1)} %bitcast.194), channel_id=1, source_target_pairs={{1,0},{3,2},{5,4},{7,6},{9,8},{11,10},{13,12},{15,14},{17,16},{19,... | collective-permute-start | bytes 98312 | tf_op jit(solution)/shard_map/ppermute | solution.py:508
  325.3 16.5 %copy-start.20 = (f32[1,512,1024]{2,1,0:T(8,128)S(1)}, f32[1,512,1024]{2,1,0:T(8,128)}, u32[]{:S(2)}) copy-start(f32[1,512,1024]{2,1,0:T(8,128)} %get-tuple-element.22) | copy-start | bytes 6291460
  362.4 7.3 %copy-start.30 = (bf16[1,512,1024]{2,1,0:T(8,128)(2,1)}, bf16[1,512,1024]{2,1,0:T(8,128)(2,1)S(1)}, u32[]{:S(2)}) copy-start(bf16[1,512,1024]{2,1,0:T(8,128)(2,1)S(1)} %get-tuple-element.32) | copy-start | bytes 3145732
  362.4 7.4 %copy-start.7 = (f32[1,512,1024]{2,1,0:T(8,128)S(1)}, f32[1,512,1024]{2,1,0:T(8,128)}, u32[]{:S(2)}) copy-start(f32[1,512,1024]{2,1,0:T(8,128)} %copy-done.5) | copy-start | bytes 6291460
  382.6 135.1 %all-reduce.6.cloned.1.call-start = ((), (), s32[]{:S(2)}) async-start(), calls=%async_computation.4 | async-start | bytes 1671168 | tf_op jit(solution)/shard_map/psum | solution.py:349
  382.7 18.6 %collective-permute-start.11 = (bf16[1,352,1024]{2,1,0:T(8,128)(2,1)}, bf16[1,352,1024]{2,1,0:T(8,128)(2,1)S(1)}, u32[]{:S(2)}, u32[]{:S(2)}) collective-permute-start(bf16[1,352,1024]{2,1,0:T(8,128)(2,1)} %reduce-scatter.8.cloned.1.call-done), channel_id=1, source_target_pairs={{0,8},{24,16},{1,9},{25,17},{2,10},{26,18},{3,11},{27,19},{4,12},{... | collective-permute-start | bytes 2162696 | tf_op jit(solution)/shard_map/ppermute | solution.py:325
  402.6 13.1 %collective-permute-start.12 = (bf16[1,352,1024]{2,1,0:T(8,128)(2,1)S(1)}, bf16[1,352,1024]{2,1,0:T(8,128)(2,1)}, u32[]{:S(2)}, u32[]{:S(2)}) collective-permute-start(bf16[1,352,1024]{2,1,0:T(8,128)(2,1)S(1)} %add_convert_fusion.6), channel_id=1, source_target_pairs={{8,16},{16,8},{9,17},{17,9},{10,18},{18,10},{11,19},{19,11},{12,20... | collective-permute-start | bytes 2162696 | tf_op jit(solution)/shard_map/ppermute | solution.py:327
  407.2 56.9 %copy-start.9 = (bf16[1,128,6656]{2,1,0:T(8,128)(2,1)S(1)}, bf16[1,128,6656]{2,1,0:T(8,128)(2,1)}, u32[]{:S(2)}) copy-start(bf16[1,128,6656]{2,1,0:T(8,128)(2,1)} %reduce-scatter.6.cloned.1.call-done) | copy-start | bytes 5111812
  407.2 56.0 %collective-permute-start.5 = (bf16[1,64,6656]{2,1,0:T(8,128)(2,1)}, bf16[1,64,6656]{2,1,0:T(8,128)(2,1)S(1)}, u32[]{:S(2)}, u32[]{:S(2)}) collective-permute-start(bf16[1,64,6656]{2,1,0:T(8,128)(2,1)} %get-tuple-element.63), channel_id=1, source_target_pairs={{0,8},{24,16},{1,9},{25,17},{2,10},{26,18},{3,11},{27,19},{4,12},{... | collective-permute-start | bytes 2555912 | tf_op jit(solution)/shard_map/ppermute | solution.py:325
  413.5 50.6 %collective-permute-start.8 = (bf16[1,64,6656]{2,1,0:T(8,128)(2,1)}, bf16[1,64,6656]{2,1,0:T(8,128)(2,1)}, u32[]{:S(2)}, u32[]{:S(2)}) collective-permute-start(bf16[1,64,6656]{2,1,0:T(8,128)(2,1)} %get-tuple-element.64), channel_id=1, source_target_pairs={{0,8},{24,16},{1,9},{25,17},{2,10},{26,18},{3,11},{27,19},{4,12},{... | collective-permute-start | bytes 2555912 | tf_op jit(solution)/shard_map/ppermute | solution.py:325
  418.0 59.0 %collective-permute-start.13 = (bf16[1,352,1024]{2,1,0:T(8,128)(2,1)}, bf16[1,352,1024]{2,1,0:T(8,128)(2,1)}, u32[]{:S(2)}, u32[]{:S(2)}) collective-permute-start(bf16[1,352,1024]{2,1,0:T(8,128)(2,1)} %add_convert_fusion.5), channel_id=1, source_target_pairs={{8,0},{16,24},{9,1},{17,25},{10,2},{18,26},{11,3},{19,27},{12,4},{... | collective-permute-start | bytes 2162696 | tf_op jit(solution)/shard_map/ppermute | solution.py:329
  465.9 55.7 %collective-permute-start.9 = (bf16[1,64,6656]{2,1,0:T(8,128)(2,1)S(1)}, bf16[1,64,6656]{2,1,0:T(8,128)(2,1)S(1)}, u32[]{:S(2)}, u32[]{:S(2)}) collective-permute-start(bf16[1,64,6656]{2,1,0:T(8,128)(2,1)S(1)} %get-tuple-element.62), channel_id=1, source_target_pairs={{8,16},{16,8},{9,17},{17,9},{10,18},{18,10},{11,19},{19,11},{12,20... | collective-permute-start | bytes 2555912 | tf_op jit(solution)/shard_map/ppermute | solution.py:327
  520.8 2.2 collective-permute-start.6
  521.8 22.7 %collective-permute-start.10 = (bf16[1,64,6656]{2,1,0:T(8,128)(2,1)S(1)}, bf16[1,64,6656]{2,1,0:T(8,128)(2,1)S(1)}, u32[]{:S(2)}, u32[]{:S(2)}) collective-permute-start(bf16[1,64,6656]{2,1,0:T(8,128)(2,1)S(1)} %add_convert_fusion.1), channel_id=1, source_target_pairs={{8,0},{16,24},{9,1},{17,25},{10,2},{18,26},{11,3},{19,27},{12,4},{... | collective-permute-start | bytes 2555912 | tf_op jit(solution)/shard_map/ppermute | solution.py:329
  523.3 39.4 %collective-permute-start.7 = (bf16[1,64,6656]{2,1,0:T(8,128)(2,1)S(1)}, bf16[1,64,6656]{2,1,0:T(8,128)(2,1)S(1)}, u32[]{:S(2)}, u32[]{:S(2)}) collective-permute-start(bf16[1,64,6656]{2,1,0:T(8,128)(2,1)S(1)} %add_convert_fusion.3), channel_id=1, source_target_pairs={{8,0},{16,24},{9,1},{17,25},{10,2},{18,26},{11,3},{19,27},{12,4},{... | collective-permute-start | bytes 2555912 | tf_op jit(solution)/shard_map/ppermute | solution.py:329
  (26 other events, 68.4 us)
Sparse Core Ops, SparseCore 0:
  10.5 72.8 all-gather.8
  85.3 31.7 all-gather.10
  119.5 67.5 all-gather.12
  188.8 43.1 all-gather.14
  235.3 59.7 reduce-scatter.7
  298.4 97.4 reduce-scatter.5
  399.4 63.6 reduce-scatter.3
  465.5 52.2 all-reduce.5

commit v13 on v11

--- a/solution.py
+++ b/solution.py
@@ -320,10 +320,7 @@
     return fulls
 
 
-def rep_sum(x):
-    n_rep = lax.axis_size("rep")
-    if n_rep != 4:
-        return lax.psum(x, "rep")
+def rep_chain(x):
     me = lax.axis_index("rep")
     arrived = lax.ppermute(x, "rep", [(0, 1), (3, 2)])
     folded = (x.astype(jnp.float32) + arrived.astype(jnp.float32)).astype(x.dtype)
@@ -333,10 +330,25 @@
     return jnp.where((me == 0) | (me == 3), sent_out, total)
 
 
-def scatter_blocks(blocks, by_permutes):
+def rep_sum(x, pieces=1):
+    if lax.axis_size("rep") != 4:
+        return lax.psum(x, "rep")
+    rows = x.shape[1]
+    if pieces == 1 or rows % (8 * pieces):
+        return rep_chain(x)
+    step = rows // pieces
+    parts = []
+    for i in range(pieces):
+        parts.append(rep_chain(x[:, i * step : (i + 1) * step]))
+    return jnp.concatenate(parts, axis=1)
+
+
+def scatter_blocks(blocks, by_permutes, pieces=1):
     packed = jnp.concatenate(blocks, axis=1).astype(jnp.bfloat16)
     summed = lax.psum_scatter(packed, GROUP, scatter_dimension=0, tiled=True)
-    summed = (rep_sum(summed) if by_permutes else lax.psum(summed, "rep"))[0].astype(jnp.float32)
+    summed = (rep_sum(summed, pieces) if by_permutes else lax.psum(summed, "rep"))[0].astype(
+        jnp.float32
+    )
     parts, offset = [], 0
     for block in blocks:
         parts.append(summed[offset : offset + block.shape[1], :])
@@ -485,7 +497,7 @@
         .astype(jnp.bfloat16)
         .reshape(head_shape)
     )
-    (part_gu,) = scatter_blocks([gu_block], True)
+    (part_gu,) = scatter_blocks([gu_block], True, 2)
     row_dots = jnp.sum(g_attended.astype(jnp.float32) * attended.astype(jnp.float32), axis=-1)
     if paired:
         dot_rows = jnp.transpose(row_dots, (0, 2, 1))

time: 610 us -> 584 us (0.957)
  waiting for transfers between devices: 282 us -> 245 us
  starting transfers between devices: 23 us -> 30.7 us
    ppermute x3, waiting for transfers between devices: 27.6 us -> 5.88 us  [shards(): lax.ppermute((g_attended, dot_rows, lse_rows), 'ctx', [(1, 0)])]
    reduce_scatter x3, waiting for transfers between devices: 53.4 us -> 38.4 us  [scatter_blocks(): summed = lax.psum_scatter(packed, GROUP, scatter_dimension=0, tiled=True)]
    psum x1, waiting for transfers between devices: 47.1 us -> 59.6 us  [scatter_blocks(): lax.psum(summed, 'rep')]
    all_gather x4, waiting for transfers between devices: 90.7 us -> 79.1 us  [gather_blocks(): gathered = lax.all_gather(packed, GROUP, axis=0, tiled=False)]
    ppermute x6 -> x9, starting transfers between devices: 12.4 us -> 19.7 us  [the longest x3 12.9 us: rep_chain(): arrived = lax.ppermute(x, 'rep', [(0, 1), (3, 2)])]
    ppermute x6 -> x9, waiting for transfers between devices: 34.9 us -> 34.8 us  [the longest x3 32.8 us: rep_chain(): sent_out = lax.ppermute(total, 'rep', [(1, 0), (2, 3)])]
  transfers between devices with their start and end apart: 19 -> 22, of which waited for: 12 -> 11; matrix products, arithmetic and copies ran while one was open for 30% -> 38% of each run, Pallas kernels for 9% -> 10%
where the time goes in v13:
time: 584 us; the launch traced here: 578 us
  waiting for transfers between devices  245 us (42%)
  matrix products  103 us (18%)
  other arithmetic  75.2 us (13%)
  Pallas kernels  55.4 us (9%)
  local copies, waits for them, and re-layouts  53 us (9%)
  starting transfers between devices  30.7 us (5%)
  between operations  15.8 us (3%)
    all_gather x4, waiting for transfers between devices, gather_blocks(): gathered = lax.all_gather(packed, GROUP, axis=0, tiled=False)  79.1 us
    psum x1, waiting for transfers between devices, scatter_blocks(): lax.psum(summed, 'rep')  59.6 us
    reduce_scatter x3, waiting for transfers between devices, scatter_blocks(): summed = lax.psum_scatter(packed, GROUP, scatter_dimension=0, tiled=True)  38.4 us
    ppermute x3, waiting for transfers between devices, rep_chain(): sent_out = lax.ppermute(total, 'rep', [(1, 0), (2, 3)])  32.8 us
    pallas_call x2, Pallas kernels, block_backward(): pl.pallas_call(kernel, grid=(n_slots, n_heads // 2), in_specs=[q_spec, k_...  32.8 us
    ppermute x1, waiting for transfers between devices, shards(): other_tokens = lax.ppermute(tokens, 'ctx', [(0, 1), (1, 0)])  26.2 us
    pallas_call x1, Pallas kernels, block_forward(): pl.pallas_call(kernel, grid=(n_slots, n_heads // 2), in_specs=[q_spec, k_...  22.6 us
    dot_general x1, matrix products, shards(): jnp.einsum('srf,df->srd', gu_gradient, full_gu, preferred_element_type=jn...  13.6 us
  transfers between devices with their start and end apart: 22, of which 11 were waited for; matrix products, arithmetic and copies ran while one was open for 38% of the time, Pallas kernels for 10%

profile of v13, /device:TPU:0, one launch (start us, length us, event | category | flops | bytes accessed | tf_op | source)
XLA Modules:
  0.0 578.3 jit_solution(15283355338701797719)
XLA Ops:
  22.3 26.2 %collective-permute-done = bf16[1,512,1024]{2,1,0:T(8,128)(2,1)S(1)} collective-permute-done((bf16[1,512,1024]{2,1,0:T(8,128)(2,1)S(1)}, bf16[1,512,1024]{2,1,0:T(8,128)(2,1)S(1)}, u32[]{:S(2)}, u32[]{:S(2)}) %collective-permute-start) | collective-permute-done | bytes 1048608 | tf_op jit(solution)/shard_map/ppermute | solution.py:409
  48.7 34.6 %all-gather.9.cloned.1.call-done = bf16[1088,3072]{1,0:T(8,128)(2,1)} async-done(((bf16[136,3072]{1,0:T(8,128)(2,1)}), bf16[1088,3072]{1,0:T(8,128)(2,1)}) %all-gather.9.cloned.1.call-update) | async-done | bytes 6684688 | tf_op jit(solution)/shard_map/all_gather | solution.py:315
  87.4 3.6 convolution_bitcast_fusion.2
  102.2 8.2 %convolution_bitcast_fusion.1 = f32[1,512,3072]{2,1,0:T(8,128)} fusion(bf16[1024,3072]{1,0:T(8,128)(2,1)} %bitcast.179, bf16[1,512,1024]{2,1,0:T(8,128)(2,1)S(1)} %collective-permute-done, f32[512]{0:T(512)S(1)} %add_rsqrt_fusion.1, f32[1024]{0:T(1024)S(1)} %bitcast.200), kind=kOutput, calls=%fused_computation.22 | convolution fusion | flops 3223322624 | bytes 13637632 | tf_op jit(solution)/shard_map/srd,de->sre/dot_general | solution.py:419
  112.4 5.2 fusion.93
  127.8 5.2 broadcast_select_fusion.1
  135.5 22.6 %shard_map.220 = (bf16[1,512,1024]{2,1,0:T(8,128)(2,1)}, f32[1,16,512]{2,1,0:T(8,128)}) custom-call(bf16[1,512,1024]{2,1,0:T(8,128)(2,1)} %copy.91.q_ref, bf16[1,1024,1024]{2,1,0:T(8,128)(2,1)} %pad_maximum_fusion.4.k_ref, bf16[1,1024,1024]{2,1,0:T(8,128)(2,1)} %pad_maximum_fusion.5.v_ref, s32[1,512]{1,0:T(1,128)} %iota_add_fusion.1.qpos_ref, ...), custom_call_target="tpu_custom_call" | custom-call | flops 2147483648 | bytes 6291456 | tf_op jit(solution)/shard_map/pallas_call | solution.py:247
  161.5 25.6 %all-gather.13.cloned.1.call-done = bf16[1024,5632]{1,0:T(8,128)(2,1)} async-done(((bf16[128,5632]{1,0:T(8,128)(2,1)}), bf16[1024,5632]{1,0:T(8,128)(2,1)}) %all-gather.13.cloned.1.call-update) | async-done | bytes 11534352 | tf_op jit(solution)/shard_map/all_gather | solution.py:315
  187.1 9.3 %convolution_bitcast_fusion = f32[1,512,5632]{2,1,0:T(8,128)S(1)} fusion(bf16[1024,5632]{1,0:T(8,128)(2,1)} %all-gather.13.cloned.1.call-done, f32[1,512,1024]{2,1,0:T(8,128)S(1)} %get-tuple-element.87, f32[1024]{0:T(1024)S(1)} %bitcast.196, f32[512]{0:T(512)S(1)} %add_rsqrt_fusion), kind=kOutput, calls=%fused_computation.3 | convolution fusion | flops 5907152896 | bytes 25171968 | tf_op jit(solution)/shard_map/srd,df->srf/dot_general | solution.py:456
  196.4 4.2 copy-done
  205.3 7.8 %convolution_convert_fusion.2 = bf16[8,352,1024]{2,1,0:T(8,128)(2,1)} fusion(bf16[8,352,512]{2,1,0:T(8,128)(2,1)} %bitcast.190, bf16[1,512,1024]{2,1,0:T(8,128)(2,1)} %param.15, pred[512]{0:T(512)(128)(4,1)S(1)} %fusion.80), kind=kOutput, calls=%fused_computation.24 | convolution fusion | flops 2957246464 | bytes 9699840 | tf_op jit(solution)/shard_map/srf,srd->fd/dot_general | solution.py:472
  213.2 18.8 %all-gather.15.cloned.1.call-done = bf16[2816,1024]{1,0:T(8,128)(2,1)} async-done(((bf16[352,1024]{1,0:T(8,128)(2,1)}), bf16[2816,1024]{1,0:T(8,128)(2,1)}) %all-gather.15.cloned.1.call-update) | async-done | bytes 5767184 | tf_op jit(solution)/shard_map/all_gather | solution.py:315
  232.0 11.3 %fusion.8 = (bf16[1,512,2816]{2,1,0:T(8,128)(2,1)}, bf16[1,512,2816]{2,1,0:T(8,128)(2,1)}) fusion(f32[1,512,5632]{2,1,0:T(8,128)} %copy-done, bf16[2816,1024]{1,0:T(8,128)(2,1)} %all-gather.15.cloned.1.call-done, bf16[1,512,1024]{2,1,0:T(8,128)(2,1)S(1)} %copy-done.24, pred[512]{0:T(512)(128)(4,1)S(1)} %fusion.80), kind=kOutput, calls=%fused_computation.16 | convolution fusion | flops 2973106176 | bytes 24117760 | tf_op jit(solution)/shard_map/srd,fd->srf/dot_general | solution.py:478
  243.3 13.6 %fusion.32 = (bf16[1024]{0:T(1024)(128)(2,1)S(1)}, f32[512]{0:T(512)S(1)}, f32[512,1024]{1,0:T(8,128)S(1)}) fusion(f32[1,512,1024]{2,1,0:T(8,128)S(1)} %copy-done.17, f32[512]{0:T(512)S(1)} %add_rsqrt_fusion, f32[1024]{0:T(1024)S(1)} %bitcast.197, bf16[1024,5632]{1,0:T(8,128)(2,1)} %all-gather.13.cloned.1.call-done, ...), kind=kOutput, calls=%fused_computation.57 | convolution fusion | flops 5920258560 | bytes 21506048 | tf_op jit(solution)/shard_map/srf,df->srd/dot_general | solution.py:485
  259.6 11.5 %convolution_convert_fusion = bf16[8,128,5632]{2,1,0:T(8,128)(2,1)} fusion(bf16[8,128,512]{2,1,0:T(8,128)(2,1)S(1)} %bitcast.193, bf16[1,512,2816]{2,1,0:T(8,128)(2,1)} %get-tuple-element.40, bf16[1,512,2816]{2,1,0:T(8,128)(2,1)} %get-tuple-element.39), kind=kOutput, calls=%fused_computation.2 | convolution fusion | flops 5922881536 | bytes 18350080 | tf_op jit(solution)/shard_map/srd,srf->df/dot_general | solution.py:482
  282.5 4.9 convolution_convert_fusion.4
  295.2 16.3 %shard_map.221 = (f32[1,512,1024]{2,1,0:T(8,128)}, f32[1,512,1024]{2,1,0:T(8,128)}, f32[1,512,1024]{2,1,0:T(8,128)}) custom-call(bf16[1,512,1024]{2,1,0:T(8,128)(2,1)} %copy.91.q_ref, bf16[1,512,1024]{2,1,0:T(8,128)(2,1)} %copy-done.1, bf16[1,512,1024]{2,1,0:T(8,128)(2,1)} %copy-done.12, bf16[1,512,1024]{2,1,0:T(8,128)(2,1)} %bitcast.192, ...), custom_call_target="tpu_custom_call" | custom-call | flops 2684354560 | bytes 10485760 | tf_op jit(solution)/shard_map/pallas_call | solution.py:285
  311.5 4.6 collective-permute-done.4
  319.5 16.5 %shard_map.222 = (f32[1,512,1024]{2,1,0:T(8,128)}, f32[1,512,1024]{2,1,0:T(8,128)}, f32[1,512,1024]{2,1,0:T(8,128)}) custom-call(bf16[1,512,1024]{2,1,0:T(8,128)(2,1)} %broadcast_select_fusion.3.q_ref, bf16[1,512,1024]{2,1,0:T(8,128)(2,1)} %broadcast_select_fusion.2.k_ref, bf16[1,512,1024]{2,1,0:T(8,128)(2,1)} %get-tuple-element.34.v_ref, ...), custom_call_target="tpu_custom_call" | custom-call | flops 2684354560 | bytes 10485760 | tf_op jit(solution)/shard_map/pallas_call | solution.py:285
  339.7 4.4 select_add_fusion
  351.7 4.6 fusion.90
  356.2 7.9 %fusion.26 = (bf16[1024]{0:T(1024)(128)(2,1)S(1)}, f32[512]{0:T(512)S(1)}, f32[512,1024]{1,0:T(8,128)}) fusion(bf16[1,512,1024]{2,1,0:T(8,128)(2,1)S(1)} %copy-done.15, f32[512]{0:T(512)S(1)} %add_rsqrt_fusion.2, f32[1024]{0:T(1024)S(1)} %bitcast.201, bf16[1024,3072]{1,0:T(8,128)(2,1)} %bitcast.180, bf16[1,512,1024]{2,1,0:T(8,128)(2,1)S(1)} %get-tuple-element.32, ...), kind=kOutput, calls=%fused_computation.46 | convolution fusion | flops 3234331136 | bytes 12593152 | tf_op jit(solution)/shard_map/sre,de->srd/dot_general | solution.py:546
  364.2 7.7 %convolution_convert_fusion.1 = bf16[1024,3072]{1,0:T(8,128)(2,1)} fusion(bf16[1,512,1024]{2,1,0:T(8,128)(2,1)S(1)} %get-tuple-element.32, bf16[1,512,1024]{2,1,0:T(8,128)(2,1)} %copy-done.28, bf16[1,512,1024]{2,1,0:T(8,128)(2,1)S(1)} %copy-done.29, bf16[1,512,1024]{2,1,0:T(8,128)(2,1)S(1)} %copy-done.15, f32[1024]{0:T(1024)S(1)} %bitcast.202, ...), kind=kOutput, calls=%fused_computation.21 | convolution fusion | flops 3235905536 | bytes 10491904 | tf_op jit(solution)/shard_map/srd,sre->de/dot_general | solution.py:545
  371.9 7.0 %pad_maximum_fusion = bf16[1024,4096]{1,0:T(8,128)(2,1)} fusion(bf16[1024,1024]{1,0:T(8,128)(2,1)S(1)} %copy-done.23, bf16[1024,3072]{1,0:T(8,128)(2,1)} %convolution_convert_fusion.1), kind=kLoop, calls=%fused_computation.5 | loop fusion | flops 16777216 | bytes 16777216 | tf_op jit(solution)/shard_map/concatenate | solution.py:551
  378.9 8.4 %fusion.1 = bf16[8,136,4096]{2,1,0:T(8,128)(2,1)} fusion(bf16[8,1,4096]{2,1,0:T(2,128)(2,1)S(1)} %copy.112, bf16[8,128,4096]{2,1,0:T(8,128)(2,1)} %bitcast.168), kind=kLoop, calls=%fused_computation.4 | loop fusion | flops 26738688 | bytes 17367040 | tf_op jit(solution)/shard_map/concatenate | solution.py:347
  387.4 3.6 collective-permute-start.11
  391.0 11.7 %fusion.37 = bf16[1,512,1024]{2,1,0:T(8,128)(2,1)} fusion(f32[1,512,1024]{2,1,0:T(8,128)S(1)} %copy-done.18, bf16[2816,1024]{1,0:T(8,128)(2,1)} %all-gather.15.cloned.1.call-done, f32[1,512,5632]{2,1,0:T(8,128)} %copy-done, pred[512]{0:T(512)(128)(4,1)S(1)} %fusion.80), kind=kOutput, calls=%fused_computation.65 | convolution fusion | flops 2963013632 | bytes 20447744 | tf_op jit(solution)/shard_map/srf,fd->srd/dot_general | solution.py:461
  410.1 7.0 %collective-permute-start.5 = (bf16[1,64,5632]{2,1,0:T(8,128)(2,1)}, bf16[1,64,5632]{2,1,0:T(8,128)(2,1)}, u32[]{:S(2)}, u32[]{:S(2)}) collective-permute-start(bf16[1,64,5632]{2,1,0:T(8,128)(2,1)} %get-tuple-element.67), channel_id=1, source_target_pairs={{0,8},{24,16},{1,9},{25,17},{2,10},{26,18},{3,11},{27,19},{4,12},{... | collective-permute-start | bytes 2162696 | tf_op jit(solution)/shard_map/ppermute | solution.py:325
  424.3 38.4 %reduce-scatter.4.cloned.1.call-done = bf16[1,136,4096]{2,1,0:T(8,128)(2,1)} async-done(((bf16[8,136,4096]{2,1,0:T(8,128)(2,1)}), bf16[1,136,4096]{2,1,0:T(8,128)(2,1)}) %reduce-scatter.4.cloned.1.call-update) | async-done | bytes 1114128 | tf_op jit(solution)/shard_map/reduce_scatter | solution.py:348
  468.3 59.6 %all-reduce.6.cloned.1.call-done = bf16[136,4096]{1,0:T(8,128)(2,1)} async-done(((bf16[136,4096]{1,0:T(8,128)(2,1)}), bf16[136,4096]{1,0:T(8,128)(2,1)}) %all-reduce.6.cloned.1.call-update) | async-done | bytes 1114128 | tf_op jit(solution)/shard_map/psum | solution.py:349
  536.2 18.8 %collective-permute-done.10 = bf16[1,64,5632]{2,1,0:T(8,128)(2,1)S(1)} collective-permute-done((bf16[1,64,5632]{2,1,0:T(8,128)(2,1)S(1)}, bf16[1,64,5632]{2,1,0:T(8,128)(2,1)S(1)}, u32[]{:S(2)}, u32[]{:S(2)}) %collective-permute-start.10) | collective-permute-done | bytes 720928 | tf_op jit(solution)/shard_map/ppermute | solution.py:329
  555.1 14.0 %collective-permute-done.7 = bf16[1,64,5632]{2,1,0:T(8,128)(2,1)S(1)} collective-permute-done((bf16[1,64,5632]{2,1,0:T(8,128)(2,1)S(1)}, bf16[1,64,5632]{2,1,0:T(8,128)(2,1)S(1)}, u32[]{:S(2)}, u32[]{:S(2)}) %collective-permute-start.7) | collective-permute-done | bytes 720928 | tf_op jit(solution)/shard_map/ppermute | solution.py:329
  (197 shorter events, 119.3 us)
Async XLA Ops:
  7.2 76.2 %all-gather.9.cloned.1.call-start = ((), (), s32[]{:S(2)}) async-start(), calls=%async_computation.7 | async-start | bytes 7520256 | tf_op jit(solution)/shard_map/all_gather | solution.py:315
  10.1 148.0 %all-gather.11.cloned.1.call-start = ((), (), s32[]{:S(2)}) async-start(), calls=%async_computation.8 | async-start | bytes 2359296 | tf_op jit(solution)/shard_map/all_gather | solution.py:315
  10.9 176.2 %all-gather.13.cloned.1.call-start = ((), (), s32[]{:S(2)}) async-start(), calls=%async_computation.9 | async-start | bytes 12976128 | tf_op jit(solution)/shard_map/all_gather | solution.py:315
  12.2 219.8 %all-gather.15.cloned.1.call-start = ((), (), s32[]{:S(2)}) async-start(), calls=%async_computation.10 | async-start | bytes 6488064 | tf_op jit(solution)/shard_map/all_gather | solution.py:315
  12.4 36.0 %collective-permute-start = (bf16[1,512,1024]{2,1,0:T(8,128)(2,1)S(1)}, bf16[1,512,1024]{2,1,0:T(8,128)(2,1)S(1)}, u32[]{:S(2)}, u32[]{:S(2)}) collective-permute-start(bf16[1,512,1024]{2,1,0:T(8,128)(2,1)S(1)} %copy-done.13), channel_id=1, source_target_pairs={{0,1},{1,0},{2,3},{3,2},{4,5},{5,4},{6,7},{7,6},{8,9},{9,8},{10,11... | collective-permute-start | bytes 3145736 | tf_op jit(solution)/shard_map/ppermute | solution.py:409
  15.4 112.4 %collective-permute-start.1 = (bf16[1,512,1024]{2,1,0:T(8,128)(2,1)}, bf16[1,512,1024]{2,1,0:T(8,128)(2,1)}, u32[]{:S(2)}, u32[]{:S(2)}) collective-permute-start(bf16[1,512,1024]{2,1,0:T(8,128)(2,1)} %param.14), channel_id=1, source_target_pairs={{0,1},{2,3},{4,5},{6,7},{8,9},{10,11},{12,13},{14,15},{16,17},{18,... | collective-permute-start | bytes 3145736 | tf_op jit(solution)/shard_map/ppermute | solution.py:410
  18.4 369.0 %reduce-scatter.8.cloned.1.call-start = ((), (), s32[]{:S(2)}) async-start(), calls=%async_computation.6 | async-start | bytes 6488064 | tf_op jit(solution)/shard_map/reduce_scatter | solution.py:348
  112.4 13.8 %copy-start.1 = (bf16[1,512,1024]{2,1,0:T(8,128)(2,1)}, bf16[1,512,1024]{2,1,0:T(8,128)(2,1)S(1)}, u32[]{:S(2)}) copy-start(bf16[1,512,1024]{2,1,0:T(8,128)(2,1)S(1)} %copy.87.k_ref) | copy-start | bytes 3145732
  135.5 22.6 %copy-start.14 = (bf16[1,512,1024]{2,1,0:T(8,128)(2,1)S(1)}, bf16[1,512,1024]{2,1,0:T(8,128)(2,1)}, u32[]{:S(2)}) copy-start(bf16[1,512,1024]{2,1,0:T(8,128)(2,1)} %param.13) | copy-start | bytes 3145732
  161.5 25.6 %copy-start.16 = (f32[1,512,1024]{2,1,0:T(8,128)}, f32[1,512,1024]{2,1,0:T(8,128)S(1)}, u32[]{:S(2)}) copy-start(f32[1,512,1024]{2,1,0:T(8,128)S(1)} %get-tuple-element.87) | copy-start | bytes 6291460
  213.1 18.9 %copy-start.24 = (bf16[1,512,1024]{2,1,0:T(8,128)(2,1)S(1)}, bf16[1,512,1024]{2,1,0:T(8,128)(2,1)}, u32[]{:S(2)}) copy-start(bf16[1,512,1024]{2,1,0:T(8,128)(2,1)} %param.15) | copy-start | bytes 3145732
  213.1 30.2 %copy-start.17 = (f32[1,512,1024]{2,1,0:T(8,128)S(1)}, f32[1,512,1024]{2,1,0:T(8,128)}, u32[]{:S(2)}) copy-start(f32[1,512,1024]{2,1,0:T(8,128)} %copy-done.16) | copy-start | bytes 6291460
  213.1 194.3 %reduce-scatter.6.cloned.1.call-start = ((), (), s32[]{:S(2)}) async-start(), calls=%async_computation.5 | async-start | bytes 12976128 | tf_op jit(solution)/shard_map/reduce_scatter | solution.py:348
  271.1 191.6 %reduce-scatter.4.cloned.1.call-start = ((), (), s32[]{:S(2)}) async-start(), calls=%async_computation.3 | async-start | bytes 10027008 | tf_op jit(solution)/shard_map/reduce_scatter | solution.py:348
  275.9 5.9 %collective-permute-start.3 = (f32[1,16,512]{2,1,0:T(8,128)S(1)}, f32[1,16,512]{2,1,0:T(8,128)S(1)}, u32[]{:S(2)}, u32[]{:S(2)}) collective-permute-start(f32[1,16,512]{2,1,0:T(8,128)S(1)} %copy-done.35), channel_id=1, source_target_pairs={{1,0},{3,2},{5,4},{7,6},{9,8},{11,10},{13,12},{15,14},{17,16},{19,... | collective-permute-start | bytes 98312 | tf_op jit(solution)/shard_map/ppermute | solution.py:504
  288.9 27.9 %collective-permute-start.2 = (bf16[1,512,16,64]{1,3,2,0:T(8,128)(2,1)S(1)}, bf16[1,512,16,64]{1,3,2,0:T(8,128)(2,1)}, u32[]{:S(2)}, u32[]{:S(2)}) collective-permute-start(bf16[1,512,16,64]{1,3,2,0:T(8,128)(2,1)S(1)} %bitcast.169), channel_id=1, source_target_pairs={{1,0},{3,2},{5,4},{7,6},{9,8},{11,10},{13,12},{15,14},{17,16},{19,... | collective-permute-start | bytes 3145736 | tf_op jit(solution)/shard_map/ppermute | solution.py:504
  290.8 25.3 %collective-permute-start.4 = (f32[1,16,512]{2,1,0:T(8,128)S(1)}, f32[1,16,512]{2,1,0:T(8,128)S(1)}, u32[]{:S(2)}, u32[]{:S(2)}) collective-permute-start(f32[1,16,512]{2,1,0:T(8,128)S(1)} %bitcast.194), channel_id=1, source_target_pairs={{1,0},{3,2},{5,4},{7,6},{9,8},{11,10},{13,12},{15,14},{17,16},{19,... | collective-permute-start | bytes 98312 | tf_op jit(solution)/shard_map/ppermute | solution.py:504
  295.2 20.9 %copy-start.34 = (f32[512,16]{0,1:T(8,128)S(1)}, f32[512,16]{0,1:T(8,128)}, u32[]{:S(2)}) copy-start(f32[512,16]{0,1:T(8,128)} %copy-done.33) | copy-start | bytes 98308
  319.5 16.5 %copy-start.19 = (f32[1,512,1024]{2,1,0:T(8,128)S(1)}, f32[1,512,1024]{2,1,0:T(8,128)}, u32[]{:S(2)}) copy-start(f32[1,512,1024]{2,1,0:T(8,128)} %get-tuple-element.22) | copy-start | bytes 6291460
  387.3 140.6 %all-reduce.6.cloned.1.call-start = ((), (), s32[]{:S(2)}) async-start(), calls=%async_computation.4 | async-start | bytes 2228224 | tf_op jit(solution)/shard_map/psum | solution.py:349
  387.4 17.3 %copy-start.30 = (bf16[1,352,1024]{2,1,0:T(8,128)(2,1)S(1)}, bf16[1,352,1024]{2,1,0:T(8,128)(2,1)}, u32[]{:S(2)}) copy-start(bf16[1,352,1024]{2,1,0:T(8,128)(2,1)} %reduce-scatter.8.cloned.1.call-done) | copy-start | bytes 2162692
  387.4 17.3 %collective-permute-start.11 = (bf16[1,352,1024]{2,1,0:T(8,128)(2,1)}, bf16[1,352,1024]{2,1,0:T(8,128)(2,1)S(1)}, u32[]{:S(2)}, u32[]{:S(2)}) collective-permute-start(bf16[1,352,1024]{2,1,0:T(8,128)(2,1)} %reduce-scatter.8.cloned.1.call-done), channel_id=1, source_target_pairs={{0,8},{24,16},{1,9},{25,17},{2,10},{26,18},{3,11},{27,19},{4,12},{... | collective-permute-start | bytes 2162696 | tf_op jit(solution)/shard_map/ppermute | solution.py:325
  402.8 16.7 %copy-start.7 = (f32[1,512,1024]{2,1,0:T(8,128)S(1)}, f32[1,512,1024]{2,1,0:T(8,128)}, u32[]{:S(2)}) copy-start(f32[1,512,1024]{2,1,0:T(8,128)} %get-tuple-element.64) | copy-start | bytes 6291460
  405.8 15.5 %collective-permute-start.12 = (bf16[1,352,1024]{2,1,0:T(8,128)(2,1)}, bf16[1,352,1024]{2,1,0:T(8,128)(2,1)}, u32[]{:S(2)}, u32[]{:S(2)}) collective-permute-start(bf16[1,352,1024]{2,1,0:T(8,128)(2,1)} %add_convert_fusion.2), channel_id=1, source_target_pairs={{8,16},{16,8},{9,17},{17,9},{10,18},{18,10},{11,19},{19,11},{12,20... | collective-permute-start | bytes 2162696 | tf_op jit(solution)/shard_map/ppermute | solution.py:327
  410.1 52.7 %collective-permute-start.5 = (bf16[1,64,5632]{2,1,0:T(8,128)(2,1)}, bf16[1,64,5632]{2,1,0:T(8,128)(2,1)}, u32[]{:S(2)}, u32[]{:S(2)}) collective-permute-start(bf16[1,64,5632]{2,1,0:T(8,128)(2,1)} %get-tuple-element.67), channel_id=1, source_target_pairs={{0,8},{24,16},{1,9},{25,17},{2,10},{26,18},{3,11},{27,19},{4,12},{... | collective-permute-start | bytes 2162696 | tf_op jit(solution)/shard_map/ppermute | solution.py:325
  417.1 45.7 %collective-permute-start.8 = (bf16[1,64,5632]{2,1,0:T(8,128)(2,1)}, bf16[1,64,5632]{2,1,0:T(8,128)(2,1)}, u32[]{:S(2)}, u32[]{:S(2)}) collective-permute-start(bf16[1,64,5632]{2,1,0:T(8,128)(2,1)} %get-tuple-element.68), channel_id=1, source_target_pairs={{0,8},{24,16},{1,9},{25,17},{2,10},{26,18},{3,11},{27,19},{4,12},{... | collective-permute-start | bytes 2162696 | tf_op jit(solution)/shard_map/ppermute | solution.py:325
  421.3 41.4 %copy-start.10 = (bf16[1,128,5632]{2,1,0:T(8,128)(2,1)S(1)}, bf16[1,128,5632]{2,1,0:T(8,128)(2,1)}, u32[]{:S(2)}) copy-start(bf16[1,128,5632]{2,1,0:T(8,128)(2,1)} %reduce-scatter.6.cloned.1.call-done) | copy-start | bytes 4325380
  423.0 43.0 %collective-permute-start.13 = (bf16[1,352,1024]{2,1,0:T(8,128)(2,1)S(1)}, bf16[1,352,1024]{2,1,0:T(8,128)(2,1)}, u32[]{:S(2)}, u32[]{:S(2)}) collective-permute-start(bf16[1,352,1024]{2,1,0:T(8,128)(2,1)S(1)} %add_convert_fusion.1), channel_id=1, source_target_pairs={{8,0},{16,24},{9,1},{17,25},{10,2},{18,26},{11,3},{19,27},{12,4},{... | collective-permute-start | bytes 2162696 | tf_op jit(solution)/shard_map/ppermute | solution.py:329
  465.3 66.9 %collective-permute-start.9 = (bf16[1,64,5632]{2,1,0:T(8,128)(2,1)}, bf16[1,64,5632]{2,1,0:T(8,128)(2,1)S(1)}, u32[]{:S(2)}, u32[]{:S(2)}) collective-permute-start(bf16[1,64,5632]{2,1,0:T(8,128)(2,1)} %get-tuple-element.66), channel_id=1, source_target_pairs={{8,16},{16,8},{9,17},{17,9},{10,18},{18,10},{11,19},{19,11},{12,20... | collective-permute-start | bytes 2162696 | tf_op jit(solution)/shard_map/ppermute | solution.py:327
  531.4 3.3 collective-permute-start.6
  533.4 21.6 %collective-permute-start.10 = (bf16[1,64,5632]{2,1,0:T(8,128)(2,1)S(1)}, bf16[1,64,5632]{2,1,0:T(8,128)(2,1)S(1)}, u32[]{:S(2)}, u32[]{:S(2)}) collective-permute-start(bf16[1,64,5632]{2,1,0:T(8,128)(2,1)S(1)} %add_convert_fusion.3), channel_id=1, source_target_pairs={{8,0},{16,24},{9,1},{17,25},{10,2},{18,26},{11,3},{19,27},{12,4},{... | collective-permute-start | bytes 2162696 | tf_op jit(solution)/shard_map/ppermute | solution.py:329
  534.9 34.2 %collective-permute-start.7 = (bf16[1,64,5632]{2,1,0:T(8,128)(2,1)S(1)}, bf16[1,64,5632]{2,1,0:T(8,128)(2,1)S(1)}, u32[]{:S(2)}, u32[]{:S(2)}) collective-permute-start(bf16[1,64,5632]{2,1,0:T(8,128)(2,1)S(1)} %add_convert_fusion.5), channel_id=1, source_target_pairs={{8,0},{16,24},{9,1},{17,25},{10,2},{18,26},{11,3},{19,27},{12,4},{... | collective-permute-start | bytes 2162696 | tf_op jit(solution)/shard_map/ppermute | solution.py:329
  (26 other events, 109.9 us)
Sparse Core Ops, SparseCore 0:
  10.5 72.8 all-gather.8
  85.3 31.7 all-gather.10
  119.5 67.5 all-gather.12
  188.8 43.1 all-gather.14
  235.3 59.1 reduce-scatter.7
  297.8 87.0 reduce-scatter.5
  388.5 74.1 reduce-scatter.3
  465.1 62.8 all-reduce.5

commit v14 on v13

--- a/solution.py
+++ b/solution.py
@@ -385,17 +385,18 @@
     ff_width = w_gate.shape[1]
     attn_width = w_query.shape[1]
     qkv_width = 3 * attn_width
-    (qkv_blocks, gain_rows) = gather_blocks(
+    qkvo_width = qkv_width + model_width
+    (qkvo_blocks, gain_rows) = gather_blocks(
         [
-            jnp.concatenate([w_query, w_key, w_value], axis=1),
-            gain_block(gain_attn, gain_mlp, qkv_width),
+            jnp.concatenate([w_query, w_key, w_value, w_out], axis=1),
+            gain_block(gain_attn, gain_mlp, qkvo_width),
         ]
     )
-    full_qkv = qkv_blocks.reshape(n_group * own_rows, qkv_width)
+    full_qkvo = qkvo_blocks.reshape(n_group * own_rows, qkvo_width)
+    full_qkv = full_qkvo[:, :qkv_width]
+    full_out = full_qkvo[:, qkv_width:]
     full_gain_attn = gain_rows[:, 0, :own_rows].reshape(-1)
     full_gain_mlp = gain_rows[:, 0, own_rows : 2 * own_rows].reshape(-1)
-    (out_blocks,) = gather_blocks([w_out])
-    full_out = out_blocks.reshape(-1, model_width)
     (gu_blocks,) = gather_blocks([jnp.concatenate([w_gate, w_up], axis=1)])
     full_gu = gu_blocks.reshape(n_group * own_rows, 2 * ff_width)
     (down_blocks,) = gather_blocks([w_down])

time: 584 us -> 565 us (0.967)
  waiting for transfers between devices: 245 us -> 219 us
  local copies, waits for them, and re-layouts: 53 us -> 59.6 us
    all_gather x4 -> x3, waiting for transfers between devices: 79.1 us -> 51.5 us  [gather_blocks(): gathered = lax.all_gather(packed, GROUP, axis=0, tiled=False)]
  transfers between devices with their start and end apart: 22 -> 21, of which waited for: 11 -> 10; matrix products, arithmetic and copies ran while one was open for 38% -> 40% of each run, Pallas kernels for 10% -> 10%
where the time goes in v14:
time: 565 us; the launch traced here: 561 us
  waiting for transfers between devices  219 us (39%)
  matrix products  106 us (19%)
  other arithmetic  74.9 us (13%)
  local copies, waits for them, and re-layouts  59.6 us (11%)
  Pallas kernels  55.4 us (10%)
  starting transfers between devices  30.5 us (5%)
  between operations  15.8 us (3%)
    psum x1, waiting for transfers between devices, scatter_blocks(): lax.psum(summed, 'rep')  59.6 us
    all_gather x3, waiting for transfers between devices, gather_blocks(): gathered = lax.all_gather(packed, GROUP, axis=0, tiled=False)  51.5 us
    reduce_scatter x3, waiting for transfers between devices, scatter_blocks(): summed = lax.psum_scatter(packed, GROUP, scatter_dimension=0, tiled=True)  38.1 us
    ppermute x3, waiting for transfers between devices, rep_chain(): sent_out = lax.ppermute(total, 'rep', [(1, 0), (2, 3)])  32.8 us
    pallas_call x2, Pallas kernels, block_backward(): pl.pallas_call(kernel, grid=(n_slots, n_heads // 2), in_specs=[q_spec, k_...  32.7 us
    ppermute x1, waiting for transfers between devices, shards(): other_tokens = lax.ppermute(tokens, 'ctx', [(0, 1), (1, 0)])  28.6 us
    pallas_call x1, Pallas kernels, block_forward(): pl.pallas_call(kernel, grid=(n_slots, n_heads // 2), in_specs=[q_spec, k_...  22.6 us
    dot_general x2, matrix products, project(): jnp.einsum('srd,de->sre', chunk_low, full_qkv, preferred_element_type=jnp...  14.1 us
  transfers between devices with their start and end apart: 21, of which 10 were waited for; matrix products, arithmetic and copies ran while one was open for 40% of the time, Pallas kernels for 10%

profile of v14, /device:TPU:0, one launch (start us, length us, event | category | flops | bytes accessed | tf_op | source)
XLA Modules:
  0.0 561.2 jit_solution(5034984361538680940)
XLA Ops:
  21.8 28.6 %collective-permute-done = bf16[1,512,1024]{2,1,0:T(8,128)(2,1)S(1)} collective-permute-done((bf16[1,512,1024]{2,1,0:T(8,128)(2,1)S(1)}, bf16[1,512,1024]{2,1,0:T(8,128)(2,1)S(1)}, u32[]{:S(2)}, u32[]{:S(2)}) %collective-permute-start) | collective-permute-done | bytes 1048608 | tf_op jit(solution)/shard_map/ppermute | solution.py:410
  50.7 45.1 %all-gather.7.cloned.1.call-done = bf16[1088,4096]{1,0:T(8,128)(2,1)} async-done(((bf16[136,4096]{1,0:T(8,128)(2,1)}), bf16[1088,4096]{1,0:T(8,128)(2,1)}) %all-gather.7.cloned.1.call-update) | async-done | bytes 8912912 | tf_op jit(solution)/shard_map/all_gather | solution.py:315
  95.7 7.8 %slice.162 = bf16[8,128,4096]{2,1,0:T(8,128)(2,1)} slice(bf16[8,136,4096]{2,1,0:T(8,128)(2,1)} %bitcast.178), slice={[0:8], [0:128], [0:4096]} | slice | bytes 16777216 | tf_op jit(solution)/shard_map/slice | solution.py:318
  104.3 5.9 %convolution_bitcast_fusion.2 = f32[1,512,3072]{2,1,0:T(8,128)S(1)} fusion(bf16[1024,4096]{1,0:T(8,128)(2,1)} %bitcast.173, bf16[1,512,1024]{2,1,0:T(8,128)(2,1)S(1)} %copy-done.12, f32[1024]{0:T(1024)S(1)} %bitcast.196, f32[512]{0:T(512)S(1)} %add_rsqrt_fusion.2), kind=kOutput, calls=%fused_computation.23 | convolution fusion | flops 3223322624 | bytes 13637632 | tf_op jit(solution)/shard_map/srd,de->sre/dot_general | solution.py:420
  121.3 8.2 %convolution_bitcast_fusion.1 = f32[1,512,3072]{2,1,0:T(8,128)} fusion(bf16[1024,4096]{1,0:T(8,128)(2,1)} %bitcast.174, bf16[1,512,1024]{2,1,0:T(8,128)(2,1)S(1)} %collective-permute-done, f32[512]{0:T(512)S(1)} %add_rsqrt_fusion.1, f32[1024]{0:T(1024)S(1)} %bitcast.197), kind=kOutput, calls=%fused_computation.22 | convolution fusion | flops 3223322624 | bytes 13637632 | tf_op jit(solution)/shard_map/srd,de->sre/dot_general | solution.py:420
  131.4 5.8 %fusion.105 = (f32[1,512,1024]{2,1,0:T(8,128)}, f32[1,512,1024]{2,1,0:T(8,128)}) fusion(f32[1,512,3072]{2,1,0:T(8,128)} %convolution_bitcast_fusion.1), kind=kLoop, calls=%fused_computation.194 | loop fusion | bytes 8388608 | tf_op jit(solution)/shard_map/slice | solution.py:423
  147.5 4.7 broadcast_select_fusion.1
  154.7 22.6 %shard_map.220 = (bf16[1,512,1024]{2,1,0:T(8,128)(2,1)}, f32[1,16,512]{2,1,0:T(8,128)}) custom-call(bf16[1,512,1024]{2,1,0:T(8,128)(2,1)} %copy.91.q_ref, bf16[1,1024,1024]{2,1,0:T(8,128)(2,1)} %pad_maximum_fusion.4.k_ref, bf16[1,1024,1024]{2,1,0:T(8,128)(2,1)} %pad_maximum_fusion.5.v_ref, s32[1,512]{1,0:T(1,128)} %iota_add_fusion.1.qpos_ref, ...), custom_call_target="tpu_custom_call" | custom-call | flops 2147483648 | bytes 6291456 | tf_op jit(solution)/shard_map/pallas_call | solution.py:247
  182.2 9.5 %convolution_bitcast_fusion = f32[1,512,5632]{2,1,0:T(8,128)S(1)} fusion(bf16[1024,5632]{1,0:T(8,128)(2,1)} %all-gather.9.cloned.1.call-done, f32[1,512,1024]{2,1,0:T(8,128)S(1)} %get-tuple-element.87, f32[1024]{0:T(1024)S(1)} %bitcast.193, f32[512]{0:T(512)S(1)} %add_rsqrt_fusion), kind=kOutput, calls=%fused_computation.3 | convolution fusion | flops 5907152896 | bytes 25171968 | tf_op jit(solution)/shard_map/srd,df->srf/dot_general | solution.py:457
  191.6 4.4 copy-done
  200.7 7.8 %convolution_convert_fusion.2 = bf16[8,352,1024]{2,1,0:T(8,128)(2,1)} fusion(bf16[8,352,512]{2,1,0:T(8,128)(2,1)} %bitcast.187, bf16[1,512,1024]{2,1,0:T(8,128)(2,1)} %param.15, pred[512]{0:T(512)(128)(4,1)S(1)} %fusion.92), kind=kOutput, calls=%fused_computation.28 | convolution fusion | flops 2957246464 | bytes 9699840 | tf_op jit(solution)/shard_map/srf,srd->fd/dot_general | solution.py:473
  208.5 6.4 %all-gather.11.cloned.1.call-done = bf16[2816,1024]{1,0:T(8,128)(2,1)} async-done(((bf16[352,1024]{1,0:T(8,128)(2,1)}), bf16[2816,1024]{1,0:T(8,128)(2,1)}) %all-gather.11.cloned.1.call-update) | async-done | bytes 5767184 | tf_op jit(solution)/shard_map/all_gather | solution.py:315
  215.0 11.1 %fusion.8 = (bf16[1,512,2816]{2,1,0:T(8,128)(2,1)}, bf16[1,512,2816]{2,1,0:T(8,128)(2,1)}) fusion(f32[1,512,5632]{2,1,0:T(8,128)} %copy-done, bf16[2816,1024]{1,0:T(8,128)(2,1)} %all-gather.11.cloned.1.call-done, bf16[1,512,1024]{2,1,0:T(8,128)(2,1)S(1)} %copy-done.23, pred[512]{0:T(512)(128)(4,1)S(1)} %fusion.92), kind=kOutput, calls=%fused_computation.16 | convolution fusion | flops 2973106176 | bytes 24117760 | tf_op jit(solution)/shard_map/srd,fd->srf/dot_general | solution.py:479
  226.1 13.6 %fusion.37 = (bf16[1024]{0:T(1024)(128)(2,1)S(1)}, f32[512]{0:T(512)S(1)}, f32[512,1024]{1,0:T(8,128)S(1)}) fusion(f32[1,512,1024]{2,1,0:T(8,128)S(1)} %copy-done.16, f32[512]{0:T(512)S(1)} %add_rsqrt_fusion, f32[1024]{0:T(1024)S(1)} %bitcast.194, bf16[1024,5632]{1,0:T(8,128)(2,1)} %all-gather.9.cloned.1.call-done, ...), kind=kOutput, calls=%fused_computation.63 | convolution fusion | flops 5920258560 | bytes 21506048 | tf_op jit(solution)/shard_map/srf,df->srd/dot_general | solution.py:486
  242.4 11.5 %convolution_convert_fusion = bf16[8,128,5632]{2,1,0:T(8,128)(2,1)} fusion(bf16[8,128,512]{2,1,0:T(8,128)(2,1)S(1)} %bitcast.190, bf16[1,512,2816]{2,1,0:T(8,128)(2,1)} %get-tuple-element.40, bf16[1,512,2816]{2,1,0:T(8,128)(2,1)} %get-tuple-element.39), kind=kOutput, calls=%fused_computation.2 | convolution fusion | flops 5922881536 | bytes 18350080 | tf_op jit(solution)/shard_map/srd,srf->df/dot_general | solution.py:483
  265.3 4.9 fusion.52
  277.8 16.3 %shard_map.221 = (f32[1,512,1024]{2,1,0:T(8,128)}, f32[1,512,1024]{2,1,0:T(8,128)}, f32[1,512,1024]{2,1,0:T(8,128)}) custom-call(bf16[1,512,1024]{2,1,0:T(8,128)(2,1)} %copy.91.q_ref, bf16[1,512,1024]{2,1,0:T(8,128)(2,1)} %copy-done.1, bf16[1,512,1024]{2,1,0:T(8,128)(2,1)} %copy-done.11, bf16[1,512,1024]{2,1,0:T(8,128)(2,1)} %bitcast.189, ...), custom_call_target="tpu_custom_call" | custom-call | flops 2684354560 | bytes 10485760 | tf_op jit(solution)/shard_map/pallas_call | solution.py:285
  294.1 5.0 collective-permute-done.4
  302.5 16.5 %shard_map.222 = (f32[1,512,1024]{2,1,0:T(8,128)}, f32[1,512,1024]{2,1,0:T(8,128)}, f32[1,512,1024]{2,1,0:T(8,128)}) custom-call(bf16[1,512,1024]{2,1,0:T(8,128)(2,1)} %broadcast_select_fusion.3.q_ref, bf16[1,512,1024]{2,1,0:T(8,128)(2,1)} %broadcast_select_fusion.2.k_ref, bf16[1,512,1024]{2,1,0:T(8,128)(2,1)} %get-tuple-element.34.v_ref, ...), custom_call_target="tpu_custom_call" | custom-call | flops 2684354560 | bytes 10485760 | tf_op jit(solution)/shard_map/pallas_call | solution.py:285
  322.6 4.4 select_add_fusion
  334.4 4.6 fusion.102
  339.0 7.9 %fusion.31 = (bf16[1024]{0:T(1024)(128)(2,1)S(1)}, f32[512]{0:T(512)S(1)}, f32[512,1024]{1,0:T(8,128)}) fusion(bf16[1,512,1024]{2,1,0:T(8,128)(2,1)S(1)} %copy-done.14, f32[512]{0:T(512)S(1)} %add_rsqrt_fusion.2, f32[1024]{0:T(1024)S(1)} %bitcast.198, bf16[1024,4096]{1,0:T(8,128)(2,1)} %bitcast.177, bf16[1,512,1024]{2,1,0:T(8,128)(2,1)S(1)} %get-tuple-element.32, ...), kind=kOutput, calls=%fused_computation.52 | convolution fusion | flops 3234331136 | bytes 12593152 | tf_op jit(solution)/shard_map/sre,de->srd/dot_general | solution.py:547
  347.1 7.6 %convolution_convert_fusion.1 = bf16[1024,3072]{1,0:T(8,128)(2,1)} fusion(bf16[1,512,1024]{2,1,0:T(8,128)(2,1)S(1)} %get-tuple-element.32, bf16[1,512,1024]{2,1,0:T(8,128)(2,1)} %copy-done.27, bf16[1,512,1024]{2,1,0:T(8,128)(2,1)S(1)} %copy-done.28, bf16[1,512,1024]{2,1,0:T(8,128)(2,1)S(1)} %copy-done.14, f32[1024]{0:T(1024)S(1)} %bitcast.199, ...), kind=kOutput, calls=%fused_computation.21 | convolution fusion | flops 3235905536 | bytes 10491904 | tf_op jit(solution)/shard_map/srd,sre->de/dot_general | solution.py:546
  354.6 7.1 %pad_maximum_fusion = bf16[1024,4096]{1,0:T(8,128)(2,1)} fusion(bf16[1024,1024]{1,0:T(8,128)(2,1)S(1)} %copy-done.22, bf16[1024,3072]{1,0:T(8,128)(2,1)} %convolution_convert_fusion.1), kind=kLoop, calls=%fused_computation.5 | loop fusion | flops 16777216 | bytes 16777216 | tf_op jit(solution)/shard_map/concatenate | solution.py:552
  361.7 8.4 %fusion.1 = bf16[8,136,4096]{2,1,0:T(8,128)(2,1)} fusion(bf16[8,1,4096]{2,1,0:T(2,128)(2,1)S(1)} %copy.112, bf16[8,128,4096]{2,1,0:T(8,128)(2,1)} %bitcast.163), kind=kLoop, calls=%fused_computation.4 | loop fusion | flops 26738688 | bytes 17367040 | tf_op jit(solution)/shard_map/concatenate | solution.py:347
  370.2 3.6 collective-permute-start.11
  373.8 11.7 %fusion.42 = bf16[1,512,1024]{2,1,0:T(8,128)(2,1)} fusion(f32[1,512,1024]{2,1,0:T(8,128)S(1)} %copy-done.17, bf16[2816,1024]{1,0:T(8,128)(2,1)} %all-gather.11.cloned.1.call-done, f32[1,512,5632]{2,1,0:T(8,128)} %copy-done, pred[512]{0:T(512)(128)(4,1)S(1)} %fusion.92), kind=kOutput, calls=%fused_computation.71 | convolution fusion | flops 2963013632 | bytes 20447744 | tf_op jit(solution)/shard_map/srf,fd->srd/dot_general | solution.py:462
  393.1 7.0 %collective-permute-start.5 = (bf16[1,64,5632]{2,1,0:T(8,128)(2,1)}, bf16[1,64,5632]{2,1,0:T(8,128)(2,1)}, u32[]{:S(2)}, u32[]{:S(2)}) collective-permute-start(bf16[1,64,5632]{2,1,0:T(8,128)(2,1)} %get-tuple-element.67), channel_id=1, source_target_pairs={{0,8},{24,16},{1,9},{25,17},{2,10},{26,18},{3,11},{27,19},{4,12},{... | collective-permute-start | bytes 2162696 | tf_op jit(solution)/shard_map/ppermute | solution.py:325
  407.5 38.1 %reduce-scatter.4.cloned.1.call-done = bf16[1,136,4096]{2,1,0:T(8,128)(2,1)} async-done(((bf16[8,136,4096]{2,1,0:T(8,128)(2,1)}), bf16[1,136,4096]{2,1,0:T(8,128)(2,1)}) %reduce-scatter.4.cloned.1.call-update) | async-done | bytes 1114128 | tf_op jit(solution)/shard_map/reduce_scatter | solution.py:348
  451.2 59.6 %all-reduce.6.cloned.1.call-done = bf16[136,4096]{1,0:T(8,128)(2,1)} async-done(((bf16[136,4096]{1,0:T(8,128)(2,1)}), bf16[136,4096]{1,0:T(8,128)(2,1)}) %all-reduce.6.cloned.1.call-update) | async-done | bytes 1114128 | tf_op jit(solution)/shard_map/psum | solution.py:349
  519.1 18.8 %collective-permute-done.10 = bf16[1,64,5632]{2,1,0:T(8,128)(2,1)S(1)} collective-permute-done((bf16[1,64,5632]{2,1,0:T(8,128)(2,1)S(1)}, bf16[1,64,5632]{2,1,0:T(8,128)(2,1)S(1)}, u32[]{:S(2)}, u32[]{:S(2)}) %collective-permute-start.10) | collective-permute-done | bytes 720928 | tf_op jit(solution)/shard_map/ppermute | solution.py:329
  538.0 14.0 %collective-permute-done.7 = bf16[1,64,5632]{2,1,0:T(8,128)(2,1)S(1)} collective-permute-done((bf16[1,64,5632]{2,1,0:T(8,128)(2,1)S(1)}, bf16[1,64,5632]{2,1,0:T(8,128)(2,1)S(1)}, u32[]{:S(2)}, u32[]{:S(2)}) %collective-permute-start.7) | collective-permute-done | bytes 720928 | tf_op jit(solution)/shard_map/ppermute | solution.py:329
  (192 shorter events, 117.0 us)
Async XLA Ops:
  7.2 88.5 %all-gather.7.cloned.1.call-start = ((), (), s32[]{:S(2)}) async-start(), calls=%async_computation.7 | async-start | bytes 10027008 | tf_op jit(solution)/shard_map/all_gather | solution.py:315
  10.4 170.5 %all-gather.9.cloned.1.call-start = ((), (), s32[]{:S(2)}) async-start(), calls=%async_computation.8 | async-start | bytes 12976128 | tf_op jit(solution)/shard_map/all_gather | solution.py:315
  11.7 203.3 %all-gather.11.cloned.1.call-start = ((), (), s32[]{:S(2)}) async-start(), calls=%async_computation.9 | async-start | bytes 6488064 | tf_op jit(solution)/shard_map/all_gather | solution.py:315
  11.9 38.5 %collective-permute-start = (bf16[1,512,1024]{2,1,0:T(8,128)(2,1)S(1)}, bf16[1,512,1024]{2,1,0:T(8,128)(2,1)S(1)}, u32[]{:S(2)}, u32[]{:S(2)}) collective-permute-start(bf16[1,512,1024]{2,1,0:T(8,128)(2,1)S(1)} %copy-done.12), channel_id=1, source_target_pairs={{0,1},{1,0},{2,3},{3,2},{4,5},{5,4},{6,7},{7,6},{8,9},{9,8},{10,11... | collective-permute-start | bytes 3145736 | tf_op jit(solution)/shard_map/ppermute | solution.py:410
  14.9 132.6 %collective-permute-start.1 = (bf16[1,512,1024]{2,1,0:T(8,128)(2,1)}, bf16[1,512,1024]{2,1,0:T(8,128)(2,1)}, u32[]{:S(2)}, u32[]{:S(2)}) collective-permute-start(bf16[1,512,1024]{2,1,0:T(8,128)(2,1)} %param.14), channel_id=1, source_target_pairs={{0,1},{2,3},{4,5},{6,7},{8,9},{10,11},{12,13},{14,15},{16,17},{18,... | collective-permute-start | bytes 3145736 | tf_op jit(solution)/shard_map/ppermute | solution.py:411
  17.8 352.4 %reduce-scatter.8.cloned.1.call-start = ((), (), s32[]{:S(2)}) async-start(), calls=%async_computation.6 | async-start | bytes 6488064 | tf_op jit(solution)/shard_map/reduce_scatter | solution.py:348
  131.4 14.4 %copy-start.1 = (bf16[1,512,1024]{2,1,0:T(8,128)(2,1)}, bf16[1,512,1024]{2,1,0:T(8,128)(2,1)S(1)}, u32[]{:S(2)}) copy-start(bf16[1,512,1024]{2,1,0:T(8,128)(2,1)S(1)} %copy.87.k_ref) | copy-start | bytes 3145732
  154.7 22.6 %copy-start.13 = (bf16[1,512,1024]{2,1,0:T(8,128)(2,1)S(1)}, bf16[1,512,1024]{2,1,0:T(8,128)(2,1)}, u32[]{:S(2)}) copy-start(bf16[1,512,1024]{2,1,0:T(8,128)(2,1)} %param.13) | copy-start | bytes 3145732
  208.5 17.6 %copy-start.16 = (f32[1,512,1024]{2,1,0:T(8,128)S(1)}, f32[1,512,1024]{2,1,0:T(8,128)}, u32[]{:S(2)}) copy-start(f32[1,512,1024]{2,1,0:T(8,128)} %copy-done.15) | copy-start | bytes 6291460
  208.5 181.9 %reduce-scatter.6.cloned.1.call-start = ((), (), s32[]{:S(2)}) async-start(), calls=%async_computation.5 | async-start | bytes 12976128 | tf_op jit(solution)/shard_map/reduce_scatter | solution.py:348
  226.0 13.6 %copy-start.24 = (bf16[1,512,1024]{2,1,0:T(8,128)(2,1)S(1)}, bf16[1,512,1024]{2,1,0:T(8,128)(2,1)}, u32[]{:S(2)}) copy-start(bf16[1,512,1024]{2,1,0:T(8,128)(2,1)} %param.15) | copy-start | bytes 3145732
  254.0 191.6 %reduce-scatter.4.cloned.1.call-start = ((), (), s32[]{:S(2)}) async-start(), calls=%async_computation.3 | async-start | bytes 10027008 | tf_op jit(solution)/shard_map/reduce_scatter | solution.py:348
  258.8 5.9 %collective-permute-start.3 = (f32[1,16,512]{2,1,0:T(8,128)S(1)}, f32[1,16,512]{2,1,0:T(8,128)S(1)}, u32[]{:S(2)}, u32[]{:S(2)}) collective-permute-start(f32[1,16,512]{2,1,0:T(8,128)S(1)} %copy-done.34), channel_id=1, source_target_pairs={{1,0},{3,2},{5,4},{7,6},{9,8},{11,10},{13,12},{15,14},{17,16},{19,... | collective-permute-start | bytes 98312 | tf_op jit(solution)/shard_map/ppermute | solution.py:505
  271.8 28.0 %collective-permute-start.2 = (bf16[1,512,16,64]{1,3,2,0:T(8,128)(2,1)S(1)}, bf16[1,512,16,64]{1,3,2,0:T(8,128)(2,1)}, u32[]{:S(2)}, u32[]{:S(2)}) collective-permute-start(bf16[1,512,16,64]{1,3,2,0:T(8,128)(2,1)S(1)} %bitcast.164), channel_id=1, source_target_pairs={{1,0},{3,2},{5,4},{7,6},{9,8},{11,10},{13,12},{15,14},{17,16},{19,... | collective-permute-start | bytes 3145736 | tf_op jit(solution)/shard_map/ppermute | solution.py:505
  273.7 25.4 %collective-permute-start.4 = (f32[1,16,512]{2,1,0:T(8,128)S(1)}, f32[1,16,512]{2,1,0:T(8,128)S(1)}, u32[]{:S(2)}, u32[]{:S(2)}) collective-permute-start(f32[1,16,512]{2,1,0:T(8,128)S(1)} %bitcast.191), channel_id=1, source_target_pairs={{1,0},{3,2},{5,4},{7,6},{9,8},{11,10},{13,12},{15,14},{17,16},{19,... | collective-permute-start | bytes 98312 | tf_op jit(solution)/shard_map/ppermute | solution.py:505
  277.8 21.3 %copy-start.33 = (f32[512,16]{0,1:T(8,128)S(1)}, f32[512,16]{0,1:T(8,128)}, u32[]{:S(2)}) copy-start(f32[512,16]{0,1:T(8,128)} %copy-done.32) | copy-start | bytes 98308
  302.5 16.5 %copy-start.18 = (f32[1,512,1024]{2,1,0:T(8,128)S(1)}, f32[1,512,1024]{2,1,0:T(8,128)}, u32[]{:S(2)}) copy-start(f32[1,512,1024]{2,1,0:T(8,128)} %get-tuple-element.22) | copy-start | bytes 6291460
  347.1 7.6 %copy-start.22 = (bf16[1024,1024]{1,0:T(8,128)(2,1)S(1)}, bf16[1024,1024]{1,0:T(8,128)(2,1)}, u32[]{:S(2)}) copy-start(bf16[1024,1024]{1,0:T(8,128)(2,1)} %convolution_convert_fusion.3) | copy-start | bytes 6291460
  370.1 140.7 %all-reduce.6.cloned.1.call-start = ((), (), s32[]{:S(2)}) async-start(), calls=%async_computation.4 | async-start | bytes 2228224 | tf_op jit(solution)/shard_map/psum | solution.py:349
  370.2 17.6 %copy-start.29 = (bf16[1,352,1024]{2,1,0:T(8,128)(2,1)S(1)}, bf16[1,352,1024]{2,1,0:T(8,128)(2,1)}, u32[]{:S(2)}) copy-start(bf16[1,352,1024]{2,1,0:T(8,128)(2,1)} %reduce-scatter.8.cloned.1.call-done) | copy-start | bytes 2162692
  370.2 17.6 %collective-permute-start.11 = (bf16[1,352,1024]{2,1,0:T(8,128)(2,1)}, bf16[1,352,1024]{2,1,0:T(8,128)(2,1)S(1)}, u32[]{:S(2)}, u32[]{:S(2)}) collective-permute-start(bf16[1,352,1024]{2,1,0:T(8,128)(2,1)} %reduce-scatter.8.cloned.1.call-done), channel_id=1, source_target_pairs={{0,8},{24,16},{1,9},{25,17},{2,10},{26,18},{3,11},{27,19},{4,12},{... | collective-permute-start | bytes 2162696 | tf_op jit(solution)/shard_map/ppermute | solution.py:325
  385.5 17.0 %copy-start.7 = (f32[1,512,1024]{2,1,0:T(8,128)S(1)}, f32[1,512,1024]{2,1,0:T(8,128)}, u32[]{:S(2)}) copy-start(f32[1,512,1024]{2,1,0:T(8,128)} %get-tuple-element.64) | copy-start | bytes 6291460
  388.9 15.6 %collective-permute-start.12 = (bf16[1,352,1024]{2,1,0:T(8,128)(2,1)}, bf16[1,352,1024]{2,1,0:T(8,128)(2,1)}, u32[]{:S(2)}, u32[]{:S(2)}) collective-permute-start(bf16[1,352,1024]{2,1,0:T(8,128)(2,1)} %add_convert_fusion.2), channel_id=1, source_target_pairs={{8,16},{16,8},{9,17},{17,9},{10,18},{18,10},{11,19},{19,11},{12,20... | collective-permute-start | bytes 2162696 | tf_op jit(solution)/shard_map/ppermute | solution.py:327
  390.4 12.1 %copy-start.21 = (f32[512,1024]{1,0:T(8,128)S(1)}, f32[512,1024]{1,0:T(8,128)}, u32[]{:S(2)}) copy-start(f32[512,1024]{1,0:T(8,128)} %get-tuple-element.89) | copy-start | bytes 6291460
  393.1 52.5 %collective-permute-start.5 = (bf16[1,64,5632]{2,1,0:T(8,128)(2,1)}, bf16[1,64,5632]{2,1,0:T(8,128)(2,1)}, u32[]{:S(2)}, u32[]{:S(2)}) collective-permute-start(bf16[1,64,5632]{2,1,0:T(8,128)(2,1)} %get-tuple-element.67), channel_id=1, source_target_pairs={{0,8},{24,16},{1,9},{25,17},{2,10},{26,18},{3,11},{27,19},{4,12},{... | collective-permute-start | bytes 2162696 | tf_op jit(solution)/shard_map/ppermute | solution.py:325
  400.1 45.5 %collective-permute-start.8 = (bf16[1,64,5632]{2,1,0:T(8,128)(2,1)}, bf16[1,64,5632]{2,1,0:T(8,128)(2,1)}, u32[]{:S(2)}, u32[]{:S(2)}) collective-permute-start(bf16[1,64,5632]{2,1,0:T(8,128)(2,1)} %get-tuple-element.68), channel_id=1, source_target_pairs={{0,8},{24,16},{1,9},{25,17},{2,10},{26,18},{3,11},{27,19},{4,12},{... | collective-permute-start | bytes 2162696 | tf_op jit(solution)/shard_map/ppermute | solution.py:325
  404.5 41.2 %copy-start.9 = (bf16[1,128,5632]{2,1,0:T(8,128)(2,1)S(1)}, bf16[1,128,5632]{2,1,0:T(8,128)(2,1)}, u32[]{:S(2)}) copy-start(bf16[1,128,5632]{2,1,0:T(8,128)(2,1)} %reduce-scatter.6.cloned.1.call-done) | copy-start | bytes 4325380
  406.2 42.7 %collective-permute-start.13 = (bf16[1,352,1024]{2,1,0:T(8,128)(2,1)S(1)}, bf16[1,352,1024]{2,1,0:T(8,128)(2,1)}, u32[]{:S(2)}, u32[]{:S(2)}) collective-permute-start(bf16[1,352,1024]{2,1,0:T(8,128)(2,1)S(1)} %add_convert_fusion.1), channel_id=1, source_target_pairs={{8,0},{16,24},{9,1},{17,25},{10,2},{18,26},{11,3},{19,27},{12,4},{... | collective-permute-start | bytes 2162696 | tf_op jit(solution)/shard_map/ppermute | solution.py:329
  448.2 66.9 %collective-permute-start.9 = (bf16[1,64,5632]{2,1,0:T(8,128)(2,1)}, bf16[1,64,5632]{2,1,0:T(8,128)(2,1)S(1)}, u32[]{:S(2)}, u32[]{:S(2)}) collective-permute-start(bf16[1,64,5632]{2,1,0:T(8,128)(2,1)} %get-tuple-element.66), channel_id=1, source_target_pairs={{8,16},{16,8},{9,17},{17,9},{10,18},{18,10},{11,19},{19,11},{12,20... | collective-permute-start | bytes 2162696 | tf_op jit(solution)/shard_map/ppermute | solution.py:327
  514.3 3.3 collective-permute-start.6
  516.3 21.6 %collective-permute-start.10 = (bf16[1,64,5632]{2,1,0:T(8,128)(2,1)S(1)}, bf16[1,64,5632]{2,1,0:T(8,128)(2,1)S(1)}, u32[]{:S(2)}, u32[]{:S(2)}) collective-permute-start(bf16[1,64,5632]{2,1,0:T(8,128)(2,1)S(1)} %add_convert_fusion.3), channel_id=1, source_target_pairs={{8,0},{16,24},{9,1},{17,25},{10,2},{18,26},{11,3},{19,27},{12,4},{... | collective-permute-start | bytes 2162696 | tf_op jit(solution)/shard_map/ppermute | solution.py:329
  517.8 34.2 %collective-permute-start.7 = (bf16[1,64,5632]{2,1,0:T(8,128)(2,1)S(1)}, bf16[1,64,5632]{2,1,0:T(8,128)(2,1)S(1)}, u32[]{:S(2)}, u32[]{:S(2)}) collective-permute-start(bf16[1,64,5632]{2,1,0:T(8,128)(2,1)S(1)} %add_convert_fusion.5), channel_id=1, source_target_pairs={{8,0},{16,24},{9,1},{17,25},{10,2},{18,26},{11,3},{19,27},{12,4},{... | collective-permute-start | bytes 2162696 | tf_op jit(solution)/shard_map/ppermute | solution.py:329
  (24 other events, 78.5 us)
Sparse Core Ops, SparseCore 0:
  10.5 85.2 all-gather.6
  98.2 71.6 all-gather.8
  171.8 43.1 all-gather.10
  218.3 59.2 reduce-scatter.7
  281.0 87.0 reduce-scatter.5
  371.5 74.0 reduce-scatter.3
  448.0 62.8 all-reduce.5

commit v15 on v14

--- a/solution.py
+++ b/solution.py
@@ -386,12 +386,14 @@
     attn_width = w_query.shape[1]
     qkv_width = 3 * attn_width
     qkvo_width = qkv_width + model_width
-    (qkvo_blocks, gain_rows) = gather_blocks(
+    (qkvo_blocks, gain_rows, down_wide) = gather_blocks(
         [
             jnp.concatenate([w_query, w_key, w_value, w_out], axis=1),
             gain_block(gain_attn, gain_mlp, qkvo_width),
+            w_down.reshape(-1, qkvo_width),
         ]
     )
+    full_down = down_wide.reshape(-1, model_width)
     full_qkvo = qkvo_blocks.reshape(n_group * own_rows, qkvo_width)
     full_qkv = full_qkvo[:, :qkv_width]
     full_out = full_qkvo[:, qkv_width:]
@@ -399,8 +401,6 @@
     full_gain_mlp = gain_rows[:, 0, own_rows : 2 * own_rows].reshape(-1)
     (gu_blocks,) = gather_blocks([jnp.concatenate([w_gate, w_up], axis=1)])
     full_gu = gu_blocks.reshape(n_group * own_rows, 2 * ff_width)
-    (down_blocks,) = gather_blocks([w_down])
-    full_down = down_blocks.reshape(-1, model_width)
     ctx_index = lax.axis_index("ctx")
     q_pos = ctx_index * slot_rows + jnp.arange(slot_rows)
     live_rows = q_pos[None, :] < lengths[:, None]

time: 565 us -> 602 us (1.065)
  local copies, waits for them, and re-layouts: 59.6 us -> 81 us
  waiting for transfers between devices: 219 us -> 233 us
    all_gather x3 -> x2, waiting for transfers between devices: 51.5 us -> 64.8 us  [gather_blocks(): gathered = lax.all_gather(packed, GROUP, axis=0, tiled=False)]
    reshape x0 -> x2, local copies, waits for them, and re-layouts: none -> 11.9 us  [the longest x1 10.4 us: shards(): full_down = down_wide.reshape(-1, model_width)]
    slice x1 -> x2, local copies, waits for them, and re-layouts: 7.82 us -> 13.7 us  [gather_blocks(): fulls.append(gathered[:, offset:offset + piece.shape[0], :])]
  transfers between devices with their start and end apart: 21 -> 20, of which waited for: 10 -> 9; matrix products, arithmetic and copies ran while one was open for 40% -> 37% of each run, Pallas kernels for 10% -> 9%
where the time goes in v15:
time: 602 us; the launch traced here: 597 us
  waiting for transfers between devices  233 us (39%)
  matrix products  104 us (17%)
  local copies, waits for them, and re-layouts  81 us (13%)
  other arithmetic  76 us (13%)
  Pallas kernels  56 us (9%)
  starting transfers between devices  31.1 us (5%)
  between operations  15.8 us (3%)
    all_gather x2, waiting for transfers between devices, gather_blocks(): gathered = lax.all_gather(packed, GROUP, axis=0, tiled=False)  64.8 us
    psum x1, waiting for transfers between devices, scatter_blocks(): lax.psum(summed, 'rep')  59.5 us
    reduce_scatter x3, waiting for transfers between devices, scatter_blocks(): summed = lax.psum_scatter(packed, GROUP, scatter_dimension=0, tiled=True)  37.7 us
    pallas_call x2, Pallas kernels, block_backward(): pl.pallas_call(kernel, grid=(n_slots, n_heads // 2), in_specs=[q_spec, k_...  33.4 us
    ppermute x3, waiting for transfers between devices, rep_chain(): sent_out = lax.ppermute(total, 'rep', [(1, 0), (2, 3)])  32.8 us
    ppermute x1, waiting for transfers between devices, shards(): other_tokens = lax.ppermute(tokens, 'ctx', [(0, 1), (1, 0)])  32.2 us
    pallas_call x1, Pallas kernels, block_forward(): pl.pallas_call(kernel, grid=(n_slots, n_heads // 2), in_specs=[q_spec, k_...  22.6 us
    dot_general x2, matrix products, project(): jnp.einsum('srd,de->sre', chunk_low, full_qkv, preferred_element_type=jnp...  14.1 us
  transfers between devices with their start and end apart: 20, of which 9 were waited for; matrix products, arithmetic and copies ran while one was open for 37% of the time, Pallas kernels for 9%

profile of v15, /device:TPU:0, one launch (start us, length us, event | category | flops | bytes accessed | tf_op | source)
XLA Modules:
  0.0 596.9 jit_solution(9289989566787762821)
XLA Ops:
  23.8 32.2 %collective-permute-done = bf16[1,512,1024]{2,1,0:T(8,128)(2,1)S(1)} collective-permute-done((bf16[1,512,1024]{2,1,0:T(8,128)(2,1)S(1)}, bf16[1,512,1024]{2,1,0:T(8,128)(2,1)S(1)}, u32[]{:S(2)}, u32[]{:S(2)}) %collective-permute-start) | collective-permute-done | bytes 1048608 | tf_op jit(solution)/shard_map/ppermute | solution.py:410
  56.3 64.7 %all-gather.5.cloned.1.call-done = bf16[1792,4096]{1,0:T(8,128)(2,1)} async-done(((bf16[224,4096]{1,0:T(8,128)(2,1)}), bf16[1792,4096]{1,0:T(8,128)(2,1)}) %all-gather.5.cloned.1.call-update) | async-done | bytes 14680080 | tf_op jit(solution)/shard_map/all_gather | solution.py:315
  121.1 7.8 %slice.166 = bf16[8,128,4096]{2,1,0:T(8,128)(2,1)} slice(bf16[8,224,4096]{2,1,0:T(8,128)(2,1)} %bitcast.164), slice={[0:8], [0:128], [0:4096]} | slice | bytes 16777216 | tf_op jit(solution)/shard_map/slice | solution.py:318
  129.6 5.9 convolution_bitcast_fusion.2
  146.7 8.2 %convolution_bitcast_fusion.1 = f32[1,512,3072]{2,1,0:T(8,128)} fusion(bf16[1024,4096]{1,0:T(8,128)(2,1)} %bitcast.177, bf16[1,512,1024]{2,1,0:T(8,128)(2,1)S(1)} %collective-permute-done, f32[512]{0:T(512)S(1)} %add_rsqrt_fusion.1, f32[1024]{0:T(1024)S(1)} %bitcast.198), kind=kOutput, calls=%fused_computation.24 | convolution fusion | flops 3223322624 | bytes 13637632 | tf_op jit(solution)/shard_map/srd,de->sre/dot_general | solution.py:420
  156.8 6.0 %fusion.107 = (f32[1,512,1024]{2,1,0:T(8,128)}, f32[1,512,1024]{2,1,0:T(8,128)}) fusion(f32[1,512,3072]{2,1,0:T(8,128)} %convolution_bitcast_fusion.1), kind=kLoop, calls=%fused_computation.197 | loop fusion | bytes 8388608 | tf_op jit(solution)/shard_map/slice | solution.py:423
  173.2 4.7 broadcast_select_fusion.1
  180.4 22.6 %shard_map.220 = (bf16[1,512,1024]{2,1,0:T(8,128)(2,1)}, f32[1,16,512]{2,1,0:T(8,128)}) custom-call(bf16[1,512,1024]{2,1,0:T(8,128)(2,1)} %copy.91.q_ref, bf16[1,1024,1024]{2,1,0:T(8,128)(2,1)} %pad_maximum_fusion.4.k_ref, bf16[1,1024,1024]{2,1,0:T(8,128)(2,1)} %pad_maximum_fusion.5.v_ref, s32[1,512]{1,0:T(1,128)} %iota_add_fusion.1.qpos_ref, ...), custom_call_target="tpu_custom_call" | custom-call | flops 2147483648 | bytes 6291456 | tf_op jit(solution)/shard_map/pallas_call | solution.py:247
  207.6 9.5 %convolution_bitcast_fusion = f32[1,512,5632]{2,1,0:T(8,128)S(1)} fusion(bf16[1024,5632]{1,0:T(8,128)(2,1)} %all-gather.7.cloned.1.call-done, f32[1,512,1024]{2,1,0:T(8,128)S(1)} %get-tuple-element.87, f32[1024]{0:T(1024)S(1)} %bitcast.194, f32[512]{0:T(512)S(1)} %add_rsqrt_fusion), kind=kOutput, calls=%fused_computation.3 | convolution fusion | flops 5907152896 | bytes 25171968 | tf_op jit(solution)/shard_map/srd,df->srf/dot_general | solution.py:457
  217.1 4.3 copy-done
  226.0 7.7 %convolution_convert_fusion.2 = bf16[8,352,1024]{2,1,0:T(8,128)(2,1)} fusion(bf16[8,352,512]{2,1,0:T(8,128)(2,1)} %bitcast.188, bf16[1,512,1024]{2,1,0:T(8,128)(2,1)} %param.15, pred[512]{0:T(512)(128)(4,1)S(1)} %fusion.94), kind=kOutput, calls=%fused_computation.32 | convolution fusion | flops 2957246464 | bytes 9699840 | tf_op jit(solution)/shard_map/srf,srd->fd/dot_general | solution.py:473
  233.8 5.9 slice.183
  239.7 10.4 %reshape.782 = bf16[2816,1024]{1,0:T(8,128)(2,1)} reshape(bf16[8,88,4096]{2,1,0:T(8,128)(2,1)} %slice.183) | data formatting | bytes 11534336 | tf_op jit(solution)/shard_map/reshape | solution.py:396
  250.1 12.0 %fusion.8 = (bf16[1,512,2816]{2,1,0:T(8,128)(2,1)}, bf16[1,512,2816]{2,1,0:T(8,128)(2,1)}) fusion(f32[1,512,5632]{2,1,0:T(8,128)} %copy-done, bf16[2816,1024]{1,0:T(8,128)(2,1)} %reshape.782, bf16[1,512,1024]{2,1,0:T(8,128)(2,1)S(1)} %copy-done.25, pred[512]{0:T(512)(128)(4,1)S(1)} %fusion.94), kind=kOutput, calls=%fused_computation.16 | convolution fusion | flops 2973106176 | bytes 24117760 | tf_op jit(solution)/shard_map/srd,fd->srf/dot_general | solution.py:479
  262.1 13.0 %fusion.38 = (bf16[1024]{0:T(1024)(128)(2,1)S(1)}, f32[512]{0:T(512)S(1)}, f32[512,1024]{1,0:T(8,128)}) fusion(f32[1,512,1024]{2,1,0:T(8,128)S(1)} %copy-done.18, f32[512]{0:T(512)S(1)} %add_rsqrt_fusion, f32[1024]{0:T(1024)S(1)} %bitcast.195, bf16[1024,5632]{1,0:T(8,128)(2,1)} %all-gather.7.cloned.1.call-done, ...), kind=kOutput, calls=%fused_computation.65 | convolution fusion | flops 5920258560 | bytes 21506048 | tf_op jit(solution)/shard_map/srf,df->srd/dot_general | solution.py:486
  279.1 11.8 %convolution_convert_fusion = bf16[8,128,5632]{2,1,0:T(8,128)(2,1)} fusion(bf16[8,128,512]{2,1,0:T(8,128)(2,1)} %bitcast.191, bf16[1,512,2816]{2,1,0:T(8,128)(2,1)} %get-tuple-element.40, bf16[1,512,2816]{2,1,0:T(8,128)(2,1)} %get-tuple-element.39), kind=kOutput, calls=%fused_computation.2 | convolution fusion | flops 5922881536 | bytes 18350080 | tf_op jit(solution)/shard_map/srd,srf->df/dot_general | solution.py:483
  314.9 16.7 %shard_map.221 = (f32[1,512,1024]{2,1,0:T(8,128)}, f32[1,512,1024]{2,1,0:T(8,128)}, f32[1,512,1024]{2,1,0:T(8,128)}) custom-call(bf16[1,512,1024]{2,1,0:T(8,128)(2,1)} %copy.91.q_ref, bf16[1,512,1024]{2,1,0:T(8,128)(2,1)} %copy-done.1, bf16[1,512,1024]{2,1,0:T(8,128)(2,1)} %copy-done.12, bf16[1,512,1024]{2,1,0:T(8,128)(2,1)} %bitcast.190, ...), custom_call_target="tpu_custom_call" | custom-call | flops 2684354560 | bytes 10485760 | tf_op jit(solution)/shard_map/pallas_call | solution.py:285
  336.6 16.8 %shard_map.222 = (f32[1,512,1024]{2,1,0:T(8,128)}, f32[1,512,1024]{2,1,0:T(8,128)}, f32[1,512,1024]{2,1,0:T(8,128)}) custom-call(bf16[1,512,1024]{2,1,0:T(8,128)(2,1)} %broadcast_select_fusion.3.q_ref, bf16[1,512,1024]{2,1,0:T(8,128)(2,1)} %broadcast_select_fusion.2.k_ref, bf16[1,512,1024]{2,1,0:T(8,128)(2,1)} %get-tuple-element.34.v_ref, ...), custom_call_target="tpu_custom_call" | custom-call | flops 2684354560 | bytes 10485760 | tf_op jit(solution)/shard_map/pallas_call | solution.py:285
  357.0 4.2 select_add_fusion
  368.6 4.5 fusion.104
  373.1 7.9 %fusion.32 = (bf16[1024]{0:T(1024)(128)(2,1)S(1)}, f32[512]{0:T(512)S(1)}, f32[512,1024]{1,0:T(8,128)}) fusion(bf16[1,512,1024]{2,1,0:T(8,128)(2,1)S(1)} %copy-done.16, f32[512]{0:T(512)S(1)} %add_rsqrt_fusion.2, f32[1024]{0:T(1024)S(1)} %bitcast.199, bf16[1024,4096]{1,0:T(8,128)(2,1)} %bitcast.180, bf16[1,512,1024]{2,1,0:T(8,128)(2,1)S(1)} %get-tuple-element.32, ...), kind=kOutput, calls=%fused_computation.54 | convolution fusion | flops 3234331136 | bytes 12593152 | tf_op jit(solution)/shard_map/sre,de->srd/dot_general | solution.py:547
  381.1 7.6 %convolution_convert_fusion.1 = bf16[1024,3072]{1,0:T(8,128)(2,1)} fusion(bf16[1,512,1024]{2,1,0:T(8,128)(2,1)S(1)} %get-tuple-element.32, bf16[1,512,1024]{2,1,0:T(8,128)(2,1)} %copy-done.29, bf16[1,512,1024]{2,1,0:T(8,128)(2,1)S(1)} %copy-done.30, bf16[1,512,1024]{2,1,0:T(8,128)(2,1)S(1)} %copy-done.16, f32[1024]{0:T(1024)S(1)} %bitcast.200, ...), kind=kOutput, calls=%fused_computation.21 | convolution fusion | flops 3235905536 | bytes 10491904 | tf_op jit(solution)/shard_map/srd,sre->de/dot_general | solution.py:546
  388.7 7.1 %pad_maximum_fusion = bf16[1024,4096]{1,0:T(8,128)(2,1)} fusion(bf16[1024,1024]{1,0:T(8,128)(2,1)S(1)} %copy-done.24, bf16[1024,3072]{1,0:T(8,128)(2,1)} %convolution_convert_fusion.1), kind=kLoop, calls=%fused_computation.5 | loop fusion | flops 16777216 | bytes 16777216 | tf_op jit(solution)/shard_map/concatenate | solution.py:552
  395.8 8.3 %fusion.1 = bf16[8,136,4096]{2,1,0:T(8,128)(2,1)} fusion(bf16[8,1,4096]{2,1,0:T(2,128)(2,1)S(1)} %copy.112, bf16[8,128,4096]{2,1,0:T(8,128)(2,1)} %bitcast.163), kind=kLoop, calls=%fused_computation.4 | loop fusion | flops 26738688 | bytes 17367040 | tf_op jit(solution)/shard_map/concatenate | solution.py:347
  404.2 4.0 collective-permute-start.11
  408.2 10.9 %fusion.43 = bf16[1,512,1024]{2,1,0:T(8,128)(2,1)} fusion(f32[1,512,1024]{2,1,0:T(8,128)S(1)} %copy-done.19, bf16[2816,1024]{1,0:T(8,128)(2,1)} %reshape.782, f32[1,512,5632]{2,1,0:T(8,128)} %copy-done, pred[512]{0:T(512)(128)(4,1)S(1)} %fusion.94), kind=kOutput, calls=%fused_computation.73 | convolution fusion | flops 2963013632 | bytes 20447744 | tf_op jit(solution)/shard_map/srf,fd->srd/dot_general | solution.py:462
  419.1 4.5 collective-permute-done.11
  428.9 7.5 %collective-permute-start.5 = (bf16[1,64,5632]{2,1,0:T(8,128)(2,1)}, bf16[1,64,5632]{2,1,0:T(8,128)(2,1)}, u32[]{:S(2)}, u32[]{:S(2)}) collective-permute-start(bf16[1,64,5632]{2,1,0:T(8,128)(2,1)} %get-tuple-element.67), channel_id=1, source_target_pairs={{0,8},{24,16},{1,9},{25,17},{2,10},{26,18},{3,11},{27,19},{4,12},{... | collective-permute-start | bytes 2162696 | tf_op jit(solution)/shard_map/ppermute | solution.py:325
  443.7 37.7 %reduce-scatter.4.cloned.1.call-done = bf16[1,136,4096]{2,1,0:T(8,128)(2,1)} async-done(((bf16[8,136,4096]{2,1,0:T(8,128)(2,1)}), bf16[1,136,4096]{2,1,0:T(8,128)(2,1)}) %reduce-scatter.4.cloned.1.call-update) | async-done | bytes 1114128 | tf_op jit(solution)/shard_map/reduce_scatter | solution.py:348
  487.1 59.5 %all-reduce.6.cloned.1.call-done = bf16[136,4096]{1,0:T(8,128)(2,1)} async-done(((bf16[136,4096]{1,0:T(8,128)(2,1)}), bf16[136,4096]{1,0:T(8,128)(2,1)}) %all-reduce.6.cloned.1.call-update) | async-done | bytes 1114128 | tf_op jit(solution)/shard_map/psum | solution.py:349
  554.8 18.8 %collective-permute-done.10 = bf16[1,64,5632]{2,1,0:T(8,128)(2,1)S(1)} collective-permute-done((bf16[1,64,5632]{2,1,0:T(8,128)(2,1)S(1)}, bf16[1,64,5632]{2,1,0:T(8,128)(2,1)S(1)}, u32[]{:S(2)}, u32[]{:S(2)}) %collective-permute-start.10) | collective-permute-done | bytes 720928 | tf_op jit(solution)/shard_map/ppermute | solution.py:329
  573.7 14.0 %collective-permute-done.7 = bf16[1,64,5632]{2,1,0:T(8,128)(2,1)S(1)} collective-permute-done((bf16[1,64,5632]{2,1,0:T(8,128)(2,1)S(1)}, bf16[1,64,5632]{2,1,0:T(8,128)(2,1)S(1)}, u32[]{:S(2)}, u32[]{:S(2)}) %collective-permute-start.7) | collective-permute-done | bytes 720928 | tf_op jit(solution)/shard_map/ppermute | solution.py:329
  (198 shorter events, 124.6 us)
Async XLA Ops:
  7.2 113.9 %all-gather.5.cloned.1.call-start = ((), (), s32[]{:S(2)}) async-start(), calls=%async_computation.7 | async-start | bytes 16515072 | tf_op jit(solution)/shard_map/all_gather | solution.py:315
  12.5 193.8 %all-gather.7.cloned.1.call-start = ((), (), s32[]{:S(2)}) async-start(), calls=%async_computation.8 | async-start | bytes 12976128 | tf_op jit(solution)/shard_map/all_gather | solution.py:315
  13.8 390.3 %reduce-scatter.8.cloned.1.call-start = ((), (), s32[]{:S(2)}) async-start(), calls=%async_computation.6 | async-start | bytes 6488064 | tf_op jit(solution)/shard_map/reduce_scatter | solution.py:348
  14.0 42.0 %collective-permute-start = (bf16[1,512,1024]{2,1,0:T(8,128)(2,1)S(1)}, bf16[1,512,1024]{2,1,0:T(8,128)(2,1)S(1)}, u32[]{:S(2)}, u32[]{:S(2)}) collective-permute-start(bf16[1,512,1024]{2,1,0:T(8,128)(2,1)S(1)} %copy-done.14), channel_id=1, source_target_pairs={{0,1},{1,0},{2,3},{3,2},{4,5},{5,4},{6,7},{7,6},{8,9},{9,8},{10,11... | collective-permute-start | bytes 3145736 | tf_op jit(solution)/shard_map/ppermute | solution.py:410
  17.0 156.1 %collective-permute-start.1 = (bf16[1,512,1024]{2,1,0:T(8,128)(2,1)}, bf16[1,512,1024]{2,1,0:T(8,128)(2,1)}, u32[]{:S(2)}, u32[]{:S(2)}) collective-permute-start(bf16[1,512,1024]{2,1,0:T(8,128)(2,1)} %param.14), channel_id=1, source_target_pairs={{0,1},{2,3},{4,5},{6,7},{8,9},{10,11},{12,13},{14,15},{16,17},{18,... | collective-permute-start | bytes 3145736 | tf_op jit(solution)/shard_map/ppermute | solution.py:411
  156.8 14.7 %copy-start.1 = (bf16[1,512,1024]{2,1,0:T(8,128)(2,1)}, bf16[1,512,1024]{2,1,0:T(8,128)(2,1)S(1)}, u32[]{:S(2)}) copy-start(bf16[1,512,1024]{2,1,0:T(8,128)(2,1)S(1)} %copy.87.k_ref) | copy-start | bytes 3145732
  180.4 22.6 %copy-start.15 = (bf16[1,512,1024]{2,1,0:T(8,128)(2,1)S(1)}, bf16[1,512,1024]{2,1,0:T(8,128)(2,1)}, u32[]{:S(2)}) copy-start(bf16[1,512,1024]{2,1,0:T(8,128)(2,1)} %param.13) | copy-start | bytes 3145732
  233.7 192.5 %reduce-scatter.6.cloned.1.call-start = ((), (), s32[]{:S(2)}) async-start(), calls=%async_computation.5 | async-start | bytes 12976128 | tf_op jit(solution)/shard_map/reduce_scatter | solution.py:348
  250.1 12.0 %copy-start.18 = (f32[1,512,1024]{2,1,0:T(8,128)S(1)}, f32[1,512,1024]{2,1,0:T(8,128)}, u32[]{:S(2)}) copy-start(f32[1,512,1024]{2,1,0:T(8,128)} %copy-done.17) | copy-start | bytes 6291460
  262.1 13.0 %copy-start.26 = (bf16[1,512,1024]{2,1,0:T(8,128)(2,1)S(1)}, bf16[1,512,1024]{2,1,0:T(8,128)(2,1)}, u32[]{:S(2)}) copy-start(bf16[1,512,1024]{2,1,0:T(8,128)(2,1)} %param.15) | copy-start | bytes 3145732
  277.5 17.3 %copy-start.6 = (f32[1,512,1024]{2,1,0:T(8,128)}, f32[1,512,1024]{2,1,0:T(8,128)S(1)}, u32[]{:S(2)}) copy-start(f32[1,512,1024]{2,1,0:T(8,128)S(1)} %get-tuple-element.64) | copy-start | bytes 6291460
  291.0 190.5 %reduce-scatter.4.cloned.1.call-start = ((), (), s32[]{:S(2)}) async-start(), calls=%async_computation.3 | async-start | bytes 10027008 | tf_op jit(solution)/shard_map/reduce_scatter | solution.py:348
  301.7 32.2 %collective-permute-start.2 = (bf16[1,512,16,64]{1,3,2,0:T(8,128)(2,1)S(1)}, bf16[1,512,16,64]{1,3,2,0:T(8,128)(2,1)}, u32[]{:S(2)}, u32[]{:S(2)}) collective-permute-start(bf16[1,512,16,64]{1,3,2,0:T(8,128)(2,1)S(1)} %bitcast.167), channel_id=1, source_target_pairs={{1,0},{3,2},{5,4},{7,6},{9,8},{11,10},{13,12},{15,14},{17,16},{19,... | collective-permute-start | bytes 3145736 | tf_op jit(solution)/shard_map/ppermute | solution.py:505
  303.1 29.1 %collective-permute-start.3 = (f32[1,16,512]{2,1,0:T(8,128)S(1)}, f32[1,16,512]{2,1,0:T(8,128)S(1)}, u32[]{:S(2)}, u32[]{:S(2)}) collective-permute-start(f32[1,16,512]{2,1,0:T(8,128)S(1)} %copy-done.36), channel_id=1, source_target_pairs={{1,0},{3,2},{5,4},{7,6},{9,8},{11,10},{13,12},{15,14},{17,16},{19,... | collective-permute-start | bytes 98312 | tf_op jit(solution)/shard_map/ppermute | solution.py:505
  306.4 26.9 %collective-permute-start.4 = (f32[1,16,512]{2,1,0:T(8,128)S(1)}, f32[1,16,512]{2,1,0:T(8,128)S(1)}, u32[]{:S(2)}, u32[]{:S(2)}) collective-permute-start(f32[1,16,512]{2,1,0:T(8,128)S(1)} %bitcast.192), channel_id=1, source_target_pairs={{1,0},{3,2},{5,4},{7,6},{9,8},{11,10},{13,12},{15,14},{17,16},{19,... | collective-permute-start | bytes 98312 | tf_op jit(solution)/shard_map/ppermute | solution.py:505
  314.9 17.4 %copy-start.37 = (f32[1,16,512]{2,1,0:T(8,128)S(1)}, f32[1,16,512]{2,1,0:T(8,128)}, u32[]{:S(2)}) copy-start(f32[1,16,512]{2,1,0:T(8,128)} %get-tuple-element.21.lse_ref) | copy-start | bytes 98308
  314.9 18.4 %copy-start.35 = (f32[512,16]{0,1:T(8,128)S(1)}, f32[512,16]{0,1:T(8,128)}, u32[]{:S(2)}) copy-start(f32[512,16]{0,1:T(8,128)} %copy-done.34) | copy-start | bytes 98308
  336.6 16.8 %copy-start.20 = (f32[1,512,1024]{2,1,0:T(8,128)S(1)}, f32[1,512,1024]{2,1,0:T(8,128)}, u32[]{:S(2)}) copy-start(f32[1,512,1024]{2,1,0:T(8,128)} %get-tuple-element.22) | copy-start | bytes 6291460
  404.1 142.5 %all-reduce.6.cloned.1.call-start = ((), (), s32[]{:S(2)}) async-start(), calls=%async_computation.4 | async-start | bytes 2228224 | tf_op jit(solution)/shard_map/psum | solution.py:349
  404.2 19.4 %copy-start.31 = (bf16[1,352,1024]{2,1,0:T(8,128)(2,1)S(1)}, bf16[1,352,1024]{2,1,0:T(8,128)(2,1)}, u32[]{:S(2)}) copy-start(bf16[1,352,1024]{2,1,0:T(8,128)(2,1)} %reduce-scatter.8.cloned.1.call-done) | copy-start | bytes 2162692
  404.2 19.4 %collective-permute-start.11 = (bf16[1,352,1024]{2,1,0:T(8,128)(2,1)}, bf16[1,352,1024]{2,1,0:T(8,128)(2,1)S(1)}, u32[]{:S(2)}, u32[]{:S(2)}) collective-permute-start(bf16[1,352,1024]{2,1,0:T(8,128)(2,1)} %reduce-scatter.8.cloned.1.call-done), channel_id=1, source_target_pairs={{0,8},{24,16},{1,9},{25,17},{2,10},{26,18},{3,11},{27,19},{4,12},{... | collective-permute-start | bytes 2162696 | tf_op jit(solution)/shard_map/ppermute | solution.py:325
  419.1 19.7 %copy-start.8 = (f32[1,512,1024]{2,1,0:T(8,128)S(1)}, f32[1,512,1024]{2,1,0:T(8,128)}, u32[]{:S(2)}) copy-start(f32[1,512,1024]{2,1,0:T(8,128)} %copy-done.6) | copy-start | bytes 6291460
  424.7 16.0 %collective-permute-start.12 = (bf16[1,352,1024]{2,1,0:T(8,128)(2,1)}, bf16[1,352,1024]{2,1,0:T(8,128)(2,1)}, u32[]{:S(2)}, u32[]{:S(2)}) collective-permute-start(bf16[1,352,1024]{2,1,0:T(8,128)(2,1)} %add_convert_fusion.2), channel_id=1, source_target_pairs={{8,16},{16,8},{9,17},{17,9},{10,18},{18,10},{11,19},{19,11},{12,20... | collective-permute-start | bytes 2162696 | tf_op jit(solution)/shard_map/ppermute | solution.py:327
  426.2 12.6 %copy-start.23 = (f32[512,1024]{1,0:T(8,128)S(1)}, f32[512,1024]{1,0:T(8,128)}, u32[]{:S(2)}) copy-start(f32[512,1024]{1,0:T(8,128)} %get-tuple-element.89) | copy-start | bytes 6291460
  428.9 52.6 %collective-permute-start.5 = (bf16[1,64,5632]{2,1,0:T(8,128)(2,1)}, bf16[1,64,5632]{2,1,0:T(8,128)(2,1)}, u32[]{:S(2)}, u32[]{:S(2)}) collective-permute-start(bf16[1,64,5632]{2,1,0:T(8,128)(2,1)} %get-tuple-element.67), channel_id=1, source_target_pairs={{0,8},{24,16},{1,9},{25,17},{2,10},{26,18},{3,11},{27,19},{4,12},{... | collective-permute-start | bytes 2162696 | tf_op jit(solution)/shard_map/ppermute | solution.py:325
  436.4 45.1 %collective-permute-start.8 = (bf16[1,64,5632]{2,1,0:T(8,128)(2,1)}, bf16[1,64,5632]{2,1,0:T(8,128)(2,1)}, u32[]{:S(2)}, u32[]{:S(2)}) collective-permute-start(bf16[1,64,5632]{2,1,0:T(8,128)(2,1)} %get-tuple-element.68), channel_id=1, source_target_pairs={{0,8},{24,16},{1,9},{25,17},{2,10},{26,18},{3,11},{27,19},{4,12},{... | collective-permute-start | bytes 2162696 | tf_op jit(solution)/shard_map/ppermute | solution.py:325
  440.7 40.8 %copy-start.10 = (bf16[1,128,5632]{2,1,0:T(8,128)(2,1)S(1)}, bf16[1,128,5632]{2,1,0:T(8,128)(2,1)}, u32[]{:S(2)}) copy-start(bf16[1,128,5632]{2,1,0:T(8,128)(2,1)} %reduce-scatter.6.cloned.1.call-done) | copy-start | bytes 4325380
  442.4 42.3 %collective-permute-start.13 = (bf16[1,352,1024]{2,1,0:T(8,128)(2,1)S(1)}, bf16[1,352,1024]{2,1,0:T(8,128)(2,1)}, u32[]{:S(2)}, u32[]{:S(2)}) collective-permute-start(bf16[1,352,1024]{2,1,0:T(8,128)(2,1)S(1)} %add_convert_fusion.1), channel_id=1, source_target_pairs={{8,0},{16,24},{9,1},{17,25},{10,2},{18,26},{11,3},{19,27},{12,4},{... | collective-permute-start | bytes 2162696 | tf_op jit(solution)/shard_map/ppermute | solution.py:329
  484.0 66.7 %collective-permute-start.9 = (bf16[1,64,5632]{2,1,0:T(8,128)(2,1)}, bf16[1,64,5632]{2,1,0:T(8,128)(2,1)S(1)}, u32[]{:S(2)}, u32[]{:S(2)}) collective-permute-start(bf16[1,64,5632]{2,1,0:T(8,128)(2,1)} %get-tuple-element.66), channel_id=1, source_target_pairs={{8,16},{16,8},{9,17},{17,9},{10,18},{18,10},{11,19},{19,11},{12,20... | collective-permute-start | bytes 2162696 | tf_op jit(solution)/shard_map/ppermute | solution.py:327
  550.1 3.3 collective-permute-start.6
  552.1 21.6 %collective-permute-start.10 = (bf16[1,64,5632]{2,1,0:T(8,128)(2,1)S(1)}, bf16[1,64,5632]{2,1,0:T(8,128)(2,1)S(1)}, u32[]{:S(2)}, u32[]{:S(2)}) collective-permute-start(bf16[1,64,5632]{2,1,0:T(8,128)(2,1)S(1)} %add_convert_fusion.3), channel_id=1, source_target_pairs={{8,0},{16,24},{9,1},{17,25},{10,2},{18,26},{11,3},{19,27},{12,4},{... | collective-permute-start | bytes 2162696 | tf_op jit(solution)/shard_map/ppermute | solution.py:329
  553.5 34.2 %collective-permute-start.7 = (bf16[1,64,5632]{2,1,0:T(8,128)(2,1)S(1)}, bf16[1,64,5632]{2,1,0:T(8,128)(2,1)S(1)}, u32[]{:S(2)}, u32[]{:S(2)}) collective-permute-start(bf16[1,64,5632]{2,1,0:T(8,128)(2,1)S(1)} %add_convert_fusion.5), channel_id=1, source_target_pairs={{8,0},{16,24},{9,1},{17,25},{10,2},{18,26},{11,3},{19,27},{12,4},{... | collective-permute-start | bytes 2162696 | tf_op jit(solution)/shard_map/ppermute | solution.py:329
  (26 other events, 95.4 us)
Sparse Core Ops, SparseCore 0:
  12.6 108.3 all-gather.4
  123.5 72.0 all-gather.6
  233.9 63.8 reduce-scatter.7
  301.1 88.9 reduce-scatter.5
  404.2 77.2 reduce-scatter.3
  483.7 62.8 all-reduce.5

commit v16 on v14

--- a/solution.py
+++ b/solution.py
@@ -407,7 +407,8 @@
     head_shape = (n_slots, slot_rows, HEADS, HEAD_DIM)
     paired = n_ctx == 2
     if paired:
-        other_tokens = lax.ppermute(tokens, "ctx", [(0, 1), (1, 0)])
+        earlier_tokens = lax.ppermute(tokens, "ctx", [(0, 1)])
+        later_tokens = lax.ppermute(tokens, "ctx", [(1, 0)])
         other_first = lax.ppermute(initial_layer_values, "ctx", [(0, 1)])
         other_pos = (1 - ctx_index) * slot_rows + jnp.arange(slot_rows)
     inputs = tokens.astype(jnp.float32)
@@ -434,7 +435,8 @@
 
     normed_low, inv_attn, queries, keys, values = project(tokens, initial_layer_values, q_pos)
     if paired:
-        _, _, other_q, other_k, other_v = project(other_tokens, other_first, other_pos)
+        _, _, _, other_k, other_v = project(earlier_tokens, other_first, other_pos)
+        _, _, other_q, _, _ = project(later_tokens, other_first, other_pos)
         slot_k = jnp.concatenate([other_k, keys], axis=1)
         slot_v = jnp.concatenate([other_v, values], axis=1)
         k_pos = jnp.concatenate([other_pos, q_pos])

time: 565 us -> 574 us (1.016)
  matrix products: 106 us -> 117 us
  waiting for transfers between devices: 219 us -> 208 us
    dot_general x2 -> x3, matrix products: 14.1 us -> 24.5 us  [project(): jnp.einsum('srd,de->sre', chunk_low, full_qkv, preferred_element_type=jnp...]
    all_gather x3, waiting for transfers between devices: 51.5 us -> 43.6 us  [gather_blocks(): gathered = lax.all_gather(packed, GROUP, axis=0, tiled=False)]
    ppermute x1 -> x2, waiting for transfers between devices: 28.6 us -> 27.3 us  [the longest x1 25.3 us: shards(): later_tokens = lax.ppermute(tokens, 'ctx', [(1, 0)])]
  transfers between devices with their start and end apart: 21 -> 22, of which waited for: 10 -> 10; matrix products, arithmetic and copies ran while one was open for 40% -> 42% of each run, Pallas kernels for 10% -> 10%
where the time goes in v16:
time: 574 us; the launch traced here: 569 us
  waiting for transfers between devices  208 us (36%)
  matrix products  117 us (20%)
  other arithmetic  76 us (13%)
  local copies, waits for them, and re-layouts  62 us (11%)
  Pallas kernels  55.7 us (10%)
  starting transfers between devices  34.9 us (6%)
  between operations  15.8 us (3%)
    psum x1, waiting for transfers between devices, scatter_blocks(): lax.psum(summed, 'rep')  59.6 us
    all_gather x3, waiting for transfers between devices, gather_blocks(): gathered = lax.all_gather(packed, GROUP, axis=0, tiled=False)  43.6 us
    reduce_scatter x3, waiting for transfers between devices, scatter_blocks(): summed = lax.psum_scatter(packed, GROUP, scatter_dimension=0, tiled=True)  36 us
    ppermute x3, waiting for transfers between devices, rep_chain(): sent_out = lax.ppermute(total, 'rep', [(1, 0), (2, 3)])  32.8 us
    pallas_call x2, Pallas kernels, block_backward(): pl.pallas_call(kernel, grid=(n_slots, n_heads // 2), in_specs=[q_spec, k_...  32.8 us
    ppermute x1, waiting for transfers between devices, shards(): later_tokens = lax.ppermute(tokens, 'ctx', [(1, 0)])  25.3 us
    dot_general x3, matrix products, project(): jnp.einsum('srd,de->sre', chunk_low, full_qkv, preferred_element_type=jnp...  24.5 us
    pallas_call x1, Pallas kernels, block_forward(): pl.pallas_call(kernel, grid=(n_slots, n_heads // 2), in_specs=[q_spec, k_...  22.9 us
  transfers between devices with their start and end apart: 22, of which 10 were waited for; matrix products, arithmetic and copies ran while one was open for 42% of the time, Pallas kernels for 10%

profile of v16, /device:TPU:0, one launch (start us, length us, event | category | flops | bytes accessed | tf_op | source)
XLA Modules:
  0.0 569.5 jit_solution(4330227716212962665)
XLA Ops:
  13.2 6.0 %collective-permute-start = (bf16[1,512,1024]{2,1,0:T(8,128)(2,1)S(1)}, bf16[1,512,1024]{2,1,0:T(8,128)(2,1)}, u32[]{:S(2)}, u32[]{:S(2)}) collective-permute-start(bf16[1,512,1024]{2,1,0:T(8,128)(2,1)S(1)} %copy-done.13), channel_id=1, source_target_pairs={{0,1},{2,3},{4,5},{6,7},{8,9},{10,11},{12,13},{14,15},{16,17},{18,... | collective-permute-start | bytes 3145736 | tf_op jit(solution)/shard_map/ppermute | solution.py:410
  26.0 25.3 %collective-permute-done.2 = bf16[1,512,1024]{2,1,0:T(8,128)(2,1)S(1)} collective-permute-done((bf16[1,512,1024]{2,1,0:T(8,128)(2,1)S(1)}, bf16[1,512,1024]{2,1,0:T(8,128)(2,1)S(1)}, u32[]{:S(2)}, u32[]{:S(2)}) %collective-permute-start.2) | collective-permute-done | bytes 1048608 | tf_op jit(solution)/shard_map/ppermute | solution.py:411
  55.5 43.5 %all-gather.7.cloned.1.call-done = bf16[1088,4096]{1,0:T(8,128)(2,1)} async-done(((bf16[136,4096]{1,0:T(8,128)(2,1)}), bf16[1088,4096]{1,0:T(8,128)(2,1)}) %all-gather.7.cloned.1.call-update) | async-done | bytes 8912912 | tf_op jit(solution)/shard_map/all_gather | solution.py:315
  99.0 7.8 %slice.162 = bf16[8,128,4096]{2,1,0:T(8,128)(2,1)} slice(bf16[8,136,4096]{2,1,0:T(8,128)(2,1)} %bitcast.184), slice={[0:8], [0:128], [0:4096]} | slice | bytes 16777216 | tf_op jit(solution)/shard_map/slice | solution.py:318
  107.6 5.9 %convolution_bitcast_fusion.3 = f32[1,512,3072]{2,1,0:T(8,128)S(1)} fusion(bf16[1024,4096]{1,0:T(8,128)(2,1)} %bitcast.178, bf16[1,512,1024]{2,1,0:T(8,128)(2,1)S(1)} %copy-done.13, f32[1024]{0:T(1024)S(1)} %bitcast.202, f32[512]{0:T(512)S(1)} %add_rsqrt_fusion.3), kind=kOutput, calls=%fused_computation.24 | convolution fusion | flops 3223322624 | bytes 13637632 | tf_op jit(solution)/shard_map/srd,de->sre/dot_general | solution.py:421
  122.5 8.2 %convolution_bitcast_fusion.1 = f32[1,512,3072]{2,1,0:T(8,128)} fusion(bf16[1024,4096]{1,0:T(8,128)(2,1)} %bitcast.179, bf16[1,512,1024]{2,1,0:T(8,128)(2,1)S(1)} %collective-permute-done.2, f32[512]{0:T(512)S(1)} %add_rsqrt_fusion, f32[1024]{0:T(1024)S(1)} %bitcast.203), kind=kOutput, calls=%fused_computation.22 | convolution fusion | flops 3223322624 | bytes 13637632 | tf_op jit(solution)/shard_map/srd,de->sre/dot_general | solution.py:421
  130.8 10.4 %convolution_bitcast_fusion.2 = f32[1,512,3072]{2,1,0:T(8,128)} fusion(bf16[1024,4096]{1,0:T(8,128)(2,1)} %bitcast.180, bf16[1,512,1024]{2,1,0:T(8,128)(2,1)} %collective-permute-done, f32[512]{0:T(512)S(1)} %add_rsqrt_fusion.2, f32[1024]{0:T(1024)S(1)} %bitcast.204), kind=kOutput, calls=%fused_computation.23 | convolution fusion | flops 3223322624 | bytes 13637632 | tf_op jit(solution)/shard_map/srd,de->sre/dot_general | solution.py:421
  161.0 4.7 broadcast_select_fusion.1
  168.2 22.9 %shard_map.220 = (bf16[1,512,1024]{2,1,0:T(8,128)(2,1)}, f32[1,16,512]{2,1,0:T(8,128)}) custom-call(bf16[1,512,1024]{2,1,0:T(8,128)(2,1)} %copy.91.q_ref, bf16[1,1024,1024]{2,1,0:T(8,128)(2,1)} %pad_maximum_fusion.4.k_ref, bf16[1,1024,1024]{2,1,0:T(8,128)(2,1)} %pad_maximum_fusion.5.v_ref, s32[1,512]{1,0:T(1,128)} %iota_add_fusion.1.qpos_ref, ...), custom_call_target="tpu_custom_call" | custom-call | flops 2147483648 | bytes 6291456 | tf_op jit(solution)/shard_map/pallas_call | solution.py:247
  195.7 9.1 %convolution_bitcast_fusion = f32[1,512,5632]{2,1,0:T(8,128)S(1)} fusion(bf16[1024,5632]{1,0:T(8,128)(2,1)} %all-gather.9.cloned.1.call-done, f32[1,512,1024]{2,1,0:T(8,128)S(1)} %get-tuple-element.85, f32[1024]{0:T(1024)S(1)} %bitcast.199, f32[512]{0:T(512)S(1)} %add_rsqrt_fusion.1), kind=kOutput, calls=%fused_computation.3 | convolution fusion | flops 5907152896 | bytes 25171968 | tf_op jit(solution)/shard_map/srd,df->srf/dot_general | solution.py:459
  204.7 4.2 copy-done
  213.7 7.9 %convolution_convert_fusion.2 = bf16[8,352,1024]{2,1,0:T(8,128)(2,1)} fusion(bf16[8,352,512]{2,1,0:T(8,128)(2,1)} %bitcast.193, bf16[1,512,1024]{2,1,0:T(8,128)(2,1)} %param.15, pred[512]{0:T(512)(128)(4,1)S(1)} %fusion.100), kind=kOutput, calls=%fused_computation.30 | convolution fusion | flops 2957246464 | bytes 9699840 | tf_op jit(solution)/shard_map/srf,srd->fd/dot_general | solution.py:475
  222.8 11.5 %fusion.8 = (bf16[1,512,2816]{2,1,0:T(8,128)(2,1)}, bf16[1,512,2816]{2,1,0:T(8,128)(2,1)}) fusion(f32[1,512,5632]{2,1,0:T(8,128)} %copy-done, bf16[2816,1024]{1,0:T(8,128)(2,1)} %all-gather.11.cloned.1.call-done, bf16[1,512,1024]{2,1,0:T(8,128)(2,1)S(1)} %copy-done.24, pred[512]{0:T(512)(128)(4,1)S(1)} %fusion.100), kind=kOutput, calls=%fused_computation.16 | convolution fusion | flops 2973106176 | bytes 24117760 | tf_op jit(solution)/shard_map/srd,fd->srf/dot_general | solution.py:481
  234.3 13.6 %fusion.41 = (bf16[1024]{0:T(1024)(128)(2,1)S(1)}, f32[512]{0:T(512)S(1)}, f32[512,1024]{1,0:T(8,128)S(1)}) fusion(f32[1,512,1024]{2,1,0:T(8,128)S(1)} %copy-done.17, f32[512]{0:T(512)S(1)} %add_rsqrt_fusion.1, f32[1024]{0:T(1024)S(1)} %bitcast.200, bf16[1024,5632]{1,0:T(8,128)(2,1)} %all-gather.9.cloned.1.call-done, ...), kind=kOutput, calls=%fused_computation.70 | convolution fusion | flops 5920258560 | bytes 21506048 | tf_op jit(solution)/shard_map/srf,df->srd/dot_general | solution.py:488
  250.5 11.5 %convolution_convert_fusion = bf16[8,128,5632]{2,1,0:T(8,128)(2,1)} fusion(bf16[8,128,512]{2,1,0:T(8,128)(2,1)S(1)} %bitcast.196, bf16[1,512,2816]{2,1,0:T(8,128)(2,1)} %get-tuple-element.40, bf16[1,512,2816]{2,1,0:T(8,128)(2,1)} %get-tuple-element.39), kind=kOutput, calls=%fused_computation.2 | convolution fusion | flops 5922881536 | bytes 18350080 | tf_op jit(solution)/shard_map/srd,srf->df/dot_general | solution.py:485
  273.5 4.9 fusion.56
  286.0 16.3 %shard_map.221 = (f32[1,512,1024]{2,1,0:T(8,128)}, f32[1,512,1024]{2,1,0:T(8,128)}, f32[1,512,1024]{2,1,0:T(8,128)}) custom-call(bf16[1,512,1024]{2,1,0:T(8,128)(2,1)} %copy.91.q_ref, bf16[1,512,1024]{2,1,0:T(8,128)(2,1)} %copy-done.1, bf16[1,512,1024]{2,1,0:T(8,128)(2,1)} %copy-done.12, bf16[1,512,1024]{2,1,0:T(8,128)(2,1)} %bitcast.195, ...), custom_call_target="tpu_custom_call" | custom-call | flops 2684354560 | bytes 10485760 | tf_op jit(solution)/shard_map/pallas_call | solution.py:285
  302.3 5.0 collective-permute-done.5
  310.7 16.5 %shard_map.222 = (f32[1,512,1024]{2,1,0:T(8,128)}, f32[1,512,1024]{2,1,0:T(8,128)}, f32[1,512,1024]{2,1,0:T(8,128)}) custom-call(bf16[1,512,1024]{2,1,0:T(8,128)(2,1)} %broadcast_select_fusion.3.q_ref, bf16[1,512,1024]{2,1,0:T(8,128)(2,1)} %broadcast_select_fusion.2.k_ref, bf16[1,512,1024]{2,1,0:T(8,128)(2,1)} %get-tuple-element.34.v_ref, ...), custom_call_target="tpu_custom_call" | custom-call | flops 2684354560 | bytes 10485760 | tf_op jit(solution)/shard_map/pallas_call | solution.py:285
  330.9 4.5 select_add_fusion
  343.0 4.5 fusion.110
  347.6 7.8 %fusion.35 = (bf16[1024]{0:T(1024)(128)(2,1)S(1)}, f32[512]{0:T(512)S(1)}, f32[512,1024]{1,0:T(8,128)}) fusion(bf16[1,512,1024]{2,1,0:T(8,128)(2,1)S(1)} %copy-done.15, f32[512]{0:T(512)S(1)} %add_rsqrt_fusion.3, f32[1024]{0:T(1024)S(1)} %bitcast.205, bf16[1024,4096]{1,0:T(8,128)(2,1)} %bitcast.183, bf16[1,512,1024]{2,1,0:T(8,128)(2,1)S(1)} %get-tuple-element.32, ...), kind=kOutput, calls=%fused_computation.59 | convolution fusion | flops 3234331136 | bytes 12593152 | tf_op jit(solution)/shard_map/sre,de->srd/dot_general | solution.py:549
  355.5 7.8 %convolution_convert_fusion.1 = bf16[1024,3072]{1,0:T(8,128)(2,1)} fusion(bf16[1,512,1024]{2,1,0:T(8,128)(2,1)S(1)} %get-tuple-element.32, bf16[1,512,1024]{2,1,0:T(8,128)(2,1)} %copy-done.28, bf16[1,512,1024]{2,1,0:T(8,128)(2,1)S(1)} %copy-done.29, bf16[1,512,1024]{2,1,0:T(8,128)(2,1)S(1)} %copy-done.15, f32[1024]{0:T(1024)S(1)} %bitcast.206, ...), kind=kOutput, calls=%fused_computation.21 | convolution fusion | flops 3235905536 | bytes 10491904 | tf_op jit(solution)/shard_map/srd,sre->de/dot_general | solution.py:548
  363.3 7.0 %pad_maximum_fusion = bf16[1024,4096]{1,0:T(8,128)(2,1)} fusion(bf16[1024,1024]{1,0:T(8,128)(2,1)S(1)} %copy-done.23, bf16[1024,3072]{1,0:T(8,128)(2,1)} %convolution_convert_fusion.1), kind=kLoop, calls=%fused_computation.5 | loop fusion | flops 16777216 | bytes 16777216 | tf_op jit(solution)/shard_map/concatenate | solution.py:554
  370.3 8.4 %fusion.1 = bf16[8,136,4096]{2,1,0:T(8,128)(2,1)} fusion(bf16[8,1,4096]{2,1,0:T(2,128)(2,1)S(1)} %copy.112, bf16[8,128,4096]{2,1,0:T(8,128)(2,1)} %bitcast.168), kind=kLoop, calls=%fused_computation.4 | loop fusion | flops 26738688 | bytes 17367040 | tf_op jit(solution)/shard_map/concatenate | solution.py:347
  378.8 4.4 collective-permute-start.12
  383.3 12.5 %fusion.46 = bf16[1,512,1024]{2,1,0:T(8,128)(2,1)} fusion(f32[1,512,1024]{2,1,0:T(8,128)S(1)} %copy-done.18, bf16[2816,1024]{1,0:T(8,128)(2,1)} %all-gather.11.cloned.1.call-done, f32[1,512,5632]{2,1,0:T(8,128)} %copy-done, pred[512]{0:T(512)(128)(4,1)S(1)} %fusion.100), kind=kOutput, calls=%fused_computation.78 | convolution fusion | flops 2963013632 | bytes 20447744 | tf_op jit(solution)/shard_map/srf,fd->srd/dot_general | solution.py:464
  403.4 7.0 %collective-permute-start.6 = (bf16[1,64,5632]{2,1,0:T(8,128)(2,1)}, bf16[1,64,5632]{2,1,0:T(8,128)(2,1)}, u32[]{:S(2)}, u32[]{:S(2)}) collective-permute-start(bf16[1,64,5632]{2,1,0:T(8,128)(2,1)} %get-tuple-element.65), channel_id=1, source_target_pairs={{0,8},{24,16},{1,9},{25,17},{2,10},{26,18},{3,11},{27,19},{4,12},{... | collective-permute-start | bytes 2162696 | tf_op jit(solution)/shard_map/ppermute | solution.py:325
  417.9 36.0 %reduce-scatter.4.cloned.1.call-done = bf16[1,136,4096]{2,1,0:T(8,128)(2,1)} async-done(((bf16[8,136,4096]{2,1,0:T(8,128)(2,1)}), bf16[1,136,4096]{2,1,0:T(8,128)(2,1)}) %reduce-scatter.4.cloned.1.call-update) | async-done | bytes 1114128 | tf_op jit(solution)/shard_map/reduce_scatter | solution.py:348
  459.5 59.6 %all-reduce.6.cloned.1.call-done = bf16[136,4096]{1,0:T(8,128)(2,1)} async-done(((bf16[136,4096]{1,0:T(8,128)(2,1)}), bf16[136,4096]{1,0:T(8,128)(2,1)}) %all-reduce.6.cloned.1.call-update) | async-done | bytes 1114128 | tf_op jit(solution)/shard_map/psum | solution.py:349
  527.4 18.8 %collective-permute-done.11 = bf16[1,64,5632]{2,1,0:T(8,128)(2,1)S(1)} collective-permute-done((bf16[1,64,5632]{2,1,0:T(8,128)(2,1)S(1)}, bf16[1,64,5632]{2,1,0:T(8,128)(2,1)S(1)}, u32[]{:S(2)}, u32[]{:S(2)}) %collective-permute-start.11) | collective-permute-done | bytes 720928 | tf_op jit(solution)/shard_map/ppermute | solution.py:329
  546.2 14.0 %collective-permute-done.8 = bf16[1,64,5632]{2,1,0:T(8,128)(2,1)S(1)} collective-permute-done((bf16[1,64,5632]{2,1,0:T(8,128)(2,1)S(1)}, bf16[1,64,5632]{2,1,0:T(8,128)(2,1)S(1)}, u32[]{:S(2)}, u32[]{:S(2)}) %collective-permute-start.8) | collective-permute-done | bytes 720928 | tf_op jit(solution)/shard_map/ppermute | solution.py:329
  (202 shorter events, 126.0 us)
Async XLA Ops:
  7.2 91.8 %all-gather.7.cloned.1.call-start = ((), (), s32[]{:S(2)}) async-start(), calls=%async_computation.7 | async-start | bytes 10027008 | tf_op jit(solution)/shard_map/all_gather | solution.py:315
  10.4 184.0 %all-gather.9.cloned.1.call-start = ((), (), s32[]{:S(2)}) async-start(), calls=%async_computation.8 | async-start | bytes 12976128 | tf_op jit(solution)/shard_map/all_gather | solution.py:315
  11.7 210.0 %all-gather.11.cloned.1.call-start = ((), (), s32[]{:S(2)}) async-start(), calls=%async_computation.9 | async-start | bytes 6488064 | tf_op jit(solution)/shard_map/all_gather | solution.py:315
  11.9 39.4 %collective-permute-start.2 = (bf16[1,512,1024]{2,1,0:T(8,128)(2,1)S(1)}, bf16[1,512,1024]{2,1,0:T(8,128)(2,1)S(1)}, u32[]{:S(2)}, u32[]{:S(2)}) collective-permute-start(bf16[1,512,1024]{2,1,0:T(8,128)(2,1)S(1)} %copy-done.13), channel_id=1, source_target_pairs={{1,0},{3,2},{5,4},{7,6},{9,8},{11,10},{13,12},{15,14},{17,16},{19,... | collective-permute-start | bytes 3145736 | tf_op jit(solution)/shard_map/ppermute | solution.py:411
  13.2 40.4 %collective-permute-start = (bf16[1,512,1024]{2,1,0:T(8,128)(2,1)S(1)}, bf16[1,512,1024]{2,1,0:T(8,128)(2,1)}, u32[]{:S(2)}, u32[]{:S(2)}) collective-permute-start(bf16[1,512,1024]{2,1,0:T(8,128)(2,1)S(1)} %copy-done.13), channel_id=1, source_target_pairs={{0,1},{2,3},{4,5},{6,7},{8,9},{10,11},{12,13},{14,15},{16,17},{18,... | collective-permute-start | bytes 3145736 | tf_op jit(solution)/shard_map/ppermute | solution.py:410
  19.1 141.9 %collective-permute-start.1 = (bf16[1,512,1024]{2,1,0:T(8,128)(2,1)}, bf16[1,512,1024]{2,1,0:T(8,128)(2,1)}, u32[]{:S(2)}, u32[]{:S(2)}) collective-permute-start(bf16[1,512,1024]{2,1,0:T(8,128)(2,1)} %param.14), channel_id=1, source_target_pairs={{0,1},{2,3},{4,5},{6,7},{8,9},{10,11},{12,13},{14,15},{16,17},{18,... | collective-permute-start | bytes 3145736 | tf_op jit(solution)/shard_map/ppermute | solution.py:412
  21.5 357.3 %reduce-scatter.8.cloned.1.call-start = ((), (), s32[]{:S(2)}) async-start(), calls=%async_computation.6 | async-start | bytes 6488064 | tf_op jit(solution)/shard_map/reduce_scatter | solution.py:348
  143.9 15.4 %copy-start.1 = (bf16[1,512,1024]{2,1,0:T(8,128)(2,1)}, bf16[1,512,1024]{2,1,0:T(8,128)(2,1)S(1)}, u32[]{:S(2)}) copy-start(bf16[1,512,1024]{2,1,0:T(8,128)(2,1)S(1)} %copy.87.k_ref) | copy-start | bytes 3145732
  168.2 22.9 %copy-start.14 = (bf16[1,512,1024]{2,1,0:T(8,128)(2,1)S(1)}, bf16[1,512,1024]{2,1,0:T(8,128)(2,1)}, u32[]{:S(2)}) copy-start(bf16[1,512,1024]{2,1,0:T(8,128)(2,1)} %param.13) | copy-start | bytes 3145732
  221.6 12.7 %copy-start.17 = (f32[1,512,1024]{2,1,0:T(8,128)S(1)}, f32[1,512,1024]{2,1,0:T(8,128)}, u32[]{:S(2)}) copy-start(f32[1,512,1024]{2,1,0:T(8,128)} %copy-done.16) | copy-start | bytes 6291460
  221.6 179.2 %reduce-scatter.6.cloned.1.call-start = ((), (), s32[]{:S(2)}) async-start(), calls=%async_computation.5 | async-start | bytes 12976128 | tf_op jit(solution)/shard_map/reduce_scatter | solution.py:348
  234.3 13.6 %copy-start.25 = (bf16[1,512,1024]{2,1,0:T(8,128)(2,1)S(1)}, bf16[1,512,1024]{2,1,0:T(8,128)(2,1)}, u32[]{:S(2)}) copy-start(bf16[1,512,1024]{2,1,0:T(8,128)(2,1)} %param.15) | copy-start | bytes 3145732
  262.1 191.8 %reduce-scatter.4.cloned.1.call-start = ((), (), s32[]{:S(2)}) async-start(), calls=%async_computation.3 | async-start | bytes 10027008 | tf_op jit(solution)/shard_map/reduce_scatter | solution.py:348
  266.9 5.9 %collective-permute-start.4 = (f32[1,16,512]{2,1,0:T(8,128)S(1)}, f32[1,16,512]{2,1,0:T(8,128)S(1)}, u32[]{:S(2)}, u32[]{:S(2)}) collective-permute-start(f32[1,16,512]{2,1,0:T(8,128)S(1)} %copy-done.36), channel_id=1, source_target_pairs={{1,0},{3,2},{5,4},{7,6},{9,8},{11,10},{13,12},{15,14},{17,16},{19,... | collective-permute-start | bytes 98312 | tf_op jit(solution)/shard_map/ppermute | solution.py:507
  279.9 28.0 %collective-permute-start.3 = (bf16[1,512,16,64]{1,3,2,0:T(8,128)(2,1)S(1)}, bf16[1,512,16,64]{1,3,2,0:T(8,128)(2,1)}, u32[]{:S(2)}, u32[]{:S(2)}) collective-permute-start(bf16[1,512,16,64]{1,3,2,0:T(8,128)(2,1)S(1)} %bitcast.169), channel_id=1, source_target_pairs={{1,0},{3,2},{5,4},{7,6},{9,8},{11,10},{13,12},{15,14},{17,16},{19,... | collective-permute-start | bytes 3145736 | tf_op jit(solution)/shard_map/ppermute | solution.py:507
  281.9 25.4 %collective-permute-start.5 = (f32[1,16,512]{2,1,0:T(8,128)S(1)}, f32[1,16,512]{2,1,0:T(8,128)S(1)}, u32[]{:S(2)}, u32[]{:S(2)}) collective-permute-start(f32[1,16,512]{2,1,0:T(8,128)S(1)} %bitcast.197), channel_id=1, source_target_pairs={{1,0},{3,2},{5,4},{7,6},{9,8},{11,10},{13,12},{15,14},{17,16},{19,... | collective-permute-start | bytes 98312 | tf_op jit(solution)/shard_map/ppermute | solution.py:507
  286.0 21.3 %copy-start.35 = (f32[512,16]{0,1:T(8,128)S(1)}, f32[512,16]{0,1:T(8,128)}, u32[]{:S(2)}) copy-start(f32[512,16]{0,1:T(8,128)} %copy-done.34) | copy-start | bytes 98308
  310.7 16.5 %copy-start.19 = (f32[1,512,1024]{2,1,0:T(8,128)S(1)}, f32[1,512,1024]{2,1,0:T(8,128)}, u32[]{:S(2)}) copy-start(f32[1,512,1024]{2,1,0:T(8,128)} %get-tuple-element.22) | copy-start | bytes 6291460
  378.7 140.4 %all-reduce.6.cloned.1.call-start = ((), (), s32[]{:S(2)}) async-start(), calls=%async_computation.4 | async-start | bytes 2228224 | tf_op jit(solution)/shard_map/psum | solution.py:349
  378.8 19.2 %copy-start.30 = (bf16[1,352,1024]{2,1,0:T(8,128)(2,1)S(1)}, bf16[1,352,1024]{2,1,0:T(8,128)(2,1)}, u32[]{:S(2)}) copy-start(bf16[1,352,1024]{2,1,0:T(8,128)(2,1)} %reduce-scatter.8.cloned.1.call-done) | copy-start | bytes 2162692
  378.8 19.2 %collective-permute-start.12 = (bf16[1,352,1024]{2,1,0:T(8,128)(2,1)}, bf16[1,352,1024]{2,1,0:T(8,128)(2,1)S(1)}, u32[]{:S(2)}, u32[]{:S(2)}) collective-permute-start(bf16[1,352,1024]{2,1,0:T(8,128)(2,1)} %reduce-scatter.8.cloned.1.call-done), channel_id=1, source_target_pairs={{0,8},{24,16},{1,9},{25,17},{2,10},{26,18},{3,11},{27,19},{4,12},{... | collective-permute-start | bytes 2162696 | tf_op jit(solution)/shard_map/ppermute | solution.py:325
  395.8 17.0 %copy-start.8 = (f32[1,512,1024]{2,1,0:T(8,128)S(1)}, f32[1,512,1024]{2,1,0:T(8,128)}, u32[]{:S(2)}) copy-start(f32[1,512,1024]{2,1,0:T(8,128)} %get-tuple-element.62) | copy-start | bytes 6291460
  399.2 15.5 %collective-permute-start.13 = (bf16[1,352,1024]{2,1,0:T(8,128)(2,1)}, bf16[1,352,1024]{2,1,0:T(8,128)(2,1)}, u32[]{:S(2)}, u32[]{:S(2)}) collective-permute-start(bf16[1,352,1024]{2,1,0:T(8,128)(2,1)} %add_convert_fusion.2), channel_id=1, source_target_pairs={{8,16},{16,8},{9,17},{17,9},{10,18},{18,10},{11,19},{19,11},{12,20... | collective-permute-start | bytes 2162696 | tf_op jit(solution)/shard_map/ppermute | solution.py:327
  400.7 12.0 %copy-start.22 = (f32[512,1024]{1,0:T(8,128)S(1)}, f32[512,1024]{1,0:T(8,128)}, u32[]{:S(2)}) copy-start(f32[512,1024]{1,0:T(8,128)} %get-tuple-element.87) | copy-start | bytes 6291460
  403.4 50.5 %collective-permute-start.6 = (bf16[1,64,5632]{2,1,0:T(8,128)(2,1)}, bf16[1,64,5632]{2,1,0:T(8,128)(2,1)}, u32[]{:S(2)}, u32[]{:S(2)}) collective-permute-start(bf16[1,64,5632]{2,1,0:T(8,128)(2,1)} %get-tuple-element.65), channel_id=1, source_target_pairs={{0,8},{24,16},{1,9},{25,17},{2,10},{26,18},{3,11},{27,19},{4,12},{... | collective-permute-start | bytes 2162696 | tf_op jit(solution)/shard_map/ppermute | solution.py:325
  410.4 43.5 %collective-permute-start.9 = (bf16[1,64,5632]{2,1,0:T(8,128)(2,1)}, bf16[1,64,5632]{2,1,0:T(8,128)(2,1)}, u32[]{:S(2)}, u32[]{:S(2)}) collective-permute-start(bf16[1,64,5632]{2,1,0:T(8,128)(2,1)} %get-tuple-element.66), channel_id=1, source_target_pairs={{0,8},{24,16},{1,9},{25,17},{2,10},{26,18},{3,11},{27,19},{4,12},{... | collective-permute-start | bytes 2162696 | tf_op jit(solution)/shard_map/ppermute | solution.py:325
  414.7 39.2 %copy-start.10 = (bf16[1,128,5632]{2,1,0:T(8,128)(2,1)S(1)}, bf16[1,128,5632]{2,1,0:T(8,128)(2,1)}, u32[]{:S(2)}) copy-start(bf16[1,128,5632]{2,1,0:T(8,128)(2,1)} %reduce-scatter.6.cloned.1.call-done) | copy-start | bytes 4325380
  416.6 40.5 %collective-permute-start.14 = (bf16[1,352,1024]{2,1,0:T(8,128)(2,1)S(1)}, bf16[1,352,1024]{2,1,0:T(8,128)(2,1)}, u32[]{:S(2)}, u32[]{:S(2)}) collective-permute-start(bf16[1,352,1024]{2,1,0:T(8,128)(2,1)S(1)} %add_convert_fusion.1), channel_id=1, source_target_pairs={{8,0},{16,24},{9,1},{17,25},{10,2},{18,26},{11,3},{19,27},{12,4},{... | collective-permute-start | bytes 2162696 | tf_op jit(solution)/shard_map/ppermute | solution.py:329
  456.4 66.9 %collective-permute-start.10 = (bf16[1,64,5632]{2,1,0:T(8,128)(2,1)}, bf16[1,64,5632]{2,1,0:T(8,128)(2,1)S(1)}, u32[]{:S(2)}, u32[]{:S(2)}) collective-permute-start(bf16[1,64,5632]{2,1,0:T(8,128)(2,1)} %get-tuple-element.64), channel_id=1, source_target_pairs={{8,16},{16,8},{9,17},{17,9},{10,18},{18,10},{11,19},{19,11},{12,20... | collective-permute-start | bytes 2162696 | tf_op jit(solution)/shard_map/ppermute | solution.py:327
  522.6 3.3 collective-permute-start.7
  524.6 21.6 %collective-permute-start.11 = (bf16[1,64,5632]{2,1,0:T(8,128)(2,1)S(1)}, bf16[1,64,5632]{2,1,0:T(8,128)(2,1)S(1)}, u32[]{:S(2)}, u32[]{:S(2)}) collective-permute-start(bf16[1,64,5632]{2,1,0:T(8,128)(2,1)S(1)} %add_convert_fusion.3), channel_id=1, source_target_pairs={{8,0},{16,24},{9,1},{17,25},{10,2},{18,26},{11,3},{19,27},{12,4},{... | collective-permute-start | bytes 2162696 | tf_op jit(solution)/shard_map/ppermute | solution.py:329
  526.1 34.2 %collective-permute-start.8 = (bf16[1,64,5632]{2,1,0:T(8,128)(2,1)S(1)}, bf16[1,64,5632]{2,1,0:T(8,128)(2,1)S(1)}, u32[]{:S(2)}, u32[]{:S(2)}) collective-permute-start(bf16[1,64,5632]{2,1,0:T(8,128)(2,1)S(1)} %add_convert_fusion.5), channel_id=1, source_target_pairs={{8,0},{16,24},{9,1},{17,25},{10,2},{18,26},{11,3},{19,27},{12,4},{... | collective-permute-start | bytes 2162696 | tf_op jit(solution)/shard_map/ppermute | solution.py:329
  (27 other events, 95.6 us)
Sparse Core Ops, SparseCore 0:
  10.5 88.4 all-gather.6
  101.5 72.4 all-gather.8
  175.8 43.1 all-gather.10
  222.4 63.0 reduce-scatter.7
  288.8 87.1 reduce-scatter.5
  379.4 74.3 reduce-scatter.3
  456.2 62.8 all-reduce.5
